TPU v7x, 128 devices: a whole 4x4x4 slice. The times are simulated.
128 devices in a mesh: kvh: 4 (over z), blk: 32 (over y, x, core).
Axes of the slice: x: 4, y: 4, z: 4, core: 2. Of those that a mesh axis runs over, the one named last changes fastest.
Arguments:
- queries: bfloat16 [4096, 4096], P('blk', 'kvh')
- suffix_key_rows: bfloat16 [4096, 1024], P('blk', 'kvh')
- suffix_value_rows: bfloat16 [4096, 1024], P('blk', 'kvh'), may hold values from -6 to 6
- prefix_block_keys: bfloat16 [512, 128, 1024], P('blk', None, 'kvh')
- prefix_block_values: bfloat16 [512, 128, 1024], P('blk', None, 'kvh'), may hold values from -6 to 6
- block_group: int32 [512], P('blk'), may hold values from 0 to 15, as said below
- suffix_len: int32 [64], replicated, may hold values from 32 to 96, as said below
- request_group: int32 [64], replicated, may hold values from 0 to 15, as said below
- w_out: bfloat16 [4096, 4096], P('kvh'), may hold values from -1.5 to 1.5
Outputs:
- output: bfloat16 [4096, 4096], P('blk', 'kvh')
Inputs may be any that keep to these rules, and one draw needn't show every extreme that they name: `block_group`: every group owns exactly 32 blocks; no index of blk holds more than 1 block of one group, and some holds exactly 1. `request_group`: every group has exactly 4 requests. `suffix_len`: the lengths sum to 4096; both ends of the range are reached; no request begins at a multiple of 128 other than 0.
All inputs are finite; a program needn't handle non-finite values.
Results may differ from a plain program's by a relative error of at most 0.005.
Values may be sent and summed in bfloat16 or wider, within the bound.
No kernel may reach another device: no remote copies, remote signals or barrier semaphores. Data moves between devices by JAX's collectives and lax.ppermute only.
A program may use at most 256 MiB of HBM per device.

v0:
```python
import math

import jax
import jax.numpy as jnp
from jax import lax
from jax.sharding import PartitionSpec as P

HEAD_SIZE = 128


def from_behind(block, axis, distance):
    devices = range(lax.axis_size(axis))
    route = [(i - distance, i) for i in devices if i - distance in devices]
    return lax.ppermute(block, axis, route)


def slot_table(suffix_len, request_group, tok_dev, row_count):
    req_count = suffix_len.shape[0]
    group_count = req_count // 4
    row_ends = jnp.cumsum(suffix_len)
    starts = row_ends - suffix_len
    member = (request_group[None, :] == jnp.arange(group_count, dtype=jnp.int32)[:, None]).astype(
        jnp.int32
    )
    rank_of = jnp.cumsum(member, axis=1) - 1
    slot_ids = jnp.arange(4 * tok_dev, dtype=jnp.int32)
    which_req = slot_ids // tok_dev
    offset = slot_ids % tok_dev
    picked = member[:, None, :] * (rank_of[:, None, :] == which_req[None, :, None]).astype(
        jnp.int32
    )
    length = jnp.sum(picked * suffix_len[None, None, :], axis=2)
    row_begin = jnp.sum(picked * starts[None, None, :], axis=2)
    slot_valid = offset[None, :] < length
    return (jnp.where(slot_valid, row_begin + offset[None, :], row_count), slot_valid)


def request_of(row_ids, starts, row_ends):
    inside = (row_ids[:, None] >= starts[None, :]) & (row_ids[:, None] < row_ends[None, :])
    req_ids = jnp.arange(starts.shape[0], dtype=jnp.int32)
    return jnp.sum(jnp.where(inside, req_ids[None, :], 0), axis=1)


def per_device(
    queries,
    suffix_key_rows,
    suffix_value_rows,
    prefix_block_keys,
    prefix_block_values,
    block_group,
    suffix_len,
    request_group,
    w_out,
):
    tok_dev = queries.shape[0]
    q_cols = queries.shape[1]
    kv_cols = suffix_key_rows.shape[1]
    local_kv = kv_cols // HEAD_SIZE
    local_heads = q_cols // HEAD_SIZE
    query_group_width = local_heads // local_kv
    blocks = prefix_block_keys.shape[0]
    block_len = prefix_block_keys.shape[1]
    blk_count = lax.axis_size("blk")
    row_count = blk_count * tok_dev
    blk_index = lax.axis_index("blk")
    score_scale = 1.0 / math.sqrt(HEAD_SIZE)
    row_ends = jnp.cumsum(suffix_len)
    starts = row_ends - suffix_len
    own_rows = blk_index * tok_dev + jnp.arange(tok_dev, dtype=jnp.int32)
    earlier_keys, earlier_values = from_behind((suffix_key_rows, suffix_value_rows), "blk", 1)
    near_keys = jnp.concatenate([earlier_keys, suffix_key_rows], axis=0).reshape(
        2 * tok_dev, local_kv, HEAD_SIZE
    )
    near_values = jnp.concatenate([earlier_values, suffix_value_rows], axis=0).reshape(
        2 * tok_dev, local_kv, HEAD_SIZE
    )
    near_rows = (blk_index - 1) * tok_dev + jnp.arange(2 * tok_dev, dtype=jnp.int32)
    own_req = request_of(own_rows, starts, row_ends)
    near_req = request_of(near_rows, starts, row_ends)
    allowed = (
        (own_req[:, None] == near_req[None, :])
        & (near_rows[None, :] <= own_rows[:, None])
        & (near_rows[None, :] >= 0)
    )
    own_queries = queries.reshape(tok_dev, local_kv, query_group_width, HEAD_SIZE)
    near_scores = (
        jnp.einsum("sgjd,tgd->sgjt", own_queries, near_keys, preferred_element_type=jnp.float32)
        * score_scale
    )
    near_scores = jnp.where(allowed[:, None, None, :], near_scores, -jnp.inf)
    near_max = jnp.max(near_scores, axis=3)
    gathered = lax.all_gather(queries, "blk", axis=0, tiled=True)
    slot_rows, slot_valid = slot_table(suffix_len, request_group, tok_dev, row_count)
    slot_count = slot_rows.shape[1]
    block_rows = slot_rows[block_group]
    block_valid = slot_valid[block_group]
    padded = jnp.concatenate([gathered, jnp.zeros((1, q_cols), gathered.dtype)], axis=0)
    chosen = padded[block_rows].reshape(blocks, slot_count, local_kv, query_group_width, HEAD_SIZE)
    far_keys = prefix_block_keys.reshape(blocks, block_len, local_kv, HEAD_SIZE)
    far_scores = (
        jnp.einsum("bsgjd,btgd->bsgjt", chosen, far_keys, preferred_element_type=jnp.float32)
        * score_scale
    )
    far_max = jnp.max(far_scores, axis=4).reshape(-1, local_heads)
    flat_rows = block_rows.reshape(-1)
    row_max = (
        jnp.full((row_count + 1, local_heads), -jnp.inf, jnp.float32).at[flat_rows].max(far_max)
    )
    own_part = lax.dynamic_slice_in_dim(row_max, blk_index * tok_dev, tok_dev, 0)
    row_max = lax.dynamic_update_slice_in_dim(
        row_max,
        jnp.maximum(own_part, near_max.reshape(tok_dev, local_heads)),
        blk_index * tok_dev,
        0,
    )
    top_score = lax.pmax(row_max[:row_count], "blk")
    slot_top = jnp.concatenate([top_score, jnp.zeros((1, local_heads), jnp.float32)], axis=0)[
        block_rows
    ]
    slot_top = slot_top.reshape(blocks, slot_count, local_kv, query_group_width, 1)
    far_prob = jnp.exp(far_scores - slot_top) * block_valid[:, :, None, None, None].astype(
        jnp.float32
    )
    far_total = jnp.sum(far_prob, axis=4).reshape(-1, local_heads)
    far_values = prefix_block_values.reshape(blocks, block_len, local_kv, HEAD_SIZE)
    far_context = jnp.einsum(
        "bsgjt,btgd->bsgjd",
        far_prob.astype(jnp.bfloat16),
        far_values,
        preferred_element_type=jnp.float32,
    ).reshape(-1, q_cols)
    context_rows = (
        jnp.zeros((row_count + 1, q_cols), jnp.float32).at[flat_rows].add(far_context)[:row_count]
    )
    total_rows = (
        jnp.zeros((row_count + 1, local_heads), jnp.float32)
        .at[flat_rows]
        .add(far_total)[:row_count]
    )
    got_context, got_total = (
        lax.psum_scatter(context_rows, "blk", scatter_dimension=0, tiled=True),
        lax.psum_scatter(total_rows, "blk", scatter_dimension=0, tiled=True),
    )
    own_top = lax.dynamic_slice_in_dim(top_score, blk_index * tok_dev, tok_dev, 0)
    near_prob = jnp.exp(near_scores - own_top.reshape(tok_dev, local_kv, query_group_width, 1))
    near_total = jnp.sum(near_prob, axis=3).reshape(tok_dev, local_heads)
    near_context = jnp.einsum(
        "sgjt,tgd->sgjd",
        near_prob.astype(jnp.bfloat16),
        near_values,
        preferred_element_type=jnp.float32,
    ).reshape(tok_dev, q_cols)
    denominator = (got_total + near_total)[:, :, None]
    attention = (
        ((got_context + near_context).reshape(tok_dev, local_heads, HEAD_SIZE) / denominator)
        .reshape(tok_dev, q_cols)
        .astype(jnp.bfloat16)
    )
    projected = jnp.dot(attention, w_out, preferred_element_type=jnp.float32)
    return lax.psum_scatter(projected, "kvh", scatter_dimension=1, tiled=True).astype(jnp.bfloat16)


def solution(mesh):
    placed = (
        P("blk", "kvh"),
        P("blk", "kvh"),
        P("blk", "kvh"),
        P("blk", None, "kvh"),
        P("blk", None, "kvh"),
        P("blk"),
        P(),
        P(),
        P("kvh", None),
    )
    return jax.shard_map(
        per_device, mesh=mesh, in_specs=placed, out_specs=P("blk", "kvh"), check_vma=False
    )
```

profile of v0, /device:TPU:0, one launch (start us, length us, event | category | flops | bytes accessed | tf_op | source)
XLA Modules:
  0.0 777.4 jit_solution(996612331615580433)
XLA Ops:
  8.3 1.3 collective-permute-start
  12.7 1.6 fusion.17
  15.5 1.1 reshape.259
  16.7 1.3 reshape.256
  18.1 1.3 fusion.43
  19.5 45.2 %all-gather.2.cloned.1.call-done = bf16[4096,1024]{1,0:T(8,128)(2,1)} async-done(((bf16[128,1024]{1,0:T(8,128)(2,1)}), bf16[4096,1024]{1,0:T(8,128)(2,1)}) %all-gather.2.cloned.1.call-update) | async-done | bytes 8388624 | tf_op jit(solution)/shard_map/all_gather | solution.py:92
  64.7 7.6 concatenate.12
  72.3 45.1 %gather_fusion.1 = bf16[8192,1024]{1,0:T(8,128)(2,1)} fusion(bf16[4097,1024]{1,0:T(8,128)(2,1)} %concatenate.12, s32[8192]{0:T(1024)S(1)} %broadcast_clamp_fusion), kind=kCustom, calls=%fused_computation.1 | custom fusion | bytes 33587200 | tf_op jit(solution)/shard_map/gather | solution.py:98
  117.5 27.4 %reshape.255 = bf16[16,512,2,4,128]{4,3,2,1,0:T(4,128)(2,1)} reshape(bf16[8192,1024]{1,0:T(8,128)(2,1)} %gather_fusion.1) | data formatting | bytes 33554432 | tf_op jit(solution)/shard_map/reshape | solution.py:98
  144.8 19.2 %bitcast_reduce_fusion = (f32[16,512,2,4]{1,3,2,0:T(4,128)S(1)}, f32[16,2,512,4,128]{2,4,3,1,0:T(8,128)}) fusion(bf16[16,128,2,128,1]{3,2,1,0,4:T(2,128)(2,1)S(1)} %bitcast.75, bf16[16,512,2,4,128]{4,3,2,1,0:T(4,128)(2,1)} %reshape.255), kind=kOutput, calls=%fused_computation.8 | convolution fusion | flops 2164195328 | bytes 51642368 | tf_op jit(solution)/shard_map/bsgjd,btgd->bsgjt/dot_general | solution.py:101
  164.3 2.7 copy.86
  167.0 50.0 %scatter_custom_fusion = f32[4097,8]{1,0:T(8,128)S(1)} fusion(s32[8192]{0:T(1024)S(1)} %bitcast.91, f32[8192,8]{1,0:T(8,128)} %copy.86, f32[]{:T(128)} %constant.71.clone.1), kind=kCustom, calls=%fused_computation.31 | custom fusion | flops 65536 | bytes 131616 | tf_op jit(solution)/shard_map/scatter-max | solution.py:107
  217.6 1.5 slice.20
  219.9 1.3 reshape.261
  221.2 104.9 %all-reduce.4.cloned.1.call-done = f32[4096,8]{1,0:T(8,128)} async-done(((f32[4096,8]{1,0:T(8,128)}), f32[4096,8]{1,0:T(8,128)}) %all-reduce.4.cloned.1.call-update) | async-done | bytes 131088 | tf_op jit(solution)/shard_map/pmax | solution.py:116
  326.1 1.7 concatenate.14
  327.9 27.7 %gather_fusion.2 = f32[8192,8]{1,0:T(8,128)} fusion(f32[4097,8]{1,0:T(8,128)S(1)} %concatenate.14, s32[8192]{0:T(1024)S(1)} %broadcast_clamp_fusion), kind=kCustom, calls=%fused_computation.2 | custom fusion | bytes 557056 | tf_op jit(solution)/shard_map/gather | solution.py:117
  355.6 2.8 copy.92
  358.7 15.4 %fusion.2 = f32[16,512,2,4]{1,3,2,0:T(4,128)S(1)} fusion(f32[16,2,512,4,128]{2,4,3,1,0:T(8,128)} %get-tuple-element.10, f32[16,512]{1,0:T(8,128)S(1)} %convert_element_type.33, f32[16,512,2,4]{1,3,2,0:T(4,128)S(1)} %copy.93), kind=kLoop, calls=%fused_computation.11 | loop fusion | flops 33488896 | bytes 34111488 | tf_op jit(solution)/shard_map/reduce_sum | solution.py:124
  374.4 2.7 copy.103
  377.1 50.0 %scatter_custom_fusion.2 = f32[4097,8]{1,0:T(8,128)S(1)} fusion(s32[8192]{0:T(1024)S(1)} %bitcast.92, f32[8192,8]{1,0:T(8,128)} %copy.103, f32[]{:T(128)} %constant.32.clone.1), kind=kCustom, calls=%fused_computation.29 | custom fusion | flops 65536 | bytes 131616 | tf_op jit(solution)/shard_map/scatter-add | solution.py:138
  427.1 1.5 slice.22
  428.6 22.8 %fusion.11 = f32[16,512,2,4,128]{4,1,3,2,0:T(8,128)} fusion(f32[16,2,512,4,128]{2,4,3,1,0:T(8,128)} %get-tuple-element.10, f32[16,512]{1,0:T(8,128)S(1)} %convert_element_type.33, f32[16,512,2,4]{1,3,2,0:T(4,128)S(1)} %copy.93, bf16[16,128,2,128,1]{3,2,1,0,4:T(2,128)(2,1)S(1)} %bitcast.74), kind=kOutput, calls=%fused_computation.19 | convolution fusion | flops 2181038080 | bytes 68452352 | tf_op jit(solution)/shard_map/bsgjt,btgd->bsgjd/dot_general | solution.py:126
  451.4 37.8 %copy.117 = f32[16,512,2,4,128]{4,3,2,1,0:T(4,128)} copy(f32[16,512,2,4,128]{4,1,3,2,0:T(8,128)} %fusion.11) | data formatting | bytes 67108864 | tf_op jit(solution)/shard_map/reshape | solution.py:131
  489.3 39.1 %reshape.333 = f32[8192,1024]{1,0:T(8,128)} reshape(f32[16,512,2,4,128]{4,3,2,1,0:T(4,128)} %copy.117) | data formatting | bytes 67108864 | tf_op jit(solution)/shard_map/reshape | solution.py:131
  528.4 77.7 %scatter_custom_fusion.1 = f32[4097,1024]{1,0:T(8,128)} fusion(s32[8192]{0:T(1024)S(1)} %bitcast.93, f32[8192,1024]{1,0:T(8,128)} %reshape.333, f32[]{:T(128)} %constant.32.clone.1), kind=kCustom, calls=%fused_computation.20 | custom fusion | flops 8388608 | bytes 16781824 | tf_op jit(solution)/shard_map/scatter-add | solution.py:133
  606.1 11.8 %slice.21 = f32[4096,1024]{1,0:T(8,128)} slice(f32[4097,1024]{1,0:T(8,128)} %scatter_custom_fusion.1), slice={[0:4096], [0:1024]} | slice | bytes 33554432 | tf_op jit(solution)/shard_map/slice | solution.py:133
  618.7 1.7 collective-permute-start.1
  624.0 109.1 %reduce-scatter.4.cloned.1.call-done = f32[128,1024]{1,0:T(8,128)} async-done(((f32[4096,1024]{1,0:T(8,128)}), f32[128,1024]{1,0:T(8,128)}) %reduce-scatter.4.cloned.1.call-update) | async-done | bytes 524304 | tf_op jit(solution)/shard_map/reduce_scatter | solution.py:141
  733.4 6.3 fusion.32
  739.6 29.5 %reduce-scatter.8.cloned.1.call-done = f32[128,1024]{1,0:T(8,128)} async-done(((f32[128,4096]{1,0:T(8,128)}), f32[128,1024]{1,0:T(8,128)}) %reduce-scatter.8.cloned.1.call-update) | async-done | bytes 524304 | tf_op jit(solution)/shard_map/reduce_scatter | solution.py:160
  769.1 1.8 convert_element_type.37
  (64 shorter events, 13.1 us)
Async XLA Ops:
  6.5 58.2 %all-gather.2.cloned.1.call-start = ((), (), s32[]{:S(2)}) async-start(), calls=%async_computation.3 | async-start | bytes 8650752 | tf_op jit(solution)/shard_map/all_gather | solution.py:92
  7.3 318.9 %all-reduce.4.cloned.1.call-start = ((), (), s32[]{:S(2)}) async-start(), calls=%async_computation.4 | async-start | bytes 4194304 | tf_op jit(solution)/shard_map/pmax | solution.py:116
  8.3 9.8 %collective-permute-start = (bf16[128,256]{0,1:T(8,128)(2,1)S(1)}, bf16[128,256]{0,1:T(8,128)(2,1)S(1)}, u32[]{:S(2)}, u32[]{:S(2)}) collective-permute-start(bf16[128,256]{0,1:T(8,128)(2,1)S(1)} %copy.87), channel_id=1, source_target_pairs={{0,1},{1,2},{2,3},{3,4},{4,5},{5,6},{6,7},{7,8},{8,9},{9,10},{10,1... | collective-permute-start | bytes 196616 | tf_op jit(solution)/shard_map/ppermute | solution.py:14
  219.1 404.1 %reduce-scatter.6.cloned.1.call-start = ((), (), s32[]{:S(2)}) async-start(), calls=%async_computation.6 | async-start | bytes 2162688 | tf_op jit(solution)/shard_map/reduce_scatter | solution.py:142
  428.6 304.6 %reduce-scatter.4.cloned.1.call-start = ((), (), s32[]{:S(2)}) async-start(), calls=%async_computation.5 | async-start | bytes 17301504 | tf_op jit(solution)/shard_map/reduce_scatter | solution.py:141
  617.9 0.8 copy-start.1
  617.9 4.4 copy-start
  617.9 151.2 %reduce-scatter.8.cloned.1.call-start = ((), (), s32[]{:S(2)}) async-start(), calls=%async_computation.7 | async-start | bytes 2621440 | tf_op jit(solution)/shard_map/reduce_scatter | solution.py:160
  618.7 2.6 collective-permute-start.1
Sparse Core Ops, SparseCore 0:
  9.6 55.1 all-gather.1
  219.2 106.9 all-reduce.3
  428.7 78.6 reduce-scatter.5
  618.1 115.0 reduce-scatter.3
  739.8 29.2 reduce-scatter.7
where the time goes:
time: 780 us; the launch traced here: 777 us
  waiting for transfers between devices  290 us (37%)
  local copies, waits for them, and re-layouts  220 us (28%)
  other arithmetic  200 us (26%)
  matrix products  49.9 us (6%)
  between operations  13.4 us (2%)
    reduce_scatter x1, waiting for transfers between devices, per_device(): lax.psum_scatter(context_rows, 'blk', scatter_dimension=0, tiled=True)  109 us
    pmax x1, waiting for transfers between devices, per_device(): top_score = lax.pmax(row_max[:row_count], 'blk')  105 us
    scatter-add x1, other arithmetic, per_device(): jnp.zeros((row_count + 1, q_cols), jnp.float32).at[flat_rows]  77.7 us
    reshape x2, local copies, waits for them, and re-layouts, per_device(): far_context = jnp.einsum('bsgjt,btgd->bsgjd', far_prob.astype(jnp.bfloat1...  77 us
    another operation x1, other arithmetic, per_device(): jnp.full((row_count + 1, local_heads), -jnp.inf, jnp.float32).at[flat_rows]  50 us
    scatter-add x1, other arithmetic, per_device(): total_rows = jnp.zeros((row_count + 1, local_heads), jnp.float32).at[flat...  50 us
    all_gather x1, waiting for transfers between devices, per_device(): gathered = lax.all_gather(queries, 'blk', axis=0, tiled=True)  45.2 us
    gather x1, local copies, waits for them, and re-layouts, per_device(): padded[block_rows]  45.1 us
  transfers between devices with their start and end apart: 7, of which 5 were waited for; matrix products, arithmetic and copies ran while one was open for 26% of the time, Pallas kernels for 0%

commit v1 on v0

v1 whole, which is shorter than its diff:
```python
import functools
import math

import jax
import jax.numpy as jnp
from jax import lax
from jax.experimental import pallas as pl
from jax.experimental.pallas import tpu as pltpu
from jax.sharding import PartitionSpec as P

HEAD_SIZE = 128
SLOTS = 5
STAT_LANES = 128


def from_behind(block, axis, distance):
    devices = range(lax.axis_size(axis))
    route = [(i - distance, i) for i in devices if i - distance in devices]
    return lax.ppermute(block, axis, route)


def request_of(row_ids, starts, row_ends):
    inside = (row_ids[:, None] >= starts[None, :]) & (row_ids[:, None] < row_ends[None, :])
    req_ids = jnp.arange(starts.shape[0], dtype=jnp.int32)
    return jnp.sum(jnp.where(inside, req_ids[None, :], 0), axis=1)


def tile_tables(suffix_len, request_group, block_group, n_tiles, tile):
    row_ends = jnp.cumsum(suffix_len).astype(jnp.int32)
    starts = row_ends - suffix_len
    tile_lo = jnp.arange(n_tiles, dtype=jnp.int32) * tile
    first = jnp.sum((row_ends[None, :] <= tile_lo[:, None]).astype(jnp.int32), axis=1)
    last = jnp.sum((row_ends[None, :] <= (tile_lo + tile - 1)[:, None]).astype(jnp.int32), axis=1)
    req = first[:, None] + jnp.arange(SLOTS, dtype=jnp.int32)[None, :]
    valid = req <= last[:, None]
    req_v = jnp.minimum(req, last[:, None])
    lo = jnp.where(valid, starts[req_v], 0).astype(jnp.int32)
    hi = jnp.where(valid, row_ends[req_v], 0).astype(jnp.int32)
    group_count = suffix_len.shape[0] // 4
    blocks = block_group.shape[0]
    owns = block_group[None, :] == jnp.arange(group_count, dtype=jnp.int32)[:, None]
    block_of_group = jnp.sum(
        jnp.where(owns, jnp.arange(blocks, dtype=jnp.int32)[None, :], 0), axis=1
    ).astype(jnp.int32)
    blk = block_of_group[request_group[req_v]].astype(jnp.int32)
    return lo.reshape(-1), hi.reshape(-1), blk.reshape(-1)


def _scores(q_ref, k_ref, j, h, query_group_width, scale):
    kv = h // query_group_width
    q = q_ref[:, h * HEAD_SIZE : (h + 1) * HEAD_SIZE]
    k = k_ref[j, :, kv * HEAD_SIZE : (kv + 1) * HEAD_SIZE]
    s = lax.dot_general(q, k, (((1,), (1,)), ((), ())), preferred_element_type=jnp.float32)
    return s * scale


def max_kernel(lo_ref, hi_ref, blk_ref, q_ref, k_ref, m_ref, *, heads, qgw, scale):
    i = pl.program_id(0)
    tile = q_ref.shape[0]
    rows = i * tile + lax.broadcasted_iota(jnp.int32, (tile, 1), 0)
    m_ref[...] = jnp.full(m_ref.shape, -jnp.inf, jnp.float32)
    for s in range(SLOTS):
        a = lo_ref[i * SLOTS + s]
        b = hi_ref[i * SLOTS + s]
        j = blk_ref[i * SLOTS + s]

        @pl.when(a < b)
        def _():
            mask = (rows >= a) & (rows < b)
            for h in range(heads):
                sc = _scores(q_ref, k_ref, j, h, qgw, scale)
                mx = jnp.max(sc, axis=1, keepdims=True)
                m_ref[:, h : h + 1] = jnp.where(mask, mx, m_ref[:, h : h + 1])


def ctx_kernel(lo_ref, hi_ref, blk_ref, q_ref, k_ref, v_ref, m_ref, o_ref, *, heads, qgw, scale):
    i = pl.program_id(0)
    tile = q_ref.shape[0]
    rows = i * tile + lax.broadcasted_iota(jnp.int32, (tile, 1), 0)
    o_ref[...] = jnp.zeros(o_ref.shape, jnp.float32)
    for s in range(SLOTS):
        a = lo_ref[i * SLOTS + s]
        b = hi_ref[i * SLOTS + s]
        j = blk_ref[i * SLOTS + s]

        @pl.when(a < b)
        def _():
            mask = (rows >= a) & (rows < b)
            for h in range(heads):
                kv = h // qgw
                sc = _scores(q_ref, k_ref, j, h, qgw, scale)
                p = jnp.where(mask, jnp.exp(sc - m_ref[:, h : h + 1]), 0.0)
                v = v_ref[j, :, kv * HEAD_SIZE : (kv + 1) * HEAD_SIZE]
                ctx = jnp.dot(p.astype(jnp.bfloat16), v, preferred_element_type=jnp.float32)
                cols = slice(h * HEAD_SIZE, (h + 1) * HEAD_SIZE)
                o_ref[:, cols] = o_ref[:, cols] + ctx
                tcol = slice(heads * HEAD_SIZE + h, heads * HEAD_SIZE + h + 1)
                o_ref[:, tcol] = o_ref[:, tcol] + jnp.sum(p, axis=1, keepdims=True)


def per_device(
    queries,
    suffix_key_rows,
    suffix_value_rows,
    prefix_block_keys,
    prefix_block_values,
    block_group,
    suffix_len,
    request_group,
    w_out,
):
    tok_dev = queries.shape[0]
    q_cols = queries.shape[1]
    kv_cols = suffix_key_rows.shape[1]
    local_kv = kv_cols // HEAD_SIZE
    local_heads = q_cols // HEAD_SIZE
    qgw = local_heads // local_kv
    blocks, block_len, _ = prefix_block_keys.shape
    blk_count = lax.axis_size("blk")
    row_count = blk_count * tok_dev
    blk_index = lax.axis_index("blk")
    scale = 1.0 / math.sqrt(HEAD_SIZE)
    tile = tok_dev
    n_tiles = row_count // tile

    gathered = lax.all_gather(queries, "blk", axis=0, tiled=True)
    lo, hi, blk = tile_tables(suffix_len, request_group, block_group, n_tiles, tile)

    q_spec = pl.BlockSpec((tile, q_cols), lambda i, *_: (i, 0))
    kv_spec = pl.BlockSpec((blocks, block_len, kv_cols), lambda i, *_: (0, 0, 0))
    m_spec = pl.BlockSpec((tile, local_heads), lambda i, *_: (i, 0))
    kw = dict(heads=local_heads, qgw=qgw, scale=scale)

    local_max = pl.pallas_call(
        functools.partial(max_kernel, **kw),
        out_shape=jax.ShapeDtypeStruct((row_count, local_heads), jnp.float32),
        grid_spec=pltpu.PrefetchScalarGridSpec(
            num_scalar_prefetch=3,
            grid=(n_tiles,),
            in_specs=[q_spec, kv_spec],
            out_specs=m_spec,
        ),
    )(lo, hi, blk, gathered, prefix_block_keys)
    far_max = lax.pmax(local_max, "blk")

    width = q_cols + STAT_LANES
    partial = pl.pallas_call(
        functools.partial(ctx_kernel, **kw),
        out_shape=jax.ShapeDtypeStruct((row_count, width), jnp.float32),
        grid_spec=pltpu.PrefetchScalarGridSpec(
            num_scalar_prefetch=3,
            grid=(n_tiles,),
            in_specs=[q_spec, kv_spec, kv_spec, m_spec],
            out_specs=pl.BlockSpec((tile, width), lambda i, *_: (i, 0)),
        ),
    )(lo, hi, blk, gathered, prefix_block_keys, prefix_block_values, far_max)
    got = lax.psum_scatter(partial, "blk", scatter_dimension=0, tiled=True)
    far_context = got[:, :q_cols].reshape(tok_dev, local_kv, qgw, HEAD_SIZE)
    far_total = got[:, q_cols : q_cols + local_heads].reshape(tok_dev, local_kv, qgw)
    own_far_max = lax.dynamic_slice_in_dim(far_max, blk_index * tok_dev, tok_dev, 0).reshape(
        tok_dev, local_kv, qgw
    )

    row_ends = jnp.cumsum(suffix_len)
    starts = row_ends - suffix_len
    own_rows = blk_index * tok_dev + jnp.arange(tok_dev, dtype=jnp.int32)
    earlier_keys, earlier_values = from_behind((suffix_key_rows, suffix_value_rows), "blk", 1)
    near_keys = jnp.concatenate([earlier_keys, suffix_key_rows], axis=0).reshape(
        2 * tok_dev, local_kv, HEAD_SIZE
    )
    near_values = jnp.concatenate([earlier_values, suffix_value_rows], axis=0).reshape(
        2 * tok_dev, local_kv, HEAD_SIZE
    )
    near_rows = (blk_index - 1) * tok_dev + jnp.arange(2 * tok_dev, dtype=jnp.int32)
    own_req = request_of(own_rows, starts, row_ends)
    near_req = request_of(near_rows, starts, row_ends)
    allowed = (
        (own_req[:, None] == near_req[None, :])
        & (near_rows[None, :] <= own_rows[:, None])
        & (near_rows[None, :] >= 0)
    )
    own_queries = queries.reshape(tok_dev, local_kv, qgw, HEAD_SIZE)
    near_scores = (
        jnp.einsum("sgjd,tgd->sgjt", own_queries, near_keys, preferred_element_type=jnp.float32)
        * scale
    )
    near_scores = jnp.where(allowed[:, None, None, :], near_scores, -jnp.inf)
    near_max = jnp.max(near_scores, axis=3)
    top = jnp.maximum(own_far_max, near_max)
    near_prob = jnp.exp(near_scores - top[..., None])
    near_total = jnp.sum(near_prob, axis=3)
    near_context = jnp.einsum(
        "sgjt,tgd->sgjd",
        near_prob.astype(jnp.bfloat16),
        near_values,
        preferred_element_type=jnp.float32,
    )
    far_scale = jnp.exp(own_far_max - top)
    context = far_context * far_scale[..., None] + near_context
    denominator = far_total * far_scale + near_total
    attention = (context / denominator[..., None]).reshape(tok_dev, q_cols).astype(jnp.bfloat16)
    projected = jnp.dot(attention, w_out, preferred_element_type=jnp.float32)
    return lax.psum_scatter(projected, "kvh", scatter_dimension=1, tiled=True).astype(jnp.bfloat16)


def solution(mesh):
    placed = (
        P("blk", "kvh"),
        P("blk", "kvh"),
        P("blk", "kvh"),
        P("blk", None, "kvh"),
        P("blk", None, "kvh"),
        P("blk"),
        P(),
        P(),
        P("kvh", None),
    )
    return jax.shard_map(
        per_device, mesh=mesh, in_specs=placed, out_specs=P("blk", "kvh"), check_vma=False
    )
```

time: 780 us -> 528 us (0.68)
  local copies, waits for them, and re-layouts: 220 us -> 13.6 us
  other arithmetic: 200 us -> 3.75 us
  Pallas kernels: 0 us -> 187 us
  matrix products: 49.9 us -> 6.72 us
    pallas_call x0 -> x2, Pallas kernels: none -> 187 us  [the longest x1 141 us: per_device(): pl.pallas_call(functools.partial(ctx_kernel, **kw), out_shape=jax.ShapeDt...]
    scatter-add x2 -> x0, other arithmetic: 128 us -> none  [the longest x1 77.7 us: per_device(): jnp.zeros((row_count + 1, q_cols), jnp.float32).at[flat_rows]]
    reshape x11 -> x2, local copies, waits for them, and re-layouts: 114 us -> 0.36 us  [the longest x1 0.19 us: per_device(): far_context = got[:, :q_cols].reshape(tok_dev, local_kv, qgw, HEAD_SIZE)]
    gather x5 -> x7, local copies, waits for them, and re-layouts: 76.8 us -> 7.07 us  [the longest x3 3.77 us: tile_tables(): blk = block_of_group[request_group[req_v]].astype(jnp.int32)]
    another operation x4 -> x2, other arithmetic: 50.4 us -> 0.2 us  [the longest x1 50 us: per_device(): jnp.full((row_count + 1, local_heads), -jnp.inf, jnp.float32).at[flat_rows]]
    dot_general x2 -> x0, matrix products: 42 us -> none  [the longest x1 22.8 us: per_device(): jnp.einsum('bsgjt,btgd->bsgjd', far_prob.astype(jnp.bfloat16), far_values...]
    reduce_sum x3, other arithmetic: 17.2 us -> 0.48 us  [the longest x1 0.18 us: per_device(): near_total = jnp.sum(near_prob, axis=3)]
    slice x3, local copies, waits for them, and re-layouts: 14.7 us -> 1.99 us  [the longest x1 1.1 us: per_device(): far_context = got[:, :q_cols].reshape(tok_dev, local_kv, qgw, HEAD_SIZE)]
  transfers between devices with their start and end apart: 7 -> 6, of which waited for: 5 -> 5; matrix products, arithmetic and copies ran while one was open for 26% -> 2% of each run, Pallas kernels for 0% -> 0%
where the time goes in v1:
time: 528 us; the launch traced here: 527 us
  waiting for transfers between devices  297 us (56%)
  Pallas kernels  187 us (35%)
  local copies, waits for them, and re-layouts  13.6 us (3%)
  between operations  13.3 us (3%)
  matrix products  6.72 us (1%)
    pallas_call x1, Pallas kernels, per_device(): pl.pallas_call(functools.partial(ctx_kernel, **kw), out_shape=jax.ShapeDt...  141 us
    reduce_scatter x1, waiting for transfers between devices, per_device(): got = lax.psum_scatter(partial, 'blk', scatter_dimension=0, tiled=True)  113 us
    pmax x1, waiting for transfers between devices, per_device(): far_max = lax.pmax(local_max, 'blk')  107 us
    all_gather x1, waiting for transfers between devices, per_device(): gathered = lax.all_gather(queries, 'blk', axis=0, tiled=True)  46.6 us
    pallas_call x1, Pallas kernels, per_device(): pl.pallas_call(functools.partial(max_kernel, **kw), out_shape=jax.ShapeDt...  46.4 us
    reduce_scatter x1, waiting for transfers between devices, per_device(): lax.psum_scatter(projected, 'kvh', scatter_dimension=1, tiled=True)  29.5 us
  transfers between devices with their start and end apart: 6, of which 5 were waited for; matrix products, arithmetic and copies ran while one was open for 2% of the time, Pallas kernels for 0%

profile of v1, /device:TPU:0, one launch (start us, length us, event | category | flops | bytes accessed | tf_op | source)
XLA Modules:
  0.0 527.1 jit_solution(3733478937105935372)
XLA Ops:
  6.5 0.7 all-gather.2.cloned.1.call-update
  7.3 0.7 copy.28
  8.3 0.7 sub.33
  8.9 0.2 convert_reduce_fusion.1
  9.3 1.6 gather_fusion.1
  10.9 1.6 gather_fusion
  12.7 0.7 select_n.58.lo_ref
  13.4 0.7 select_n.60.hi_ref
  14.1 1.5 gather_fusion.2
  15.9 0.1 select_reduce_fusion.2
  16.0 2.1 gather_fusion.3
  18.1 46.6 %all-gather.2.cloned.1.call-done.q_ref = bf16[4096,1024]{1,0:T(8,128)(2,1)} async-done(((bf16[128,1024]{1,0:T(8,128)(2,1)}), bf16[4096,1024]{1,0:T(8,128)(2,1)}) %all-gather.2.cloned.1.call-update) | async-done | bytes 8388624 | tf_op jit(solution)/shard_map/all_gather | solution.py:126
  64.8 46.4 %shard_map.91 = f32[4096,8]{1,0:T(8,128)} custom-call(s32[160]{0:T(256)} %select_n.58.lo_ref, s32[160]{0:T(256)} %select_n.60.hi_ref, s32[160]{0:T(256)} %gather_fusion.3, bf16[4096,1024]{1,0:T(8,128)(2,1)} %all-gather.2.cloned.1.call-done.q_ref, bf16[16,128,256]{2,1,0:T(8,128)(2,1)} %k_ref.3), custom_call_target="tpu_custom_call" | custom-call | tf_op jit(solution)/shard_map/pallas_call | solution.py:134
  111.2 107.0 %all-reduce.2.cloned.1.call-done.m_ref = f32[4096,8]{1,0:T(8,128)} async-done(((f32[4096,8]{1,0:T(8,128)}), f32[4096,8]{1,0:T(8,128)}) %all-reduce.2.cloned.1.call-update) | async-done | bytes 131088 | tf_op jit(solution)/shard_map/pmax | solution.py:144
  218.3 140.9 %shard_map.92 = f32[4096,1152]{1,0:T(8,128)} custom-call(s32[160]{0:T(256)} %select_n.58.lo_ref, s32[160]{0:T(256)} %select_n.60.hi_ref, s32[160]{0:T(256)} %gather_fusion.3, bf16[4096,1024]{1,0:T(8,128)(2,1)} %all-gather.2.cloned.1.call-done.q_ref, bf16[16,128,256]{2,1,0:T(8,128)(2,1)} %k_ref.3, bf16[16,128,256]{2,1,0:T(8,128)(2,1)} %v_ref.1, ...), custom_call_target="tpu_custom_call" | custom-call | tf_op jit(solution)/shard_map/pallas_call | solution.py:147
  359.2 0.8 copy-done.2
  360.1 1.7 collective-permute-start
  361.8 3.2 collective-permute-start.1
  365.2 0.2 and_and_fusion
  365.4 0.2 reshape.260
  365.6 0.3 collective-permute-done.1
  366.0 0.4 fusion.12
  366.4 0.9 constant_dynamic-slice_fusion
  367.3 0.2 fusion.5
  367.5 113.3 %reduce-scatter.3.cloned.1.call-done = f32[128,1152]{1,0:T(8,128)} async-done(((f32[4096,1152]{1,0:T(8,128)}), f32[128,1152]{1,0:T(8,128)}) %reduce-scatter.3.cloned.1.call-update) | async-done | bytes 589840 | tf_op jit(solution)/shard_map/reduce_scatter | solution.py:157
  480.7 0.8 slice.17
  481.6 1.1 slice.16
  482.7 0.2 copy.41
  482.9 0.3 fusion.4
  483.3 6.0 %fusion.13 = f32[128,4096]{1,0:T(8,128)} fusion(bf16[128,1024]{0,1:T(8,128)(2,1)S(1)} %bitcast.41, bf16[1024,4096]{1,0:T(8,128)(2,1)} %param.17), kind=kOutput, calls=%fused_computation.41 | convolution fusion | flops 1073741824 | bytes 10747904 | tf_op jit(solution)/shard_map/dot_general | solution.py:202
  489.3 29.5 %reduce-scatter.5.cloned.1.call-done = f32[128,1024]{1,0:T(8,128)} async-done(((f32[128,4096]{1,0:T(8,128)}), f32[128,1024]{1,0:T(8,128)}) %reduce-scatter.5.cloned.1.call-update) | async-done | bytes 524304 | tf_op jit(solution)/shard_map/reduce_scatter | solution.py:203
  518.8 1.8 convert_element_type.23
  (43 shorter events, 1.7 us)
Async XLA Ops:
  6.5 7.6 %copy-start = (s32[64]{0:T(128)S(1)}, s32[64]{0:T(128)}, u32[]{:S(2)}) copy-start(s32[64]{0:T(128)} %param.16) | copy-start | bytes 772
  6.5 58.2 %all-gather.2.cloned.1.call-start = ((), (), s32[]{:S(2)}) async-start(), calls=%async_computation.2 | async-start | bytes 8650752 | tf_op jit(solution)/shard_map/all_gather | solution.py:126
  7.3 211.0 %all-reduce.2.cloned.1.call-start = ((), (), s32[]{:S(2)}) async-start(), calls=%async_computation.3 | async-start | bytes 4194304 | tf_op jit(solution)/shard_map/pmax | solution.py:144
  14.1 1.8 copy-start.4
  111.2 369.6 %reduce-scatter.3.cloned.1.call-start = ((), (), s32[]{:S(2)}) async-start(), calls=%async_computation.4 | async-start | bytes 19464192 | tf_op jit(solution)/shard_map/reduce_scatter | solution.py:157
  359.1 0.8 copy-start.2
  359.1 2.7 copy-start.3
  359.1 6.2 %copy-start.1 = (bf16[128,1024]{1,0:T(8,128)(2,1)S(1)}, bf16[128,1024]{1,0:T(8,128)(2,1)}, u32[]{:S(2)}) copy-start(bf16[128,1024]{1,0:T(8,128)(2,1)} %param.9) | copy-start | bytes 786436
  359.2 159.6 %reduce-scatter.5.cloned.1.call-start = ((), (), s32[]{:S(2)}) async-start(), calls=%async_computation.5 | async-start | bytes 2621440 | tf_op jit(solution)/shard_map/reduce_scatter | solution.py:203
  360.1 5.9 %collective-permute-start = (bf16[128,256]{0,1:T(8,128)(2,1)S(1)}, bf16[128,256]{0,1:T(8,128)(2,1)S(1)}, u32[]{:S(2)}, u32[]{:S(2)}) collective-permute-start(bf16[128,256]{0,1:T(8,128)(2,1)S(1)} %copy.30), channel_id=1, source_target_pairs={{0,1},{1,2},{2,3},{3,4},{4,5},{5,6},{6,7},{7,8},{8,9},{9,10},{10,1... | collective-permute-start | bytes 196616 | tf_op jit(solution)/shard_map/ppermute | solution.py:19
  361.8 4.0 collective-permute-start.1
Sparse Core Ops, SparseCore 0:
  9.6 55.1 all-gather.1
  111.3 106.9 all-reduce.1
  359.3 121.4 reduce-scatter.2
  489.5 29.3 reduce-scatter.4

commit v2 on v1

--- a/solution.py
+++ b/solution.py
@@ -46,56 +46,75 @@
     return lo.reshape(-1), hi.reshape(-1), blk.reshape(-1)
 
 
-def _scores(q_ref, k_ref, j, h, query_group_width, scale):
-    kv = h // query_group_width
-    q = q_ref[:, h * HEAD_SIZE : (h + 1) * HEAD_SIZE]
-    k = k_ref[j, :, kv * HEAD_SIZE : (kv + 1) * HEAD_SIZE]
-    s = lax.dot_general(q, k, (((1,), (1,)), ((), ())), preferred_element_type=jnp.float32)
-    return s * scale
-
-
-def max_kernel(lo_ref, hi_ref, blk_ref, q_ref, k_ref, m_ref, *, heads, qgw, scale):
+def _slot_mask(lo_ref, hi_ref, base, rows):
+    seg = lax.broadcasted_iota(jnp.int32, (1, SLOTS * HEAD_SIZE), 1) // HEAD_SIZE
+    lo = jnp.zeros(seg.shape, jnp.int32)
+    hi = jnp.zeros(seg.shape, jnp.int32)
+    for s in range(SLOTS):
+        lo = jnp.where(seg == s, lo_ref[base + s], lo)
+        hi = jnp.where(seg == s, hi_ref[base + s], hi)
+    return (rows >= lo) & (rows < hi)
+
+
+def _slot_keys(kt_ref, blk_ref, base, kv):
+    cols = slice(kv * HEAD_SIZE, (kv + 1) * HEAD_SIZE)
+    return jnp.concatenate([kt_ref[blk_ref[base + s], cols, :] for s in range(SLOTS)], axis=1)
+
+
+def _slot_values(v_ref, blk_ref, base, kv):
+    cols = slice(kv * HEAD_SIZE, (kv + 1) * HEAD_SIZE)
+    return jnp.concatenate([v_ref[blk_ref[base + s], :, cols] for s in range(SLOTS)], axis=0)
+
+
+def max_kernel(lo_ref, hi_ref, blk_ref, q_ref, kt_ref, m_ref, *, heads, qgw, scale):
     i = pl.program_id(0)
     tile = q_ref.shape[0]
+    base = i * SLOTS
     rows = i * tile + lax.broadcasted_iota(jnp.int32, (tile, 1), 0)
-    m_ref[...] = jnp.full(m_ref.shape, -jnp.inf, jnp.float32)
-    for s in range(SLOTS):
-        a = lo_ref[i * SLOTS + s]
-        b = hi_ref[i * SLOTS + s]
-        j = blk_ref[i * SLOTS + s]
-
-        @pl.when(a < b)
-        def _():
-            mask = (rows >= a) & (rows < b)
-            for h in range(heads):
-                sc = _scores(q_ref, k_ref, j, h, qgw, scale)
-                mx = jnp.max(sc, axis=1, keepdims=True)
-                m_ref[:, h : h + 1] = jnp.where(mask, mx, m_ref[:, h : h + 1])
-
-
-def ctx_kernel(lo_ref, hi_ref, blk_ref, q_ref, k_ref, v_ref, m_ref, o_ref, *, heads, qgw, scale):
+    mask = _slot_mask(lo_ref, hi_ref, base, rows)
+    lane = lax.broadcasted_iota(jnp.int32, (1, STAT_LANES), 1)
+    stats = jnp.full((tile, STAT_LANES), -jnp.inf, jnp.float32)
+    for kv in range(heads // qgw):
+        keys = _slot_keys(kt_ref, blk_ref, base, kv)
+        for j in range(qgw):
+            h = kv * qgw + j
+            q = q_ref[:, h * HEAD_SIZE : (h + 1) * HEAD_SIZE]
+            sc = jnp.dot(q, keys, preferred_element_type=jnp.float32) * scale
+            mx = jnp.max(jnp.where(mask, sc, -jnp.inf), axis=1, keepdims=True)
+            stats = jnp.where(lane == h, mx, stats)
+    m_ref[...] = stats[:, :heads]
+
+
+def ctx_kernel(lo_ref, hi_ref, blk_ref, q_ref, kt_ref, v_ref, m_ref, o_ref, *, heads, qgw, scale):
     i = pl.program_id(0)
     tile = q_ref.shape[0]
+    base = i * SLOTS
     rows = i * tile + lax.broadcasted_iota(jnp.int32, (tile, 1), 0)
-    o_ref[...] = jnp.zeros(o_ref.shape, jnp.float32)
-    for s in range(SLOTS):
-        a = lo_ref[i * SLOTS + s]
-        b = hi_ref[i * SLOTS + s]
-        j = blk_ref[i * SLOTS + s]
-
-        @pl.when(a < b)
-        def _():
-            mask = (rows >= a) & (rows < b)
-            for h in range(heads):
-                kv = h // qgw
-                sc = _scores(q_ref, k_ref, j, h, qgw, scale)
-                p = jnp.where(mask, jnp.exp(sc - m_ref[:, h : h + 1]), 0.0)
-                v = v_ref[j, :, kv * HEAD_SIZE : (kv + 1) * HEAD_SIZE]
-                ctx = jnp.dot(p.astype(jnp.bfloat16), v, preferred_element_type=jnp.float32)
-                cols = slice(h * HEAD_SIZE, (h + 1) * HEAD_SIZE)
-                o_ref[:, cols] = o_ref[:, cols] + ctx
-                tcol = slice(heads * HEAD_SIZE + h, heads * HEAD_SIZE + h + 1)
-                o_ref[:, tcol] = o_ref[:, tcol] + jnp.sum(p, axis=1, keepdims=True)
+    mask = _slot_mask(lo_ref, hi_ref, base, rows)
+    lane = lax.broadcasted_iota(jnp.int32, (1, STAT_LANES), 1)
+    totals = jnp.zeros((tile, STAT_LANES), jnp.float32)
+    top = m_ref[...]
+    for kv in range(heads // qgw):
+        keys = _slot_keys(kt_ref, blk_ref, base, kv)
+        values = _slot_values(v_ref, blk_ref, base, kv)
+        for j in range(qgw):
+            h = kv * qgw + j
+            q = q_ref[:, h * HEAD_SIZE : (h + 1) * HEAD_SIZE]
+            sc = jnp.dot(q, keys, preferred_element_type=jnp.float32) * scale
+            p = jnp.exp(jnp.where(mask, sc - top[:, h : h + 1], -jnp.inf))
+            ctx = jnp.dot(p.astype(jnp.bfloat16), values, preferred_element_type=jnp.float32)
+            o_ref[:, h * HEAD_SIZE : (h + 1) * HEAD_SIZE] = ctx
+            totals = jnp.where(lane == h, jnp.sum(p, axis=1, keepdims=True), totals)
+    o_ref[:, heads * HEAD_SIZE :] = totals
+
+
+def butterfly_max(x, axis):
+    n = lax.axis_size(axis)
+    d = 1
+    while d < n:
+        x = jnp.maximum(x, lax.ppermute(x, axis, [(i, i ^ d) for i in range(n)]))
+        d *= 2
+    return x
 
 
 def per_device(
@@ -128,6 +147,8 @@
 
     q_spec = pl.BlockSpec((tile, q_cols), lambda i, *_: (i, 0))
     kv_spec = pl.BlockSpec((blocks, block_len, kv_cols), lambda i, *_: (0, 0, 0))
+    kt_spec = pl.BlockSpec((blocks, kv_cols, block_len), lambda i, *_: (0, 0, 0))
+    keys_t = jnp.swapaxes(prefix_block_keys, 1, 2)
     m_spec = pl.BlockSpec((tile, local_heads), lambda i, *_: (i, 0))
     kw = dict(heads=local_heads, qgw=qgw, scale=scale)
 
@@ -137,11 +158,11 @@
         grid_spec=pltpu.PrefetchScalarGridSpec(
             num_scalar_prefetch=3,
             grid=(n_tiles,),
-            in_specs=[q_spec, kv_spec],
+            in_specs=[q_spec, kt_spec],
             out_specs=m_spec,
         ),
-    )(lo, hi, blk, gathered, prefix_block_keys)
-    far_max = lax.pmax(local_max, "blk")
+    )(lo, hi, blk, gathered, keys_t)
+    far_max = butterfly_max(local_max, "blk")
 
     width = q_cols + STAT_LANES
     partial = pl.pallas_call(
@@ -150,10 +171,10 @@
         grid_spec=pltpu.PrefetchScalarGridSpec(
             num_scalar_prefetch=3,
             grid=(n_tiles,),
-            in_specs=[q_spec, kv_spec, kv_spec, m_spec],
+            in_specs=[q_spec, kt_spec, kv_spec, m_spec],
             out_specs=pl.BlockSpec((tile, width), lambda i, *_: (i, 0)),
         ),
-    )(lo, hi, blk, gathered, prefix_block_keys, prefix_block_values, far_max)
+    )(lo, hi, blk, gathered, keys_t, prefix_block_values, far_max)
     got = lax.psum_scatter(partial, "blk", scatter_dimension=0, tiled=True)
     far_context = got[:, :q_cols].reshape(tok_dev, local_kv, qgw, HEAD_SIZE)
     far_total = got[:, q_cols : q_cols + local_heads].reshape(tok_dev, local_kv, qgw)

time: 528 us -> 385 us (0.73)
  Pallas kernels: 187 us -> 91.5 us
  waiting for transfers between devices: 297 us -> 204 us
  local copies, waits for them, and re-layouts: 13.6 us -> 34.1 us
  other arithmetic: 3.75 us -> 18.6 us
  starting transfers between devices: 4.97 us -> 14.7 us
    pmax x1 -> x0, waiting for transfers between devices: 107 us -> none  [per_device(): far_max = lax.pmax(local_max, 'blk')]
    pallas_call x1, Pallas kernels: 141 us -> 62.2 us  [per_device(): pl.pallas_call(functools.partial(ctx_kernel, **kw), out_shape=jax.ShapeDt...]
    pallas_call x1, Pallas kernels: 46.4 us -> 29.2 us  [per_device(): pl.pallas_call(functools.partial(max_kernel, **kw), out_shape=jax.ShapeDt...]
    ppermute x0 -> x5, waiting for transfers between devices: none -> 16.2 us  [butterfly_max(): x = jnp.maximum(x, lax.ppermute(x, axis, [(i, i ^ d) for i in range(n)]))]
    max x0 -> x5, other arithmetic: none -> 14.8 us  [butterfly_max(): x = jnp.maximum(x, lax.ppermute(x, axis, [(i, i ^ d) for i in range(n)]))]
    ppermute x0 -> x5, local copies, waits for them, and re-layouts: none -> 9.58 us  [butterfly_max(): x = jnp.maximum(x, lax.ppermute(x, axis, [(i, i ^ d) for i in range(n)]))]
    ppermute x0 -> x5, starting transfers between devices: none -> 9.04 us  [butterfly_max(): x = jnp.maximum(x, lax.ppermute(x, axis, [(i, i ^ d) for i in range(n)]))]
    max x0 -> x4, local copies, waits for them, and re-layouts: none -> 7.47 us  [butterfly_max(): x = jnp.maximum(x, lax.ppermute(x, axis, [(i, i ^ d) for i in range(n)]))]
  transfers between devices with their start and end apart: 6 -> 10, of which waited for: 5 -> 9; matrix products, arithmetic and copies ran while one was open for 2% -> 4% of each run, Pallas kernels for 0% -> 0%
where the time goes in v2:
time: 385 us; the launch traced here: 383 us
  waiting for transfers between devices  204 us (53%)
  Pallas kernels  91.5 us (24%)
  local copies, waits for them, and re-layouts  34.1 us (9%)
  other arithmetic  18.6 us (5%)
  starting transfers between devices  14.7 us (4%)
  between operations  13.4 us (3%)
  matrix products  6.72 us (2%)
    reduce_scatter x1, waiting for transfers between devices, per_device(): got = lax.psum_scatter(partial, 'blk', scatter_dimension=0, tiled=True)  113 us
    pallas_call x1, Pallas kernels, per_device(): pl.pallas_call(functools.partial(ctx_kernel, **kw), out_shape=jax.ShapeDt...  62.2 us
    all_gather x1, waiting for transfers between devices, per_device(): gathered = lax.all_gather(queries, 'blk', axis=0, tiled=True)  45.3 us
    reduce_scatter x1, waiting for transfers between devices, per_device(): lax.psum_scatter(projected, 'kvh', scatter_dimension=1, tiled=True)  29.5 us
    pallas_call x1, Pallas kernels, per_device(): pl.pallas_call(functools.partial(max_kernel, **kw), out_shape=jax.ShapeDt...  29.2 us
    ppermute x5, waiting for transfers between devices, butterfly_max(): x = jnp.maximum(x, lax.ppermute(x, axis, [(i, i ^ d) for i in range(n)]))  16.2 us
    max x5, other arithmetic, butterfly_max(): x = jnp.maximum(x, lax.ppermute(x, axis, [(i, i ^ d) for i in range(n)]))  14.8 us
    ppermute x5, local copies, waits for them, and re-layouts, butterfly_max(): x = jnp.maximum(x, lax.ppermute(x, axis, [(i, i ^ d) for i in range(n)]))  9.58 us
  transfers between devices with their start and end apart: 10, of which 9 were waited for; matrix products, arithmetic and copies ran while one was open for 4% of the time, Pallas kernels for 0%

profile of v2, /device:TPU:0, one launch (start us, length us, event | category | flops | bytes accessed | tf_op | source)
XLA Modules:
  0.0 383.3 jit_solution(6520209706422626402)
XLA Ops:
  9.3 1.6 gather_fusion.1
  10.9 1.6 gather_fusion
  14.1 1.5 gather_fusion.2
  17.3 2.1 gather_fusion.3
  19.4 45.3 %all-gather.2.cloned.1.call-done.q_ref = bf16[4096,1024]{1,0:T(8,128)(2,1)} async-done(((bf16[128,1024]{1,0:T(8,128)(2,1)}), bf16[4096,1024]{1,0:T(8,128)(2,1)}) %all-gather.2.cloned.1.call-update) | async-done | bytes 8388624 | tf_op jit(solution)/shard_map/all_gather | solution.py:145
  64.8 29.2 %shard_map.91 = f32[4096,8]{1,0:T(8,128)} custom-call(s32[160]{0:T(256)} %select_n.58.lo_ref, s32[160]{0:T(256)} %select_n.60.hi_ref, s32[160]{0:T(256)} %gather_fusion.3, bf16[4096,1024]{1,0:T(8,128)(2,1)} %all-gather.2.cloned.1.call-done.q_ref, bf16[16,256,128]{2,1,0:T(8,128)(2,1)} %bitcast.42), custom_call_target="tpu_custom_call" | custom-call | tf_op jit(solution)/shard_map/pallas_call | solution.py:155
  94.0 2.2 copy.74
  97.6 1.9 copy.75
  99.5 2.4 max.28
  104.0 4.2 %collective-permute-done.1 = f32[4096,8]{0,1:T(8,128)S(1)} collective-permute-done((f32[4096,8]{0,1:T(8,128)S(1)}, f32[4096,8]{0,1:T(8,128)S(1)}, u32[]{:S(2)}, u32[]{:S(2)}) %collective-permute-start.1) | collective-permute-done | bytes 131104 | tf_op jit(solution)/shard_map/ppermute | solution.py:115
  108.2 1.9 copy.77
  110.1 3.1 max.29
  113.2 2.3 copy.78
  115.5 3.0 collective-permute-start.2
  118.5 3.5 collective-permute-done.2
  122.0 2.0 copy.79
  124.0 3.1 max.30
  127.1 2.3 copy.80
  130.7 3.7 collective-permute-done.3
  134.4 1.9 copy.81
  136.3 3.1 max.31
  139.4 2.3 copy.82
  141.7 2.9 collective-permute-start.4
  144.6 3.7 collective-permute-done.4
  148.3 1.9 copy.83
  150.2 3.1 max.32.m_ref
  153.3 62.2 %shard_map.92 = f32[4096,1152]{1,0:T(8,128)} custom-call(s32[160]{0:T(256)} %select_n.58.lo_ref, s32[160]{0:T(256)} %select_n.60.hi_ref, s32[160]{0:T(256)} %gather_fusion.3, bf16[4096,1024]{1,0:T(8,128)(2,1)} %all-gather.2.cloned.1.call-done.q_ref, bf16[16,256,128]{2,1,0:T(8,128)(2,1)} %bitcast.43, bf16[16,128,256]{2,1,0:T(8,128)(2,1)} %v_ref.1, ...), custom_call_target="tpu_custom_call" | custom-call | tf_op jit(solution)/shard_map/pallas_call | solution.py:168
  217.8 4.3 %collective-permute-start.6 = (bf16[128,256]{1,0:T(8,128)(2,1)S(1)}, bf16[128,256]{1,0:T(8,128)(2,1)S(1)}, u32[]{:S(2)}, u32[]{:S(2)}) collective-permute-start(bf16[128,256]{1,0:T(8,128)(2,1)S(1)} %copy-done.8), channel_id=1, source_target_pairs={{0,1},{1,2},{2,3},{3,4},{4,5},{5,6},{6,7},{7,8},{8,9},{9,10},{10,1... | collective-permute-start | bytes 196616 | tf_op jit(solution)/shard_map/ppermute | solution.py:19
  224.4 112.5 %reduce-scatter.3.cloned.1.call-done = f32[128,1152]{1,0:T(8,128)} async-done(((f32[4096,1152]{1,0:T(8,128)}), f32[128,1152]{1,0:T(8,128)}) %reduce-scatter.3.cloned.1.call-update) | async-done | bytes 589840 | tf_op jit(solution)/shard_map/reduce_scatter | solution.py:178
  339.5 6.0 %fusion.13 = f32[128,4096]{1,0:T(8,128)} fusion(bf16[128,1024]{0,1:T(8,128)(2,1)S(1)} %bitcast.44, bf16[1024,4096]{1,0:T(8,128)(2,1)} %param.17), kind=kOutput, calls=%fused_computation.41 | convolution fusion | flops 1073741824 | bytes 10747904 | tf_op jit(solution)/shard_map/dot_general | solution.py:223
  345.5 29.5 %reduce-scatter.5.cloned.1.call-done = f32[128,1024]{1,0:T(8,128)} async-done(((f32[128,4096]{1,0:T(8,128)}), f32[128,1024]{1,0:T(8,128)}) %reduce-scatter.5.cloned.1.call-update) | async-done | bytes 524304 | tf_op jit(solution)/shard_map/reduce_scatter | solution.py:224
  375.0 1.8 convert_element_type.23
  (76 shorter events, 17.9 us)
Async XLA Ops:
  6.5 7.5 %copy-start = (s32[64]{0:T(128)S(1)}, s32[64]{0:T(128)}, u32[]{:S(2)}) copy-start(s32[64]{0:T(128)} %param.16) | copy-start | bytes 772
  6.5 58.2 %all-gather.2.cloned.1.call-start = ((), (), s32[]{:S(2)}) async-start(), calls=%async_computation.2 | async-start | bytes 8650752 | tf_op jit(solution)/shard_map/all_gather | solution.py:145
  7.3 329.6 %reduce-scatter.3.cloned.1.call-start = ((), (), s32[]{:S(2)}) async-start(), calls=%async_computation.3 | async-start | bytes 19464192 | tf_op jit(solution)/shard_map/reduce_scatter | solution.py:178
  14.1 1.8 copy-start.5
  15.6 1.6 copy-start.9
  96.1 1.4 collective-permute-start
  102.5 5.7 %collective-permute-start.1 = (f32[4096,8]{0,1:T(8,128)S(1)}, f32[4096,8]{0,1:T(8,128)S(1)}, u32[]{:S(2)}, u32[]{:S(2)}) collective-permute-start(f32[4096,8]{0,1:T(8,128)S(1)} %copy.76), channel_id=1, source_target_pairs={{0,2},{1,3},{2,0},{3,1},{4,6},{5,7},{6,4},{7,5},{8,10},{9,11},{10,... | collective-permute-start | bytes 393224 | tf_op jit(solution)/shard_map/ppermute | solution.py:115
  113.2 10.8 %copy-start.2 = (f32[4096,8]{1,0:T(8,128)S(1)}, f32[4096,8]{1,0:T(8,128)}, u32[]{:S(2)}) copy-start(f32[4096,8]{1,0:T(8,128)} %max.29) | copy-start | bytes 393220
  115.5 6.5 %collective-permute-start.2 = (f32[4096,8]{0,1:T(8,128)S(1)}, f32[4096,8]{0,1:T(8,128)S(1)}, u32[]{:S(2)}, u32[]{:S(2)}) collective-permute-start(f32[4096,8]{0,1:T(8,128)S(1)} %copy.78), channel_id=1, source_target_pairs={{0,4},{1,5},{2,6},{3,7},{4,0},{5,1},{6,2},{7,3},{8,12},{9,13},{10,... | collective-permute-start | bytes 393224 | tf_op jit(solution)/shard_map/ppermute | solution.py:115
  127.1 9.2 %copy-start.3 = (f32[4096,8]{1,0:T(8,128)S(1)}, f32[4096,8]{1,0:T(8,128)}, u32[]{:S(2)}) copy-start(f32[4096,8]{1,0:T(8,128)} %max.30) | copy-start | bytes 393220
  129.4 5.0 %collective-permute-start.3 = (f32[4096,8]{0,1:T(8,128)S(1)}, f32[4096,8]{0,1:T(8,128)S(1)}, u32[]{:S(2)}, u32[]{:S(2)}) collective-permute-start(f32[4096,8]{0,1:T(8,128)S(1)} %copy.80), channel_id=1, source_target_pairs={{0,8},{1,9},{2,10},{3,11},{4,12},{5,13},{6,14},{7,15},{8,0},{9,1},... | collective-permute-start | bytes 393224 | tf_op jit(solution)/shard_map/ppermute | solution.py:115
  139.4 10.7 %copy-start.4 = (f32[4096,8]{1,0:T(8,128)S(1)}, f32[4096,8]{1,0:T(8,128)}, u32[]{:S(2)}) copy-start(f32[4096,8]{1,0:T(8,128)} %max.31) | copy-start | bytes 393220
  141.7 6.5 %collective-permute-start.4 = (f32[4096,8]{0,1:T(8,128)S(1)}, f32[4096,8]{0,1:T(8,128)S(1)}, u32[]{:S(2)}, u32[]{:S(2)}) collective-permute-start(f32[4096,8]{0,1:T(8,128)S(1)} %copy.82), channel_id=1, source_target_pairs={{0,16},{1,17},{2,18},{3,19},{4,20},{5,21},{6,22},{7,23},{8,24},{9,... | collective-permute-start | bytes 393224 | tf_op jit(solution)/shard_map/ppermute | solution.py:115
  215.5 0.8 copy-start.7
  215.5 2.3 copy-start.8
  215.5 7.0 %copy-start.6 = (bf16[128,1024]{1,0:T(8,128)(2,1)S(1)}, bf16[128,1024]{1,0:T(8,128)(2,1)}, u32[]{:S(2)}) copy-start(bf16[128,1024]{1,0:T(8,128)(2,1)} %param.9) | copy-start | bytes 786436
  215.5 159.5 %reduce-scatter.5.cloned.1.call-start = ((), (), s32[]{:S(2)}) async-start(), calls=%async_computation.4 | async-start | bytes 2621440 | tf_op jit(solution)/shard_map/reduce_scatter | solution.py:224
  216.5 6.4 %collective-permute-start.5 = (bf16[128,256]{0,1:T(8,128)(2,1)S(1)}, bf16[128,256]{0,1:T(8,128)(2,1)S(1)}, u32[]{:S(2)}, u32[]{:S(2)}) collective-permute-start(bf16[128,256]{0,1:T(8,128)(2,1)S(1)} %copy.85), channel_id=1, source_target_pairs={{0,1},{1,2},{2,3},{3,4},{4,5},{5,6},{6,7},{7,8},{8,9},{9,10},{10,1... | collective-permute-start | bytes 196616 | tf_op jit(solution)/shard_map/ppermute | solution.py:19
  217.8 5.0 %collective-permute-start.6 = (bf16[128,256]{1,0:T(8,128)(2,1)S(1)}, bf16[128,256]{1,0:T(8,128)(2,1)S(1)}, u32[]{:S(2)}, u32[]{:S(2)}) collective-permute-start(bf16[128,256]{1,0:T(8,128)(2,1)S(1)} %copy-done.8), channel_id=1, source_target_pairs={{0,1},{1,2},{2,3},{3,4},{4,5},{5,6},{6,7},{7,8},{8,9},{9,10},{10,1... | collective-permute-start | bytes 196616 | tf_op jit(solution)/shard_map/ppermute | solution.py:19
  339.5 37.3 %copy-start.1 = (s32[64]{0:T(128)S(1)}, s32[64]{0:T(128)}, u32[]{:S(2)}) copy-start(s32[64]{0:T(128)} %param.16) | copy-start | bytes 772
Sparse Core Ops, SparseCore 0:
  9.6 55.1 all-gather.1
  215.7 121.2 reduce-scatter.2
  345.6 29.3 reduce-scatter.4

commit v3 on v2

--- a/solution.py
+++ b/solution.py
@@ -56,17 +56,15 @@
     return (rows >= lo) & (rows < hi)
 
 
-def _slot_keys(kt_ref, blk_ref, base, kv):
-    cols = slice(kv * HEAD_SIZE, (kv + 1) * HEAD_SIZE)
-    return jnp.concatenate([kt_ref[blk_ref[base + s], cols, :] for s in range(SLOTS)], axis=1)
-
-
-def _slot_values(v_ref, blk_ref, base, kv):
-    cols = slice(kv * HEAD_SIZE, (kv + 1) * HEAD_SIZE)
-    return jnp.concatenate([v_ref[blk_ref[base + s], :, cols] for s in range(SLOTS)], axis=0)
-
-
-def max_kernel(lo_ref, hi_ref, blk_ref, q_ref, kt_ref, m_ref, *, heads, qgw, scale):
+def _slot_keys(kt_ref, blk_ref, base):
+    return jnp.concatenate([kt_ref[blk_ref[base + s]] for s in range(SLOTS)], axis=1)
+
+
+def _slot_values(v_ref, blk_ref, base):
+    return jnp.concatenate([v_ref[blk_ref[base + s]] for s in range(SLOTS)], axis=0)
+
+
+def max_kernel(lo_ref, hi_ref, blk_ref, q_ref, kt_ref, m_ref, *, heads, scale):
     i = pl.program_id(0)
     tile = q_ref.shape[0]
     base = i * SLOTS
@@ -74,18 +72,16 @@
     mask = _slot_mask(lo_ref, hi_ref, base, rows)
     lane = lax.broadcasted_iota(jnp.int32, (1, STAT_LANES), 1)
     stats = jnp.full((tile, STAT_LANES), -jnp.inf, jnp.float32)
-    for kv in range(heads // qgw):
-        keys = _slot_keys(kt_ref, blk_ref, base, kv)
-        for j in range(qgw):
-            h = kv * qgw + j
-            q = q_ref[:, h * HEAD_SIZE : (h + 1) * HEAD_SIZE]
-            sc = jnp.dot(q, keys, preferred_element_type=jnp.float32) * scale
-            mx = jnp.max(jnp.where(mask, sc, -jnp.inf), axis=1, keepdims=True)
-            stats = jnp.where(lane == h, mx, stats)
-    m_ref[...] = stats[:, :heads]
-
-
-def ctx_kernel(lo_ref, hi_ref, blk_ref, q_ref, kt_ref, v_ref, m_ref, o_ref, *, heads, qgw, scale):
+    keys = _slot_keys(kt_ref, blk_ref, base)
+    for h in range(heads):
+        q = q_ref[:, h * HEAD_SIZE : (h + 1) * HEAD_SIZE]
+        sc = jnp.dot(q, keys, preferred_element_type=jnp.float32) * scale
+        mx = jnp.max(jnp.where(mask, sc, -jnp.inf), axis=1, keepdims=True)
+        stats = jnp.where(lane == h, mx, stats)
+    m_ref[...] = jnp.transpose(stats)[: m_ref.shape[0], :]
+
+
+def ctx_kernel(lo_ref, hi_ref, blk_ref, q_ref, kt_ref, v_ref, m_ref, o_ref, t_ref, *, heads, scale):
     i = pl.program_id(0)
     tile = q_ref.shape[0]
     base = i * SLOTS
@@ -93,28 +89,65 @@
     mask = _slot_mask(lo_ref, hi_ref, base, rows)
     lane = lax.broadcasted_iota(jnp.int32, (1, STAT_LANES), 1)
     totals = jnp.zeros((tile, STAT_LANES), jnp.float32)
-    top = m_ref[...]
-    for kv in range(heads // qgw):
-        keys = _slot_keys(kt_ref, blk_ref, base, kv)
-        values = _slot_values(v_ref, blk_ref, base, kv)
-        for j in range(qgw):
-            h = kv * qgw + j
-            q = q_ref[:, h * HEAD_SIZE : (h + 1) * HEAD_SIZE]
-            sc = jnp.dot(q, keys, preferred_element_type=jnp.float32) * scale
-            p = jnp.exp(jnp.where(mask, sc - top[:, h : h + 1], -jnp.inf))
-            ctx = jnp.dot(p.astype(jnp.bfloat16), values, preferred_element_type=jnp.float32)
-            o_ref[:, h * HEAD_SIZE : (h + 1) * HEAD_SIZE] = ctx
-            totals = jnp.where(lane == h, jnp.sum(p, axis=1, keepdims=True), totals)
-    o_ref[:, heads * HEAD_SIZE :] = totals
-
-
-def butterfly_max(x, axis):
+    top = jnp.transpose(m_ref[...])
+    keys = _slot_keys(kt_ref, blk_ref, base)
+    values = _slot_values(v_ref, blk_ref, base)
+    for h in range(heads):
+        q = q_ref[:, h * HEAD_SIZE : (h + 1) * HEAD_SIZE]
+        sc = jnp.dot(q, keys, preferred_element_type=jnp.float32) * scale
+        p = jnp.exp(jnp.where(mask, sc - top[:, h : h + 1], -jnp.inf))
+        ctx = jnp.dot(p.astype(jnp.bfloat16), values, preferred_element_type=jnp.float32)
+        o_ref[:, h * HEAD_SIZE : (h + 1) * HEAD_SIZE] = ctx
+        totals = jnp.where(lane == h, jnp.sum(p, axis=1, keepdims=True), totals)
+    t_ref[...] = jnp.transpose(totals)[: t_ref.shape[0], :]
+
+
+def butterfly(x, axis, combine):
     n = lax.axis_size(axis)
     d = 1
     while d < n:
-        x = jnp.maximum(x, lax.ppermute(x, axis, [(i, i ^ d) for i in range(n)]))
+        x = combine(x, lax.ppermute(x, axis, [(i, i ^ d) for i in range(n)]))
         d *= 2
     return x
+
+
+def far_part(queries_kv, keys_t, values, lo, hi, blk, kv, heads, blk_index, scale):
+    tok_dev, q_cols = queries_kv.shape
+    blocks, _, block_len = keys_t.shape
+    gathered = lax.all_gather(queries_kv, "blk", axis=0, tiled=True)
+    row_count = gathered.shape[0]
+    n_tiles = row_count // tok_dev
+    stat_rows = 8
+    q_spec = pl.BlockSpec((tok_dev, q_cols), lambda i, *_: (i, 0))
+    kt_spec = pl.BlockSpec((blocks, HEAD_SIZE, block_len), lambda i, *_: (0, kv, 0))
+    v_spec = pl.BlockSpec((blocks, block_len, HEAD_SIZE), lambda i, *_: (0, 0, kv))
+    s_spec = pl.BlockSpec((stat_rows, tok_dev), lambda i, *_: (i, 0))
+    stat_shape = jax.ShapeDtypeStruct((n_tiles * stat_rows, tok_dev), jnp.float32)
+    kw = dict(heads=heads, scale=scale)
+    local_max = pl.pallas_call(
+        functools.partial(max_kernel, **kw),
+        out_shape=stat_shape,
+        grid_spec=pltpu.PrefetchScalarGridSpec(
+            num_scalar_prefetch=3, grid=(n_tiles,), in_specs=[q_spec, kt_spec], out_specs=s_spec
+        ),
+    )(lo, hi, blk, gathered, keys_t)
+    far_max = butterfly(local_max, "blk", jnp.maximum)
+    partial, totals = pl.pallas_call(
+        functools.partial(ctx_kernel, **kw),
+        out_shape=(jax.ShapeDtypeStruct((row_count, q_cols), jnp.float32), stat_shape),
+        grid_spec=pltpu.PrefetchScalarGridSpec(
+            num_scalar_prefetch=3,
+            grid=(n_tiles,),
+            in_specs=[q_spec, kt_spec, v_spec, s_spec],
+            out_specs=(pl.BlockSpec((tok_dev, q_cols), lambda i, *_: (i, 0)), s_spec),
+        ),
+    )(lo, hi, blk, gathered, keys_t, values, far_max)
+    context = lax.psum_scatter(partial, "blk", scatter_dimension=0, tiled=True)
+    totals = butterfly(totals, "blk", jnp.add)
+    own = lambda a: jnp.transpose(
+        lax.dynamic_slice_in_dim(a, blk_index * stat_rows, stat_rows, 0)[:heads]
+    )
+    return context, own(totals), own(far_max)
 
 
 def per_device(
@@ -142,43 +175,28 @@
     tile = tok_dev
     n_tiles = row_count // tile
 
-    gathered = lax.all_gather(queries, "blk", axis=0, tiled=True)
     lo, hi, blk = tile_tables(suffix_len, request_group, block_group, n_tiles, tile)
-
-    q_spec = pl.BlockSpec((tile, q_cols), lambda i, *_: (i, 0))
-    kv_spec = pl.BlockSpec((blocks, block_len, kv_cols), lambda i, *_: (0, 0, 0))
-    kt_spec = pl.BlockSpec((blocks, kv_cols, block_len), lambda i, *_: (0, 0, 0))
     keys_t = jnp.swapaxes(prefix_block_keys, 1, 2)
-    m_spec = pl.BlockSpec((tile, local_heads), lambda i, *_: (i, 0))
-    kw = dict(heads=local_heads, qgw=qgw, scale=scale)
-
-    local_max = pl.pallas_call(
-        functools.partial(max_kernel, **kw),
-        out_shape=jax.ShapeDtypeStruct((row_count, local_heads), jnp.float32),
-        grid_spec=pltpu.PrefetchScalarGridSpec(
-            num_scalar_prefetch=3,
-            grid=(n_tiles,),
-            in_specs=[q_spec, kt_spec],
-            out_specs=m_spec,
-        ),
-    )(lo, hi, blk, gathered, keys_t)
-    far_max = butterfly_max(local_max, "blk")
-
-    width = q_cols + STAT_LANES
-    partial = pl.pallas_call(
-        functools.partial(ctx_kernel, **kw),
-        out_shape=jax.ShapeDtypeStruct((row_count, width), jnp.float32),
-        grid_spec=pltpu.PrefetchScalarGridSpec(
-            num_scalar_prefetch=3,
-            grid=(n_tiles,),
-            in_specs=[q_spec, kt_spec, kv_spec, m_spec],
-            out_specs=pl.BlockSpec((tile, width), lambda i, *_: (i, 0)),
-        ),
-    )(lo, hi, blk, gathered, keys_t, prefix_block_values, far_max)
-    got = lax.psum_scatter(partial, "blk", scatter_dimension=0, tiled=True)
-    far_context = got[:, :q_cols].reshape(tok_dev, local_kv, qgw, HEAD_SIZE)
-    far_total = got[:, q_cols : q_cols + local_heads].reshape(tok_dev, local_kv, qgw)
-    own_far_max = lax.dynamic_slice_in_dim(far_max, blk_index * tok_dev, tok_dev, 0).reshape(
+    parts = [
+        far_part(
+            queries[:, kv * qgw * HEAD_SIZE : (kv + 1) * qgw * HEAD_SIZE],
+            keys_t,
+            prefix_block_values,
+            lo,
+            hi,
+            blk,
+            kv,
+            qgw,
+            blk_index,
+            scale,
+        )
+        for kv in range(local_kv)
+    ]
+    far_context = jnp.concatenate([c for c, _, _ in parts], axis=1).reshape(
+        tok_dev, local_kv, qgw, HEAD_SIZE
+    )
+    far_total = jnp.concatenate([t for _, t, _ in parts], axis=1).reshape(tok_dev, local_kv, qgw)
+    own_far_max = jnp.concatenate([m for _, _, m in parts], axis=1).reshape(
         tok_dev, local_kv, qgw
     )
 

time: 385 us -> 386 us (level)
  Pallas kernels: 91.5 us -> 124 us
  waiting for transfers between devices: 204 us -> 173 us
  starting transfers between devices: 14.7 us -> 44.1 us
  local copies, waits for them, and re-layouts: 34.1 us -> 14.4 us
  other arithmetic: 18.6 us -> 8.24 us
    reduce_scatter x1 -> x2, waiting for transfers between devices: 113 us -> 55.2 us  [far_part(): context = lax.psum_scatter(partial, 'blk', scatter_dimension=0, tiled=True)]
    ppermute x5 -> x20, waiting for transfers between devices: 16.2 us -> 50.8 us  [butterfly(): x = combine(x, lax.ppermute(x, axis, [(i, i ^ d) for i in range(n)]))]
    pallas_call x2 -> x4, Pallas kernels: 91.5 us -> 124 us  [the longest x2 73.9 us: far_part(): pl.pallas_call(functools.partial(ctx_kernel, **kw), out_shape=(jax.ShapeD...]
    ppermute x5 -> x20, starting transfers between devices: 9.04 us -> 40.2 us  [butterfly(): x = combine(x, lax.ppermute(x, axis, [(i, i ^ d) for i in range(n)]))]
    max x5 -> x10, other arithmetic: 14.8 us -> 3.31 us  [butterfly(): x = combine(x, lax.ppermute(x, axis, [(i, i ^ d) for i in range(n)]))]
    ppermute x5 -> x0, local copies, waits for them, and re-layouts: 9.58 us -> none  [butterfly_max(): x = jnp.maximum(x, lax.ppermute(x, axis, [(i, i ^ d) for i in range(n)]))]
    all_gather x1 -> x2, waiting for transfers between devices: 45.3 us -> 36.9 us  [far_part(): gathered = lax.all_gather(queries_kv, 'blk', axis=0, tiled=True)]
    max x4 -> x0, local copies, waits for them, and re-layouts: 7.47 us -> none  [butterfly_max(): x = jnp.maximum(x, lax.ppermute(x, axis, [(i, i ^ d) for i in range(n)]))]
  transfers between devices with their start and end apart: 10 -> 27, of which waited for: 9 -> 20; matrix products, arithmetic and copies ran while one was open for 4% -> 5% of each run, Pallas kernels for 0% -> 32%
where the time goes in v3:
time: 386 us; the launch traced here: 384 us
  waiting for transfers between devices  173 us (45%)
  Pallas kernels  124 us (32%)
  starting transfers between devices  44.1 us (11%)
  local copies, waits for them, and re-layouts  14.4 us (4%)
  between operations  13.5 us (3%)
  other arithmetic  8.24 us (2%)
  matrix products  6.71 us (2%)
    pallas_call x2, Pallas kernels, far_part(): pl.pallas_call(functools.partial(ctx_kernel, **kw), out_shape=(jax.ShapeD...  73.9 us
    reduce_scatter x2, waiting for transfers between devices, far_part(): context = lax.psum_scatter(partial, 'blk', scatter_dimension=0, tiled=True)  55.2 us
    ppermute x20, waiting for transfers between devices, butterfly(): x = combine(x, lax.ppermute(x, axis, [(i, i ^ d) for i in range(n)]))  50.8 us
    pallas_call x2, Pallas kernels, far_part(): pl.pallas_call(functools.partial(max_kernel, **kw), out_shape=stat_shape,...  49.6 us
    ppermute x20, starting transfers between devices, butterfly(): x = combine(x, lax.ppermute(x, axis, [(i, i ^ d) for i in range(n)]))  40.2 us
    all_gather x2, waiting for transfers between devices, far_part(): gathered = lax.all_gather(queries_kv, 'blk', axis=0, tiled=True)  36.9 us
    reduce_scatter x1, waiting for transfers between devices, per_device(): lax.psum_scatter(projected, 'kvh', scatter_dimension=1, tiled=True)  29.4 us
  transfers between devices with their start and end apart: 27, of which 20 were waited for; matrix products, arithmetic and copies ran while one was open for 5% of the time, Pallas kernels for 32%

profile of v3, /device:TPU:0, one launch (start us, length us, event | category | flops | bytes accessed | tf_op | source)
XLA Modules:
  0.0 383.6 jit_solution(10240766046033670346)
XLA Ops:
  19.0 2.1 gather_fusion.3
  21.2 36.9 %all-gather.5.cloned.1.call-done.q_ref = bf16[4096,512]{1,0:T(8,128)(2,1)} async-done(((bf16[128,512]{1,0:T(8,128)(2,1)}), bf16[4096,512]{1,0:T(8,128)(2,1)}) %all-gather.5.cloned.1.call-update) | async-done | bytes 4194320 | tf_op jit(solution)/shard_map/all_gather | solution.py:117
  58.0 24.8 %shard_map.93 = f32[256,128]{1,0:T(8,128)} custom-call(s32[160]{0:T(256)} %select_n.61.lo_ref, s32[160]{0:T(256)} %select_n.63.hi_ref, s32[160]{0:T(256)} %gather_fusion.3, bf16[4096,512]{1,0:T(8,128)(2,1)} %all-gather.5.cloned.1.call-done.q_ref, bf16[16,256,128]{2,1,0:T(8,128)(2,1)} %bitcast.50), custom_call_target="tpu_custom_call" | custom-call | tf_op jit(solution)/shard_map/pallas_call | solution.py:127
  86.5 4.5 %collective-permute-done.6 = f32[256,128]{1,0:T(8,128)S(1)} collective-permute-done((f32[256,128]{1,0:T(8,128)S(1)}, f32[256,128]{1,0:T(8,128)S(1)}, u32[]{:S(2)}, u32[]{:S(2)}) %collective-permute-start.6) | collective-permute-done | bytes 131104 | tf_op jit(solution)/shard_map/ppermute | solution.py:109
  91.0 2.2 collective-permute-start.7
  93.3 6.9 %collective-permute-done.7 = f32[256,128]{1,0:T(8,128)S(1)} collective-permute-done((f32[256,128]{1,0:T(8,128)S(1)}, f32[256,128]{1,0:T(8,128)S(1)}, u32[]{:S(2)}, u32[]{:S(2)}) %collective-permute-start.7) | collective-permute-done | bytes 131104 | tf_op jit(solution)/shard_map/ppermute | solution.py:109
  100.2 2.3 collective-permute-start.8
  102.5 3.5 collective-permute-done.8
  106.0 2.7 collective-permute-start.9
  108.7 3.9 %collective-permute-done.9 = f32[256,128]{1,0:T(8,128)S(1)} collective-permute-done((f32[256,128]{1,0:T(8,128)S(1)}, f32[256,128]{1,0:T(8,128)S(1)}, u32[]{:S(2)}, u32[]{:S(2)}) %collective-permute-start.9) | collective-permute-done | bytes 131104 | tf_op jit(solution)/shard_map/ppermute | solution.py:109
  113.3 36.9 %shard_map.94 = (f32[4096,512]{1,0:T(8,128)}, f32[256,128]{1,0:T(8,128)}) custom-call(s32[160]{0:T(256)} %select_n.61.lo_ref, s32[160]{0:T(256)} %select_n.63.hi_ref, s32[160]{0:T(256)} %gather_fusion.3, bf16[4096,512]{1,0:T(8,128)(2,1)} %all-gather.5.cloned.1.call-done.q_ref, bf16[16,256,128]{2,1,0:T(8,128)(2,1)} %bitcast.51, bf16[16,128,256]{2,1,0:T(8,128)(2,1)} %v_ref.3, ...), custom_call_target="tpu_custom_call" | custom-call | tf_op jit(solution)/shard_map/pallas_call | solution.py:135
  150.3 24.9 %shard_map.91 = f32[256,128]{1,0:T(8,128)} custom-call(s32[160]{0:T(256)} %select_n.61.lo_ref, s32[160]{0:T(256)} %select_n.63.hi_ref, s32[160]{0:T(256)} %gather_fusion.3, bf16[4096,512]{1,0:T(8,128)(2,1)} %all-gather.3.cloned.1.call-done.q_ref, bf16[16,256,128]{2,1,0:T(8,128)(2,1)} %bitcast.52), custom_call_target="tpu_custom_call" | custom-call | tf_op jit(solution)/shard_map/pallas_call | solution.py:127
  178.1 5.3 %collective-permute-done.1 = f32[256,128]{1,0:T(8,128)S(1)} collective-permute-done((f32[256,128]{1,0:T(8,128)S(1)}, f32[256,128]{1,0:T(8,128)S(1)}, u32[]{:S(2)}, u32[]{:S(2)}) %collective-permute-start.1) | collective-permute-done | bytes 131104 | tf_op jit(solution)/shard_map/ppermute | solution.py:109
  185.0 4.9 %collective-permute-done.2 = f32[256,128]{1,0:T(8,128)S(1)} collective-permute-done((f32[256,128]{1,0:T(8,128)S(1)}, f32[256,128]{1,0:T(8,128)S(1)}, u32[]{:S(2)}, u32[]{:S(2)}) %collective-permute-start.2) | collective-permute-done | bytes 131104 | tf_op jit(solution)/shard_map/ppermute | solution.py:109
  191.6 3.4 collective-permute-done.3
  195.0 3.0 collective-permute-start.4
  198.0 4.1 %collective-permute-done.4 = f32[256,128]{1,0:T(8,128)S(1)} collective-permute-done((f32[256,128]{1,0:T(8,128)S(1)}, f32[256,128]{1,0:T(8,128)S(1)}, u32[]{:S(2)}, u32[]{:S(2)}) %collective-permute-start.4) | collective-permute-done | bytes 131104 | tf_op jit(solution)/shard_map/ppermute | solution.py:109
  202.7 36.9 %shard_map.92 = (f32[4096,512]{1,0:T(8,128)}, f32[256,128]{1,0:T(8,128)}) custom-call(s32[160]{0:T(256)} %select_n.61.lo_ref, s32[160]{0:T(256)} %select_n.63.hi_ref, s32[160]{0:T(256)} %gather_fusion.3, bf16[4096,512]{1,0:T(8,128)(2,1)} %all-gather.3.cloned.1.call-done.q_ref, bf16[16,256,128]{2,1,0:T(8,128)(2,1)} %bitcast.53, bf16[16,128,256]{2,1,0:T(8,128)(2,1)} %v_ref.3, ...), custom_call_target="tpu_custom_call" | custom-call | tf_op jit(solution)/shard_map/pallas_call | solution.py:135
  241.1 2.5 collective-permute-start.10
  246.1 2.7 collective-permute-start.18
  249.7 3.4 collective-permute-done.18
  253.1 3.9 %collective-permute-start.19 = (f32[256,128]{1,0:T(8,128)S(1)}, f32[256,128]{1,0:T(8,128)S(1)}, u32[]{:S(2)}, u32[]{:S(2)}) collective-permute-start(f32[256,128]{1,0:T(8,128)S(1)} %add.164), channel_id=1, source_target_pairs={{0,4},{1,5},{2,6},{3,7},{4,0},{5,1},{6,2},{7,3},{8,12},{9,13},{10,... | collective-permute-start | bytes 393224 | tf_op jit(solution)/shard_map/ppermute | solution.py:109
  257.1 2.8 collective-permute-start.14
  260.6 2.0 collective-permute-done.19
  262.6 4.7 %collective-permute-start.20 = (f32[256,128]{1,0:T(8,128)S(1)}, f32[256,128]{1,0:T(8,128)S(1)}, u32[]{:S(2)}, u32[]{:S(2)}) collective-permute-start(f32[256,128]{1,0:T(8,128)S(1)} %add.165), channel_id=1, source_target_pairs={{0,8},{1,9},{2,10},{3,11},{4,12},{5,13},{6,14},{7,15},{8,0},{9,1},... | collective-permute-start | bytes 393224 | tf_op jit(solution)/shard_map/ppermute | solution.py:109
  269.1 2.1 collective-permute-done.20
  271.1 5.4 %collective-permute-start.21 = (f32[256,128]{1,0:T(8,128)S(1)}, f32[256,128]{1,0:T(8,128)S(1)}, u32[]{:S(2)}, u32[]{:S(2)}) collective-permute-start(f32[256,128]{1,0:T(8,128)S(1)} %add.166), channel_id=1, source_target_pairs={{0,16},{1,17},{2,18},{3,19},{4,20},{5,21},{6,22},{7,23},{8,24},{9,... | collective-permute-start | bytes 393224 | tf_op jit(solution)/shard_map/ppermute | solution.py:109
  276.5 2.8 collective-permute-start.16
  281.2 1.9 collective-permute-done.16
  283.1 55.1 %reduce-scatter.4.cloned.1.call-done = f32[128,512]{1,0:T(8,128)} async-done(((f32[4096,512]{1,0:T(8,128)}), f32[128,512]{1,0:T(8,128)}) %reduce-scatter.4.cloned.1.call-update) | async-done | bytes 262160 | tf_op jit(solution)/shard_map/reduce_scatter | solution.py:145
  339.9 6.0 %fusion.14 = f32[128,4096]{1,0:T(8,128)} fusion(bf16[128,1024]{0,1:T(8,128)(2,1)S(1)} %bitcast.54, bf16[1024,4096]{1,0:T(8,128)(2,1)} %param.17), kind=kOutput, calls=%fused_computation.52 | convolution fusion | flops 1073741824 | bytes 10747904 | tf_op jit(solution)/shard_map/dot_general | solution.py:241
  345.9 29.4 %reduce-scatter.8.cloned.1.call-done = f32[128,1024]{1,0:T(8,128)} async-done(((f32[128,4096]{1,0:T(8,128)}), f32[128,1024]{1,0:T(8,128)}) %reduce-scatter.8.cloned.1.call-update) | async-done | bytes 524304 | tf_op jit(solution)/shard_map/reduce_scatter | solution.py:242
  (120 shorter events, 36.5 us)
Async XLA Ops:
  6.5 9.3 %copy-start = (s32[64]{0:T(128)S(1)}, s32[64]{0:T(128)}, u32[]{:S(2)}) copy-start(s32[64]{0:T(128)} %param.16) | copy-start | bytes 772
  6.5 51.5 %all-gather.5.cloned.1.call-start = ((), (), s32[]{:S(2)}) async-start(), calls=%async_computation.5 | async-start | bytes 4325376 | tf_op jit(solution)/shard_map/all_gather | solution.py:117
  8.2 142.0 %all-gather.3.cloned.1.call-start = ((), (), s32[]{:S(2)}) async-start(), calls=%async_computation.3 | async-start | bytes 4325376 | tf_op jit(solution)/shard_map/all_gather | solution.py:117
  9.0 274.1 %reduce-scatter.6.cloned.1.call-start = ((), (), s32[]{:S(2)}) async-start(), calls=%async_computation.6 | async-start | bytes 8650752 | tf_op jit(solution)/shard_map/reduce_scatter | solution.py:145
  82.8 1.6 collective-permute-start.5
  85.3 5.7 %collective-permute-start.6 = (f32[256,128]{1,0:T(8,128)S(1)}, f32[256,128]{1,0:T(8,128)S(1)}, u32[]{:S(2)}, u32[]{:S(2)}) collective-permute-start(f32[256,128]{1,0:T(8,128)S(1)} %max.48), channel_id=1, source_target_pairs={{0,2},{1,3},{2,0},{3,1},{4,6},{5,7},{6,4},{7,5},{8,10},{9,11},{10,... | collective-permute-start | bytes 393224 | tf_op jit(solution)/shard_map/ppermute | solution.py:109
  91.0 9.2 %collective-permute-start.7 = (f32[256,128]{1,0:T(8,128)S(1)}, f32[256,128]{1,0:T(8,128)S(1)}, u32[]{:S(2)}, u32[]{:S(2)}) collective-permute-start(f32[256,128]{1,0:T(8,128)S(1)} %max.49), channel_id=1, source_target_pairs={{0,4},{1,5},{2,6},{3,7},{4,0},{5,1},{6,2},{7,3},{8,12},{9,13},{10,... | collective-permute-start | bytes 393224 | tf_op jit(solution)/shard_map/ppermute | solution.py:109
  100.2 5.8 %collective-permute-start.8 = (f32[256,128]{1,0:T(8,128)S(1)}, f32[256,128]{1,0:T(8,128)S(1)}, u32[]{:S(2)}, u32[]{:S(2)}) collective-permute-start(f32[256,128]{1,0:T(8,128)S(1)} %max.50), channel_id=1, source_target_pairs={{0,8},{1,9},{2,10},{3,11},{4,12},{5,13},{6,14},{7,15},{8,0},{9,1},... | collective-permute-start | bytes 393224 | tf_op jit(solution)/shard_map/ppermute | solution.py:109
  106.0 6.6 %collective-permute-start.9 = (f32[256,128]{1,0:T(8,128)S(1)}, f32[256,128]{1,0:T(8,128)S(1)}, u32[]{:S(2)}, u32[]{:S(2)}) collective-permute-start(f32[256,128]{1,0:T(8,128)S(1)} %max.51), channel_id=1, source_target_pairs={{0,16},{1,17},{2,18},{3,19},{4,20},{5,21},{6,22},{7,23},{8,24},{9,... | collective-permute-start | bytes 393224 | tf_op jit(solution)/shard_map/ppermute | solution.py:109
  150.2 188.0 %reduce-scatter.4.cloned.1.call-start = ((), (), s32[]{:S(2)}) async-start(), calls=%async_computation.4 | async-start | bytes 8650752 | tf_op jit(solution)/shard_map/reduce_scatter | solution.py:145
  175.2 64.5 %copy-start.6 = (bf16[128,256]{1,0:T(8,128)(2,1)S(1)}, bf16[128,256]{1,0:T(8,128)(2,1)}, u32[]{:S(2)}) copy-start(bf16[128,256]{1,0:T(8,128)(2,1)} %param.11) | copy-start | bytes 196612
  175.2 65.8 %copy-start.5 = (bf16[128,256]{1,0:T(8,128)(2,1)S(1)}, bf16[128,256]{1,0:T(8,128)(2,1)}, u32[]{:S(2)}) copy-start(bf16[128,256]{1,0:T(8,128)(2,1)} %param.10) | copy-start | bytes 196612
  175.2 1.6 collective-permute-start
  177.7 66.3 %copy-start.2 = (bf16[128,1024]{1,0:T(8,128)(2,1)S(1)}, bf16[128,1024]{1,0:T(8,128)(2,1)}, u32[]{:S(2)}) copy-start(bf16[128,1024]{1,0:T(8,128)(2,1)} %param.9) | copy-start | bytes 786436
  177.7 5.6 %collective-permute-start.1 = (f32[256,128]{1,0:T(8,128)S(1)}, f32[256,128]{1,0:T(8,128)S(1)}, u32[]{:S(2)}, u32[]{:S(2)}) collective-permute-start(f32[256,128]{1,0:T(8,128)S(1)} %max.43), channel_id=1, source_target_pairs={{0,2},{1,3},{2,0},{3,1},{4,6},{5,7},{6,4},{7,5},{8,10},{9,11},{10,... | collective-permute-start | bytes 393224 | tf_op jit(solution)/shard_map/ppermute | solution.py:109
  183.4 6.6 %collective-permute-start.2 = (f32[256,128]{1,0:T(8,128)S(1)}, f32[256,128]{1,0:T(8,128)S(1)}, u32[]{:S(2)}, u32[]{:S(2)}) collective-permute-start(f32[256,128]{1,0:T(8,128)S(1)} %max.44), channel_id=1, source_target_pairs={{0,4},{1,5},{2,6},{3,7},{4,0},{5,1},{6,2},{7,3},{8,12},{9,13},{10,... | collective-permute-start | bytes 393224 | tf_op jit(solution)/shard_map/ppermute | solution.py:109
  189.9 54.6 %copy-start.3 = (f32[256,128]{1,0:T(8,128)S(1)}, f32[256,128]{1,0:T(8,128)}, u32[]{:S(2)}) copy-start(f32[256,128]{1,0:T(8,128)} %get-tuple-element.12) | copy-start | bytes 393220
  189.9 5.0 %collective-permute-start.3 = (f32[256,128]{1,0:T(8,128)S(1)}, f32[256,128]{1,0:T(8,128)S(1)}, u32[]{:S(2)}, u32[]{:S(2)}) collective-permute-start(f32[256,128]{1,0:T(8,128)S(1)} %max.45), channel_id=1, source_target_pairs={{0,8},{1,9},{2,10},{3,11},{4,12},{5,13},{6,14},{7,15},{8,0},{9,1},... | collective-permute-start | bytes 393224 | tf_op jit(solution)/shard_map/ppermute | solution.py:109
  195.0 7.0 %collective-permute-start.4 = (f32[256,128]{1,0:T(8,128)S(1)}, f32[256,128]{1,0:T(8,128)S(1)}, u32[]{:S(2)}, u32[]{:S(2)}) collective-permute-start(f32[256,128]{1,0:T(8,128)S(1)} %max.46), channel_id=1, source_target_pairs={{0,16},{1,17},{2,18},{3,19},{4,20},{5,21},{6,22},{7,23},{8,24},{9,... | collective-permute-start | bytes 393224 | tf_op jit(solution)/shard_map/ppermute | solution.py:109
  239.7 135.7 %reduce-scatter.8.cloned.1.call-start = ((), (), s32[]{:S(2)}) async-start(), calls=%async_computation.7 | async-start | bytes 2621440 | tf_op jit(solution)/shard_map/reduce_scatter | solution.py:242
  239.7 9.2 %collective-permute-start.11 = (bf16[128,256]{1,0:T(8,128)(2,1)S(1)}, bf16[128,256]{1,0:T(8,128)(2,1)S(1)}, u32[]{:S(2)}, u32[]{:S(2)}) collective-permute-start(bf16[128,256]{1,0:T(8,128)(2,1)S(1)} %copy-done.6), channel_id=1, source_target_pairs={{0,1},{1,2},{2,3},{3,4},{4,5},{5,6},{6,7},{7,8},{8,9},{9,10},{10,1... | collective-permute-start | bytes 196616 | tf_op jit(solution)/shard_map/ppermute | solution.py:19
  241.1 3.4 collective-permute-start.10
  244.5 1.5 collective-permute-start.17
  245.1 3.7 collective-permute-start.12
  246.1 7.0 %collective-permute-start.18 = (f32[256,128]{1,0:T(8,128)S(1)}, f32[256,128]{1,0:T(8,128)S(1)}, u32[]{:S(2)}, u32[]{:S(2)}) collective-permute-start(f32[256,128]{1,0:T(8,128)S(1)} %add.163), channel_id=1, source_target_pairs={{0,2},{1,3},{2,0},{3,1},{4,6},{5,7},{6,4},{7,5},{8,10},{9,11},{10,... | collective-permute-start | bytes 393224 | tf_op jit(solution)/shard_map/ppermute | solution.py:109
  248.8 8.3 %collective-permute-start.13 = (f32[256,128]{1,0:T(8,128)S(1)}, f32[256,128]{1,0:T(8,128)S(1)}, u32[]{:S(2)}, u32[]{:S(2)}) collective-permute-start(f32[256,128]{1,0:T(8,128)S(1)} %add.158), channel_id=1, source_target_pairs={{0,2},{1,3},{2,0},{3,1},{4,6},{5,7},{6,4},{7,5},{8,10},{9,11},{10,... | collective-permute-start | bytes 393224 | tf_op jit(solution)/shard_map/ppermute | solution.py:109
  253.1 9.5 %collective-permute-start.19 = (f32[256,128]{1,0:T(8,128)S(1)}, f32[256,128]{1,0:T(8,128)S(1)}, u32[]{:S(2)}, u32[]{:S(2)}) collective-permute-start(f32[256,128]{1,0:T(8,128)S(1)} %add.164), channel_id=1, source_target_pairs={{0,4},{1,5},{2,6},{3,7},{4,0},{5,1},{6,2},{7,3},{8,12},{9,13},{10,... | collective-permute-start | bytes 393224 | tf_op jit(solution)/shard_map/ppermute | solution.py:109
  257.1 10.2 %collective-permute-start.14 = (f32[256,128]{1,0:T(8,128)S(1)}, f32[256,128]{1,0:T(8,128)S(1)}, u32[]{:S(2)}, u32[]{:S(2)}) collective-permute-start(f32[256,128]{1,0:T(8,128)S(1)} %add.159), channel_id=1, source_target_pairs={{0,4},{1,5},{2,6},{3,7},{4,0},{5,1},{6,2},{7,3},{8,12},{9,13},{10,... | collective-permute-start | bytes 393224 | tf_op jit(solution)/shard_map/ppermute | solution.py:109
  262.6 8.5 %collective-permute-start.20 = (f32[256,128]{1,0:T(8,128)S(1)}, f32[256,128]{1,0:T(8,128)S(1)}, u32[]{:S(2)}, u32[]{:S(2)}) collective-permute-start(f32[256,128]{1,0:T(8,128)S(1)} %add.165), channel_id=1, source_target_pairs={{0,8},{1,9},{2,10},{3,11},{4,12},{5,13},{6,14},{7,15},{8,0},{9,1},... | collective-permute-start | bytes 393224 | tf_op jit(solution)/shard_map/ppermute | solution.py:109
  267.3 9.2 %collective-permute-start.15 = (f32[256,128]{1,0:T(8,128)S(1)}, f32[256,128]{1,0:T(8,128)S(1)}, u32[]{:S(2)}, u32[]{:S(2)}) collective-permute-start(f32[256,128]{1,0:T(8,128)S(1)} %add.160), channel_id=1, source_target_pairs={{0,8},{1,9},{2,10},{3,11},{4,12},{5,13},{6,14},{7,15},{8,0},{9,1},... | collective-permute-start | bytes 393224 | tf_op jit(solution)/shard_map/ppermute | solution.py:109
  271.1 10.1 %collective-permute-start.21 = (f32[256,128]{1,0:T(8,128)S(1)}, f32[256,128]{1,0:T(8,128)S(1)}, u32[]{:S(2)}, u32[]{:S(2)}) collective-permute-start(f32[256,128]{1,0:T(8,128)S(1)} %add.166), channel_id=1, source_target_pairs={{0,16},{1,17},{2,18},{3,19},{4,20},{5,21},{6,22},{7,23},{8,24},{9,... | collective-permute-start | bytes 393224 | tf_op jit(solution)/shard_map/ppermute | solution.py:109
  276.5 6.6 %collective-permute-start.16 = (f32[256,128]{1,0:T(8,128)S(1)}, f32[256,128]{1,0:T(8,128)S(1)}, u32[]{:S(2)}, u32[]{:S(2)}) collective-permute-start(f32[256,128]{1,0:T(8,128)S(1)} %add.161), channel_id=1, source_target_pairs={{0,16},{1,17},{2,18},{3,19},{4,20},{5,21},{6,22},{7,23},{8,24},{9,... | collective-permute-start | bytes 393224 | tf_op jit(solution)/shard_map/ppermute | solution.py:109
  (3 other events, 10.3 us)
Sparse Core Ops, SparseCore 0:
  9.6 48.4 all-gather.4
  60.3 46.9 all-gather.2
  150.4 92.3 reduce-scatter.5
  246.3 91.9 reduce-scatter.3
  346.0 29.2 reduce-scatter.7

commit v4 on v3

--- a/solution.py
+++ b/solution.py
@@ -56,15 +56,17 @@
     return (rows >= lo) & (rows < hi)
 
 
-def _slot_keys(kt_ref, blk_ref, base):
-    return jnp.concatenate([kt_ref[blk_ref[base + s]] for s in range(SLOTS)], axis=1)
-
-
-def _slot_values(v_ref, blk_ref, base):
-    return jnp.concatenate([v_ref[blk_ref[base + s]] for s in range(SLOTS)], axis=0)
-
-
-def max_kernel(lo_ref, hi_ref, blk_ref, q_ref, kt_ref, m_ref, *, heads, scale):
+def _slot_keys(kt_ref, blk_ref, base, kv):
+    cols = slice(kv * HEAD_SIZE, (kv + 1) * HEAD_SIZE)
+    return jnp.concatenate([kt_ref[blk_ref[base + s], cols, :] for s in range(SLOTS)], axis=1)
+
+
+def _slot_values(v_ref, blk_ref, base, kv):
+    cols = slice(kv * HEAD_SIZE, (kv + 1) * HEAD_SIZE)
+    return jnp.concatenate([v_ref[blk_ref[base + s], :, cols] for s in range(SLOTS)], axis=0)
+
+
+def max_kernel(lo_ref, hi_ref, blk_ref, q_ref, kt_ref, m_ref, *, heads, qgw, scale):
     i = pl.program_id(0)
     tile = q_ref.shape[0]
     base = i * SLOTS
@@ -72,8 +74,9 @@
     mask = _slot_mask(lo_ref, hi_ref, base, rows)
     lane = lax.broadcasted_iota(jnp.int32, (1, STAT_LANES), 1)
     stats = jnp.full((tile, STAT_LANES), -jnp.inf, jnp.float32)
-    keys = _slot_keys(kt_ref, blk_ref, base)
     for h in range(heads):
+        if h % qgw == 0:
+            keys = _slot_keys(kt_ref, blk_ref, base, h // qgw)
         q = q_ref[:, h * HEAD_SIZE : (h + 1) * HEAD_SIZE]
         sc = jnp.dot(q, keys, preferred_element_type=jnp.float32) * scale
         mx = jnp.max(jnp.where(mask, sc, -jnp.inf), axis=1, keepdims=True)
@@ -81,7 +84,9 @@
     m_ref[...] = jnp.transpose(stats)[: m_ref.shape[0], :]
 
 
-def ctx_kernel(lo_ref, hi_ref, blk_ref, q_ref, kt_ref, v_ref, m_ref, o_ref, t_ref, *, heads, scale):
+def ctx_kernel(
+    lo_ref, hi_ref, blk_ref, q_ref, kt_ref, v_ref, m_ref, o_ref, t_ref, *, heads, qgw, scale
+):
     i = pl.program_id(0)
     tile = q_ref.shape[0]
     base = i * SLOTS
@@ -90,9 +95,10 @@
     lane = lax.broadcasted_iota(jnp.int32, (1, STAT_LANES), 1)
     totals = jnp.zeros((tile, STAT_LANES), jnp.float32)
     top = jnp.transpose(m_ref[...])
-    keys = _slot_keys(kt_ref, blk_ref, base)
-    values = _slot_values(v_ref, blk_ref, base)
     for h in range(heads):
+        if h % qgw == 0:
+            keys = _slot_keys(kt_ref, blk_ref, base, h // qgw)
+            values = _slot_values(v_ref, blk_ref, base, h // qgw)
         q = q_ref[:, h * HEAD_SIZE : (h + 1) * HEAD_SIZE]
         sc = jnp.dot(q, keys, preferred_element_type=jnp.float32) * scale
         p = jnp.exp(jnp.where(mask, sc - top[:, h : h + 1], -jnp.inf))
@@ -111,19 +117,20 @@
     return x
 
 
-def far_part(queries_kv, keys_t, values, lo, hi, blk, kv, heads, blk_index, scale):
-    tok_dev, q_cols = queries_kv.shape
-    blocks, _, block_len = keys_t.shape
-    gathered = lax.all_gather(queries_kv, "blk", axis=0, tiled=True)
+def far_part(queries, keys_t, values, lo, hi, blk, qgw, blk_index, scale):
+    tok_dev, q_cols = queries.shape
+    heads = q_cols // HEAD_SIZE
+    blocks, kv_cols, block_len = keys_t.shape
+    gathered = lax.all_gather(queries, "blk", axis=0, tiled=True)
     row_count = gathered.shape[0]
     n_tiles = row_count // tok_dev
     stat_rows = 8
     q_spec = pl.BlockSpec((tok_dev, q_cols), lambda i, *_: (i, 0))
-    kt_spec = pl.BlockSpec((blocks, HEAD_SIZE, block_len), lambda i, *_: (0, kv, 0))
-    v_spec = pl.BlockSpec((blocks, block_len, HEAD_SIZE), lambda i, *_: (0, 0, kv))
+    kt_spec = pl.BlockSpec((blocks, kv_cols, block_len), lambda i, *_: (0, 0, 0))
+    v_spec = pl.BlockSpec((blocks, block_len, kv_cols), lambda i, *_: (0, 0, 0))
     s_spec = pl.BlockSpec((stat_rows, tok_dev), lambda i, *_: (i, 0))
     stat_shape = jax.ShapeDtypeStruct((n_tiles * stat_rows, tok_dev), jnp.float32)
-    kw = dict(heads=heads, scale=scale)
+    kw = dict(heads=heads, qgw=qgw, scale=scale)
     local_max = pl.pallas_call(
         functools.partial(max_kernel, **kw),
         out_shape=stat_shape,
@@ -148,6 +155,17 @@
         lax.dynamic_slice_in_dim(a, blk_index * stat_rows, stat_rows, 0)[:heads]
     )
     return context, own(totals), own(far_max)
+
+
+def column_sum(x, axis):
+    n = lax.axis_size(axis)
+    me = lax.axis_index(axis)
+    width = x.shape[1] // n
+    chunk = lambda k: lax.dynamic_slice_in_dim(x, (k % n) * width, width, 1)
+    total = chunk(me)
+    for d in range(1, n):
+        total = total + lax.ppermute(chunk(me + d), axis, [(i, (i + d) % n) for i in range(n)])
+    return total
 
 
 def per_device(
@@ -177,28 +195,12 @@
 
     lo, hi, blk = tile_tables(suffix_len, request_group, block_group, n_tiles, tile)
     keys_t = jnp.swapaxes(prefix_block_keys, 1, 2)
-    parts = [
-        far_part(
-            queries[:, kv * qgw * HEAD_SIZE : (kv + 1) * qgw * HEAD_SIZE],
-            keys_t,
-            prefix_block_values,
-            lo,
-            hi,
-            blk,
-            kv,
-            qgw,
-            blk_index,
-            scale,
-        )
-        for kv in range(local_kv)
-    ]
-    far_context = jnp.concatenate([c for c, _, _ in parts], axis=1).reshape(
-        tok_dev, local_kv, qgw, HEAD_SIZE
-    )
-    far_total = jnp.concatenate([t for _, t, _ in parts], axis=1).reshape(tok_dev, local_kv, qgw)
-    own_far_max = jnp.concatenate([m for _, _, m in parts], axis=1).reshape(
-        tok_dev, local_kv, qgw
-    )
+    far_context, far_total, own_far_max = far_part(
+        queries, keys_t, prefix_block_values, lo, hi, blk, qgw, blk_index, scale
+    )
+    far_context = far_context.reshape(tok_dev, local_kv, qgw, HEAD_SIZE)
+    far_total = far_total.reshape(tok_dev, local_kv, qgw)
+    own_far_max = own_far_max.reshape(tok_dev, local_kv, qgw)
 
     row_ends = jnp.cumsum(suffix_len)
     starts = row_ends - suffix_len
@@ -239,7 +241,7 @@
     denominator = far_total * far_scale + near_total
     attention = (context / denominator[..., None]).reshape(tok_dev, q_cols).astype(jnp.bfloat16)
     projected = jnp.dot(attention, w_out, preferred_element_type=jnp.float32)
-    return lax.psum_scatter(projected, "kvh", scatter_dimension=1, tiled=True).astype(jnp.bfloat16)
+    return column_sum(projected, "kvh").astype(jnp.bfloat16)
 
 
 def solution(mesh):

time: 386 us -> 346 us (0.90)
  Pallas kernels: 124 us -> 95.2 us
  starting transfers between devices: 44.1 us -> 27.7 us
  waiting for transfers between devices: 173 us -> 182 us
    reduce_scatter x1 -> x0, waiting for transfers between devices: 29.4 us -> none  [per_device(): lax.psum_scatter(projected, 'kvh', scatter_dimension=1, tiled=True)]
    reduce_scatter x2 -> x1, waiting for transfers between devices: 55.2 us -> 82.9 us  [far_part(): context = lax.psum_scatter(partial, 'blk', scatter_dimension=0, tiled=True)]
    ppermute x20 -> x10, starting transfers between devices: 40.2 us -> 16.5 us  [butterfly(): x = combine(x, lax.ppermute(x, axis, [(i, i ^ d) for i in range(n)]))]
    ppermute x0 -> x3, waiting for transfers between devices: none -> 20.4 us  [column_sum(): lax.ppermute(chunk(me + d), axis, [(i, (i + d) % n) for i in range(n)])]
    pallas_call x2 -> x1, Pallas kernels: 49.6 us -> 29.8 us  [far_part(): pl.pallas_call(functools.partial(max_kernel, **kw), out_shape=stat_shape,...]
    ppermute x20 -> x10, waiting for transfers between devices: 50.8 us -> 32.6 us  [butterfly(): x = combine(x, lax.ppermute(x, axis, [(i, i ^ d) for i in range(n)]))]
    pallas_call x2 -> x1, Pallas kernels: 73.9 us -> 65.4 us  [far_part(): pl.pallas_call(functools.partial(ctx_kernel, **kw), out_shape=(jax.ShapeD...]
    all_gather x2 -> x1, waiting for transfers between devices: 36.9 us -> 45.3 us  [far_part(): gathered = lax.all_gather(queries, 'blk', axis=0, tiled=True)]
  transfers between devices with their start and end apart: 27 -> 17, of which waited for: 20 -> 14; matrix products, arithmetic and copies ran while one was open for 5% -> 4% of each run, Pallas kernels for 32% -> 0%
where the time goes in v4:
time: 346 us; the launch traced here: 345 us
  waiting for transfers between devices  182 us (53%)
  Pallas kernels  95.2 us (28%)
  starting transfers between devices  27.7 us (8%)
  local copies, waits for them, and re-layouts  15 us (4%)
  between operations  13.7 us (4%)
  other arithmetic  5.75 us (2%)
  matrix products  5.36 us (2%)
    reduce_scatter x1, waiting for transfers between devices, far_part(): context = lax.psum_scatter(partial, 'blk', scatter_dimension=0, tiled=True)  82.9 us
    pallas_call x1, Pallas kernels, far_part(): pl.pallas_call(functools.partial(ctx_kernel, **kw), out_shape=(jax.ShapeD...  65.4 us
    all_gather x1, waiting for transfers between devices, far_part(): gathered = lax.all_gather(queries, 'blk', axis=0, tiled=True)  45.3 us
    ppermute x10, waiting for transfers between devices, butterfly(): x = combine(x, lax.ppermute(x, axis, [(i, i ^ d) for i in range(n)]))  32.6 us
    pallas_call x1, Pallas kernels, far_part(): pl.pallas_call(functools.partial(max_kernel, **kw), out_shape=stat_shape,...  29.8 us
    ppermute x3, waiting for transfers between devices, column_sum(): lax.ppermute(chunk(me + d), axis, [(i, (i + d) % n) for i in range(n)])  20.4 us
    ppermute x10, starting transfers between devices, butterfly(): x = combine(x, lax.ppermute(x, axis, [(i, i ^ d) for i in range(n)]))  16.5 us
  transfers between devices with their start and end apart: 17, of which 14 were waited for; matrix products, arithmetic and copies ran while one was open for 4% of the time, Pallas kernels for 0%

profile of v4, /device:TPU:0, one launch (start us, length us, event | category | flops | bytes accessed | tf_op | source)
XLA Modules:
  0.0 344.7 jit_solution(2025051350813928193)
XLA Ops:
  9.3 1.6 gather_fusion.1
  10.9 1.6 gather_fusion
  14.1 1.5 gather_fusion.2
  15.9 1.3 copy.26
  17.4 2.1 gather_fusion.3
  19.5 45.3 %all-gather.2.cloned.1.call-done.q_ref = bf16[4096,1024]{1,0:T(8,128)(2,1)} async-done(((bf16[128,1024]{1,0:T(8,128)(2,1)}), bf16[4096,1024]{1,0:T(8,128)(2,1)}) %all-gather.2.cloned.1.call-update) | async-done | bytes 8388624 | tf_op jit(solution)/shard_map/all_gather | solution.py:124
  64.8 29.8 %shard_map.91 = f32[256,128]{1,0:T(8,128)} custom-call(s32[160]{0:T(256)} %select_n.90.lo_ref, s32[160]{0:T(256)} %select_n.92.hi_ref, s32[160]{0:T(256)} %gather_fusion.3, bf16[4096,1024]{1,0:T(8,128)(2,1)} %all-gather.2.cloned.1.call-done.q_ref, bf16[16,256,128]{2,1,0:T(8,128)(2,1)} %bitcast.46), custom_call_target="tpu_custom_call" | custom-call | tf_op jit(solution)/shard_map/pallas_call | solution.py:134
  97.1 1.5 collective-permute-start.1
  98.6 4.2 %collective-permute-done.1 = f32[256,128]{1,0:T(8,128)S(1)} collective-permute-done((f32[256,128]{1,0:T(8,128)S(1)}, f32[256,128]{1,0:T(8,128)S(1)}, u32[]{:S(2)}, u32[]{:S(2)}) %collective-permute-start.1) | collective-permute-done | bytes 131104 | tf_op jit(solution)/shard_map/ppermute | solution.py:115
  102.8 3.1 collective-permute-start.2
  105.9 3.5 %collective-permute-done.2 = f32[256,128]{1,0:T(8,128)S(1)} collective-permute-done((f32[256,128]{1,0:T(8,128)S(1)}, f32[256,128]{1,0:T(8,128)S(1)}, u32[]{:S(2)}, u32[]{:S(2)}) %collective-permute-start.2) | collective-permute-done | bytes 131104 | tf_op jit(solution)/shard_map/ppermute | solution.py:115
  109.4 1.3 collective-permute-start.3
  110.7 3.7 %collective-permute-done.3 = f32[256,128]{1,0:T(8,128)S(1)} collective-permute-done((f32[256,128]{1,0:T(8,128)S(1)}, f32[256,128]{1,0:T(8,128)S(1)}, u32[]{:S(2)}, u32[]{:S(2)}) %collective-permute-start.3) | collective-permute-done | bytes 131104 | tf_op jit(solution)/shard_map/ppermute | solution.py:115
  114.5 2.9 collective-permute-start.4
  117.3 3.7 %collective-permute-done.4 = f32[256,128]{1,0:T(8,128)S(1)} collective-permute-done((f32[256,128]{1,0:T(8,128)S(1)}, f32[256,128]{1,0:T(8,128)S(1)}, u32[]{:S(2)}, u32[]{:S(2)}) %collective-permute-start.4) | collective-permute-done | bytes 131104 | tf_op jit(solution)/shard_map/ppermute | solution.py:115
  121.7 65.4 %shard_map.92 = (f32[4096,1024]{1,0:T(8,128)}, f32[256,128]{1,0:T(8,128)}) custom-call(s32[160]{0:T(256)} %select_n.90.lo_ref, s32[160]{0:T(256)} %select_n.92.hi_ref, s32[160]{0:T(256)} %gather_fusion.3, bf16[4096,1024]{1,0:T(8,128)(2,1)} %all-gather.2.cloned.1.call-done.q_ref, bf16[16,256,128]{2,1,0:T(8,128)(2,1)} %bitcast.47, ...), custom_call_target="tpu_custom_call" | custom-call | tf_op jit(solution)/shard_map/pallas_call | solution.py:142
  189.4 4.1 %collective-permute-start.6 = (bf16[128,256]{1,0:T(8,128)(2,1)S(1)}, bf16[128,256]{1,0:T(8,128)(2,1)S(1)}, u32[]{:S(2)}, u32[]{:S(2)}) collective-permute-start(bf16[128,256]{1,0:T(8,128)(2,1)S(1)} %copy-done.5), channel_id=1, source_target_pairs={{0,1},{1,2},{2,3},{3,4},{4,5},{5,6},{6,7},{7,8},{8,9},{9,10},{10,1... | collective-permute-start | bytes 196616 | tf_op jit(solution)/shard_map/ppermute | solution.py:19
  195.1 2.2 collective-permute-start.8
  197.7 3.4 collective-permute-done.8
  201.1 3.0 collective-permute-start.9
  204.5 3.1 collective-permute-done.9
  208.6 4.1 %collective-permute-done.10 = f32[256,128]{1,0:T(8,128)S(1)} collective-permute-done((f32[256,128]{1,0:T(8,128)S(1)}, f32[256,128]{1,0:T(8,128)S(1)}, u32[]{:S(2)}, u32[]{:S(2)}) %collective-permute-start.10) | collective-permute-done | bytes 131104 | tf_op jit(solution)/shard_map/ppermute | solution.py:115
  212.8 2.0 collective-permute-start.11
  215.0 4.4 %collective-permute-done.11 = f32[256,128]{1,0:T(8,128)S(1)} collective-permute-done((f32[256,128]{1,0:T(8,128)S(1)}, f32[256,128]{1,0:T(8,128)S(1)}, u32[]{:S(2)}, u32[]{:S(2)}) %collective-permute-start.11) | collective-permute-done | bytes 131104 | tf_op jit(solution)/shard_map/ppermute | solution.py:115
  219.3 82.9 %reduce-scatter.2.cloned.1.call-done = f32[128,1024]{1,0:T(8,128)} async-done(((f32[4096,1024]{1,0:T(8,128)}), f32[128,1024]{1,0:T(8,128)}) %reduce-scatter.2.cloned.1.call-update) | async-done | bytes 524304 | tf_op jit(solution)/shard_map/reduce_scatter | solution.py:152
  303.8 4.7 %fusion.13 = f32[128,4096]{1,0:T(8,128)S(1)} fusion(bf16[128,1024]{0,1:T(8,128)(2,1)S(1)} %bitcast.48, bf16[1024,4096]{1,0:T(8,128)(2,1)} %param.17), kind=kOutput, calls=%fused_computation.46 | convolution fusion | flops 1073741824 | bytes 10747904 | tf_op jit(solution)/shard_map/dot_general | solution.py:243
  309.6 1.6 collective-permute-start.12
  311.2 2.9 collective-permute-start.13
  314.0 1.3 collective-permute-start.14
  315.4 9.3 %collective-permute-done.12 = f32[128,1024]{1,0:T(8,128)S(1)} collective-permute-done((f32[128,1024]{1,0:T(8,128)}, f32[128,1024]{1,0:T(8,128)S(1)}, u32[]{:S(2)}, u32[]{:S(2)}) %collective-permute-start.12) | collective-permute-done | bytes 524320 | tf_op jit(solution)/shard_map/ppermute | solution.py:167
  324.7 11.1 %collective-permute-done.13 = f32[128,1024]{1,0:T(8,128)} collective-permute-done((f32[128,1024]{1,0:T(8,128)}, f32[128,1024]{1,0:T(8,128)}, u32[]{:S(2)}, u32[]{:S(2)}) %collective-permute-start.13) | collective-permute-done | bytes 524320 | tf_op jit(solution)/shard_map/ppermute | solution.py:167
  335.7 2.1 add_convert_fusion
  (75 shorter events, 16.3 us)
Async XLA Ops:
  6.5 7.6 %copy-start = (s32[64]{0:T(128)S(1)}, s32[64]{0:T(128)}, u32[]{:S(2)}) copy-start(s32[64]{0:T(128)} %param.16) | copy-start | bytes 772
  6.5 58.2 %all-gather.2.cloned.1.call-start = ((), (), s32[]{:S(2)}) async-start(), calls=%async_computation.1 | async-start | bytes 8650752 | tf_op jit(solution)/shard_map/all_gather | solution.py:124
  7.3 295.0 %reduce-scatter.2.cloned.1.call-start = ((), (), s32[]{:S(2)}) async-start(), calls=%async_computation.2 | async-start | bytes 17301504 | tf_op jit(solution)/shard_map/reduce_scatter | solution.py:152
  14.1 1.8 copy-start.1
  14.1 3.1 copy-start.6
  94.6 1.6 collective-permute-start
  97.1 5.7 %collective-permute-start.1 = (f32[256,128]{1,0:T(8,128)S(1)}, f32[256,128]{1,0:T(8,128)S(1)}, u32[]{:S(2)}, u32[]{:S(2)}) collective-permute-start(f32[256,128]{1,0:T(8,128)S(1)} %max.28), channel_id=1, source_target_pairs={{0,2},{1,3},{2,0},{3,1},{4,6},{5,7},{6,4},{7,5},{8,10},{9,11},{10,... | collective-permute-start | bytes 393224 | tf_op jit(solution)/shard_map/ppermute | solution.py:115
  102.8 6.6 %collective-permute-start.2 = (f32[256,128]{1,0:T(8,128)S(1)}, f32[256,128]{1,0:T(8,128)S(1)}, u32[]{:S(2)}, u32[]{:S(2)}) collective-permute-start(f32[256,128]{1,0:T(8,128)S(1)} %max.29), channel_id=1, source_target_pairs={{0,4},{1,5},{2,6},{3,7},{4,0},{5,1},{6,2},{7,3},{8,12},{9,13},{10,... | collective-permute-start | bytes 393224 | tf_op jit(solution)/shard_map/ppermute | solution.py:115
  109.4 5.0 %collective-permute-start.3 = (f32[256,128]{1,0:T(8,128)S(1)}, f32[256,128]{1,0:T(8,128)S(1)}, u32[]{:S(2)}, u32[]{:S(2)}) collective-permute-start(f32[256,128]{1,0:T(8,128)S(1)} %max.30), channel_id=1, source_target_pairs={{0,8},{1,9},{2,10},{3,11},{4,12},{5,13},{6,14},{7,15},{8,0},{9,1},... | collective-permute-start | bytes 393224 | tf_op jit(solution)/shard_map/ppermute | solution.py:115
  114.5 6.6 %collective-permute-start.4 = (f32[256,128]{1,0:T(8,128)S(1)}, f32[256,128]{1,0:T(8,128)S(1)}, u32[]{:S(2)}, u32[]{:S(2)}) collective-permute-start(f32[256,128]{1,0:T(8,128)S(1)} %max.31), channel_id=1, source_target_pairs={{0,16},{1,17},{2,18},{3,19},{4,20},{5,21},{6,22},{7,23},{8,24},{9,... | collective-permute-start | bytes 393224 | tf_op jit(solution)/shard_map/ppermute | solution.py:115
  187.1 0.8 copy-start.4
  187.1 2.3 copy-start.5
  187.1 6.5 %copy-start.3 = (f32[256,128]{1,0:T(8,128)S(1)}, f32[256,128]{1,0:T(8,128)}, u32[]{:S(2)}) copy-start(f32[256,128]{1,0:T(8,128)} %get-tuple-element.8) | copy-start | bytes 393220
  187.1 10.4 %copy-start.2 = (bf16[128,1024]{1,0:T(8,128)(2,1)S(1)}, bf16[128,1024]{1,0:T(8,128)(2,1)}, u32[]{:S(2)}) copy-start(bf16[128,1024]{1,0:T(8,128)(2,1)} %param.9) | copy-start | bytes 786436
  188.0 9.7 %collective-permute-start.5 = (bf16[128,256]{0,1:T(8,128)(2,1)S(1)}, bf16[128,256]{0,1:T(8,128)(2,1)S(1)}, u32[]{:S(2)}, u32[]{:S(2)}) collective-permute-start(bf16[128,256]{0,1:T(8,128)(2,1)S(1)} %copy.27), channel_id=1, source_target_pairs={{0,1},{1,2},{2,3},{3,4},{4,5},{5,6},{6,7},{7,8},{8,9},{9,10},{10,1... | collective-permute-start | bytes 196616 | tf_op jit(solution)/shard_map/ppermute | solution.py:19
  189.4 18.4 %collective-permute-start.6 = (bf16[128,256]{1,0:T(8,128)(2,1)S(1)}, bf16[128,256]{1,0:T(8,128)(2,1)S(1)}, u32[]{:S(2)}, u32[]{:S(2)}) collective-permute-start(bf16[128,256]{1,0:T(8,128)(2,1)S(1)} %copy-done.5), channel_id=1, source_target_pairs={{0,1},{1,2},{2,3},{3,4},{4,5},{5,6},{6,7},{7,8},{8,9},{9,10},{10,1... | collective-permute-start | bytes 196616 | tf_op jit(solution)/shard_map/ppermute | solution.py:19
  193.6 1.5 collective-permute-start.7
  195.1 6.0 %collective-permute-start.8 = (f32[256,128]{1,0:T(8,128)S(1)}, f32[256,128]{1,0:T(8,128)S(1)}, u32[]{:S(2)}, u32[]{:S(2)}) collective-permute-start(f32[256,128]{1,0:T(8,128)S(1)} %add.180), channel_id=1, source_target_pairs={{0,2},{1,3},{2,0},{3,1},{4,6},{5,7},{6,4},{7,5},{8,10},{9,11},{10,... | collective-permute-start | bytes 393224 | tf_op jit(solution)/shard_map/ppermute | solution.py:115
  201.1 6.6 %collective-permute-start.9 = (f32[256,128]{1,0:T(8,128)S(1)}, f32[256,128]{1,0:T(8,128)S(1)}, u32[]{:S(2)}, u32[]{:S(2)}) collective-permute-start(f32[256,128]{1,0:T(8,128)S(1)} %add.181), channel_id=1, source_target_pairs={{0,4},{1,5},{2,6},{3,7},{4,0},{5,1},{6,2},{7,3},{8,12},{9,13},{10,... | collective-permute-start | bytes 393224 | tf_op jit(solution)/shard_map/ppermute | solution.py:115
  207.7 5.0 %collective-permute-start.10 = (f32[256,128]{1,0:T(8,128)S(1)}, f32[256,128]{1,0:T(8,128)S(1)}, u32[]{:S(2)}, u32[]{:S(2)}) collective-permute-start(f32[256,128]{1,0:T(8,128)S(1)} %add.182), channel_id=1, source_target_pairs={{0,8},{1,9},{2,10},{3,11},{4,12},{5,13},{6,14},{7,15},{8,0},{9,1},... | collective-permute-start | bytes 393224 | tf_op jit(solution)/shard_map/ppermute | solution.py:115
  212.8 6.6 %collective-permute-start.11 = (f32[256,128]{1,0:T(8,128)S(1)}, f32[256,128]{1,0:T(8,128)S(1)}, u32[]{:S(2)}, u32[]{:S(2)}) collective-permute-start(f32[256,128]{1,0:T(8,128)S(1)} %add.183), channel_id=1, source_target_pairs={{0,16},{1,17},{2,18},{3,19},{4,20},{5,21},{6,22},{7,23},{8,24},{9,... | collective-permute-start | bytes 393224 | tf_op jit(solution)/shard_map/ppermute | solution.py:115
  309.6 15.0 %collective-permute-start.12 = (f32[128,1024]{1,0:T(8,128)}, f32[128,1024]{1,0:T(8,128)S(1)}, u32[]{:S(2)}, u32[]{:S(2)}) collective-permute-start(f32[128,1024]{1,0:T(8,128)} %get-tuple-element.13), channel_id=1, source_target_pairs={{0,32},{32,64},{64,96},{96,0},{1,33},{33,65},{65,97},{97,1},{2,34}... | collective-permute-start | bytes 1572872 | tf_op jit(solution)/shard_map/ppermute | solution.py:167
  311.2 24.6 %collective-permute-start.13 = (f32[128,1024]{1,0:T(8,128)}, f32[128,1024]{1,0:T(8,128)}, u32[]{:S(2)}, u32[]{:S(2)}) collective-permute-start(f32[128,1024]{1,0:T(8,128)} %get-tuple-element.15), channel_id=1, source_target_pairs={{0,64},{32,96},{64,0},{96,32},{1,65},{33,97},{65,1},{97,33},{2,66}... | collective-permute-start | bytes 1572872 | tf_op jit(solution)/shard_map/ppermute | solution.py:167
  314.0 21.7 %collective-permute-start.14 = (f32[128,1024]{1,0:T(8,128)S(1)}, f32[128,1024]{1,0:T(8,128)}, u32[]{:S(2)}, u32[]{:S(2)}) collective-permute-start(f32[128,1024]{1,0:T(8,128)S(1)} %get-tuple-element.14), channel_id=1, source_target_pairs={{0,96},{32,0},{64,32},{96,64},{1,97},{33,1},{65,33},{97,65},{2,98}... | collective-permute-start | bytes 1572872 | tf_op jit(solution)/shard_map/ppermute | solution.py:167
Sparse Core Ops, SparseCore 0:
  9.6 55.1 all-gather.1
  187.3 114.9 reduce-scatter.1

commit v5 on v4

--- a/solution.py
+++ b/solution.py
@@ -43,68 +43,70 @@
         jnp.where(owns, jnp.arange(blocks, dtype=jnp.int32)[None, :], 0), axis=1
     ).astype(jnp.int32)
     blk = block_of_group[request_group[req_v]].astype(jnp.int32)
-    return lo.reshape(-1), hi.reshape(-1), blk.reshape(-1)
-
-
-def _slot_mask(lo_ref, hi_ref, base, rows):
-    seg = lax.broadcasted_iota(jnp.int32, (1, SLOTS * HEAD_SIZE), 1) // HEAD_SIZE
-    lo = jnp.zeros(seg.shape, jnp.int32)
-    hi = jnp.zeros(seg.shape, jnp.int32)
-    for s in range(SLOTS):
-        lo = jnp.where(seg == s, lo_ref[base + s], lo)
-        hi = jnp.where(seg == s, hi_ref[base + s], hi)
-    return (rows >= lo) & (rows < hi)
-
-
-def _slot_keys(kt_ref, blk_ref, base, kv):
-    cols = slice(kv * HEAD_SIZE, (kv + 1) * HEAD_SIZE)
-    return jnp.concatenate([kt_ref[blk_ref[base + s], cols, :] for s in range(SLOTS)], axis=1)
-
-
-def _slot_values(v_ref, blk_ref, base, kv):
-    cols = slice(kv * HEAD_SIZE, (kv + 1) * HEAD_SIZE)
-    return jnp.concatenate([v_ref[blk_ref[base + s], :, cols] for s in range(SLOTS)], axis=0)
-
-
-def max_kernel(lo_ref, hi_ref, blk_ref, q_ref, kt_ref, m_ref, *, heads, qgw, scale):
+    count = jnp.minimum(last - first + 1, SLOTS).astype(jnp.int32)
+    return lo.reshape(-1), hi.reshape(-1), blk.reshape(-1), count
+
+
+def max_kernel(lo_ref, hi_ref, blk_ref, cnt_ref, q_ref, kt_ref, m_ref, *, heads, qgw, scale):
     i = pl.program_id(0)
     tile = q_ref.shape[0]
     base = i * SLOTS
     rows = i * tile + lax.broadcasted_iota(jnp.int32, (tile, 1), 0)
-    mask = _slot_mask(lo_ref, hi_ref, base, rows)
     lane = lax.broadcasted_iota(jnp.int32, (1, STAT_LANES), 1)
     stats = jnp.full((tile, STAT_LANES), -jnp.inf, jnp.float32)
     for h in range(heads):
-        if h % qgw == 0:
-            keys = _slot_keys(kt_ref, blk_ref, base, h // qgw)
+        kv = h // qgw
         q = q_ref[:, h * HEAD_SIZE : (h + 1) * HEAD_SIZE]
-        sc = jnp.dot(q, keys, preferred_element_type=jnp.float32) * scale
-        mx = jnp.max(jnp.where(mask, sc, -jnp.inf), axis=1, keepdims=True)
-        stats = jnp.where(lane == h, mx, stats)
+
+        def body(s, top):
+            j = blk_ref[base + s]
+            inside = (rows >= lo_ref[base + s]) & (rows < hi_ref[base + s])
+            keys = kt_ref[j, kv * HEAD_SIZE : (kv + 1) * HEAD_SIZE, :]
+            sc = jnp.dot(q, keys, preferred_element_type=jnp.float32)
+            mx = jnp.max(sc, axis=1, keepdims=True) * scale
+            return jnp.where(inside, mx, top)
+
+        top = lax.fori_loop(0, cnt_ref[i], body, jnp.full((tile, 1), -jnp.inf, jnp.float32))
+        stats = jnp.where(lane == h, top, stats)
     m_ref[...] = jnp.transpose(stats)[: m_ref.shape[0], :]
 
 
 def ctx_kernel(
-    lo_ref, hi_ref, blk_ref, q_ref, kt_ref, v_ref, m_ref, o_ref, t_ref, *, heads, qgw, scale
+    lo_ref, hi_ref, blk_ref, cnt_ref, q_ref, kt_ref, v_ref, m_ref, o_ref, t_ref, *, heads, qgw, scale
 ):
     i = pl.program_id(0)
     tile = q_ref.shape[0]
     base = i * SLOTS
     rows = i * tile + lax.broadcasted_iota(jnp.int32, (tile, 1), 0)
-    mask = _slot_mask(lo_ref, hi_ref, base, rows)
     lane = lax.broadcasted_iota(jnp.int32, (1, STAT_LANES), 1)
     totals = jnp.zeros((tile, STAT_LANES), jnp.float32)
-    top = jnp.transpose(m_ref[...])
+    tops = jnp.transpose(m_ref[...])
     for h in range(heads):
-        if h % qgw == 0:
-            keys = _slot_keys(kt_ref, blk_ref, base, h // qgw)
-            values = _slot_values(v_ref, blk_ref, base, h // qgw)
+        kv = h // qgw
+        cols = slice(kv * HEAD_SIZE, (kv + 1) * HEAD_SIZE)
         q = q_ref[:, h * HEAD_SIZE : (h + 1) * HEAD_SIZE]
-        sc = jnp.dot(q, keys, preferred_element_type=jnp.float32) * scale
-        p = jnp.exp(jnp.where(mask, sc - top[:, h : h + 1], -jnp.inf))
-        ctx = jnp.dot(p.astype(jnp.bfloat16), values, preferred_element_type=jnp.float32)
-        o_ref[:, h * HEAD_SIZE : (h + 1) * HEAD_SIZE] = ctx
-        totals = jnp.where(lane == h, jnp.sum(p, axis=1, keepdims=True), totals)
+        top = tops[:, h : h + 1]
+
+        def body(s, carry):
+            acc, tot = carry
+            j = blk_ref[base + s]
+            inside = (rows >= lo_ref[base + s]) & (rows < hi_ref[base + s])
+            shift = jnp.where(inside, top, jnp.inf)
+            sc = jnp.dot(q, kt_ref[j, cols, :], preferred_element_type=jnp.float32) * scale
+            p = jnp.exp(sc - shift)
+            acc = acc + jnp.dot(
+                p.astype(jnp.bfloat16), v_ref[j, :, cols], preferred_element_type=jnp.float32
+            )
+            return acc, tot + jnp.sum(p, axis=1, keepdims=True)
+
+        acc, tot = lax.fori_loop(
+            0,
+            cnt_ref[i],
+            body,
+            (jnp.zeros((tile, HEAD_SIZE), jnp.float32), jnp.zeros((tile, 1), jnp.float32)),
+        )
+        o_ref[:, h * HEAD_SIZE : (h + 1) * HEAD_SIZE] = acc
+        totals = jnp.where(lane == h, tot, totals)
     t_ref[...] = jnp.transpose(totals)[: t_ref.shape[0], :]
 
 
@@ -117,7 +119,7 @@
     return x
 
 
-def far_part(queries, keys_t, values, lo, hi, blk, qgw, blk_index, scale):
+def far_part(queries, keys_t, values, tables, qgw, blk_index, scale):
     tok_dev, q_cols = queries.shape
     heads = q_cols // HEAD_SIZE
     blocks, kv_cols, block_len = keys_t.shape
@@ -135,20 +137,20 @@
         functools.partial(max_kernel, **kw),
         out_shape=stat_shape,
         grid_spec=pltpu.PrefetchScalarGridSpec(
-            num_scalar_prefetch=3, grid=(n_tiles,), in_specs=[q_spec, kt_spec], out_specs=s_spec
+            num_scalar_prefetch=4, grid=(n_tiles,), in_specs=[q_spec, kt_spec], out_specs=s_spec
         ),
-    )(lo, hi, blk, gathered, keys_t)
+    )(*tables, gathered, keys_t)
     far_max = butterfly(local_max, "blk", jnp.maximum)
     partial, totals = pl.pallas_call(
         functools.partial(ctx_kernel, **kw),
         out_shape=(jax.ShapeDtypeStruct((row_count, q_cols), jnp.float32), stat_shape),
         grid_spec=pltpu.PrefetchScalarGridSpec(
-            num_scalar_prefetch=3,
+            num_scalar_prefetch=4,
             grid=(n_tiles,),
             in_specs=[q_spec, kt_spec, v_spec, s_spec],
             out_specs=(pl.BlockSpec((tok_dev, q_cols), lambda i, *_: (i, 0)), s_spec),
         ),
-    )(lo, hi, blk, gathered, keys_t, values, far_max)
+    )(*tables, gathered, keys_t, values, far_max)
     context = lax.psum_scatter(partial, "blk", scatter_dimension=0, tiled=True)
     totals = butterfly(totals, "blk", jnp.add)
     own = lambda a: jnp.transpose(
@@ -193,10 +195,10 @@
     tile = tok_dev
     n_tiles = row_count // tile
 
-    lo, hi, blk = tile_tables(suffix_len, request_group, block_group, n_tiles, tile)
+    tables = tile_tables(suffix_len, request_group, block_group, n_tiles, tile)
     keys_t = jnp.swapaxes(prefix_block_keys, 1, 2)
     far_context, far_total, own_far_max = far_part(
-        queries, keys_t, prefix_block_values, lo, hi, blk, qgw, blk_index, scale
+        queries, keys_t, prefix_block_values, tables, qgw, blk_index, scale
     )
     far_context = far_context.reshape(tok_dev, local_kv, qgw, HEAD_SIZE)
     far_total = far_total.reshape(tok_dev, local_kv, qgw)

time: 346 us -> 653 us (1.89)
  Pallas kernels: 95.2 us -> 403 us
    pallas_call x1, Pallas kernels: 65.4 us -> 224 us  [far_part(): pl.pallas_call(functools.partial(ctx_kernel, **kw), out_shape=(jax.ShapeD...]
    pallas_call x1, Pallas kernels: 29.8 us -> 179 us  [far_part(): pl.pallas_call(functools.partial(max_kernel, **kw), out_shape=stat_shape,...]
  transfers between devices with their start and end apart: 17 -> 17, of which waited for: 14 -> 14; matrix products, arithmetic and copies ran while one was open for 4% -> 2% of each run, Pallas kernels for 0% -> 0%
where the time goes in v5:
time: 653 us
  Pallas kernels  403 us (62%)
  waiting for transfers between devices  181 us (28%)
  starting transfers between devices  27.7 us (4%)
  local copies, waits for them, and re-layouts  15 us (2%)
  between operations  13.7 us (2%)
    pallas_call x1, Pallas kernels, far_part(): pl.pallas_call(functools.partial(ctx_kernel, **kw), out_shape=(jax.ShapeD...  224 us
    pallas_call x1, Pallas kernels, far_part(): pl.pallas_call(functools.partial(max_kernel, **kw), out_shape=stat_shape,...  179 us
    reduce_scatter x1, waiting for transfers between devices, far_part(): context = lax.psum_scatter(partial, 'blk', scatter_dimension=0, tiled=True)  82.9 us
    all_gather x1, waiting for transfers between devices, far_part(): gathered = lax.all_gather(queries, 'blk', axis=0, tiled=True)  44.7 us
    ppermute x10, waiting for transfers between devices, butterfly(): x = combine(x, lax.ppermute(x, axis, [(i, i ^ d) for i in range(n)]))  32.6 us
    ppermute x3, waiting for transfers between devices, column_sum(): lax.ppermute(chunk(me + d), axis, [(i, (i + d) % n) for i in range(n)])  20.4 us
    ppermute x10, starting transfers between devices, butterfly(): x = combine(x, lax.ppermute(x, axis, [(i, i ^ d) for i in range(n)]))  16.5 us
  transfers between devices with their start and end apart: 17, of which 14 were waited for; matrix products, arithmetic and copies ran while one was open for 2% of the time, Pallas kernels for 0%

profile of v5, /device:TPU:0, one launch (start us, length us, event | category | flops | bytes accessed | tf_op | source)
XLA Modules:
  0.0 652.9 jit_solution(11627835635109109523)
XLA Ops:
  9.3 1.6 gather_fusion.1
  10.9 1.6 gather_fusion
  14.1 1.5 gather_fusion.2
  15.9 1.3 copy.26
  17.4 2.1 gather_fusion.3
  20.1 44.7 %all-gather.2.cloned.1.call-done.q_ref = bf16[4096,1024]{1,0:T(8,128)(2,1)} async-done(((bf16[128,1024]{1,0:T(8,128)(2,1)}), bf16[4096,1024]{1,0:T(8,128)(2,1)}) %all-gather.2.cloned.1.call-update) | async-done | bytes 8388624 | tf_op jit(solution)/shard_map/all_gather | solution.py:126
  64.8 179.2 %shard_map.91 = f32[256,128]{1,0:T(8,128)} custom-call(s32[160]{0:T(256)} %select_n.90.lo_ref, s32[160]{0:T(256)} %select_n.92.hi_ref, s32[160]{0:T(256)} %gather_fusion.3, s32[32]{0:T(128)} %add_minimum_fusion.cnt_ref, bf16[4096,1024]{1,0:T(8,128)(2,1)} %all-gather.2.cloned.1.call-done.q_ref, bf16[16,256,128]{2,1,0:T(8,128)(2,1)} %bitcast.46), custom_call_target="tpu_custom_call" | custom-call | tf_op jit(solution)/shard_map/pallas_call | solution.py:136
  246.5 1.5 collective-permute-start.1
  248.0 4.2 collective-permute-done.1
  252.2 3.1 collective-permute-start.2
  255.3 3.5 collective-permute-done.2
  258.8 1.3 collective-permute-start.3
  260.1 3.7 collective-permute-done.3
  263.8 2.9 collective-permute-start.4
  266.7 3.7 collective-permute-done.4
  271.1 224.2 %shard_map.92 = (f32[4096,1024]{1,0:T(8,128)}, f32[256,128]{1,0:T(8,128)}) custom-call(s32[160]{0:T(256)} %select_n.90.lo_ref, s32[160]{0:T(256)} %select_n.92.hi_ref, s32[160]{0:T(256)} %gather_fusion.3, s32[32]{0:T(128)} %add_minimum_fusion.cnt_ref, bf16[4096,1024]{1,0:T(8,128)(2,1)} %all-gather.2.cloned.1.call-done.q_ref, bf16[16,256,128]{2,1,0:T(8,128)(2,1)} %bitcast.47, ...), custom_call_target="tpu_custom_call" | custom-call | tf_op jit(solution)/shard_map/pallas_call | solution.py:144
  497.5 4.1 collective-permute-start.6
  503.3 2.1 collective-permute-start.8
  505.8 3.4 collective-permute-done.8
  509.2 3.0 collective-permute-start.9
  512.6 3.2 collective-permute-done.9
  516.8 4.1 collective-permute-done.10
  520.9 2.1 collective-permute-start.11
  523.1 4.3 collective-permute-done.11
  527.4 82.9 %reduce-scatter.2.cloned.1.call-done = f32[128,1024]{1,0:T(8,128)} async-done(((f32[4096,1024]{1,0:T(8,128)}), f32[128,1024]{1,0:T(8,128)}) %reduce-scatter.2.cloned.1.call-update) | async-done | bytes 524304 | tf_op jit(solution)/shard_map/reduce_scatter | solution.py:154
  611.9 4.7 fusion.13
  617.7 1.5 collective-permute-start.12
  619.2 2.9 collective-permute-start.13
  622.1 1.4 collective-permute-start.14
  623.5 9.3 %collective-permute-done.12 = f32[128,1024]{1,0:T(8,128)S(1)} collective-permute-done((f32[128,1024]{1,0:T(8,128)}, f32[128,1024]{1,0:T(8,128)S(1)}, u32[]{:S(2)}, u32[]{:S(2)}) %collective-permute-start.12) | collective-permute-done | bytes 524320 | tf_op jit(solution)/shard_map/ppermute | solution.py:169
  632.7 11.2 %collective-permute-done.13 = f32[128,1024]{1,0:T(8,128)} collective-permute-done((f32[128,1024]{1,0:T(8,128)}, f32[128,1024]{1,0:T(8,128)}, u32[]{:S(2)}, u32[]{:S(2)}) %collective-permute-start.13) | collective-permute-done | bytes 524320 | tf_op jit(solution)/shard_map/ppermute | solution.py:169
  643.9 2.1 add_convert_fusion
  (76 shorter events, 17.0 us)
Async XLA Ops:
  6.5 7.6 %copy-start = (s32[64]{0:T(128)S(1)}, s32[64]{0:T(128)}, u32[]{:S(2)}) copy-start(s32[64]{0:T(128)} %param.16) | copy-start | bytes 772
  6.5 58.2 %all-gather.2.cloned.1.call-start = ((), (), s32[]{:S(2)}) async-start(), calls=%async_computation.1 | async-start | bytes 8650752 | tf_op jit(solution)/shard_map/all_gather | solution.py:126
  7.3 603.1 %reduce-scatter.2.cloned.1.call-start = ((), (), s32[]{:S(2)}) async-start(), calls=%async_computation.2 | async-start | bytes 17301504 | tf_op jit(solution)/shard_map/reduce_scatter | solution.py:154
  14.1 1.8 copy-start.1
  14.1 3.1 copy-start.6
  244.0 1.6 collective-permute-start
  246.5 5.7 collective-permute-start.1
  252.2 6.6 %collective-permute-start.2 = (f32[256,128]{1,0:T(8,128)S(1)}, f32[256,128]{1,0:T(8,128)S(1)}, u32[]{:S(2)}, u32[]{:S(2)}) collective-permute-start(f32[256,128]{1,0:T(8,128)S(1)} %max.29), channel_id=1, source_target_pairs={{0,4},{1,5},{2,6},{3,7},{4,0},{5,1},{6,2},{7,3},{8,12},{9,13},{10,... | collective-permute-start | bytes 393224 | tf_op jit(solution)/shard_map/ppermute | solution.py:117
  258.8 5.0 collective-permute-start.3
  263.8 6.6 %collective-permute-start.4 = (f32[256,128]{1,0:T(8,128)S(1)}, f32[256,128]{1,0:T(8,128)S(1)}, u32[]{:S(2)}, u32[]{:S(2)}) collective-permute-start(f32[256,128]{1,0:T(8,128)S(1)} %max.31), channel_id=1, source_target_pairs={{0,16},{1,17},{2,18},{3,19},{4,20},{5,21},{6,22},{7,23},{8,24},{9,... | collective-permute-start | bytes 393224 | tf_op jit(solution)/shard_map/ppermute | solution.py:117
  495.2 0.8 copy-start.4
  495.2 2.3 copy-start.5
  495.2 6.5 copy-start.3
  495.2 10.3 %copy-start.2 = (bf16[128,1024]{1,0:T(8,128)(2,1)S(1)}, bf16[128,1024]{1,0:T(8,128)(2,1)}, u32[]{:S(2)}) copy-start(bf16[128,1024]{1,0:T(8,128)(2,1)} %param.9) | copy-start | bytes 786436
  496.2 9.6 %collective-permute-start.5 = (bf16[128,256]{0,1:T(8,128)(2,1)S(1)}, bf16[128,256]{0,1:T(8,128)(2,1)S(1)}, u32[]{:S(2)}, u32[]{:S(2)}) collective-permute-start(bf16[128,256]{0,1:T(8,128)(2,1)S(1)} %copy.27), channel_id=1, source_target_pairs={{0,1},{1,2},{2,3},{3,4},{4,5},{5,6},{6,7},{7,8},{8,9},{9,10},{10,1... | collective-permute-start | bytes 196616 | tf_op jit(solution)/shard_map/ppermute | solution.py:19
  497.5 18.4 %collective-permute-start.6 = (bf16[128,256]{1,0:T(8,128)(2,1)S(1)}, bf16[128,256]{1,0:T(8,128)(2,1)S(1)}, u32[]{:S(2)}, u32[]{:S(2)}) collective-permute-start(bf16[128,256]{1,0:T(8,128)(2,1)S(1)} %copy-done.5), channel_id=1, source_target_pairs={{0,1},{1,2},{2,3},{3,4},{4,5},{5,6},{6,7},{7,8},{8,9},{9,10},{10,1... | collective-permute-start | bytes 196616 | tf_op jit(solution)/shard_map/ppermute | solution.py:19
  501.7 1.5 collective-permute-start.7
  503.3 5.9 collective-permute-start.8
  509.2 6.6 %collective-permute-start.9 = (f32[256,128]{1,0:T(8,128)S(1)}, f32[256,128]{1,0:T(8,128)S(1)}, u32[]{:S(2)}, u32[]{:S(2)}) collective-permute-start(f32[256,128]{1,0:T(8,128)S(1)} %add.185), channel_id=1, source_target_pairs={{0,4},{1,5},{2,6},{3,7},{4,0},{5,1},{6,2},{7,3},{8,12},{9,13},{10,... | collective-permute-start | bytes 393224 | tf_op jit(solution)/shard_map/ppermute | solution.py:117
  515.8 5.0 collective-permute-start.10
  520.9 6.6 %collective-permute-start.11 = (f32[256,128]{1,0:T(8,128)S(1)}, f32[256,128]{1,0:T(8,128)S(1)}, u32[]{:S(2)}, u32[]{:S(2)}) collective-permute-start(f32[256,128]{1,0:T(8,128)S(1)} %add.187), channel_id=1, source_target_pairs={{0,16},{1,17},{2,18},{3,19},{4,20},{5,21},{6,22},{7,23},{8,24},{9,... | collective-permute-start | bytes 393224 | tf_op jit(solution)/shard_map/ppermute | solution.py:117
  617.7 15.1 %collective-permute-start.12 = (f32[128,1024]{1,0:T(8,128)}, f32[128,1024]{1,0:T(8,128)S(1)}, u32[]{:S(2)}, u32[]{:S(2)}) collective-permute-start(f32[128,1024]{1,0:T(8,128)} %get-tuple-element.13), channel_id=1, source_target_pairs={{0,32},{32,64},{64,96},{96,0},{1,33},{33,65},{65,97},{97,1},{2,34}... | collective-permute-start | bytes 1572872 | tf_op jit(solution)/shard_map/ppermute | solution.py:169
  619.2 24.7 %collective-permute-start.13 = (f32[128,1024]{1,0:T(8,128)}, f32[128,1024]{1,0:T(8,128)}, u32[]{:S(2)}, u32[]{:S(2)}) collective-permute-start(f32[128,1024]{1,0:T(8,128)} %get-tuple-element.15), channel_id=1, source_target_pairs={{0,64},{32,96},{64,0},{96,32},{1,65},{33,97},{65,1},{97,33},{2,66}... | collective-permute-start | bytes 1572872 | tf_op jit(solution)/shard_map/ppermute | solution.py:169
  622.1 21.8 %collective-permute-start.14 = (f32[128,1024]{1,0:T(8,128)S(1)}, f32[128,1024]{1,0:T(8,128)}, u32[]{:S(2)}, u32[]{:S(2)}) collective-permute-start(f32[128,1024]{1,0:T(8,128)S(1)} %get-tuple-element.14), channel_id=1, source_target_pairs={{0,96},{32,0},{64,32},{96,64},{1,97},{33,1},{65,33},{97,65},{2,98}... | collective-permute-start | bytes 1572872 | tf_op jit(solution)/shard_map/ppermute | solution.py:169
Sparse Core Ops, SparseCore 0:
  9.6 55.1 all-gather.1
  495.4 114.8 reduce-scatter.1

commit v6 on v4

--- a/solution.py
+++ b/solution.py
@@ -11,10 +11,13 @@
 HEAD_SIZE = 128
 SLOTS = 5
 STAT_LANES = 128
+CHIP, CORE = "chip", "c"
+BLK = (CHIP, CORE)
+CORES = 2
 
 
 def from_behind(block, axis, distance):
-    devices = range(lax.axis_size(axis))
+    devices = range(blk_size())
     route = [(i - distance, i) for i in devices if i - distance in devices]
     return lax.ppermute(block, axis, route)
 
@@ -108,8 +111,26 @@
     t_ref[...] = jnp.transpose(totals)[: t_ref.shape[0], :]
 
 
+def blk_size():
+    return lax.axis_size(CHIP) * lax.axis_size(CORE)
+
+
+def blk_position():
+    return lax.axis_index(CHIP) * lax.axis_size(CORE) + lax.axis_index(CORE)
+
+
+def chip_then_core_sum(partial, tok_dev):
+    cores = lax.axis_size(CORE)
+    core = lax.axis_index(CORE)
+    split = partial.reshape(-1, cores, tok_dev, partial.shape[1])
+    keep = lax.dynamic_index_in_dim(split, core, 1, keepdims=False)
+    send = lax.dynamic_index_in_dim(split, 1 - core, 1, keepdims=False)
+    pair = keep + lax.ppermute(send, CORE, [(0, 1), (1, 0)])
+    return lax.psum_scatter(pair, CHIP, scatter_dimension=0, tiled=True).reshape(tok_dev, -1)
+
+
 def butterfly(x, axis, combine):
-    n = lax.axis_size(axis)
+    n = blk_size()
     d = 1
     while d < n:
         x = combine(x, lax.ppermute(x, axis, [(i, i ^ d) for i in range(n)]))
@@ -121,7 +142,7 @@
     tok_dev, q_cols = queries.shape
     heads = q_cols // HEAD_SIZE
     blocks, kv_cols, block_len = keys_t.shape
-    gathered = lax.all_gather(queries, "blk", axis=0, tiled=True)
+    gathered = lax.all_gather(queries, BLK, axis=0, tiled=True)
     row_count = gathered.shape[0]
     n_tiles = row_count // tok_dev
     stat_rows = 8
@@ -138,7 +159,7 @@
             num_scalar_prefetch=3, grid=(n_tiles,), in_specs=[q_spec, kt_spec], out_specs=s_spec
         ),
     )(lo, hi, blk, gathered, keys_t)
-    far_max = butterfly(local_max, "blk", jnp.maximum)
+    far_max = butterfly(local_max, BLK, jnp.maximum)
     partial, totals = pl.pallas_call(
         functools.partial(ctx_kernel, **kw),
         out_shape=(jax.ShapeDtypeStruct((row_count, q_cols), jnp.float32), stat_shape),
@@ -149,8 +170,8 @@
             out_specs=(pl.BlockSpec((tok_dev, q_cols), lambda i, *_: (i, 0)), s_spec),
         ),
     )(lo, hi, blk, gathered, keys_t, values, far_max)
-    context = lax.psum_scatter(partial, "blk", scatter_dimension=0, tiled=True)
-    totals = butterfly(totals, "blk", jnp.add)
+    context = chip_then_core_sum(partial, tok_dev)
+    totals = butterfly(totals, BLK, jnp.add)
     own = lambda a: jnp.transpose(
         lax.dynamic_slice_in_dim(a, blk_index * stat_rows, stat_rows, 0)[:heads]
     )
@@ -186,9 +207,9 @@
     local_heads = q_cols // HEAD_SIZE
     qgw = local_heads // local_kv
     blocks, block_len, _ = prefix_block_keys.shape
-    blk_count = lax.axis_size("blk")
+    blk_count = blk_size()
     row_count = blk_count * tok_dev
-    blk_index = lax.axis_index("blk")
+    blk_index = blk_position()
     scale = 1.0 / math.sqrt(HEAD_SIZE)
     tile = tok_dev
     n_tiles = row_count // tile
@@ -205,7 +226,7 @@
     row_ends = jnp.cumsum(suffix_len)
     starts = row_ends - suffix_len
     own_rows = blk_index * tok_dev + jnp.arange(tok_dev, dtype=jnp.int32)
-    earlier_keys, earlier_values = from_behind((suffix_key_rows, suffix_value_rows), "blk", 1)
+    earlier_keys, earlier_values = from_behind((suffix_key_rows, suffix_value_rows), BLK, 1)
     near_keys = jnp.concatenate([earlier_keys, suffix_key_rows], axis=0).reshape(
         2 * tok_dev, local_kv, HEAD_SIZE
     )
@@ -245,17 +266,21 @@
 
 
 def solution(mesh):
+    devices = mesh.devices
+    split = jax.sharding.Mesh(
+        devices.reshape(devices.shape[0], devices.shape[1] // CORES, CORES), ("kvh",) + BLK
+    )
     placed = (
-        P("blk", "kvh"),
-        P("blk", "kvh"),
-        P("blk", "kvh"),
-        P("blk", None, "kvh"),
-        P("blk", None, "kvh"),
-        P("blk"),
+        P(BLK, "kvh"),
+        P(BLK, "kvh"),
+        P(BLK, "kvh"),
+        P(BLK, None, "kvh"),
+        P(BLK, None, "kvh"),
+        P(BLK),
         P(),
         P(),
         P("kvh", None),
     )
     return jax.shard_map(
-        per_device, mesh=mesh, in_specs=placed, out_specs=P("blk", "kvh"), check_vma=False
-    )
+        per_device, mesh=split, in_specs=placed, out_specs=P(BLK, "kvh"), check_vma=False
+    )

time: 346 us -> 356 us (1.029)
  other arithmetic: 5.75 us -> 17.7 us
  waiting for transfers between devices: 182 us -> 172 us
  local copies, waits for them, and re-layouts: 15 us -> 23.3 us
    reduce_scatter x1 -> x0, waiting for transfers between devices: 82.9 us -> none  [far_part(): context = lax.psum_scatter(partial, 'blk', scatter_dimension=0, tiled=True)]
    unnamed x2 -> x3, waiting for transfers between devices: 0.73 us -> 45 us
    ppermute x0 -> x1, waiting for transfers between devices: none -> 13.5 us  [chip_then_core_sum(): pair = keep + lax.ppermute(send, CORE, [(0, 1), (1, 0)])]
    ppermute x10, waiting for transfers between devices: 32.6 us -> 45.2 us  [butterfly(): x = combine(x, lax.ppermute(x, axis, [(i, i ^ d) for i in range(n)]))]
    add x0 -> x1, other arithmetic: none -> 12 us  [chip_then_core_sum(): pair = keep + lax.ppermute(send, CORE, [(0, 1), (1, 0)])]
    squeeze x0 -> x1, local copies, waits for them, and re-layouts: none -> 8.28 us  [chip_then_core_sum(): send = lax.dynamic_index_in_dim(split, 1 - core, 1, keepdims=False)]
  transfers between devices with their start and end apart: 17 -> 18, of which waited for: 14 -> 15; matrix products, arithmetic and copies ran while one was open for 4% -> 4% of each run, Pallas kernels for 0% -> 0%
where the time goes in v6:
time: 356 us; the launch traced here: 354 us
  waiting for transfers between devices  172 us (48%)
  Pallas kernels  95.3 us (27%)
  starting transfers between devices  26.6 us (7%)
  local copies, waits for them, and re-layouts  23.3 us (7%)
  other arithmetic  17.7 us (5%)
  between operations  13.7 us (4%)
  matrix products  5.37 us (2%)
    pallas_call x1, Pallas kernels, far_part(): pl.pallas_call(functools.partial(ctx_kernel, **kw), out_shape=(jax.ShapeD...  65.4 us
    all_gather x1, waiting for transfers between devices, far_part(): gathered = lax.all_gather(queries, BLK, axis=0, tiled=True)  45.3 us
    ppermute x10, waiting for transfers between devices, butterfly(): x = combine(x, lax.ppermute(x, axis, [(i, i ^ d) for i in range(n)]))  45.2 us
    unnamed x3, waiting for transfers between devices  45 us
    pallas_call x1, Pallas kernels, far_part(): pl.pallas_call(functools.partial(max_kernel, **kw), out_shape=stat_shape,...  29.8 us
    ppermute x3, waiting for transfers between devices, column_sum(): lax.ppermute(chunk(me + d), axis, [(i, (i + d) % n) for i in range(n)])  23.2 us
    ppermute x10, starting transfers between devices, butterfly(): x = combine(x, lax.ppermute(x, axis, [(i, i ^ d) for i in range(n)]))  16.5 us
    ppermute x1, waiting for transfers between devices, chip_then_core_sum(): pair = keep + lax.ppermute(send, CORE, [(0, 1), (1, 0)])  13.5 us
  transfers between devices with their start and end apart: 18, of which 15 were waited for; matrix products, arithmetic and copies ran while one was open for 4% of the time, Pallas kernels for 0%

profile of v6, /device:TPU:0, one launch (start us, length us, event | category | flops | bytes accessed | tf_op | source)
XLA Modules:
  0.0 354.1 jit_solution(9998816082552067292)
XLA Ops:
  9.3 1.6 gather_fusion.1
  11.0 1.6 gather_fusion
  14.1 1.5 gather_fusion.2
  17.4 2.1 gather_fusion.3
  19.5 45.3 %all-gather.2.cloned.1.call-done.q_ref = bf16[4096,1024]{1,0:T(8,128)(2,1)} async-done(((bf16[128,1024]{1,0:T(8,128)(2,1)}), bf16[4096,1024]{1,0:T(8,128)(2,1)}) %all-gather.2.cloned.1.call-update) | async-done | bytes 8388624 | tf_op jit(solution)/shard_map/all_gather | solution.py:145
  64.8 29.8 %shard_map.91 = f32[256,128]{1,0:T(8,128)} custom-call(s32[160]{0:T(256)} %select_n.97.lo_ref, s32[160]{0:T(256)} %select_n.99.hi_ref, s32[160]{0:T(256)} %gather_fusion.3, bf16[4096,1024]{1,0:T(8,128)(2,1)} %all-gather.2.cloned.1.call-done.q_ref, bf16[16,256,128]{2,1,0:T(8,128)(2,1)} %bitcast.52), custom_call_target="tpu_custom_call" | custom-call | tf_op jit(solution)/shard_map/pallas_call | solution.py:155
  97.1 1.5 collective-permute-start.1
  98.6 4.2 %collective-permute-done.1 = f32[256,128]{1,0:T(8,128)S(1)} collective-permute-done((f32[256,128]{1,0:T(8,128)S(1)}, f32[256,128]{1,0:T(8,128)S(1)}, u32[]{:S(2)}, u32[]{:S(2)}) %collective-permute-start.1) | collective-permute-done | bytes 131104 | tf_op jit(solution)/shard_map/ppermute | solution.py:136
  102.8 3.0 collective-permute-start.2
  105.9 3.5 collective-permute-done.2
  110.7 3.7 %collective-permute-done.3 = f32[256,128]{1,0:T(8,128)S(1)} collective-permute-done((f32[256,128]{1,0:T(8,128)S(1)}, f32[256,128]{1,0:T(8,128)S(1)}, u32[]{:S(2)}, u32[]{:S(2)}) %collective-permute-start.3) | collective-permute-done | bytes 131104 | tf_op jit(solution)/shard_map/ppermute | solution.py:136
  114.5 2.9 collective-permute-start.4
  117.3 3.7 %collective-permute-done.4 = f32[256,128]{1,0:T(8,128)S(1)} collective-permute-done((f32[256,128]{1,0:T(8,128)S(1)}, f32[256,128]{1,0:T(8,128)S(1)}, u32[]{:S(2)}, u32[]{:S(2)}) %collective-permute-start.4) | collective-permute-done | bytes 131104 | tf_op jit(solution)/shard_map/ppermute | solution.py:136
  121.7 65.4 %shard_map.92 = (f32[4096,1024]{1,0:T(8,128)}, f32[256,128]{1,0:T(8,128)}) custom-call(s32[160]{0:T(256)} %select_n.97.lo_ref, s32[160]{0:T(256)} %select_n.99.hi_ref, s32[160]{0:T(256)} %gather_fusion.3, bf16[4096,1024]{1,0:T(8,128)(2,1)} %all-gather.2.cloned.1.call-done.q_ref, bf16[16,256,128]{2,1,0:T(8,128)(2,1)} %bitcast.53, ...), custom_call_target="tpu_custom_call" | custom-call | tf_op jit(solution)/shard_map/pallas_call | solution.py:163
  187.1 8.3 %dynamic-slice_bitcast_fusion = f32[16,128,1024]{2,1,0:T(8,128)} fusion(f32[16,2,128,1024]{3,2,1,0:T(8,128)} %bitcast.50, s32[]{:T(128)S(6)} %select_n.103), kind=kLoop, calls=%fused_computation.5 | loop fusion | bytes 16777220 | tf_op jit(solution)/shard_map/jit(dynamic_index_in_dim)/squeeze | solution.py:127
  195.4 13.5 %collective-permute-done.5 = f32[16,128,1024]{2,1,0:T(8,128)} collective-permute-done((f32[16,128,1024]{2,1,0:T(8,128)}, f32[16,128,1024]{2,1,0:T(8,128)}, u32[]{:S(2)}, u32[]{:S(2)}) %collective-permute-start.5) | collective-permute-done | bytes 8388640 | tf_op jit(solution)/shard_map/ppermute | solution.py:128
  208.9 12.0 %bitcast_add_fusion = f32[16,128,1024]{2,1,0:T(8,128)} fusion(f32[16,128,1024]{2,1,0:T(8,128)} %collective-permute-done.5, f32[16,2,128,1024]{3,2,1,0:T(8,128)} %bitcast.51, s32[]{:T(128)S(6)} %select_n.102), kind=kLoop, calls=%fused_computation.4 | loop fusion | flops 2097152 | bytes 25165828 | tf_op jit(solution)/shard_map/add | solution.py:128
  221.8 2.0 collective-permute-start.6
  223.9 3.4 collective-permute-start.7
  228.9 2.0 collective-permute-start.9
  231.2 6.3 %collective-permute-done.9 = f32[256,128]{1,0:T(8,128)S(1)} collective-permute-done((f32[256,128]{1,0:T(8,128)S(1)}, f32[256,128]{1,0:T(8,128)S(1)}, u32[]{:S(2)}, u32[]{:S(2)}) %collective-permute-start.9) | collective-permute-done | bytes 131104 | tf_op jit(solution)/shard_map/ppermute | solution.py:136
  237.6 3.4 collective-permute-start.10
  241.4 6.2 %collective-permute-done.10 = f32[256,128]{1,0:T(8,128)S(1)} collective-permute-done((f32[256,128]{1,0:T(8,128)S(1)}, f32[256,128]{1,0:T(8,128)S(1)}, u32[]{:S(2)}, u32[]{:S(2)}) %collective-permute-start.10) | collective-permute-done | bytes 131104 | tf_op jit(solution)/shard_map/ppermute | solution.py:136
  248.6 7.4 %collective-permute-done.11 = f32[256,128]{1,0:T(8,128)S(1)} collective-permute-done((f32[256,128]{1,0:T(8,128)S(1)}, f32[256,128]{1,0:T(8,128)S(1)}, u32[]{:S(2)}, u32[]{:S(2)}) %collective-permute-start.11) | collective-permute-done | bytes 131104 | tf_op jit(solution)/shard_map/ppermute | solution.py:136
  256.0 1.8 collective-permute-start.12
  258.0 7.7 %collective-permute-done.12 = f32[256,128]{1,0:T(8,128)S(1)} collective-permute-done((f32[256,128]{1,0:T(8,128)S(1)}, f32[256,128]{1,0:T(8,128)S(1)}, u32[]{:S(2)}, u32[]{:S(2)}) %collective-permute-start.12) | collective-permute-done | bytes 131104 | tf_op jit(solution)/shard_map/ppermute | solution.py:136
  265.7 44.3 %reduce-scatter.4.cloned.1.call-done = f32[1,128,1024]{2,1,0:T(8,128)} async-done(((f32[16,128,1024]{2,1,0:T(8,128)}), f32[1,128,1024]{2,1,0:T(8,128)}) %reduce-scatter.4.cloned.1.call-update) | async-done | bytes 524304
  311.6 4.7 %fusion.10 = f32[128,4096]{1,0:T(8,128)S(1)} fusion(bf16[128,1024]{0,1:T(8,128)(2,1)S(1)} %bitcast.54, bf16[1024,4096]{1,0:T(8,128)(2,1)} %param.17), kind=kOutput, calls=%fused_computation.46 | convolution fusion | flops 1073741824 | bytes 10747904 | tf_op jit(solution)/shard_map/dot_general | solution.py:264
  317.4 2.9 collective-permute-start.15
  322.0 19.6 %collective-permute-done.15 = f32[128,1024]{1,0:T(8,128)S(1)} collective-permute-done((f32[128,1024]{1,0:T(8,128)}, f32[128,1024]{1,0:T(8,128)S(1)}, u32[]{:S(2)}, u32[]{:S(2)}) %collective-permute-start.15) | collective-permute-done | bytes 524320 | tf_op jit(solution)/shard_map/ppermute | solution.py:188
  341.6 3.6 %collective-permute-done.13 = f32[128,1024]{1,0:T(8,128)} collective-permute-done((f32[128,1024]{1,0:T(8,128)S(1)}, f32[128,1024]{1,0:T(8,128)}, u32[]{:S(2)}, u32[]{:S(2)}) %collective-permute-start.13) | collective-permute-done | bytes 524320 | tf_op jit(solution)/shard_map/ppermute | solution.py:188
  345.2 2.1 add_convert_fusion
  (81 shorter events, 19.4 us)
Async XLA Ops:
  6.5 7.6 %copy-start = (s32[64]{0:T(128)S(1)}, s32[64]{0:T(128)}, u32[]{:S(2)}) copy-start(s32[64]{0:T(128)} %param.16) | copy-start | bytes 772
  6.5 58.2 %all-gather.2.cloned.1.call-start = ((), (), s32[]{:S(2)}) async-start(), calls=%async_computation.1 | async-start | bytes 8650752 | tf_op jit(solution)/shard_map/all_gather | solution.py:145
  7.3 302.7 %reduce-scatter.4.cloned.1.call-start = ((), (), s32[]{:S(2)}) async-start(), calls=%async_computation.2 | async-start | bytes 8912896
  14.1 1.8 copy-start.2
  14.1 3.1 copy-start.7
  94.6 1.6 collective-permute-start
  97.1 5.7 %collective-permute-start.1 = (f32[256,128]{1,0:T(8,128)S(1)}, f32[256,128]{1,0:T(8,128)S(1)}, u32[]{:S(2)}, u32[]{:S(2)}) collective-permute-start(f32[256,128]{1,0:T(8,128)S(1)} %max.28), channel_id=1, source_target_pairs={{0,2},{1,3},{2,0},{3,1},{4,6},{5,7},{6,4},{7,5},{8,10},{9,11},{10,... | collective-permute-start | bytes 393224 | tf_op jit(solution)/shard_map/ppermute | solution.py:136
  102.8 6.6 %collective-permute-start.2 = (f32[256,128]{1,0:T(8,128)S(1)}, f32[256,128]{1,0:T(8,128)S(1)}, u32[]{:S(2)}, u32[]{:S(2)}) collective-permute-start(f32[256,128]{1,0:T(8,128)S(1)} %max.29), channel_id=1, source_target_pairs={{0,4},{1,5},{2,6},{3,7},{4,0},{5,1},{6,2},{7,3},{8,12},{9,13},{10,... | collective-permute-start | bytes 393224 | tf_op jit(solution)/shard_map/ppermute | solution.py:136
  109.4 5.0 %collective-permute-start.3 = (f32[256,128]{1,0:T(8,128)S(1)}, f32[256,128]{1,0:T(8,128)S(1)}, u32[]{:S(2)}, u32[]{:S(2)}) collective-permute-start(f32[256,128]{1,0:T(8,128)S(1)} %max.30), channel_id=1, source_target_pairs={{0,8},{1,9},{2,10},{3,11},{4,12},{5,13},{6,14},{7,15},{8,0},{9,1},... | collective-permute-start | bytes 393224 | tf_op jit(solution)/shard_map/ppermute | solution.py:136
  114.5 6.6 %collective-permute-start.4 = (f32[256,128]{1,0:T(8,128)S(1)}, f32[256,128]{1,0:T(8,128)S(1)}, u32[]{:S(2)}, u32[]{:S(2)}) collective-permute-start(f32[256,128]{1,0:T(8,128)S(1)} %max.31), channel_id=1, source_target_pairs={{0,16},{1,17},{2,18},{3,19},{4,20},{5,21},{6,22},{7,23},{8,24},{9,... | collective-permute-start | bytes 393224 | tf_op jit(solution)/shard_map/ppermute | solution.py:136
  195.4 13.5 %collective-permute-start.5 = (f32[16,128,1024]{2,1,0:T(8,128)}, f32[16,128,1024]{2,1,0:T(8,128)}, u32[]{:S(2)}, u32[]{:S(2)}) collective-permute-start(f32[16,128,1024]{2,1,0:T(8,128)} %dynamic-slice_bitcast_fusion), channel_id=1, source_target_pairs={{0,1},{1,0},{2,3},{3,2},{4,5},{5,4},{6,7},{7,6},{8,9},{9,8},{10,11... | collective-permute-start | bytes 25165832 | tf_op jit(solution)/shard_map/ppermute | solution.py:128
  220.9 0.8 copy-start.5
  220.9 3.0 copy-start.6
  220.9 6.5 %copy-start.4 = (f32[256,128]{1,0:T(8,128)S(1)}, f32[256,128]{1,0:T(8,128)}, u32[]{:S(2)}) copy-start(f32[256,128]{1,0:T(8,128)} %get-tuple-element.8) | copy-start | bytes 393220
  220.9 10.1 %copy-start.3 = (bf16[128,1024]{1,0:T(8,128)(2,1)S(1)}, bf16[128,1024]{1,0:T(8,128)(2,1)}, u32[]{:S(2)}) copy-start(bf16[128,1024]{1,0:T(8,128)(2,1)} %param.9) | copy-start | bytes 786436
  221.8 9.4 %collective-permute-start.6 = (bf16[128,256]{0,1:T(8,128)(2,1)S(1)}, bf16[128,256]{0,1:T(8,128)(2,1)S(1)}, u32[]{:S(2)}, u32[]{:S(2)}) collective-permute-start(bf16[128,256]{0,1:T(8,128)(2,1)S(1)} %copy.42), channel_id=1, source_target_pairs={{0,1},{1,2},{2,3},{3,4},{4,5},{5,6},{6,7},{7,8},{8,9},{9,10},{10,1... | collective-permute-start | bytes 196616 | tf_op jit(solution)/shard_map/ppermute | solution.py:22
  223.9 23.8 %collective-permute-start.7 = (bf16[128,256]{1,0:T(8,128)(2,1)S(1)}, bf16[128,256]{1,0:T(8,128)(2,1)S(1)}, u32[]{:S(2)}, u32[]{:S(2)}) collective-permute-start(bf16[128,256]{1,0:T(8,128)(2,1)S(1)} %copy-done.6), channel_id=1, source_target_pairs={{0,1},{1,2},{2,3},{3,4},{4,5},{5,6},{6,7},{7,8},{8,9},{9,10},{10,1... | collective-permute-start | bytes 196616 | tf_op jit(solution)/shard_map/ppermute | solution.py:22
  227.4 1.4 collective-permute-start.8
  228.9 8.7 %collective-permute-start.9 = (f32[256,128]{1,0:T(8,128)S(1)}, f32[256,128]{1,0:T(8,128)S(1)}, u32[]{:S(2)}, u32[]{:S(2)}) collective-permute-start(f32[256,128]{1,0:T(8,128)S(1)} %add.198), channel_id=1, source_target_pairs={{0,2},{1,3},{2,0},{3,1},{4,6},{5,7},{6,4},{7,5},{8,10},{9,11},{10,... | collective-permute-start | bytes 393224 | tf_op jit(solution)/shard_map/ppermute | solution.py:136
  237.6 10.0 %collective-permute-start.10 = (f32[256,128]{1,0:T(8,128)S(1)}, f32[256,128]{1,0:T(8,128)S(1)}, u32[]{:S(2)}, u32[]{:S(2)}) collective-permute-start(f32[256,128]{1,0:T(8,128)S(1)} %add.199), channel_id=1, source_target_pairs={{0,4},{1,5},{2,6},{3,7},{4,0},{5,1},{6,2},{7,3},{8,12},{9,13},{10,... | collective-permute-start | bytes 393224 | tf_op jit(solution)/shard_map/ppermute | solution.py:136
  247.7 8.4 %collective-permute-start.11 = (f32[256,128]{1,0:T(8,128)S(1)}, f32[256,128]{1,0:T(8,128)S(1)}, u32[]{:S(2)}, u32[]{:S(2)}) collective-permute-start(f32[256,128]{1,0:T(8,128)S(1)} %add.200), channel_id=1, source_target_pairs={{0,8},{1,9},{2,10},{3,11},{4,12},{5,13},{6,14},{7,15},{8,0},{9,1},... | collective-permute-start | bytes 393224 | tf_op jit(solution)/shard_map/ppermute | solution.py:136
  256.0 9.6 %collective-permute-start.12 = (f32[256,128]{1,0:T(8,128)S(1)}, f32[256,128]{1,0:T(8,128)S(1)}, u32[]{:S(2)}, u32[]{:S(2)}) collective-permute-start(f32[256,128]{1,0:T(8,128)S(1)} %add.201), channel_id=1, source_target_pairs={{0,16},{1,17},{2,18},{3,19},{4,20},{5,21},{6,22},{7,23},{8,24},{9,... | collective-permute-start | bytes 393224 | tf_op jit(solution)/shard_map/ppermute | solution.py:136
  311.6 35.7 %copy-start.1 = (s32[64]{0:T(128)S(1)}, s32[64]{0:T(128)}, u32[]{:S(2)}) copy-start(s32[64]{0:T(128)} %param.16) | copy-start | bytes 772
  317.4 24.2 %collective-permute-start.15 = (f32[128,1024]{1,0:T(8,128)}, f32[128,1024]{1,0:T(8,128)S(1)}, u32[]{:S(2)}, u32[]{:S(2)}) collective-permute-start(f32[128,1024]{1,0:T(8,128)} %get-tuple-element.14), channel_id=1, source_target_pairs={{0,96},{32,0},{64,32},{96,64},{1,97},{33,1},{65,33},{97,65},{2,98}... | collective-permute-start | bytes 1572872 | tf_op jit(solution)/shard_map/ppermute | solution.py:188
  320.3 21.3 %collective-permute-start.14 = (f32[128,1024]{1,0:T(8,128)}, f32[128,1024]{1,0:T(8,128)}, u32[]{:S(2)}, u32[]{:S(2)}) collective-permute-start(f32[128,1024]{1,0:T(8,128)} %get-tuple-element.15), channel_id=1, source_target_pairs={{0,64},{32,96},{64,0},{96,32},{1,65},{33,97},{65,1},{97,33},{2,66}... | collective-permute-start | bytes 1572872 | tf_op jit(solution)/shard_map/ppermute | solution.py:188
  321.0 24.2 %collective-permute-start.13 = (f32[128,1024]{1,0:T(8,128)S(1)}, f32[128,1024]{1,0:T(8,128)}, u32[]{:S(2)}, u32[]{:S(2)}) collective-permute-start(f32[128,1024]{1,0:T(8,128)S(1)} %get-tuple-element.13), channel_id=1, source_target_pairs={{0,32},{32,64},{64,96},{96,0},{1,33},{33,65},{65,97},{97,1},{2,34}... | collective-permute-start | bytes 1572872 | tf_op jit(solution)/shard_map/ppermute | solution.py:188
Sparse Core Ops, SparseCore 0:
  9.6 55.1 all-gather.1
  221.0 88.8 reduce-scatter.3

commit v7 on v4

--- a/solution.py
+++ b/solution.py
@@ -110,10 +110,21 @@
 
 def butterfly(x, axis, combine):
     n = lax.axis_size(axis)
-    d = 1
-    while d < n:
-        x = combine(x, lax.ppermute(x, axis, [(i, i ^ d) for i in range(n)]))
-        d *= 2
+    stride = 1
+    while stride < n:
+        radix = 2 if stride == 1 or n % (stride * 4) else 4
+        digit = lambda i: (i // stride) % radix
+        got = [
+            lax.ppermute(
+                x,
+                axis,
+                [(i, i + ((digit(i) + d) % radix - digit(i)) * stride) for i in range(n)],
+            )
+            for d in range(1, radix)
+        ]
+        for g in got:
+            x = combine(x, g)
+        stride *= radix
     return x
 
 
@@ -164,7 +175,9 @@
     chunk = lambda k: lax.dynamic_slice_in_dim(x, (k % n) * width, width, 1)
     total = chunk(me)
     for d in range(1, n):
-        total = total + lax.ppermute(chunk(me + d), axis, [(i, (i + d) % n) for i in range(n)])
+        sent = chunk(me + d).astype(jnp.bfloat16)
+        got = lax.ppermute(sent, axis, [(i, (i + d) % n) for i in range(n)])
+        total = total + got.astype(jnp.float32)
     return total
 
 

time: 346 us -> 331 us (0.957)
  waiting for transfers between devices: 182 us -> 162 us
  starting transfers between devices: 27.7 us -> 34.3 us
    ppermute x13 -> x17, waiting for transfers between devices: 53 us -> 29.1 us  [the longest x14 20.2 us: butterfly(): lax.ppermute(x, axis, [(i, i + ((digit(i) + d) % radix - digit(i)) * stri...]
    ppermute x13 -> x17, starting transfers between devices: 22.3 us -> 28.9 us  [the longest x14 23.1 us: butterfly(): lax.ppermute(x, axis, [(i, i + ((digit(i) + d) % radix - digit(i)) * stri...]
    reduce_scatter x1, waiting for transfers between devices: 82.9 us -> 86.5 us  [far_part(): context = lax.psum_scatter(partial, 'blk', scatter_dimension=0, tiled=True)]
  transfers between devices with their start and end apart: 17 -> 21, of which waited for: 14 -> 15; matrix products, arithmetic and copies ran while one was open for 4% -> 4% of each run, Pallas kernels for 0% -> 0%
where the time goes in v7:
time: 331 us; the launch traced here: 330 us
  waiting for transfers between devices  162 us (49%)
  Pallas kernels  95.3 us (29%)
  starting transfers between devices  34.3 us (10%)
  local copies, waits for them, and re-layouts  13.9 us (4%)
  between operations  13.7 us (4%)
  other arithmetic  5.44 us (2%)
  matrix products  5.36 us (2%)
    reduce_scatter x1, waiting for transfers between devices, far_part(): context = lax.psum_scatter(partial, 'blk', scatter_dimension=0, tiled=True)  86.5 us
    pallas_call x1, Pallas kernels, far_part(): pl.pallas_call(functools.partial(ctx_kernel, **kw), out_shape=(jax.ShapeD...  65.4 us
    all_gather x1, waiting for transfers between devices, far_part(): gathered = lax.all_gather(queries, 'blk', axis=0, tiled=True)  45.3 us
    pallas_call x1, Pallas kernels, far_part(): pl.pallas_call(functools.partial(max_kernel, **kw), out_shape=stat_shape,...  29.8 us
    ppermute x14, starting transfers between devices, butterfly(): lax.ppermute(x, axis, [(i, i + ((digit(i) + d) % radix - digit(i)) * stri...  23.1 us
    ppermute x14, waiting for transfers between devices, butterfly(): lax.ppermute(x, axis, [(i, i + ((digit(i) + d) % radix - digit(i)) * stri...  20.2 us
    ppermute x3, waiting for transfers between devices, column_sum(): got = lax.ppermute(sent, axis, [(i, (i + d) % n) for i in range(n)])  8.83 us
  transfers between devices with their start and end apart: 21, of which 15 were waited for; matrix products, arithmetic and copies ran while one was open for 4% of the time, Pallas kernels for 0%

profile of v7, /device:TPU:0, one launch (start us, length us, event | category | flops | bytes accessed | tf_op | source)
XLA Modules:
  0.0 329.7 jit_solution(14176900692415682643)
XLA Ops:
  9.3 1.6 gather_fusion.1
  10.9 1.6 gather_fusion
  14.0 1.5 gather_fusion.2
  15.8 1.4 copy.26
  17.3 2.1 gather_fusion.3
  19.4 45.3 %all-gather.2.cloned.1.call-done.q_ref = bf16[4096,1024]{1,0:T(8,128)(2,1)} async-done(((bf16[128,1024]{1,0:T(8,128)(2,1)}), bf16[4096,1024]{1,0:T(8,128)(2,1)}) %all-gather.2.cloned.1.call-update) | async-done | bytes 8388624 | tf_op jit(solution)/shard_map/all_gather | solution.py:135
  64.8 29.8 %shard_map.91 = f32[256,128]{1,0:T(8,128)} custom-call(s32[160]{0:T(256)} %select_n.90.lo_ref, s32[160]{0:T(256)} %select_n.92.hi_ref, s32[160]{0:T(256)} %gather_fusion.3, bf16[4096,1024]{1,0:T(8,128)(2,1)} %all-gather.2.cloned.1.call-done.q_ref, bf16[16,256,128]{2,1,0:T(8,128)(2,1)} %bitcast.46), custom_call_target="tpu_custom_call" | custom-call | tf_op jit(solution)/shard_map/pallas_call | solution.py:145
  97.1 1.5 collective-permute-start.1
  98.6 2.7 collective-permute-start.2
  101.3 1.4 collective-permute-start.3
  104.0 3.7 %collective-permute-done.2 = f32[256,128]{1,0:T(8,128)S(1)} collective-permute-done((f32[256,128]{1,0:T(8,128)S(1)}, f32[256,128]{1,0:T(8,128)S(1)}, u32[]{:S(2)}, u32[]{:S(2)}) %collective-permute-start.2) | collective-permute-done | bytes 131104 | tf_op jit(solution)/shard_map/ppermute | solution.py:118
  108.7 2.8 collective-permute-start.5
  111.5 1.4 collective-permute-start.6
  112.9 2.4 collective-permute-done.4
  115.4 1.4 collective-permute-done.5
  117.9 65.4 %shard_map.92 = (f32[4096,1024]{1,0:T(8,128)}, f32[256,128]{1,0:T(8,128)}) custom-call(s32[160]{0:T(256)} %select_n.90.lo_ref, s32[160]{0:T(256)} %select_n.92.hi_ref, s32[160]{0:T(256)} %gather_fusion.3, bf16[4096,1024]{1,0:T(8,128)(2,1)} %all-gather.2.cloned.1.call-done.q_ref, bf16[16,256,128]{2,1,0:T(8,128)(2,1)} %bitcast.47, ...), custom_call_target="tpu_custom_call" | custom-call | tf_op jit(solution)/shard_map/pallas_call | solution.py:153
  185.6 4.1 %collective-permute-start.8 = (bf16[128,256]{1,0:T(8,128)(2,1)S(1)}, bf16[128,256]{1,0:T(8,128)(2,1)S(1)}, u32[]{:S(2)}, u32[]{:S(2)}) collective-permute-start(bf16[128,256]{1,0:T(8,128)(2,1)S(1)} %copy-done.5), channel_id=1, source_target_pairs={{0,1},{1,2},{2,3},{3,4},{4,5},{5,6},{6,7},{7,8},{8,9},{9,10},{10,1... | collective-permute-start | bytes 196616 | tf_op jit(solution)/shard_map/ppermute | solution.py:19
  192.8 3.3 %collective-permute-start.11 = (f32[256,128]{1,0:T(8,128)S(1)}, f32[256,128]{1,0:T(8,128)S(1)}, u32[]{:S(2)}, u32[]{:S(2)}) collective-permute-start(f32[256,128]{1,0:T(8,128)S(1)} %add.186), channel_id=1, source_target_pairs={{0,4},{1,5},{2,6},{3,7},{4,0},{5,1},{6,2},{7,3},{8,12},{9,13},{10,... | collective-permute-start | bytes 393224 | tf_op jit(solution)/shard_map/ppermute | solution.py:118
  196.2 1.5 collective-permute-start.12
  198.6 3.8 %collective-permute-done.11 = f32[256,128]{1,0:T(8,128)S(1)} collective-permute-done((f32[256,128]{1,0:T(8,128)S(1)}, f32[256,128]{1,0:T(8,128)S(1)}, u32[]{:S(2)}, u32[]{:S(2)}) %collective-permute-start.11) | collective-permute-done | bytes 131104 | tf_op jit(solution)/shard_map/ppermute | solution.py:118
  202.5 3.0 collective-permute-start.13
  205.6 2.6 collective-permute-start.14
  208.7 1.9 collective-permute-done.13
  210.6 2.8 collective-permute-done.14
  213.4 86.5 %reduce-scatter.2.cloned.1.call-done = f32[128,1024]{1,0:T(8,128)} async-done(((f32[4096,1024]{1,0:T(8,128)}), f32[128,1024]{1,0:T(8,128)}) %reduce-scatter.2.cloned.1.call-update) | async-done | bytes 524304 | tf_op jit(solution)/shard_map/reduce_scatter | solution.py:163
  301.5 4.7 %fusion.13 = f32[128,4096]{1,0:T(8,128)S(1)} fusion(bf16[128,1024]{0,1:T(8,128)(2,1)S(1)} %bitcast.48, bf16[1024,4096]{1,0:T(8,128)(2,1)} %param.17), kind=kOutput, calls=%fused_computation.51 | convolution fusion | flops 1073741824 | bytes 10747904 | tf_op jit(solution)/shard_map/dot_general | solution.py:256
  306.3 1.6 collective-permute-start.16
  307.9 2.9 collective-permute-start.17
  310.8 1.4 collective-permute-start.18
  312.2 3.4 %collective-permute-done.16 = bf16[128,1024]{1,0:T(8,128)(2,1)S(1)} collective-permute-done((bf16[128,1024]{1,0:T(8,128)(2,1)S(1)}, bf16[128,1024]{1,0:T(8,128)(2,1)S(1)}, u32[]{:S(2)}, u32[]{:S(2)}) %collective-permute-start.16) | collective-permute-done | bytes 262176 | tf_op jit(solution)/shard_map/ppermute | solution.py:179
  315.6 5.4 %collective-permute-done.17 = bf16[128,1024]{1,0:T(8,128)(2,1)S(1)} collective-permute-done((bf16[128,1024]{1,0:T(8,128)(2,1)S(1)}, bf16[128,1024]{1,0:T(8,128)(2,1)S(1)}, u32[]{:S(2)}, u32[]{:S(2)}) %collective-permute-start.17) | collective-permute-done | bytes 262176 | tf_op jit(solution)/shard_map/ppermute | solution.py:179
  321.0 1.8 add_convert_fusion
  (79 shorter events, 19.1 us)
Async XLA Ops:
  6.5 7.5 %copy-start = (s32[64]{0:T(128)S(1)}, s32[64]{0:T(128)}, u32[]{:S(2)}) copy-start(s32[64]{0:T(128)} %param.16) | copy-start | bytes 772
  6.5 58.2 %all-gather.2.cloned.1.call-start = ((), (), s32[]{:S(2)}) async-start(), calls=%async_computation.1 | async-start | bytes 8650752 | tf_op jit(solution)/shard_map/all_gather | solution.py:135
  7.3 292.6 %reduce-scatter.2.cloned.1.call-start = ((), (), s32[]{:S(2)}) async-start(), calls=%async_computation.2 | async-start | bytes 17301504 | tf_op jit(solution)/shard_map/reduce_scatter | solution.py:163
  14.0 1.8 copy-start.1
  14.0 3.2 copy-start.6
  94.6 1.6 collective-permute-start
  97.1 6.9 %collective-permute-start.1 = (f32[256,128]{1,0:T(8,128)S(1)}, f32[256,128]{1,0:T(8,128)S(1)}, u32[]{:S(2)}, u32[]{:S(2)}) collective-permute-start(f32[256,128]{1,0:T(8,128)S(1)} %max.34), channel_id=1, source_target_pairs={{0,2},{1,3},{2,4},{3,5},{4,6},{5,7},{6,0},{7,1},{8,10},{9,11},{10,... | collective-permute-start | bytes 393224 | tf_op jit(solution)/shard_map/ppermute | solution.py:118
  98.6 9.1 %collective-permute-start.2 = (f32[256,128]{1,0:T(8,128)S(1)}, f32[256,128]{1,0:T(8,128)S(1)}, u32[]{:S(2)}, u32[]{:S(2)}) collective-permute-start(f32[256,128]{1,0:T(8,128)S(1)} %max.34), channel_id=1, source_target_pairs={{0,4},{1,5},{2,6},{3,7},{4,0},{5,1},{6,2},{7,3},{8,12},{9,13},{10,... | collective-permute-start | bytes 393224 | tf_op jit(solution)/shard_map/ppermute | solution.py:118
  101.3 6.4 %collective-permute-start.3 = (f32[256,128]{1,0:T(8,128)S(1)}, f32[256,128]{1,0:T(8,128)S(1)}, u32[]{:S(2)}, u32[]{:S(2)}) collective-permute-start(f32[256,128]{1,0:T(8,128)S(1)} %max.34), channel_id=1, source_target_pairs={{0,6},{1,7},{2,0},{3,1},{4,2},{5,3},{6,4},{7,5},{8,14},{9,15},{10,... | collective-permute-start | bytes 393224 | tf_op jit(solution)/shard_map/ppermute | solution.py:118
  107.8 7.6 %collective-permute-start.4 = (f32[256,128]{1,0:T(8,128)S(1)}, f32[256,128]{1,0:T(8,128)S(1)}, u32[]{:S(2)}, u32[]{:S(2)}) collective-permute-start(f32[256,128]{1,0:T(8,128)S(1)} %maximum_maximum_fusion.1), channel_id=1, source_target_pairs={{0,8},{1,9},{2,10},{3,11},{4,12},{5,13},{6,14},{7,15},{8,16},{9,17... | collective-permute-start | bytes 393224 | tf_op jit(solution)/shard_map/ppermute | solution.py:118
  108.7 8.0 %collective-permute-start.5 = (f32[256,128]{1,0:T(8,128)S(1)}, f32[256,128]{1,0:T(8,128)S(1)}, u32[]{:S(2)}, u32[]{:S(2)}) collective-permute-start(f32[256,128]{1,0:T(8,128)S(1)} %maximum_maximum_fusion.1), channel_id=1, source_target_pairs={{0,16},{1,17},{2,18},{3,19},{4,20},{5,21},{6,22},{7,23},{8,24},{9,... | collective-permute-start | bytes 393224 | tf_op jit(solution)/shard_map/ppermute | solution.py:118
  111.5 5.7 %collective-permute-start.6 = (f32[256,128]{1,0:T(8,128)S(1)}, f32[256,128]{1,0:T(8,128)S(1)}, u32[]{:S(2)}, u32[]{:S(2)}) collective-permute-start(f32[256,128]{1,0:T(8,128)S(1)} %maximum_maximum_fusion.1), channel_id=1, source_target_pairs={{0,24},{1,25},{2,26},{3,27},{4,28},{5,29},{6,30},{7,31},{8,0},{9,1... | collective-permute-start | bytes 393224 | tf_op jit(solution)/shard_map/ppermute | solution.py:118
  183.3 0.8 copy-start.4
  183.3 2.3 copy-start.5
  183.3 6.7 %copy-start.2 = (bf16[128,1024]{1,0:T(8,128)(2,1)S(1)}, bf16[128,1024]{1,0:T(8,128)(2,1)}, u32[]{:S(2)}) copy-start(bf16[128,1024]{1,0:T(8,128)(2,1)} %param.9) | copy-start | bytes 786436
  183.4 7.0 %copy-start.3 = (f32[256,128]{1,0:T(8,128)S(1)}, f32[256,128]{1,0:T(8,128)}, u32[]{:S(2)}) copy-start(f32[256,128]{1,0:T(8,128)} %get-tuple-element.8) | copy-start | bytes 393220
  184.3 6.0 %collective-permute-start.7 = (bf16[128,256]{0,1:T(8,128)(2,1)S(1)}, bf16[128,256]{0,1:T(8,128)(2,1)S(1)}, u32[]{:S(2)}, u32[]{:S(2)}) collective-permute-start(bf16[128,256]{0,1:T(8,128)(2,1)S(1)} %copy.27), channel_id=1, source_target_pairs={{0,1},{1,2},{2,3},{3,4},{4,5},{5,6},{6,7},{7,8},{8,9},{9,10},{10,1... | collective-permute-start | bytes 196616 | tf_op jit(solution)/shard_map/ppermute | solution.py:19
  185.6 12.1 %collective-permute-start.8 = (bf16[128,256]{1,0:T(8,128)(2,1)S(1)}, bf16[128,256]{1,0:T(8,128)(2,1)S(1)}, u32[]{:S(2)}, u32[]{:S(2)}) collective-permute-start(bf16[128,256]{1,0:T(8,128)(2,1)S(1)} %copy-done.5), channel_id=1, source_target_pairs={{0,1},{1,2},{2,3},{3,4},{4,5},{5,6},{6,7},{7,8},{8,9},{9,10},{10,1... | collective-permute-start | bytes 196616 | tf_op jit(solution)/shard_map/ppermute | solution.py:19
  190.4 1.4 collective-permute-start.9
  191.8 6.8 %collective-permute-start.10 = (f32[256,128]{1,0:T(8,128)S(1)}, f32[256,128]{1,0:T(8,128)S(1)}, u32[]{:S(2)}, u32[]{:S(2)}) collective-permute-start(f32[256,128]{1,0:T(8,128)S(1)} %add.186), channel_id=1, source_target_pairs={{0,2},{1,3},{2,4},{3,5},{4,6},{5,7},{6,0},{7,1},{8,10},{9,11},{10,... | collective-permute-start | bytes 393224 | tf_op jit(solution)/shard_map/ppermute | solution.py:118
  192.8 9.6 %collective-permute-start.11 = (f32[256,128]{1,0:T(8,128)S(1)}, f32[256,128]{1,0:T(8,128)S(1)}, u32[]{:S(2)}, u32[]{:S(2)}) collective-permute-start(f32[256,128]{1,0:T(8,128)S(1)} %add.186), channel_id=1, source_target_pairs={{0,4},{1,5},{2,6},{3,7},{4,0},{5,1},{6,2},{7,3},{8,12},{9,13},{10,... | collective-permute-start | bytes 393224 | tf_op jit(solution)/shard_map/ppermute | solution.py:118
  196.2 6.3 %collective-permute-start.12 = (f32[256,128]{1,0:T(8,128)S(1)}, f32[256,128]{1,0:T(8,128)S(1)}, u32[]{:S(2)}, u32[]{:S(2)}) collective-permute-start(f32[256,128]{1,0:T(8,128)S(1)} %add.186), channel_id=1, source_target_pairs={{0,6},{1,7},{2,0},{3,1},{4,2},{5,3},{6,4},{7,5},{8,14},{9,15},{10,... | collective-permute-start | bytes 393224 | tf_op jit(solution)/shard_map/ppermute | solution.py:118
  202.5 8.1 %collective-permute-start.13 = (f32[256,128]{1,0:T(8,128)S(1)}, f32[256,128]{1,0:T(8,128)S(1)}, u32[]{:S(2)}, u32[]{:S(2)}) collective-permute-start(f32[256,128]{1,0:T(8,128)S(1)} %add_add_fusion), channel_id=1, source_target_pairs={{0,8},{1,9},{2,10},{3,11},{4,12},{5,13},{6,14},{7,15},{8,16},{9,17... | collective-permute-start | bytes 393224 | tf_op jit(solution)/shard_map/ppermute | solution.py:118
  205.6 7.8 %collective-permute-start.14 = (f32[256,128]{1,0:T(8,128)S(1)}, f32[256,128]{1,0:T(8,128)S(1)}, u32[]{:S(2)}, u32[]{:S(2)}) collective-permute-start(f32[256,128]{1,0:T(8,128)S(1)} %add_add_fusion), channel_id=1, source_target_pairs={{0,16},{1,17},{2,18},{3,19},{4,20},{5,21},{6,22},{7,23},{8,24},{9,... | collective-permute-start | bytes 393224 | tf_op jit(solution)/shard_map/ppermute | solution.py:118
  208.1 5.2 %collective-permute-start.15 = (f32[256,128]{1,0:T(8,128)S(1)}, f32[256,128]{1,0:T(8,128)S(1)}, u32[]{:S(2)}, u32[]{:S(2)}) collective-permute-start(f32[256,128]{1,0:T(8,128)S(1)} %add_add_fusion), channel_id=1, source_target_pairs={{0,24},{1,25},{2,26},{3,27},{4,28},{5,29},{6,30},{7,31},{8,0},{9,1... | collective-permute-start | bytes 393224 | tf_op jit(solution)/shard_map/ppermute | solution.py:118
  306.3 9.3 %collective-permute-start.16 = (bf16[128,1024]{1,0:T(8,128)(2,1)S(1)}, bf16[128,1024]{1,0:T(8,128)(2,1)S(1)}, u32[]{:S(2)}, u32[]{:S(2)}) collective-permute-start(bf16[128,1024]{1,0:T(8,128)(2,1)S(1)} %get-tuple-element.13), channel_id=1, source_target_pairs={{0,32},{32,64},{64,96},{96,0},{1,33},{33,65},{65,97},{97,1},{2,34}... | collective-permute-start | bytes 786440 | tf_op jit(solution)/shard_map/ppermute | solution.py:179
  307.9 13.1 %collective-permute-start.17 = (bf16[128,1024]{1,0:T(8,128)(2,1)S(1)}, bf16[128,1024]{1,0:T(8,128)(2,1)S(1)}, u32[]{:S(2)}, u32[]{:S(2)}) collective-permute-start(bf16[128,1024]{1,0:T(8,128)(2,1)S(1)} %get-tuple-element.15), channel_id=1, source_target_pairs={{0,64},{32,96},{64,0},{96,32},{1,65},{33,97},{65,1},{97,33},{2,66}... | collective-permute-start | bytes 786440 | tf_op jit(solution)/shard_map/ppermute | solution.py:179
  310.8 10.2 %collective-permute-start.18 = (bf16[128,1024]{1,0:T(8,128)(2,1)S(1)}, bf16[128,1024]{1,0:T(8,128)(2,1)}, u32[]{:S(2)}, u32[]{:S(2)}) collective-permute-start(bf16[128,1024]{1,0:T(8,128)(2,1)S(1)} %get-tuple-element.14), channel_id=1, source_target_pairs={{0,96},{32,0},{64,32},{96,64},{1,97},{33,1},{65,33},{97,65},{2,98}... | collective-permute-start | bytes 786440 | tf_op jit(solution)/shard_map/ppermute | solution.py:179
Sparse Core Ops, SparseCore 0:
  9.6 55.1 all-gather.1
  183.5 116.3 reduce-scatter.1

commit v8 on v7

--- a/solution.py
+++ b/solution.py
@@ -78,8 +78,8 @@
         if h % qgw == 0:
             keys = _slot_keys(kt_ref, blk_ref, base, h // qgw)
         q = q_ref[:, h * HEAD_SIZE : (h + 1) * HEAD_SIZE]
-        sc = jnp.dot(q, keys, preferred_element_type=jnp.float32) * scale
-        mx = jnp.max(jnp.where(mask, sc, -jnp.inf), axis=1, keepdims=True)
+        sc = jnp.dot(q, keys, preferred_element_type=jnp.float32)
+        mx = jnp.max(jnp.where(mask, sc, -jnp.inf), axis=1, keepdims=True) * scale
         stats = jnp.where(lane == h, mx, stats)
     m_ref[...] = jnp.transpose(stats)[: m_ref.shape[0], :]
 
@@ -94,6 +94,7 @@
     mask = _slot_mask(lo_ref, hi_ref, base, rows)
     lane = lax.broadcasted_iota(jnp.int32, (1, STAT_LANES), 1)
     totals = jnp.zeros((tile, STAT_LANES), jnp.float32)
+    ones = jnp.ones((SLOTS * HEAD_SIZE, STAT_LANES), jnp.bfloat16)
     top = jnp.transpose(m_ref[...])
     for h in range(heads):
         if h % qgw == 0:
@@ -102,9 +103,11 @@
         q = q_ref[:, h * HEAD_SIZE : (h + 1) * HEAD_SIZE]
         sc = jnp.dot(q, keys, preferred_element_type=jnp.float32) * scale
         p = jnp.exp(jnp.where(mask, sc - top[:, h : h + 1], -jnp.inf))
-        ctx = jnp.dot(p.astype(jnp.bfloat16), values, preferred_element_type=jnp.float32)
+        weights = p.astype(jnp.bfloat16)
+        ctx = jnp.dot(weights, values, preferred_element_type=jnp.float32)
         o_ref[:, h * HEAD_SIZE : (h + 1) * HEAD_SIZE] = ctx
-        totals = jnp.where(lane == h, jnp.sum(p, axis=1, keepdims=True), totals)
+        row_sum = jnp.dot(weights, ones, preferred_element_type=jnp.float32)
+        totals = jnp.where(lane == h, row_sum, totals)
     t_ref[...] = jnp.transpose(totals)[: t_ref.shape[0], :]
 
 

time: 331 us -> 341 us (1.030)
  Pallas kernels: 95.3 us -> 106 us
    pallas_call x1, Pallas kernels: 65.4 us -> 76.4 us  [far_part(): pl.pallas_call(functools.partial(ctx_kernel, **kw), out_shape=(jax.ShapeD...]
where the time goes in v8:
time: 341 us; the launch traced here: 340 us
  waiting for transfers between devices  162 us (48%)
  Pallas kernels  106 us (31%)
  starting transfers between devices  33.8 us (10%)
  local copies, waits for them, and re-layouts  13.9 us (4%)
  between operations  13.7 us (4%)
  other arithmetic  5.44 us (2%)
  matrix products  5.37 us (2%)
    reduce_scatter x1, waiting for transfers between devices, far_part(): context = lax.psum_scatter(partial, 'blk', scatter_dimension=0, tiled=True)  87.1 us
    pallas_call x1, Pallas kernels, far_part(): pl.pallas_call(functools.partial(ctx_kernel, **kw), out_shape=(jax.ShapeD...  76.4 us
    all_gather x1, waiting for transfers between devices, far_part(): gathered = lax.all_gather(queries, 'blk', axis=0, tiled=True)  45.3 us
    pallas_call x1, Pallas kernels, far_part(): pl.pallas_call(functools.partial(max_kernel, **kw), out_shape=stat_shape,...  29.1 us
    ppermute x14, starting transfers between devices, butterfly(): lax.ppermute(x, axis, [(i, i + ((digit(i) + d) % radix - digit(i)) * stri...  23.1 us
    ppermute x14, waiting for transfers between devices, butterfly(): lax.ppermute(x, axis, [(i, i + ((digit(i) + d) % radix - digit(i)) * stri...  20.2 us
    ppermute x3, waiting for transfers between devices, column_sum(): got = lax.ppermute(sent, axis, [(i, (i + d) % n) for i in range(n)])  8.83 us
  transfers between devices with their start and end apart: 21, of which 15 were waited for; matrix products, arithmetic and copies ran while one was open for 4% of the time, Pallas kernels for 0%

profile of v8, /device:TPU:0, one launch (start us, length us, event | category | flops | bytes accessed | tf_op | source)
XLA Modules:
  0.0 339.8 jit_solution(3584323245116912063)
XLA Ops:
  9.3 1.6 gather_fusion.1
  10.9 1.6 gather_fusion
  14.0 1.5 gather_fusion.2
  15.8 1.4 copy.26
  17.3 2.1 gather_fusion.3
  19.4 45.3 %all-gather.2.cloned.1.call-done.q_ref = bf16[4096,1024]{1,0:T(8,128)(2,1)} async-done(((bf16[128,1024]{1,0:T(8,128)(2,1)}), bf16[4096,1024]{1,0:T(8,128)(2,1)}) %all-gather.2.cloned.1.call-update) | async-done | bytes 8388624 | tf_op jit(solution)/shard_map/all_gather | solution.py:138
  64.8 29.1 %shard_map.91 = f32[256,128]{1,0:T(8,128)} custom-call(s32[160]{0:T(256)} %select_n.90.lo_ref, s32[160]{0:T(256)} %select_n.92.hi_ref, s32[160]{0:T(256)} %gather_fusion.3, bf16[4096,1024]{1,0:T(8,128)(2,1)} %all-gather.2.cloned.1.call-done.q_ref, bf16[16,256,128]{2,1,0:T(8,128)(2,1)} %bitcast.46), custom_call_target="tpu_custom_call" | custom-call | tf_op jit(solution)/shard_map/pallas_call | solution.py:148
  96.4 1.5 collective-permute-start.1
  97.9 2.7 collective-permute-start.2
  100.6 1.5 collective-permute-start.3
  103.3 3.7 %collective-permute-done.2 = f32[256,128]{1,0:T(8,128)S(1)} collective-permute-done((f32[256,128]{1,0:T(8,128)S(1)}, f32[256,128]{1,0:T(8,128)S(1)}, u32[]{:S(2)}, u32[]{:S(2)}) %collective-permute-start.2) | collective-permute-done | bytes 131104 | tf_op jit(solution)/shard_map/ppermute | solution.py:121
  108.1 2.7 collective-permute-start.5
  110.8 1.4 collective-permute-start.6
  112.2 2.5 collective-permute-done.4
  114.7 1.4 collective-permute-done.5
  117.2 76.4 %shard_map.92 = (f32[4096,1024]{1,0:T(8,128)}, f32[256,128]{1,0:T(8,128)}) custom-call(s32[160]{0:T(256)} %select_n.90.lo_ref, s32[160]{0:T(256)} %select_n.92.hi_ref, s32[160]{0:T(256)} %gather_fusion.3, bf16[4096,1024]{1,0:T(8,128)(2,1)} %all-gather.2.cloned.1.call-done.q_ref, bf16[16,256,128]{2,1,0:T(8,128)(2,1)} %bitcast.47, ...), custom_call_target="tpu_custom_call" | custom-call | tf_op jit(solution)/shard_map/pallas_call | solution.py:156
  195.8 3.5 %collective-permute-start.8 = (bf16[128,256]{1,0:T(8,128)(2,1)S(1)}, bf16[128,256]{1,0:T(8,128)(2,1)S(1)}, u32[]{:S(2)}, u32[]{:S(2)}) collective-permute-start(bf16[128,256]{1,0:T(8,128)(2,1)S(1)} %copy-done.5), channel_id=1, source_target_pairs={{0,1},{1,2},{2,3},{3,4},{4,5},{5,6},{6,7},{7,8},{8,9},{9,10},{10,1... | collective-permute-start | bytes 196616 | tf_op jit(solution)/shard_map/ppermute | solution.py:19
  201.5 1.6 collective-permute-start.10
  203.1 3.3 collective-permute-start.11
  208.8 4.0 %collective-permute-done.11 = f32[256,128]{1,0:T(8,128)S(1)} collective-permute-done((f32[256,128]{1,0:T(8,128)S(1)}, f32[256,128]{1,0:T(8,128)S(1)}, u32[]{:S(2)}, u32[]{:S(2)}) %collective-permute-start.11) | collective-permute-done | bytes 131104 | tf_op jit(solution)/shard_map/ppermute | solution.py:121
  212.8 3.0 collective-permute-start.13
  215.8 2.0 collective-permute-start.14
  218.9 1.3 collective-permute-done.13
  220.3 2.8 collective-permute-done.14
  223.1 87.1 %reduce-scatter.2.cloned.1.call-done = f32[128,1024]{1,0:T(8,128)} async-done(((f32[4096,1024]{1,0:T(8,128)}), f32[128,1024]{1,0:T(8,128)}) %reduce-scatter.2.cloned.1.call-update) | async-done | bytes 524304 | tf_op jit(solution)/shard_map/reduce_scatter | solution.py:166
  311.7 4.7 %fusion.13 = f32[128,4096]{1,0:T(8,128)S(1)} fusion(bf16[128,1024]{0,1:T(8,128)(2,1)S(1)} %bitcast.48, bf16[1024,4096]{1,0:T(8,128)(2,1)} %param.17), kind=kOutput, calls=%fused_computation.51 | convolution fusion | flops 1073741824 | bytes 10747904 | tf_op jit(solution)/shard_map/dot_general | solution.py:259
  316.5 1.6 collective-permute-start.16
  318.2 2.9 collective-permute-start.17
  321.0 1.3 collective-permute-start.18
  322.4 3.5 %collective-permute-done.16 = bf16[128,1024]{1,0:T(8,128)(2,1)S(1)} collective-permute-done((bf16[128,1024]{1,0:T(8,128)(2,1)S(1)}, bf16[128,1024]{1,0:T(8,128)(2,1)S(1)}, u32[]{:S(2)}, u32[]{:S(2)}) %collective-permute-start.16) | collective-permute-done | bytes 262176 | tf_op jit(solution)/shard_map/ppermute | solution.py:182
  325.8 5.4 %collective-permute-done.17 = bf16[128,1024]{1,0:T(8,128)(2,1)S(1)} collective-permute-done((bf16[128,1024]{1,0:T(8,128)(2,1)S(1)}, bf16[128,1024]{1,0:T(8,128)(2,1)S(1)}, u32[]{:S(2)}, u32[]{:S(2)}) %collective-permute-start.17) | collective-permute-done | bytes 262176 | tf_op jit(solution)/shard_map/ppermute | solution.py:182
  331.2 1.8 add_convert_fusion
  (79 shorter events, 20.0 us)
Async XLA Ops:
  6.5 7.5 %copy-start = (s32[64]{0:T(128)S(1)}, s32[64]{0:T(128)}, u32[]{:S(2)}) copy-start(s32[64]{0:T(128)} %param.16) | copy-start | bytes 772
  6.5 58.2 %all-gather.2.cloned.1.call-start = ((), (), s32[]{:S(2)}) async-start(), calls=%async_computation.1 | async-start | bytes 8650752 | tf_op jit(solution)/shard_map/all_gather | solution.py:138
  7.3 302.9 %reduce-scatter.2.cloned.1.call-start = ((), (), s32[]{:S(2)}) async-start(), calls=%async_computation.2 | async-start | bytes 17301504 | tf_op jit(solution)/shard_map/reduce_scatter | solution.py:166
  14.0 1.8 copy-start.1
  14.0 3.2 copy-start.6
  93.9 1.6 collective-permute-start
  96.4 6.9 %collective-permute-start.1 = (f32[256,128]{1,0:T(8,128)S(1)}, f32[256,128]{1,0:T(8,128)S(1)}, u32[]{:S(2)}, u32[]{:S(2)}) collective-permute-start(f32[256,128]{1,0:T(8,128)S(1)} %max.34), channel_id=1, source_target_pairs={{0,2},{1,3},{2,4},{3,5},{4,6},{5,7},{6,0},{7,1},{8,10},{9,11},{10,... | collective-permute-start | bytes 393224 | tf_op jit(solution)/shard_map/ppermute | solution.py:121
  97.9 9.1 %collective-permute-start.2 = (f32[256,128]{1,0:T(8,128)S(1)}, f32[256,128]{1,0:T(8,128)S(1)}, u32[]{:S(2)}, u32[]{:S(2)}) collective-permute-start(f32[256,128]{1,0:T(8,128)S(1)} %max.34), channel_id=1, source_target_pairs={{0,4},{1,5},{2,6},{3,7},{4,0},{5,1},{6,2},{7,3},{8,12},{9,13},{10,... | collective-permute-start | bytes 393224 | tf_op jit(solution)/shard_map/ppermute | solution.py:121
  100.6 6.4 %collective-permute-start.3 = (f32[256,128]{1,0:T(8,128)S(1)}, f32[256,128]{1,0:T(8,128)S(1)}, u32[]{:S(2)}, u32[]{:S(2)}) collective-permute-start(f32[256,128]{1,0:T(8,128)S(1)} %max.34), channel_id=1, source_target_pairs={{0,6},{1,7},{2,0},{3,1},{4,2},{5,3},{6,4},{7,5},{8,14},{9,15},{10,... | collective-permute-start | bytes 393224 | tf_op jit(solution)/shard_map/ppermute | solution.py:121
  107.1 7.6 %collective-permute-start.4 = (f32[256,128]{1,0:T(8,128)S(1)}, f32[256,128]{1,0:T(8,128)S(1)}, u32[]{:S(2)}, u32[]{:S(2)}) collective-permute-start(f32[256,128]{1,0:T(8,128)S(1)} %maximum_maximum_fusion.1), channel_id=1, source_target_pairs={{0,8},{1,9},{2,10},{3,11},{4,12},{5,13},{6,14},{7,15},{8,16},{9,17... | collective-permute-start | bytes 393224 | tf_op jit(solution)/shard_map/ppermute | solution.py:121
  108.1 8.0 %collective-permute-start.5 = (f32[256,128]{1,0:T(8,128)S(1)}, f32[256,128]{1,0:T(8,128)S(1)}, u32[]{:S(2)}, u32[]{:S(2)}) collective-permute-start(f32[256,128]{1,0:T(8,128)S(1)} %maximum_maximum_fusion.1), channel_id=1, source_target_pairs={{0,16},{1,17},{2,18},{3,19},{4,20},{5,21},{6,22},{7,23},{8,24},{9,... | collective-permute-start | bytes 393224 | tf_op jit(solution)/shard_map/ppermute | solution.py:121
  110.8 5.7 %collective-permute-start.6 = (f32[256,128]{1,0:T(8,128)S(1)}, f32[256,128]{1,0:T(8,128)S(1)}, u32[]{:S(2)}, u32[]{:S(2)}) collective-permute-start(f32[256,128]{1,0:T(8,128)S(1)} %maximum_maximum_fusion.1), channel_id=1, source_target_pairs={{0,24},{1,25},{2,26},{3,27},{4,28},{5,29},{6,30},{7,31},{8,0},{9,1... | collective-permute-start | bytes 393224 | tf_op jit(solution)/shard_map/ppermute | solution.py:121
  193.6 0.8 copy-start.4
  193.6 2.3 copy-start.5
  193.6 6.2 %copy-start.2 = (bf16[128,1024]{1,0:T(8,128)(2,1)S(1)}, bf16[128,1024]{1,0:T(8,128)(2,1)}, u32[]{:S(2)}) copy-start(bf16[128,1024]{1,0:T(8,128)(2,1)} %param.9) | copy-start | bytes 786436
  193.6 6.5 %copy-start.3 = (f32[256,128]{1,0:T(8,128)S(1)}, f32[256,128]{1,0:T(8,128)}, u32[]{:S(2)}) copy-start(f32[256,128]{1,0:T(8,128)} %get-tuple-element.8) | copy-start | bytes 393220
  194.5 5.5 %collective-permute-start.7 = (bf16[128,256]{0,1:T(8,128)(2,1)S(1)}, bf16[128,256]{0,1:T(8,128)(2,1)S(1)}, u32[]{:S(2)}, u32[]{:S(2)}) collective-permute-start(bf16[128,256]{0,1:T(8,128)(2,1)S(1)} %copy.27), channel_id=1, source_target_pairs={{0,1},{1,2},{2,3},{3,4},{4,5},{5,6},{6,7},{7,8},{8,9},{9,10},{10,1... | collective-permute-start | bytes 196616 | tf_op jit(solution)/shard_map/ppermute | solution.py:19
  195.8 11.6 %collective-permute-start.8 = (bf16[128,256]{1,0:T(8,128)(2,1)S(1)}, bf16[128,256]{1,0:T(8,128)(2,1)S(1)}, u32[]{:S(2)}, u32[]{:S(2)}) collective-permute-start(bf16[128,256]{1,0:T(8,128)(2,1)S(1)} %copy-done.5), channel_id=1, source_target_pairs={{0,1},{1,2},{2,3},{3,4},{4,5},{5,6},{6,7},{7,8},{8,9},{9,10},{10,1... | collective-permute-start | bytes 196616 | tf_op jit(solution)/shard_map/ppermute | solution.py:19
  200.1 1.4 collective-permute-start.9
  201.5 7.2 %collective-permute-start.10 = (f32[256,128]{1,0:T(8,128)S(1)}, f32[256,128]{1,0:T(8,128)S(1)}, u32[]{:S(2)}, u32[]{:S(2)}) collective-permute-start(f32[256,128]{1,0:T(8,128)S(1)} %add.186), channel_id=1, source_target_pairs={{0,2},{1,3},{2,4},{3,5},{4,6},{5,7},{6,0},{7,1},{8,10},{9,11},{10,... | collective-permute-start | bytes 393224 | tf_op jit(solution)/shard_map/ppermute | solution.py:121
  203.1 9.6 %collective-permute-start.11 = (f32[256,128]{1,0:T(8,128)S(1)}, f32[256,128]{1,0:T(8,128)S(1)}, u32[]{:S(2)}, u32[]{:S(2)}) collective-permute-start(f32[256,128]{1,0:T(8,128)S(1)} %add.186), channel_id=1, source_target_pairs={{0,4},{1,5},{2,6},{3,7},{4,0},{5,1},{6,2},{7,3},{8,12},{9,13},{10,... | collective-permute-start | bytes 393224 | tf_op jit(solution)/shard_map/ppermute | solution.py:121
  206.4 6.3 %collective-permute-start.12 = (f32[256,128]{1,0:T(8,128)S(1)}, f32[256,128]{1,0:T(8,128)S(1)}, u32[]{:S(2)}, u32[]{:S(2)}) collective-permute-start(f32[256,128]{1,0:T(8,128)S(1)} %add.186), channel_id=1, source_target_pairs={{0,6},{1,7},{2,0},{3,1},{4,2},{5,3},{6,4},{7,5},{8,14},{9,15},{10,... | collective-permute-start | bytes 393224 | tf_op jit(solution)/shard_map/ppermute | solution.py:121
  212.8 7.5 %collective-permute-start.13 = (f32[256,128]{1,0:T(8,128)S(1)}, f32[256,128]{1,0:T(8,128)S(1)}, u32[]{:S(2)}, u32[]{:S(2)}) collective-permute-start(f32[256,128]{1,0:T(8,128)S(1)} %add_add_fusion), channel_id=1, source_target_pairs={{0,8},{1,9},{2,10},{3,11},{4,12},{5,13},{6,14},{7,15},{8,16},{9,17... | collective-permute-start | bytes 393224 | tf_op jit(solution)/shard_map/ppermute | solution.py:121
  215.8 7.2 %collective-permute-start.14 = (f32[256,128]{1,0:T(8,128)S(1)}, f32[256,128]{1,0:T(8,128)S(1)}, u32[]{:S(2)}, u32[]{:S(2)}) collective-permute-start(f32[256,128]{1,0:T(8,128)S(1)} %add_add_fusion), channel_id=1, source_target_pairs={{0,16},{1,17},{2,18},{3,19},{4,20},{5,21},{6,22},{7,23},{8,24},{9,... | collective-permute-start | bytes 393224 | tf_op jit(solution)/shard_map/ppermute | solution.py:121
  217.8 5.2 %collective-permute-start.15 = (f32[256,128]{1,0:T(8,128)S(1)}, f32[256,128]{1,0:T(8,128)S(1)}, u32[]{:S(2)}, u32[]{:S(2)}) collective-permute-start(f32[256,128]{1,0:T(8,128)S(1)} %add_add_fusion), channel_id=1, source_target_pairs={{0,24},{1,25},{2,26},{3,27},{4,28},{5,29},{6,30},{7,31},{8,0},{9,1... | collective-permute-start | bytes 393224 | tf_op jit(solution)/shard_map/ppermute | solution.py:121
  316.5 9.3 %collective-permute-start.16 = (bf16[128,1024]{1,0:T(8,128)(2,1)S(1)}, bf16[128,1024]{1,0:T(8,128)(2,1)S(1)}, u32[]{:S(2)}, u32[]{:S(2)}) collective-permute-start(bf16[128,1024]{1,0:T(8,128)(2,1)S(1)} %get-tuple-element.13), channel_id=1, source_target_pairs={{0,32},{32,64},{64,96},{96,0},{1,33},{33,65},{65,97},{97,1},{2,34}... | collective-permute-start | bytes 786440 | tf_op jit(solution)/shard_map/ppermute | solution.py:182
  318.2 13.0 %collective-permute-start.17 = (bf16[128,1024]{1,0:T(8,128)(2,1)S(1)}, bf16[128,1024]{1,0:T(8,128)(2,1)S(1)}, u32[]{:S(2)}, u32[]{:S(2)}) collective-permute-start(bf16[128,1024]{1,0:T(8,128)(2,1)S(1)} %get-tuple-element.15), channel_id=1, source_target_pairs={{0,64},{32,96},{64,0},{96,32},{1,65},{33,97},{65,1},{97,33},{2,66}... | collective-permute-start | bytes 786440 | tf_op jit(solution)/shard_map/ppermute | solution.py:182
  321.0 10.2 %collective-permute-start.18 = (bf16[128,1024]{1,0:T(8,128)(2,1)S(1)}, bf16[128,1024]{1,0:T(8,128)(2,1)}, u32[]{:S(2)}, u32[]{:S(2)}) collective-permute-start(bf16[128,1024]{1,0:T(8,128)(2,1)S(1)} %get-tuple-element.14), channel_id=1, source_target_pairs={{0,96},{32,0},{64,32},{96,64},{1,97},{33,1},{65,33},{97,65},{2,98}... | collective-permute-start | bytes 786440 | tf_op jit(solution)/shard_map/ppermute | solution.py:182
Sparse Core Ops, SparseCore 0:
  9.6 55.1 all-gather.1
  193.8 116.3 reduce-scatter.1

commit v9 on v7

--- a/solution.py
+++ b/solution.py
@@ -66,21 +66,27 @@
     return jnp.concatenate([v_ref[blk_ref[base + s], :, cols] for s in range(SLOTS)], axis=0)
 
 
+def _stacked(q_ref, kv, qgw):
+    return jnp.concatenate(
+        [q_ref[:, h * HEAD_SIZE : (h + 1) * HEAD_SIZE] for h in range(kv * qgw, (kv + 1) * qgw)],
+        axis=0,
+    )
+
+
 def max_kernel(lo_ref, hi_ref, blk_ref, q_ref, kt_ref, m_ref, *, heads, qgw, scale):
     i = pl.program_id(0)
     tile = q_ref.shape[0]
     base = i * SLOTS
-    rows = i * tile + lax.broadcasted_iota(jnp.int32, (tile, 1), 0)
+    rows = i * tile + lax.broadcasted_iota(jnp.int32, (qgw * tile, 1), 0) % tile
     mask = _slot_mask(lo_ref, hi_ref, base, rows)
     lane = lax.broadcasted_iota(jnp.int32, (1, STAT_LANES), 1)
     stats = jnp.full((tile, STAT_LANES), -jnp.inf, jnp.float32)
-    for h in range(heads):
-        if h % qgw == 0:
-            keys = _slot_keys(kt_ref, blk_ref, base, h // qgw)
-        q = q_ref[:, h * HEAD_SIZE : (h + 1) * HEAD_SIZE]
-        sc = jnp.dot(q, keys, preferred_element_type=jnp.float32) * scale
+    for kv in range(heads // qgw):
+        keys = _slot_keys(kt_ref, blk_ref, base, kv)
+        sc = jnp.dot(_stacked(q_ref, kv, qgw), keys, preferred_element_type=jnp.float32) * scale
         mx = jnp.max(jnp.where(mask, sc, -jnp.inf), axis=1, keepdims=True)
-        stats = jnp.where(lane == h, mx, stats)
+        for j in range(qgw):
+            stats = jnp.where(lane == kv * qgw + j, mx[j * tile : (j + 1) * tile], stats)
     m_ref[...] = jnp.transpose(stats)[: m_ref.shape[0], :]
 
 
@@ -90,21 +96,23 @@
     i = pl.program_id(0)
     tile = q_ref.shape[0]
     base = i * SLOTS
-    rows = i * tile + lax.broadcasted_iota(jnp.int32, (tile, 1), 0)
+    rows = i * tile + lax.broadcasted_iota(jnp.int32, (qgw * tile, 1), 0) % tile
     mask = _slot_mask(lo_ref, hi_ref, base, rows)
     lane = lax.broadcasted_iota(jnp.int32, (1, STAT_LANES), 1)
     totals = jnp.zeros((tile, STAT_LANES), jnp.float32)
-    top = jnp.transpose(m_ref[...])
-    for h in range(heads):
-        if h % qgw == 0:
-            keys = _slot_keys(kt_ref, blk_ref, base, h // qgw)
-            values = _slot_values(v_ref, blk_ref, base, h // qgw)
-        q = q_ref[:, h * HEAD_SIZE : (h + 1) * HEAD_SIZE]
-        sc = jnp.dot(q, keys, preferred_element_type=jnp.float32) * scale
-        p = jnp.exp(jnp.where(mask, sc - top[:, h : h + 1], -jnp.inf))
+    tops = jnp.transpose(m_ref[...])
+    for kv in range(heads // qgw):
+        group = range(kv * qgw, (kv + 1) * qgw)
+        keys = _slot_keys(kt_ref, blk_ref, base, kv)
+        values = _slot_values(v_ref, blk_ref, base, kv)
+        sc = jnp.dot(_stacked(q_ref, kv, qgw), keys, preferred_element_type=jnp.float32) * scale
+        top = jnp.concatenate([tops[:, h : h + 1] for h in group], axis=0)
+        p = jnp.exp(jnp.where(mask, sc - top, -jnp.inf))
         ctx = jnp.dot(p.astype(jnp.bfloat16), values, preferred_element_type=jnp.float32)
-        o_ref[:, h * HEAD_SIZE : (h + 1) * HEAD_SIZE] = ctx
-        totals = jnp.where(lane == h, jnp.sum(p, axis=1, keepdims=True), totals)
+        tot = jnp.sum(p, axis=1, keepdims=True)
+        for j, h in enumerate(group):
+            o_ref[:, h * HEAD_SIZE : (h + 1) * HEAD_SIZE] = ctx[j * tile : (j + 1) * tile]
+            totals = jnp.where(lane == h, tot[j * tile : (j + 1) * tile], totals)
     t_ref[...] = jnp.transpose(totals)[: t_ref.shape[0], :]
 
 

time: 331 us -> 314 us (0.949)
  Pallas kernels: 95.3 us -> 78.3 us
    pallas_call x1, Pallas kernels: 65.4 us -> 46.9 us  [far_part(): pl.pallas_call(functools.partial(ctx_kernel, **kw), out_shape=(jax.ShapeD...]
  transfers between devices with their start and end apart: 21 -> 21, of which waited for: 15 -> 15; matrix products, arithmetic and copies ran while one was open for 4% -> 5% of each run, Pallas kernels for 0% -> 0%
where the time goes in v9:
time: 314 us; the launch traced here: 313 us
  waiting for transfers between devices  162 us (52%)
  Pallas kernels  78.3 us (25%)
  starting transfers between devices  34.4 us (11%)
  local copies, waits for them, and re-layouts  13.9 us (4%)
  between operations  13.7 us (4%)
  other arithmetic  5.44 us (2%)
  matrix products  5.36 us (2%)
    reduce_scatter x1, waiting for transfers between devices, far_part(): context = lax.psum_scatter(partial, 'blk', scatter_dimension=0, tiled=True)  86.5 us
    pallas_call x1, Pallas kernels, far_part(): pl.pallas_call(functools.partial(ctx_kernel, **kw), out_shape=(jax.ShapeD...  46.9 us
    all_gather x1, waiting for transfers between devices, far_part(): gathered = lax.all_gather(queries, 'blk', axis=0, tiled=True)  45.3 us
    pallas_call x1, Pallas kernels, far_part(): pl.pallas_call(functools.partial(max_kernel, **kw), out_shape=stat_shape,...  31.4 us
    ppermute x14, starting transfers between devices, butterfly(): lax.ppermute(x, axis, [(i, i + ((digit(i) + d) % radix - digit(i)) * stri...  23.1 us
    ppermute x14, waiting for transfers between devices, butterfly(): lax.ppermute(x, axis, [(i, i + ((digit(i) + d) % radix - digit(i)) * stri...  20.2 us
    ppermute x3, waiting for transfers between devices, column_sum(): got = lax.ppermute(sent, axis, [(i, (i + d) % n) for i in range(n)])  8.86 us
  transfers between devices with their start and end apart: 21, of which 15 were waited for; matrix products, arithmetic and copies ran while one was open for 5% of the time, Pallas kernels for 0%

profile of v9, /device:TPU:0, one launch (start us, length us, event | category | flops | bytes accessed | tf_op | source)
XLA Modules:
  0.0 312.8 jit_solution(10660771393981321718)
XLA Ops:
  9.3 1.6 gather_fusion.1
  10.9 1.6 gather_fusion
  14.0 1.5 gather_fusion.2
  15.8 1.4 copy.26
  17.3 2.1 gather_fusion.3
  19.4 45.3 %all-gather.2.cloned.1.call-done.q_ref = bf16[4096,1024]{1,0:T(8,128)(2,1)} async-done(((bf16[128,1024]{1,0:T(8,128)(2,1)}), bf16[4096,1024]{1,0:T(8,128)(2,1)}) %all-gather.2.cloned.1.call-update) | async-done | bytes 8388624 | tf_op jit(solution)/shard_map/all_gather | solution.py:143
  64.8 31.4 %shard_map.91 = f32[256,128]{1,0:T(8,128)} custom-call(s32[160]{0:T(256)} %select_n.90.lo_ref, s32[160]{0:T(256)} %select_n.92.hi_ref, s32[160]{0:T(256)} %gather_fusion.3, bf16[4096,1024]{1,0:T(8,128)(2,1)} %all-gather.2.cloned.1.call-done.q_ref, bf16[16,256,128]{2,1,0:T(8,128)(2,1)} %bitcast.46), custom_call_target="tpu_custom_call" | custom-call | tf_op jit(solution)/shard_map/pallas_call | solution.py:153
  98.7 1.5 collective-permute-start.1
  100.2 2.7 collective-permute-start.2
  102.9 1.5 collective-permute-start.3
  105.6 3.7 %collective-permute-done.2 = f32[256,128]{1,0:T(8,128)S(1)} collective-permute-done((f32[256,128]{1,0:T(8,128)S(1)}, f32[256,128]{1,0:T(8,128)S(1)}, u32[]{:S(2)}, u32[]{:S(2)}) %collective-permute-start.2) | collective-permute-done | bytes 131104 | tf_op jit(solution)/shard_map/ppermute | solution.py:126
  110.4 2.7 collective-permute-start.5
  113.1 1.4 collective-permute-start.6
  114.5 2.4 collective-permute-done.4
  117.0 1.4 collective-permute-done.5
  119.5 46.9 %shard_map.92 = (f32[4096,1024]{1,0:T(8,128)}, f32[256,128]{1,0:T(8,128)}) custom-call(s32[160]{0:T(256)} %select_n.90.lo_ref, s32[160]{0:T(256)} %select_n.92.hi_ref, s32[160]{0:T(256)} %gather_fusion.3, bf16[4096,1024]{1,0:T(8,128)(2,1)} %all-gather.2.cloned.1.call-done.q_ref, bf16[16,256,128]{2,1,0:T(8,128)(2,1)} %bitcast.47, ...), custom_call_target="tpu_custom_call" | custom-call | tf_op jit(solution)/shard_map/pallas_call | solution.py:161
  168.7 4.0 %collective-permute-start.8 = (bf16[128,256]{1,0:T(8,128)(2,1)S(1)}, bf16[128,256]{1,0:T(8,128)(2,1)S(1)}, u32[]{:S(2)}, u32[]{:S(2)}) collective-permute-start(bf16[128,256]{1,0:T(8,128)(2,1)S(1)} %copy-done.5), channel_id=1, source_target_pairs={{0,1},{1,2},{2,3},{3,4},{4,5},{5,6},{6,7},{7,8},{8,9},{9,10},{10,1... | collective-permute-start | bytes 196616 | tf_op jit(solution)/shard_map/ppermute | solution.py:19
  175.9 3.3 %collective-permute-start.11 = (f32[256,128]{1,0:T(8,128)S(1)}, f32[256,128]{1,0:T(8,128)S(1)}, u32[]{:S(2)}, u32[]{:S(2)}) collective-permute-start(f32[256,128]{1,0:T(8,128)S(1)} %add.186), channel_id=1, source_target_pairs={{0,4},{1,5},{2,6},{3,7},{4,0},{5,1},{6,2},{7,3},{8,12},{9,13},{10,... | collective-permute-start | bytes 393224 | tf_op jit(solution)/shard_map/ppermute | solution.py:126
  179.2 1.5 collective-permute-start.12
  181.7 3.9 %collective-permute-done.11 = f32[256,128]{1,0:T(8,128)S(1)} collective-permute-done((f32[256,128]{1,0:T(8,128)S(1)}, f32[256,128]{1,0:T(8,128)S(1)}, u32[]{:S(2)}, u32[]{:S(2)}) %collective-permute-start.11) | collective-permute-done | bytes 131104 | tf_op jit(solution)/shard_map/ppermute | solution.py:126
  185.6 3.0 collective-permute-start.13
  188.6 2.6 collective-permute-start.14
  191.8 1.9 collective-permute-done.13
  193.7 2.8 collective-permute-done.14
  196.5 86.5 %reduce-scatter.2.cloned.1.call-done = f32[128,1024]{1,0:T(8,128)} async-done(((f32[4096,1024]{1,0:T(8,128)}), f32[128,1024]{1,0:T(8,128)}) %reduce-scatter.2.cloned.1.call-update) | async-done | bytes 524304 | tf_op jit(solution)/shard_map/reduce_scatter | solution.py:171
  284.6 4.7 %fusion.13 = f32[128,4096]{1,0:T(8,128)S(1)} fusion(bf16[128,1024]{0,1:T(8,128)(2,1)S(1)} %bitcast.48, bf16[1024,4096]{1,0:T(8,128)(2,1)} %param.17), kind=kOutput, calls=%fused_computation.51 | convolution fusion | flops 1073741824 | bytes 10747904 | tf_op jit(solution)/shard_map/dot_general | solution.py:264
  289.4 1.6 collective-permute-start.16
  291.0 2.9 collective-permute-start.17
  293.9 1.4 collective-permute-start.18
  295.2 3.4 %collective-permute-done.16 = bf16[128,1024]{1,0:T(8,128)(2,1)S(1)} collective-permute-done((bf16[128,1024]{1,0:T(8,128)(2,1)S(1)}, bf16[128,1024]{1,0:T(8,128)(2,1)S(1)}, u32[]{:S(2)}, u32[]{:S(2)}) %collective-permute-start.16) | collective-permute-done | bytes 262176 | tf_op jit(solution)/shard_map/ppermute | solution.py:187
  298.7 5.4 %collective-permute-done.17 = bf16[128,1024]{1,0:T(8,128)(2,1)S(1)} collective-permute-done((bf16[128,1024]{1,0:T(8,128)(2,1)S(1)}, bf16[128,1024]{1,0:T(8,128)(2,1)S(1)}, u32[]{:S(2)}, u32[]{:S(2)}) %collective-permute-start.17) | collective-permute-done | bytes 262176 | tf_op jit(solution)/shard_map/ppermute | solution.py:187
  304.1 1.8 add_convert_fusion
  (79 shorter events, 19.1 us)
Async XLA Ops:
  6.5 7.5 %copy-start = (s32[64]{0:T(128)S(1)}, s32[64]{0:T(128)}, u32[]{:S(2)}) copy-start(s32[64]{0:T(128)} %param.16) | copy-start | bytes 772
  6.5 58.2 %all-gather.2.cloned.1.call-start = ((), (), s32[]{:S(2)}) async-start(), calls=%async_computation.1 | async-start | bytes 8650752 | tf_op jit(solution)/shard_map/all_gather | solution.py:143
  7.3 275.7 %reduce-scatter.2.cloned.1.call-start = ((), (), s32[]{:S(2)}) async-start(), calls=%async_computation.2 | async-start | bytes 17301504 | tf_op jit(solution)/shard_map/reduce_scatter | solution.py:171
  14.0 1.8 copy-start.1
  14.0 3.2 %copy-start.6 = (s32[16]{0:T(128)S(1)}, s32[16]{0:T(128)}, u32[]{:S(2)}) copy-start(s32[16]{0:T(128)} %param.14) | copy-start | bytes 196
  96.2 1.6 collective-permute-start
  98.7 6.9 %collective-permute-start.1 = (f32[256,128]{1,0:T(8,128)S(1)}, f32[256,128]{1,0:T(8,128)S(1)}, u32[]{:S(2)}, u32[]{:S(2)}) collective-permute-start(f32[256,128]{1,0:T(8,128)S(1)} %max.34), channel_id=1, source_target_pairs={{0,2},{1,3},{2,4},{3,5},{4,6},{5,7},{6,0},{7,1},{8,10},{9,11},{10,... | collective-permute-start | bytes 393224 | tf_op jit(solution)/shard_map/ppermute | solution.py:126
  100.2 9.1 %collective-permute-start.2 = (f32[256,128]{1,0:T(8,128)S(1)}, f32[256,128]{1,0:T(8,128)S(1)}, u32[]{:S(2)}, u32[]{:S(2)}) collective-permute-start(f32[256,128]{1,0:T(8,128)S(1)} %max.34), channel_id=1, source_target_pairs={{0,4},{1,5},{2,6},{3,7},{4,0},{5,1},{6,2},{7,3},{8,12},{9,13},{10,... | collective-permute-start | bytes 393224 | tf_op jit(solution)/shard_map/ppermute | solution.py:126
  102.9 6.4 %collective-permute-start.3 = (f32[256,128]{1,0:T(8,128)S(1)}, f32[256,128]{1,0:T(8,128)S(1)}, u32[]{:S(2)}, u32[]{:S(2)}) collective-permute-start(f32[256,128]{1,0:T(8,128)S(1)} %max.34), channel_id=1, source_target_pairs={{0,6},{1,7},{2,0},{3,1},{4,2},{5,3},{6,4},{7,5},{8,14},{9,15},{10,... | collective-permute-start | bytes 393224 | tf_op jit(solution)/shard_map/ppermute | solution.py:126
  109.4 7.6 %collective-permute-start.4 = (f32[256,128]{1,0:T(8,128)S(1)}, f32[256,128]{1,0:T(8,128)S(1)}, u32[]{:S(2)}, u32[]{:S(2)}) collective-permute-start(f32[256,128]{1,0:T(8,128)S(1)} %maximum_maximum_fusion.1), channel_id=1, source_target_pairs={{0,8},{1,9},{2,10},{3,11},{4,12},{5,13},{6,14},{7,15},{8,16},{9,17... | collective-permute-start | bytes 393224 | tf_op jit(solution)/shard_map/ppermute | solution.py:126
  110.4 8.0 %collective-permute-start.5 = (f32[256,128]{1,0:T(8,128)S(1)}, f32[256,128]{1,0:T(8,128)S(1)}, u32[]{:S(2)}, u32[]{:S(2)}) collective-permute-start(f32[256,128]{1,0:T(8,128)S(1)} %maximum_maximum_fusion.1), channel_id=1, source_target_pairs={{0,16},{1,17},{2,18},{3,19},{4,20},{5,21},{6,22},{7,23},{8,24},{9,... | collective-permute-start | bytes 393224 | tf_op jit(solution)/shard_map/ppermute | solution.py:126
  113.1 5.7 %collective-permute-start.6 = (f32[256,128]{1,0:T(8,128)S(1)}, f32[256,128]{1,0:T(8,128)S(1)}, u32[]{:S(2)}, u32[]{:S(2)}) collective-permute-start(f32[256,128]{1,0:T(8,128)S(1)} %maximum_maximum_fusion.1), channel_id=1, source_target_pairs={{0,24},{1,25},{2,26},{3,27},{4,28},{5,29},{6,30},{7,31},{8,0},{9,1... | collective-permute-start | bytes 393224 | tf_op jit(solution)/shard_map/ppermute | solution.py:126
  166.4 0.8 copy-start.4
  166.4 2.3 copy-start.5
  166.4 6.7 %copy-start.2 = (bf16[128,1024]{1,0:T(8,128)(2,1)S(1)}, bf16[128,1024]{1,0:T(8,128)(2,1)}, u32[]{:S(2)}) copy-start(bf16[128,1024]{1,0:T(8,128)(2,1)} %param.9) | copy-start | bytes 786436
  166.4 7.0 %copy-start.3 = (f32[256,128]{1,0:T(8,128)S(1)}, f32[256,128]{1,0:T(8,128)}, u32[]{:S(2)}) copy-start(f32[256,128]{1,0:T(8,128)} %get-tuple-element.8) | copy-start | bytes 393220
  167.4 6.0 %collective-permute-start.7 = (bf16[128,256]{0,1:T(8,128)(2,1)S(1)}, bf16[128,256]{0,1:T(8,128)(2,1)S(1)}, u32[]{:S(2)}, u32[]{:S(2)}) collective-permute-start(bf16[128,256]{0,1:T(8,128)(2,1)S(1)} %copy.27), channel_id=1, source_target_pairs={{0,1},{1,2},{2,3},{3,4},{4,5},{5,6},{6,7},{7,8},{8,9},{9,10},{10,1... | collective-permute-start | bytes 196616 | tf_op jit(solution)/shard_map/ppermute | solution.py:19
  168.7 12.1 %collective-permute-start.8 = (bf16[128,256]{1,0:T(8,128)(2,1)S(1)}, bf16[128,256]{1,0:T(8,128)(2,1)S(1)}, u32[]{:S(2)}, u32[]{:S(2)}) collective-permute-start(bf16[128,256]{1,0:T(8,128)(2,1)S(1)} %copy-done.5), channel_id=1, source_target_pairs={{0,1},{1,2},{2,3},{3,4},{4,5},{5,6},{6,7},{7,8},{8,9},{9,10},{10,1... | collective-permute-start | bytes 196616 | tf_op jit(solution)/shard_map/ppermute | solution.py:19
  173.4 1.4 collective-permute-start.9
  174.9 6.8 %collective-permute-start.10 = (f32[256,128]{1,0:T(8,128)S(1)}, f32[256,128]{1,0:T(8,128)S(1)}, u32[]{:S(2)}, u32[]{:S(2)}) collective-permute-start(f32[256,128]{1,0:T(8,128)S(1)} %add.186), channel_id=1, source_target_pairs={{0,2},{1,3},{2,4},{3,5},{4,6},{5,7},{6,0},{7,1},{8,10},{9,11},{10,... | collective-permute-start | bytes 393224 | tf_op jit(solution)/shard_map/ppermute | solution.py:126
  175.9 9.6 %collective-permute-start.11 = (f32[256,128]{1,0:T(8,128)S(1)}, f32[256,128]{1,0:T(8,128)S(1)}, u32[]{:S(2)}, u32[]{:S(2)}) collective-permute-start(f32[256,128]{1,0:T(8,128)S(1)} %add.186), channel_id=1, source_target_pairs={{0,4},{1,5},{2,6},{3,7},{4,0},{5,1},{6,2},{7,3},{8,12},{9,13},{10,... | collective-permute-start | bytes 393224 | tf_op jit(solution)/shard_map/ppermute | solution.py:126
  179.2 6.3 %collective-permute-start.12 = (f32[256,128]{1,0:T(8,128)S(1)}, f32[256,128]{1,0:T(8,128)S(1)}, u32[]{:S(2)}, u32[]{:S(2)}) collective-permute-start(f32[256,128]{1,0:T(8,128)S(1)} %add.186), channel_id=1, source_target_pairs={{0,6},{1,7},{2,0},{3,1},{4,2},{5,3},{6,4},{7,5},{8,14},{9,15},{10,... | collective-permute-start | bytes 393224 | tf_op jit(solution)/shard_map/ppermute | solution.py:126
  185.6 8.1 %collective-permute-start.13 = (f32[256,128]{1,0:T(8,128)S(1)}, f32[256,128]{1,0:T(8,128)S(1)}, u32[]{:S(2)}, u32[]{:S(2)}) collective-permute-start(f32[256,128]{1,0:T(8,128)S(1)} %add_add_fusion), channel_id=1, source_target_pairs={{0,8},{1,9},{2,10},{3,11},{4,12},{5,13},{6,14},{7,15},{8,16},{9,17... | collective-permute-start | bytes 393224 | tf_op jit(solution)/shard_map/ppermute | solution.py:126
  188.6 7.8 %collective-permute-start.14 = (f32[256,128]{1,0:T(8,128)S(1)}, f32[256,128]{1,0:T(8,128)S(1)}, u32[]{:S(2)}, u32[]{:S(2)}) collective-permute-start(f32[256,128]{1,0:T(8,128)S(1)} %add_add_fusion), channel_id=1, source_target_pairs={{0,16},{1,17},{2,18},{3,19},{4,20},{5,21},{6,22},{7,23},{8,24},{9,... | collective-permute-start | bytes 393224 | tf_op jit(solution)/shard_map/ppermute | solution.py:126
  191.2 5.2 %collective-permute-start.15 = (f32[256,128]{1,0:T(8,128)S(1)}, f32[256,128]{1,0:T(8,128)S(1)}, u32[]{:S(2)}, u32[]{:S(2)}) collective-permute-start(f32[256,128]{1,0:T(8,128)S(1)} %add_add_fusion), channel_id=1, source_target_pairs={{0,24},{1,25},{2,26},{3,27},{4,28},{5,29},{6,30},{7,31},{8,0},{9,1... | collective-permute-start | bytes 393224 | tf_op jit(solution)/shard_map/ppermute | solution.py:126
  289.4 9.3 %collective-permute-start.16 = (bf16[128,1024]{1,0:T(8,128)(2,1)S(1)}, bf16[128,1024]{1,0:T(8,128)(2,1)S(1)}, u32[]{:S(2)}, u32[]{:S(2)}) collective-permute-start(bf16[128,1024]{1,0:T(8,128)(2,1)S(1)} %get-tuple-element.13), channel_id=1, source_target_pairs={{0,32},{32,64},{64,96},{96,0},{1,33},{33,65},{65,97},{97,1},{2,34}... | collective-permute-start | bytes 786440 | tf_op jit(solution)/shard_map/ppermute | solution.py:187
  291.0 13.1 %collective-permute-start.17 = (bf16[128,1024]{1,0:T(8,128)(2,1)S(1)}, bf16[128,1024]{1,0:T(8,128)(2,1)S(1)}, u32[]{:S(2)}, u32[]{:S(2)}) collective-permute-start(bf16[128,1024]{1,0:T(8,128)(2,1)S(1)} %get-tuple-element.15), channel_id=1, source_target_pairs={{0,64},{32,96},{64,0},{96,32},{1,65},{33,97},{65,1},{97,33},{2,66}... | collective-permute-start | bytes 786440 | tf_op jit(solution)/shard_map/ppermute | solution.py:187
  293.9 10.2 %collective-permute-start.18 = (bf16[128,1024]{1,0:T(8,128)(2,1)S(1)}, bf16[128,1024]{1,0:T(8,128)(2,1)}, u32[]{:S(2)}, u32[]{:S(2)}) collective-permute-start(bf16[128,1024]{1,0:T(8,128)(2,1)S(1)} %get-tuple-element.14), channel_id=1, source_target_pairs={{0,96},{32,0},{64,32},{96,64},{1,97},{33,1},{65,33},{97,65},{2,98}... | collective-permute-start | bytes 786440 | tf_op jit(solution)/shard_map/ppermute | solution.py:187
Sparse Core Ops, SparseCore 0:
  9.6 55.1 all-gather.1
  166.6 116.3 reduce-scatter.1

commit v10 on v9

--- a/solution.py
+++ b/solution.py
@@ -9,7 +9,9 @@
 from jax.sharding import PartitionSpec as P
 
 HEAD_SIZE = 128
-SLOTS = 5
+TILE = 64
+MIN_LEN = 32
+SLOTS = TILE // MIN_LEN + 1
 STAT_LANES = 128
 
 
@@ -142,13 +144,14 @@
     blocks, kv_cols, block_len = keys_t.shape
     gathered = lax.all_gather(queries, "blk", axis=0, tiled=True)
     row_count = gathered.shape[0]
-    n_tiles = row_count // tok_dev
+    tile = TILE
+    n_tiles = row_count // tile
     stat_rows = 8
-    q_spec = pl.BlockSpec((tok_dev, q_cols), lambda i, *_: (i, 0))
+    q_spec = pl.BlockSpec((tile, q_cols), lambda i, *_: (i, 0))
     kt_spec = pl.BlockSpec((blocks, kv_cols, block_len), lambda i, *_: (0, 0, 0))
     v_spec = pl.BlockSpec((blocks, block_len, kv_cols), lambda i, *_: (0, 0, 0))
-    s_spec = pl.BlockSpec((stat_rows, tok_dev), lambda i, *_: (i, 0))
-    stat_shape = jax.ShapeDtypeStruct((n_tiles * stat_rows, tok_dev), jnp.float32)
+    s_spec = pl.BlockSpec((stat_rows, tile), lambda i, *_: (i, 0))
+    stat_shape = jax.ShapeDtypeStruct((n_tiles * stat_rows, tile), jnp.float32)
     kw = dict(heads=heads, qgw=qgw, scale=scale)
     local_max = pl.pallas_call(
         functools.partial(max_kernel, **kw),
@@ -165,14 +168,18 @@
             num_scalar_prefetch=3,
             grid=(n_tiles,),
             in_specs=[q_spec, kt_spec, v_spec, s_spec],
-            out_specs=(pl.BlockSpec((tok_dev, q_cols), lambda i, *_: (i, 0)), s_spec),
+            out_specs=(pl.BlockSpec((tile, q_cols), lambda i, *_: (i, 0)), s_spec),
         ),
     )(lo, hi, blk, gathered, keys_t, values, far_max)
     context = lax.psum_scatter(partial, "blk", scatter_dimension=0, tiled=True)
     totals = butterfly(totals, "blk", jnp.add)
-    own = lambda a: jnp.transpose(
-        lax.dynamic_slice_in_dim(a, blk_index * stat_rows, stat_rows, 0)[:heads]
-    )
+    per_dev = tok_dev // tile
+
+    def own(a):
+        mine = lax.dynamic_slice_in_dim(a, blk_index * per_dev * stat_rows, per_dev * stat_rows, 0)
+        mine = mine.reshape(per_dev, stat_rows, tile)[:, :heads]
+        return jnp.transpose(mine, (0, 2, 1)).reshape(tok_dev, heads)
+
     return context, own(totals), own(far_max)
 
 
@@ -211,7 +218,7 @@
     row_count = blk_count * tok_dev
     blk_index = lax.axis_index("blk")
     scale = 1.0 / math.sqrt(HEAD_SIZE)
-    tile = tok_dev
+    tile = TILE
     n_tiles = row_count // tile
 
     lo, hi, blk = tile_tables(suffix_len, request_group, block_group, n_tiles, tile)

time: 314 us -> 352 us (1.12)
  Pallas kernels: 78.3 us -> 104 us
  waiting for transfers between devices: 162 us -> 172 us
    ppermute x14, waiting for transfers between devices: 20.2 us -> 43 us  [butterfly(): lax.ppermute(x, axis, [(i, i + ((digit(i) + d) % radix - digit(i)) * stri...]
    pallas_call x1, Pallas kernels: 31.4 us -> 45.3 us  [far_part(): pl.pallas_call(functools.partial(max_kernel, **kw), out_shape=stat_shape,...]
    reduce_scatter x1, waiting for transfers between devices: 86.5 us -> 74.8 us  [far_part(): context = lax.psum_scatter(partial, 'blk', scatter_dimension=0, tiled=True)]
    pallas_call x1, Pallas kernels: 46.9 us -> 58.3 us  [far_part(): pl.pallas_call(functools.partial(ctx_kernel, **kw), out_shape=(jax.ShapeD...]
  transfers between devices with their start and end apart: 21 -> 21, of which waited for: 15 -> 15; matrix products, arithmetic and copies ran while one was open for 5% -> 4% of each run, Pallas kernels for 0% -> 0%
where the time goes in v10:
time: 352 us; the launch traced here: 350 us
  waiting for transfers between devices  172 us (49%)
  Pallas kernels  104 us (30%)
  starting transfers between devices  34.5 us (10%)
  local copies, waits for them, and re-layouts  14.5 us (4%)
  between operations  13.7 us (4%)
  other arithmetic  5.65 us (2%)
  matrix products  5.37 us (2%)
    reduce_scatter x1, waiting for transfers between devices, far_part(): context = lax.psum_scatter(partial, 'blk', scatter_dimension=0, tiled=True)  74.8 us
    pallas_call x1, Pallas kernels, far_part(): pl.pallas_call(functools.partial(ctx_kernel, **kw), out_shape=(jax.ShapeD...  58.3 us
    pallas_call x1, Pallas kernels, far_part(): pl.pallas_call(functools.partial(max_kernel, **kw), out_shape=stat_shape,...  45.3 us
    all_gather x1, waiting for transfers between devices, far_part(): gathered = lax.all_gather(queries, 'blk', axis=0, tiled=True)  45 us
    ppermute x14, waiting for transfers between devices, butterfly(): lax.ppermute(x, axis, [(i, i + ((digit(i) + d) % radix - digit(i)) * stri...  43 us
    ppermute x14, starting transfers between devices, butterfly(): lax.ppermute(x, axis, [(i, i + ((digit(i) + d) % radix - digit(i)) * stri...  23.3 us
    ppermute x3, waiting for transfers between devices, column_sum(): got = lax.ppermute(sent, axis, [(i, (i + d) % n) for i in range(n)])  8.76 us
  transfers between devices with their start and end apart: 21, of which 15 were waited for; matrix products, arithmetic and copies ran while one was open for 4% of the time, Pallas kernels for 0%

profile of v10, /device:TPU:0, one launch (start us, length us, event | category | flops | bytes accessed | tf_op | source)
XLA Modules:
  0.0 349.5 jit_solution(342226433704646641)
XLA Ops:
  9.4 1.6 gather_fusion.1
  10.9 1.6 gather_fusion
  14.3 1.5 gather_fusion.2
  17.7 2.1 gather_fusion.3
  19.8 45.0 %all-gather.2.cloned.1.call-done.q_ref = bf16[4096,1024]{1,0:T(8,128)(2,1)} async-done(((bf16[128,1024]{1,0:T(8,128)(2,1)}), bf16[4096,1024]{1,0:T(8,128)(2,1)}) %all-gather.2.cloned.1.call-update) | async-done | bytes 8388624 | tf_op jit(solution)/shard_map/all_gather | solution.py:145
  64.8 45.3 %shard_map.91 = f32[512,64]{1,0:T(8,128)} custom-call(s32[192]{0:T(256)} %select_n.90.lo_ref, s32[192]{0:T(256)} %select_n.92.hi_ref, s32[192]{0:T(256)} %gather_fusion.3, bf16[4096,1024]{1,0:T(8,128)(2,1)} %all-gather.2.cloned.1.call-done.q_ref, bf16[16,256,128]{2,1,0:T(8,128)(2,1)} %bitcast.52), custom_call_target="tpu_custom_call" | custom-call | tf_op jit(solution)/shard_map/pallas_call | solution.py:156
  110.3 1.5 collective-permute-done
  112.8 1.5 collective-permute-start.1
  114.4 2.7 collective-permute-start.2
  117.0 1.5 collective-permute-start.3
  118.5 4.1 %collective-permute-done.1 = f32[512,64]{1,0:T(8,128)S(1)} collective-permute-done((f32[512,64]{1,0:T(8,128)S(1)}, f32[512,64]{1,0:T(8,128)S(1)}, u32[]{:S(2)}, u32[]{:S(2)}) %collective-permute-start.1) | collective-permute-done | bytes 131104 | tf_op jit(solution)/shard_map/ppermute | solution.py:128
  122.5 6.5 %collective-permute-done.2 = f32[512,64]{1,0:T(8,128)S(1)} collective-permute-done((f32[512,64]{1,0:T(8,128)S(1)}, f32[512,64]{1,0:T(8,128)S(1)}, u32[]{:S(2)}, u32[]{:S(2)}) %collective-permute-start.2) | collective-permute-done | bytes 131104 | tf_op jit(solution)/shard_map/ppermute | solution.py:128
  130.2 2.7 collective-permute-start.5
  134.3 5.4 %collective-permute-done.4 = f32[512,64]{1,0:T(8,128)S(1)} collective-permute-done((f32[512,64]{1,0:T(8,128)S(1)}, f32[512,64]{1,0:T(8,128)S(1)}, u32[]{:S(2)}, u32[]{:S(2)}) %collective-permute-start.4) | collective-permute-done | bytes 131104 | tf_op jit(solution)/shard_map/ppermute | solution.py:128
  139.7 4.1 %collective-permute-done.5 = f32[512,64]{1,0:T(8,128)S(1)} collective-permute-done((f32[512,64]{1,0:T(8,128)S(1)}, f32[512,64]{1,0:T(8,128)S(1)}, u32[]{:S(2)}, u32[]{:S(2)}) %collective-permute-start.5) | collective-permute-done | bytes 131104 | tf_op jit(solution)/shard_map/ppermute | solution.py:128
  145.0 58.3 %shard_map.92 = (f32[4096,1024]{1,0:T(8,128)}, f32[512,64]{1,0:T(8,128)}) custom-call(s32[192]{0:T(256)} %select_n.90.lo_ref, s32[192]{0:T(256)} %select_n.92.hi_ref, s32[192]{0:T(256)} %gather_fusion.3, bf16[4096,1024]{1,0:T(8,128)(2,1)} %all-gather.2.cloned.1.call-done.q_ref, bf16[16,256,128]{2,1,0:T(8,128)(2,1)} %bitcast.53, bf16[16,128,256]{2,1,0:T(8,128)(2,1)} %v_ref.1, ...), custom_call_target="tpu_custom_call" | custom-call | tf_op jit(solution)/shard_map/pallas_call | solution.py:164
  205.6 4.0 %collective-permute-start.8 = (bf16[128,256]{1,0:T(8,128)(2,1)S(1)}, bf16[128,256]{1,0:T(8,128)(2,1)S(1)}, u32[]{:S(2)}, u32[]{:S(2)}) collective-permute-start(bf16[128,256]{1,0:T(8,128)(2,1)S(1)} %copy-done.5), channel_id=1, source_target_pairs={{0,1},{1,2},{2,3},{3,4},{4,5},{5,6},{6,7},{7,8},{8,9},{9,10},{10,1... | collective-permute-start | bytes 196616 | tf_op jit(solution)/shard_map/ppermute | solution.py:21
  213.0 3.3 collective-permute-start.11
  216.3 1.5 collective-permute-start.12
  218.8 2.8 collective-permute-done.10
  221.6 6.7 %collective-permute-done.11 = f32[512,64]{1,0:T(8,128)S(1)} collective-permute-done((f32[512,64]{1,0:T(8,128)S(1)}, f32[512,64]{1,0:T(8,128)S(1)}, u32[]{:S(2)}, u32[]{:S(2)}) %collective-permute-start.11) | collective-permute-done | bytes 131104 | tf_op jit(solution)/shard_map/ppermute | solution.py:128
  228.3 3.1 collective-permute-start.13
  231.4 2.7 collective-permute-start.14
  234.7 4.2 %collective-permute-done.13 = f32[512,64]{1,0:T(8,128)S(1)} collective-permute-done((f32[512,64]{1,0:T(8,128)S(1)}, f32[512,64]{1,0:T(8,128)S(1)}, u32[]{:S(2)}, u32[]{:S(2)}) %collective-permute-start.13) | collective-permute-done | bytes 131104 | tf_op jit(solution)/shard_map/ppermute | solution.py:128
  238.9 6.1 %collective-permute-done.14 = f32[512,64]{1,0:T(8,128)S(1)} collective-permute-done((f32[512,64]{1,0:T(8,128)S(1)}, f32[512,64]{1,0:T(8,128)S(1)}, u32[]{:S(2)}, u32[]{:S(2)}) %collective-permute-start.14) | collective-permute-done | bytes 131104 | tf_op jit(solution)/shard_map/ppermute | solution.py:128
  245.1 74.8 %reduce-scatter.2.cloned.1.call-done = f32[128,1024]{1,0:T(8,128)} async-done(((f32[4096,1024]{1,0:T(8,128)}), f32[128,1024]{1,0:T(8,128)}) %reduce-scatter.2.cloned.1.call-update) | async-done | bytes 524304 | tf_op jit(solution)/shard_map/reduce_scatter | solution.py:174
  321.4 4.7 %fusion.14 = f32[128,4096]{1,0:T(8,128)S(1)} fusion(bf16[128,1024]{0,1:T(8,128)(2,1)S(1)} %bitcast.54, bf16[1024,4096]{1,0:T(8,128)(2,1)} %param.17), kind=kOutput, calls=%fused_computation.52 | convolution fusion | flops 1073741824 | bytes 10747904 | tf_op jit(solution)/shard_map/dot_general | solution.py:271
  326.2 1.6 collective-permute-start.16
  327.9 2.9 collective-permute-start.17
  332.1 3.5 collective-permute-done.16
  335.6 5.3 %collective-permute-done.17 = bf16[128,1024]{1,0:T(8,128)(2,1)S(1)} collective-permute-done((bf16[128,1024]{1,0:T(8,128)(2,1)S(1)}, bf16[128,1024]{1,0:T(8,128)(2,1)S(1)}, u32[]{:S(2)}, u32[]{:S(2)}) %collective-permute-start.17) | collective-permute-done | bytes 262176 | tf_op jit(solution)/shard_map/ppermute | solution.py:194
  340.9 1.8 add_convert_fusion
  (83 shorter events, 21.6 us)
Async XLA Ops:
  6.5 7.8 %copy-start = (s32[64]{0:T(128)S(1)}, s32[64]{0:T(128)}, u32[]{:S(2)}) copy-start(s32[64]{0:T(128)} %param.16) | copy-start | bytes 772
  6.5 58.2 %all-gather.2.cloned.1.call-start = ((), (), s32[]{:S(2)}) async-start(), calls=%async_computation.1 | async-start | bytes 8650752 | tf_op jit(solution)/shard_map/all_gather | solution.py:145
  7.3 312.6 %reduce-scatter.2.cloned.1.call-start = ((), (), s32[]{:S(2)}) async-start(), calls=%async_computation.2 | async-start | bytes 17301504 | tf_op jit(solution)/shard_map/reduce_scatter | solution.py:174
  14.3 1.9 copy-start.1
  14.3 3.2 copy-start.6
  110.1 1.7 collective-permute-start
  112.8 9.7 %collective-permute-start.1 = (f32[512,64]{1,0:T(8,128)S(1)}, f32[512,64]{1,0:T(8,128)S(1)}, u32[]{:S(2)}, u32[]{:S(2)}) collective-permute-start(f32[512,64]{1,0:T(8,128)S(1)} %max.34), channel_id=1, source_target_pairs={{0,2},{1,3},{2,4},{3,5},{4,6},{5,7},{6,0},{7,1},{8,10},{9,11},{10,... | collective-permute-start | bytes 393224 | tf_op jit(solution)/shard_map/ppermute | solution.py:128
  114.4 14.7 %collective-permute-start.2 = (f32[512,64]{1,0:T(8,128)S(1)}, f32[512,64]{1,0:T(8,128)S(1)}, u32[]{:S(2)}, u32[]{:S(2)}) collective-permute-start(f32[512,64]{1,0:T(8,128)S(1)} %max.34), channel_id=1, source_target_pairs={{0,4},{1,5},{2,6},{3,7},{4,0},{5,1},{6,2},{7,3},{8,12},{9,13},{10,... | collective-permute-start | bytes 393224 | tf_op jit(solution)/shard_map/ppermute | solution.py:128
  117.0 12.1 %collective-permute-start.3 = (f32[512,64]{1,0:T(8,128)S(1)}, f32[512,64]{1,0:T(8,128)S(1)}, u32[]{:S(2)}, u32[]{:S(2)}) collective-permute-start(f32[512,64]{1,0:T(8,128)S(1)} %max.34), channel_id=1, source_target_pairs={{0,6},{1,7},{2,0},{3,1},{4,2},{5,3},{6,4},{7,5},{8,14},{9,15},{10,... | collective-permute-start | bytes 393224 | tf_op jit(solution)/shard_map/ppermute | solution.py:128
  129.1 10.6 %collective-permute-start.4 = (f32[512,64]{1,0:T(8,128)S(1)}, f32[512,64]{1,0:T(8,128)S(1)}, u32[]{:S(2)}, u32[]{:S(2)}) collective-permute-start(f32[512,64]{1,0:T(8,128)S(1)} %maximum_maximum_fusion.1), channel_id=1, source_target_pairs={{0,8},{1,9},{2,10},{3,11},{4,12},{5,13},{6,14},{7,15},{8,16},{9,17... | collective-permute-start | bytes 393224 | tf_op jit(solution)/shard_map/ppermute | solution.py:128
  130.2 13.6 %collective-permute-start.5 = (f32[512,64]{1,0:T(8,128)S(1)}, f32[512,64]{1,0:T(8,128)S(1)}, u32[]{:S(2)}, u32[]{:S(2)}) collective-permute-start(f32[512,64]{1,0:T(8,128)S(1)} %maximum_maximum_fusion.1), channel_id=1, source_target_pairs={{0,16},{1,17},{2,18},{3,19},{4,20},{5,21},{6,22},{7,23},{8,24},{9,... | collective-permute-start | bytes 393224 | tf_op jit(solution)/shard_map/ppermute | solution.py:128
  132.9 11.4 %collective-permute-start.6 = (f32[512,64]{1,0:T(8,128)S(1)}, f32[512,64]{1,0:T(8,128)S(1)}, u32[]{:S(2)}, u32[]{:S(2)}) collective-permute-start(f32[512,64]{1,0:T(8,128)S(1)} %maximum_maximum_fusion.1), channel_id=1, source_target_pairs={{0,24},{1,25},{2,26},{3,27},{4,28},{5,29},{6,30},{7,31},{8,0},{9,1... | collective-permute-start | bytes 393224 | tf_op jit(solution)/shard_map/ppermute | solution.py:128
  203.3 0.8 copy-start.4
  203.3 2.3 copy-start.5
  203.3 6.7 %copy-start.2 = (bf16[128,1024]{1,0:T(8,128)(2,1)S(1)}, bf16[128,1024]{1,0:T(8,128)(2,1)}, u32[]{:S(2)}) copy-start(bf16[128,1024]{1,0:T(8,128)(2,1)} %param.9) | copy-start | bytes 786436
  203.3 7.0 %copy-start.3 = (f32[512,64]{1,0:T(8,128)S(1)}, f32[512,64]{1,0:T(8,128)}, u32[]{:S(2)}) copy-start(f32[512,64]{1,0:T(8,128)} %get-tuple-element.8) | copy-start | bytes 393220
  204.3 6.0 %collective-permute-start.7 = (bf16[128,256]{0,1:T(8,128)(2,1)S(1)}, bf16[128,256]{0,1:T(8,128)(2,1)S(1)}, u32[]{:S(2)}, u32[]{:S(2)}) collective-permute-start(bf16[128,256]{0,1:T(8,128)(2,1)S(1)} %copy.39), channel_id=1, source_target_pairs={{0,1},{1,2},{2,3},{3,4},{4,5},{5,6},{6,7},{7,8},{8,9},{9,10},{10,1... | collective-permute-start | bytes 196616 | tf_op jit(solution)/shard_map/ppermute | solution.py:21
  205.6 12.3 %collective-permute-start.8 = (bf16[128,256]{1,0:T(8,128)(2,1)S(1)}, bf16[128,256]{1,0:T(8,128)(2,1)S(1)}, u32[]{:S(2)}, u32[]{:S(2)}) collective-permute-start(bf16[128,256]{1,0:T(8,128)(2,1)S(1)} %copy-done.5), channel_id=1, source_target_pairs={{0,1},{1,2},{2,3},{3,4},{4,5},{5,6},{6,7},{7,8},{8,9},{9,10},{10,1... | collective-permute-start | bytes 196616 | tf_op jit(solution)/shard_map/ppermute | solution.py:21
  210.3 1.6 collective-permute-start.9
  212.0 9.6 %collective-permute-start.10 = (f32[512,64]{1,0:T(8,128)S(1)}, f32[512,64]{1,0:T(8,128)S(1)}, u32[]{:S(2)}, u32[]{:S(2)}) collective-permute-start(f32[512,64]{1,0:T(8,128)S(1)} %add.186), channel_id=1, source_target_pairs={{0,2},{1,3},{2,4},{3,5},{4,6},{5,7},{6,0},{7,1},{8,10},{9,11},{10,... | collective-permute-start | bytes 393224 | tf_op jit(solution)/shard_map/ppermute | solution.py:128
  213.0 15.2 %collective-permute-start.11 = (f32[512,64]{1,0:T(8,128)S(1)}, f32[512,64]{1,0:T(8,128)S(1)}, u32[]{:S(2)}, u32[]{:S(2)}) collective-permute-start(f32[512,64]{1,0:T(8,128)S(1)} %add.186), channel_id=1, source_target_pairs={{0,4},{1,5},{2,6},{3,7},{4,0},{5,1},{6,2},{7,3},{8,12},{9,13},{10,... | collective-permute-start | bytes 393224 | tf_op jit(solution)/shard_map/ppermute | solution.py:128
  216.3 11.9 %collective-permute-start.12 = (f32[512,64]{1,0:T(8,128)S(1)}, f32[512,64]{1,0:T(8,128)S(1)}, u32[]{:S(2)}, u32[]{:S(2)}) collective-permute-start(f32[512,64]{1,0:T(8,128)S(1)} %add.186), channel_id=1, source_target_pairs={{0,6},{1,7},{2,0},{3,1},{4,2},{5,3},{6,4},{7,5},{8,14},{9,15},{10,... | collective-permute-start | bytes 393224 | tf_op jit(solution)/shard_map/ppermute | solution.py:128
  228.3 10.6 %collective-permute-start.13 = (f32[512,64]{1,0:T(8,128)S(1)}, f32[512,64]{1,0:T(8,128)S(1)}, u32[]{:S(2)}, u32[]{:S(2)}) collective-permute-start(f32[512,64]{1,0:T(8,128)S(1)} %add_add_fusion), channel_id=1, source_target_pairs={{0,8},{1,9},{2,10},{3,11},{4,12},{5,13},{6,14},{7,15},{8,16},{9,17... | collective-permute-start | bytes 393224 | tf_op jit(solution)/shard_map/ppermute | solution.py:128
  231.4 13.5 %collective-permute-start.14 = (f32[512,64]{1,0:T(8,128)S(1)}, f32[512,64]{1,0:T(8,128)S(1)}, u32[]{:S(2)}, u32[]{:S(2)}) collective-permute-start(f32[512,64]{1,0:T(8,128)S(1)} %add_add_fusion), channel_id=1, source_target_pairs={{0,16},{1,17},{2,18},{3,19},{4,20},{5,21},{6,22},{7,23},{8,24},{9,... | collective-permute-start | bytes 393224 | tf_op jit(solution)/shard_map/ppermute | solution.py:128
  234.1 10.9 %collective-permute-start.15 = (f32[512,64]{1,0:T(8,128)S(1)}, f32[512,64]{1,0:T(8,128)S(1)}, u32[]{:S(2)}, u32[]{:S(2)}) collective-permute-start(f32[512,64]{1,0:T(8,128)S(1)} %add_add_fusion), channel_id=1, source_target_pairs={{0,24},{1,25},{2,26},{3,27},{4,28},{5,29},{6,30},{7,31},{8,0},{9,1... | collective-permute-start | bytes 393224 | tf_op jit(solution)/shard_map/ppermute | solution.py:128
  326.2 9.4 %collective-permute-start.16 = (bf16[128,1024]{1,0:T(8,128)(2,1)S(1)}, bf16[128,1024]{1,0:T(8,128)(2,1)S(1)}, u32[]{:S(2)}, u32[]{:S(2)}) collective-permute-start(bf16[128,1024]{1,0:T(8,128)(2,1)S(1)} %get-tuple-element.13), channel_id=1, source_target_pairs={{0,32},{32,64},{64,96},{96,0},{1,33},{33,65},{65,97},{97,1},{2,34}... | collective-permute-start | bytes 786440 | tf_op jit(solution)/shard_map/ppermute | solution.py:194
  327.9 13.0 %collective-permute-start.17 = (bf16[128,1024]{1,0:T(8,128)(2,1)S(1)}, bf16[128,1024]{1,0:T(8,128)(2,1)S(1)}, u32[]{:S(2)}, u32[]{:S(2)}) collective-permute-start(bf16[128,1024]{1,0:T(8,128)(2,1)S(1)} %get-tuple-element.15), channel_id=1, source_target_pairs={{0,64},{32,96},{64,0},{96,32},{1,65},{33,97},{65,1},{97,33},{2,66}... | collective-permute-start | bytes 786440 | tf_op jit(solution)/shard_map/ppermute | solution.py:194
  330.7 10.1 %collective-permute-start.18 = (bf16[128,1024]{1,0:T(8,128)(2,1)S(1)}, bf16[128,1024]{1,0:T(8,128)(2,1)}, u32[]{:S(2)}, u32[]{:S(2)}) collective-permute-start(bf16[128,1024]{1,0:T(8,128)(2,1)S(1)} %get-tuple-element.14), channel_id=1, source_target_pairs={{0,96},{32,0},{64,32},{96,64},{1,97},{33,1},{65,33},{97,65},{2,98}... | collective-permute-start | bytes 786440 | tf_op jit(solution)/shard_map/ppermute | solution.py:194
Sparse Core Ops, SparseCore 0:
  9.6 55.1 all-gather.1
  203.5 116.3 reduce-scatter.1

commit v11 on v9

--- a/solution.py
+++ b/solution.py
@@ -48,12 +48,11 @@
 
 def _slot_mask(lo_ref, hi_ref, base, rows):
     seg = lax.broadcasted_iota(jnp.int32, (1, SLOTS * HEAD_SIZE), 1) // HEAD_SIZE
-    lo = jnp.zeros(seg.shape, jnp.int32)
-    hi = jnp.zeros(seg.shape, jnp.int32)
+    own = jnp.zeros(rows.shape, jnp.int32)
     for s in range(SLOTS):
-        lo = jnp.where(seg == s, lo_ref[base + s], lo)
-        hi = jnp.where(seg == s, hi_ref[base + s], hi)
-    return (rows >= lo) & (rows < hi)
+        inside = (rows >= lo_ref[base + s]) & (rows < hi_ref[base + s])
+        own = jnp.where(inside, s, own)
+    return seg == own
 
 
 def _slot_keys(kt_ref, blk_ref, base, kv):
@@ -83,8 +82,8 @@
     stats = jnp.full((tile, STAT_LANES), -jnp.inf, jnp.float32)
     for kv in range(heads // qgw):
         keys = _slot_keys(kt_ref, blk_ref, base, kv)
-        sc = jnp.dot(_stacked(q_ref, kv, qgw), keys, preferred_element_type=jnp.float32) * scale
-        mx = jnp.max(jnp.where(mask, sc, -jnp.inf), axis=1, keepdims=True)
+        sc = jnp.dot(_stacked(q_ref, kv, qgw), keys, preferred_element_type=jnp.float32)
+        mx = jnp.max(jnp.where(mask, sc, -jnp.inf), axis=1, keepdims=True) * scale
         for j in range(qgw):
             stats = jnp.where(lane == kv * qgw + j, mx[j * tile : (j + 1) * tile], stats)
     m_ref[...] = jnp.transpose(stats)[: m_ref.shape[0], :]

time: 314 us -> 310 us (0.987)
  Pallas kernels: 78.3 us -> 74.6 us
where the time goes in v11:
time: 310 us; the launch traced here: 309 us
  waiting for transfers between devices  162 us (52%)
  Pallas kernels  74.6 us (24%)
  starting transfers between devices  34.4 us (11%)
  local copies, waits for them, and re-layouts  13.9 us (4%)
  between operations  13.7 us (4%)
  other arithmetic  5.44 us (2%)
  matrix products  5.37 us (2%)
    reduce_scatter x1, waiting for transfers between devices, far_part(): context = lax.psum_scatter(partial, 'blk', scatter_dimension=0, tiled=True)  86.5 us
    pallas_call x1, Pallas kernels, far_part(): pl.pallas_call(functools.partial(ctx_kernel, **kw), out_shape=(jax.ShapeD...  45.5 us
    all_gather x1, waiting for transfers between devices, far_part(): gathered = lax.all_gather(queries, 'blk', axis=0, tiled=True)  45.3 us
    pallas_call x1, Pallas kernels, far_part(): pl.pallas_call(functools.partial(max_kernel, **kw), out_shape=stat_shape,...  29.1 us
    ppermute x14, starting transfers between devices, butterfly(): lax.ppermute(x, axis, [(i, i + ((digit(i) + d) % radix - digit(i)) * stri...  23.2 us
    ppermute x14, waiting for transfers between devices, butterfly(): lax.ppermute(x, axis, [(i, i + ((digit(i) + d) % radix - digit(i)) * stri...  20.1 us
    ppermute x3, waiting for transfers between devices, column_sum(): got = lax.ppermute(sent, axis, [(i, (i + d) % n) for i in range(n)])  8.88 us
  transfers between devices with their start and end apart: 21, of which 15 were waited for; matrix products, arithmetic and copies ran while one was open for 5% of the time, Pallas kernels for 0%

profile of v11, /device:TPU:0, one launch (start us, length us, event | category | flops | bytes accessed | tf_op | source)
XLA Modules:
  0.0 309.0 jit_solution(14412715567787841116)
XLA Ops:
  9.3 1.6 gather_fusion.1
  10.9 1.6 gather_fusion
  14.0 1.5 gather_fusion.2
  15.8 1.4 copy.26
  17.3 2.1 gather_fusion.3
  19.4 45.3 %all-gather.2.cloned.1.call-done.q_ref = bf16[4096,1024]{1,0:T(8,128)(2,1)} async-done(((bf16[128,1024]{1,0:T(8,128)(2,1)}), bf16[4096,1024]{1,0:T(8,128)(2,1)}) %all-gather.2.cloned.1.call-update) | async-done | bytes 8388624 | tf_op jit(solution)/shard_map/all_gather | solution.py:142
  64.8 29.1 %shard_map.91 = f32[256,128]{1,0:T(8,128)} custom-call(s32[160]{0:T(256)} %select_n.90.lo_ref, s32[160]{0:T(256)} %select_n.92.hi_ref, s32[160]{0:T(256)} %gather_fusion.3, bf16[4096,1024]{1,0:T(8,128)(2,1)} %all-gather.2.cloned.1.call-done.q_ref, bf16[16,256,128]{2,1,0:T(8,128)(2,1)} %bitcast.46), custom_call_target="tpu_custom_call" | custom-call | tf_op jit(solution)/shard_map/pallas_call | solution.py:152
  96.4 1.5 collective-permute-start.1
  97.9 2.7 collective-permute-start.2
  100.6 1.5 collective-permute-start.3
  103.3 3.7 %collective-permute-done.2 = f32[256,128]{1,0:T(8,128)S(1)} collective-permute-done((f32[256,128]{1,0:T(8,128)S(1)}, f32[256,128]{1,0:T(8,128)S(1)}, u32[]{:S(2)}, u32[]{:S(2)}) %collective-permute-start.2) | collective-permute-done | bytes 131104 | tf_op jit(solution)/shard_map/ppermute | solution.py:125
  108.1 2.7 collective-permute-start.5
  110.8 1.4 collective-permute-start.6
  112.2 2.5 collective-permute-done.4
  114.7 1.4 collective-permute-done.5
  117.2 45.5 %shard_map.92 = (f32[4096,1024]{1,0:T(8,128)}, f32[256,128]{1,0:T(8,128)}) custom-call(s32[160]{0:T(256)} %select_n.90.lo_ref, s32[160]{0:T(256)} %select_n.92.hi_ref, s32[160]{0:T(256)} %gather_fusion.3, bf16[4096,1024]{1,0:T(8,128)(2,1)} %all-gather.2.cloned.1.call-done.q_ref, bf16[16,256,128]{2,1,0:T(8,128)(2,1)} %bitcast.47, ...), custom_call_target="tpu_custom_call" | custom-call | tf_op jit(solution)/shard_map/pallas_call | solution.py:160
  165.0 4.0 %collective-permute-start.8 = (bf16[128,256]{1,0:T(8,128)(2,1)S(1)}, bf16[128,256]{1,0:T(8,128)(2,1)S(1)}, u32[]{:S(2)}, u32[]{:S(2)}) collective-permute-start(bf16[128,256]{1,0:T(8,128)(2,1)S(1)} %copy-done.5), channel_id=1, source_target_pairs={{0,1},{1,2},{2,3},{3,4},{4,5},{5,6},{6,7},{7,8},{8,9},{9,10},{10,1... | collective-permute-start | bytes 196616 | tf_op jit(solution)/shard_map/ppermute | solution.py:19
  172.2 3.3 %collective-permute-start.11 = (f32[256,128]{1,0:T(8,128)S(1)}, f32[256,128]{1,0:T(8,128)S(1)}, u32[]{:S(2)}, u32[]{:S(2)}) collective-permute-start(f32[256,128]{1,0:T(8,128)S(1)} %add.186), channel_id=1, source_target_pairs={{0,4},{1,5},{2,6},{3,7},{4,0},{5,1},{6,2},{7,3},{8,12},{9,13},{10,... | collective-permute-start | bytes 393224 | tf_op jit(solution)/shard_map/ppermute | solution.py:125
  175.5 1.5 collective-permute-start.12
  178.0 3.9 %collective-permute-done.11 = f32[256,128]{1,0:T(8,128)S(1)} collective-permute-done((f32[256,128]{1,0:T(8,128)S(1)}, f32[256,128]{1,0:T(8,128)S(1)}, u32[]{:S(2)}, u32[]{:S(2)}) %collective-permute-start.11) | collective-permute-done | bytes 131104 | tf_op jit(solution)/shard_map/ppermute | solution.py:125
  181.9 3.0 collective-permute-start.13
  184.9 2.6 collective-permute-start.14
  188.1 1.9 collective-permute-done.13
  190.0 2.7 collective-permute-done.14
  192.8 86.5 %reduce-scatter.2.cloned.1.call-done = f32[128,1024]{1,0:T(8,128)} async-done(((f32[4096,1024]{1,0:T(8,128)}), f32[128,1024]{1,0:T(8,128)}) %reduce-scatter.2.cloned.1.call-update) | async-done | bytes 524304 | tf_op jit(solution)/shard_map/reduce_scatter | solution.py:170
  280.8 4.7 %fusion.13 = f32[128,4096]{1,0:T(8,128)S(1)} fusion(bf16[128,1024]{0,1:T(8,128)(2,1)S(1)} %bitcast.48, bf16[1024,4096]{1,0:T(8,128)(2,1)} %param.17), kind=kOutput, calls=%fused_computation.51 | convolution fusion | flops 1073741824 | bytes 10747904 | tf_op jit(solution)/shard_map/dot_general | solution.py:263
  285.6 1.6 collective-permute-start.16
  287.2 2.9 collective-permute-start.17
  290.2 1.3 collective-permute-start.18
  291.5 3.5 %collective-permute-done.16 = bf16[128,1024]{1,0:T(8,128)(2,1)S(1)} collective-permute-done((bf16[128,1024]{1,0:T(8,128)(2,1)S(1)}, bf16[128,1024]{1,0:T(8,128)(2,1)S(1)}, u32[]{:S(2)}, u32[]{:S(2)}) %collective-permute-start.16) | collective-permute-done | bytes 262176 | tf_op jit(solution)/shard_map/ppermute | solution.py:186
  295.0 5.4 %collective-permute-done.17 = bf16[128,1024]{1,0:T(8,128)(2,1)S(1)} collective-permute-done((bf16[128,1024]{1,0:T(8,128)(2,1)S(1)}, bf16[128,1024]{1,0:T(8,128)(2,1)S(1)}, u32[]{:S(2)}, u32[]{:S(2)}) %collective-permute-start.17) | collective-permute-done | bytes 262176 | tf_op jit(solution)/shard_map/ppermute | solution.py:186
  300.4 1.8 add_convert_fusion
  (79 shorter events, 19.0 us)
Async XLA Ops:
  6.5 7.5 %copy-start = (s32[64]{0:T(128)S(1)}, s32[64]{0:T(128)}, u32[]{:S(2)}) copy-start(s32[64]{0:T(128)} %param.16) | copy-start | bytes 772
  6.5 58.2 %all-gather.2.cloned.1.call-start = ((), (), s32[]{:S(2)}) async-start(), calls=%async_computation.1 | async-start | bytes 8650752 | tf_op jit(solution)/shard_map/all_gather | solution.py:142
  7.3 272.0 %reduce-scatter.2.cloned.1.call-start = ((), (), s32[]{:S(2)}) async-start(), calls=%async_computation.2 | async-start | bytes 17301504 | tf_op jit(solution)/shard_map/reduce_scatter | solution.py:170
  14.0 1.8 copy-start.1
  14.0 3.2 %copy-start.6 = (s32[16]{0:T(128)S(1)}, s32[16]{0:T(128)}, u32[]{:S(2)}) copy-start(s32[16]{0:T(128)} %param.14) | copy-start | bytes 196
  93.9 1.6 collective-permute-start
  96.4 6.9 %collective-permute-start.1 = (f32[256,128]{1,0:T(8,128)S(1)}, f32[256,128]{1,0:T(8,128)S(1)}, u32[]{:S(2)}, u32[]{:S(2)}) collective-permute-start(f32[256,128]{1,0:T(8,128)S(1)} %max.34), channel_id=1, source_target_pairs={{0,2},{1,3},{2,4},{3,5},{4,6},{5,7},{6,0},{7,1},{8,10},{9,11},{10,... | collective-permute-start | bytes 393224 | tf_op jit(solution)/shard_map/ppermute | solution.py:125
  97.9 9.1 %collective-permute-start.2 = (f32[256,128]{1,0:T(8,128)S(1)}, f32[256,128]{1,0:T(8,128)S(1)}, u32[]{:S(2)}, u32[]{:S(2)}) collective-permute-start(f32[256,128]{1,0:T(8,128)S(1)} %max.34), channel_id=1, source_target_pairs={{0,4},{1,5},{2,6},{3,7},{4,0},{5,1},{6,2},{7,3},{8,12},{9,13},{10,... | collective-permute-start | bytes 393224 | tf_op jit(solution)/shard_map/ppermute | solution.py:125
  100.6 6.4 %collective-permute-start.3 = (f32[256,128]{1,0:T(8,128)S(1)}, f32[256,128]{1,0:T(8,128)S(1)}, u32[]{:S(2)}, u32[]{:S(2)}) collective-permute-start(f32[256,128]{1,0:T(8,128)S(1)} %max.34), channel_id=1, source_target_pairs={{0,6},{1,7},{2,0},{3,1},{4,2},{5,3},{6,4},{7,5},{8,14},{9,15},{10,... | collective-permute-start | bytes 393224 | tf_op jit(solution)/shard_map/ppermute | solution.py:125
  107.1 7.6 %collective-permute-start.4 = (f32[256,128]{1,0:T(8,128)S(1)}, f32[256,128]{1,0:T(8,128)S(1)}, u32[]{:S(2)}, u32[]{:S(2)}) collective-permute-start(f32[256,128]{1,0:T(8,128)S(1)} %maximum_maximum_fusion.1), channel_id=1, source_target_pairs={{0,8},{1,9},{2,10},{3,11},{4,12},{5,13},{6,14},{7,15},{8,16},{9,17... | collective-permute-start | bytes 393224 | tf_op jit(solution)/shard_map/ppermute | solution.py:125
  108.1 8.0 %collective-permute-start.5 = (f32[256,128]{1,0:T(8,128)S(1)}, f32[256,128]{1,0:T(8,128)S(1)}, u32[]{:S(2)}, u32[]{:S(2)}) collective-permute-start(f32[256,128]{1,0:T(8,128)S(1)} %maximum_maximum_fusion.1), channel_id=1, source_target_pairs={{0,16},{1,17},{2,18},{3,19},{4,20},{5,21},{6,22},{7,23},{8,24},{9,... | collective-permute-start | bytes 393224 | tf_op jit(solution)/shard_map/ppermute | solution.py:125
  110.8 5.7 %collective-permute-start.6 = (f32[256,128]{1,0:T(8,128)S(1)}, f32[256,128]{1,0:T(8,128)S(1)}, u32[]{:S(2)}, u32[]{:S(2)}) collective-permute-start(f32[256,128]{1,0:T(8,128)S(1)} %maximum_maximum_fusion.1), channel_id=1, source_target_pairs={{0,24},{1,25},{2,26},{3,27},{4,28},{5,29},{6,30},{7,31},{8,0},{9,1... | collective-permute-start | bytes 393224 | tf_op jit(solution)/shard_map/ppermute | solution.py:125
  162.7 0.8 copy-start.4
  162.7 2.3 copy-start.5
  162.7 6.7 %copy-start.2 = (bf16[128,1024]{1,0:T(8,128)(2,1)S(1)}, bf16[128,1024]{1,0:T(8,128)(2,1)}, u32[]{:S(2)}) copy-start(bf16[128,1024]{1,0:T(8,128)(2,1)} %param.9) | copy-start | bytes 786436
  162.7 7.0 %copy-start.3 = (f32[256,128]{1,0:T(8,128)S(1)}, f32[256,128]{1,0:T(8,128)}, u32[]{:S(2)}) copy-start(f32[256,128]{1,0:T(8,128)} %get-tuple-element.8) | copy-start | bytes 393220
  163.6 6.0 %collective-permute-start.7 = (bf16[128,256]{0,1:T(8,128)(2,1)S(1)}, bf16[128,256]{0,1:T(8,128)(2,1)S(1)}, u32[]{:S(2)}, u32[]{:S(2)}) collective-permute-start(bf16[128,256]{0,1:T(8,128)(2,1)S(1)} %copy.27), channel_id=1, source_target_pairs={{0,1},{1,2},{2,3},{3,4},{4,5},{5,6},{6,7},{7,8},{8,9},{9,10},{10,1... | collective-permute-start | bytes 196616 | tf_op jit(solution)/shard_map/ppermute | solution.py:19
  165.0 12.1 %collective-permute-start.8 = (bf16[128,256]{1,0:T(8,128)(2,1)S(1)}, bf16[128,256]{1,0:T(8,128)(2,1)S(1)}, u32[]{:S(2)}, u32[]{:S(2)}) collective-permute-start(bf16[128,256]{1,0:T(8,128)(2,1)S(1)} %copy-done.5), channel_id=1, source_target_pairs={{0,1},{1,2},{2,3},{3,4},{4,5},{5,6},{6,7},{7,8},{8,9},{9,10},{10,1... | collective-permute-start | bytes 196616 | tf_op jit(solution)/shard_map/ppermute | solution.py:19
  169.7 1.4 collective-permute-start.9
  171.1 6.8 %collective-permute-start.10 = (f32[256,128]{1,0:T(8,128)S(1)}, f32[256,128]{1,0:T(8,128)S(1)}, u32[]{:S(2)}, u32[]{:S(2)}) collective-permute-start(f32[256,128]{1,0:T(8,128)S(1)} %add.186), channel_id=1, source_target_pairs={{0,2},{1,3},{2,4},{3,5},{4,6},{5,7},{6,0},{7,1},{8,10},{9,11},{10,... | collective-permute-start | bytes 393224 | tf_op jit(solution)/shard_map/ppermute | solution.py:125
  172.2 9.7 %collective-permute-start.11 = (f32[256,128]{1,0:T(8,128)S(1)}, f32[256,128]{1,0:T(8,128)S(1)}, u32[]{:S(2)}, u32[]{:S(2)}) collective-permute-start(f32[256,128]{1,0:T(8,128)S(1)} %add.186), channel_id=1, source_target_pairs={{0,4},{1,5},{2,6},{3,7},{4,0},{5,1},{6,2},{7,3},{8,12},{9,13},{10,... | collective-permute-start | bytes 393224 | tf_op jit(solution)/shard_map/ppermute | solution.py:125
  175.5 6.3 %collective-permute-start.12 = (f32[256,128]{1,0:T(8,128)S(1)}, f32[256,128]{1,0:T(8,128)S(1)}, u32[]{:S(2)}, u32[]{:S(2)}) collective-permute-start(f32[256,128]{1,0:T(8,128)S(1)} %add.186), channel_id=1, source_target_pairs={{0,6},{1,7},{2,0},{3,1},{4,2},{5,3},{6,4},{7,5},{8,14},{9,15},{10,... | collective-permute-start | bytes 393224 | tf_op jit(solution)/shard_map/ppermute | solution.py:125
  181.9 8.1 %collective-permute-start.13 = (f32[256,128]{1,0:T(8,128)S(1)}, f32[256,128]{1,0:T(8,128)S(1)}, u32[]{:S(2)}, u32[]{:S(2)}) collective-permute-start(f32[256,128]{1,0:T(8,128)S(1)} %add_add_fusion), channel_id=1, source_target_pairs={{0,8},{1,9},{2,10},{3,11},{4,12},{5,13},{6,14},{7,15},{8,16},{9,17... | collective-permute-start | bytes 393224 | tf_op jit(solution)/shard_map/ppermute | solution.py:125
  184.9 7.8 %collective-permute-start.14 = (f32[256,128]{1,0:T(8,128)S(1)}, f32[256,128]{1,0:T(8,128)S(1)}, u32[]{:S(2)}, u32[]{:S(2)}) collective-permute-start(f32[256,128]{1,0:T(8,128)S(1)} %add_add_fusion), channel_id=1, source_target_pairs={{0,16},{1,17},{2,18},{3,19},{4,20},{5,21},{6,22},{7,23},{8,24},{9,... | collective-permute-start | bytes 393224 | tf_op jit(solution)/shard_map/ppermute | solution.py:125
  187.5 5.2 %collective-permute-start.15 = (f32[256,128]{1,0:T(8,128)S(1)}, f32[256,128]{1,0:T(8,128)S(1)}, u32[]{:S(2)}, u32[]{:S(2)}) collective-permute-start(f32[256,128]{1,0:T(8,128)S(1)} %add_add_fusion), channel_id=1, source_target_pairs={{0,24},{1,25},{2,26},{3,27},{4,28},{5,29},{6,30},{7,31},{8,0},{9,1... | collective-permute-start | bytes 393224 | tf_op jit(solution)/shard_map/ppermute | solution.py:125
  285.6 9.3 %collective-permute-start.16 = (bf16[128,1024]{1,0:T(8,128)(2,1)S(1)}, bf16[128,1024]{1,0:T(8,128)(2,1)S(1)}, u32[]{:S(2)}, u32[]{:S(2)}) collective-permute-start(bf16[128,1024]{1,0:T(8,128)(2,1)S(1)} %get-tuple-element.13), channel_id=1, source_target_pairs={{0,32},{32,64},{64,96},{96,0},{1,33},{33,65},{65,97},{97,1},{2,34}... | collective-permute-start | bytes 786440 | tf_op jit(solution)/shard_map/ppermute | solution.py:186
  287.2 13.1 %collective-permute-start.17 = (bf16[128,1024]{1,0:T(8,128)(2,1)S(1)}, bf16[128,1024]{1,0:T(8,128)(2,1)S(1)}, u32[]{:S(2)}, u32[]{:S(2)}) collective-permute-start(bf16[128,1024]{1,0:T(8,128)(2,1)S(1)} %get-tuple-element.15), channel_id=1, source_target_pairs={{0,64},{32,96},{64,0},{96,32},{1,65},{33,97},{65,1},{97,33},{2,66}... | collective-permute-start | bytes 786440 | tf_op jit(solution)/shard_map/ppermute | solution.py:186
  290.2 10.2 %collective-permute-start.18 = (bf16[128,1024]{1,0:T(8,128)(2,1)S(1)}, bf16[128,1024]{1,0:T(8,128)(2,1)}, u32[]{:S(2)}, u32[]{:S(2)}) collective-permute-start(bf16[128,1024]{1,0:T(8,128)(2,1)S(1)} %get-tuple-element.14), channel_id=1, source_target_pairs={{0,96},{32,0},{64,32},{96,64},{1,97},{33,1},{65,33},{97,65},{2,98}... | collective-permute-start | bytes 786440 | tf_op jit(solution)/shard_map/ppermute | solution.py:186
Sparse Core Ops, SparseCore 0:
  9.6 55.1 all-gather.1
  162.9 116.3 reduce-scatter.1

commit v12 on v11

--- a/solution.py
+++ b/solution.py
@@ -90,7 +90,7 @@
 
 
 def ctx_kernel(
-    lo_ref, hi_ref, blk_ref, q_ref, kt_ref, v_ref, m_ref, o_ref, t_ref, *, heads, qgw, scale
+    lo_ref, hi_ref, blk_ref, q_ref, kt_ref, v_ref, o_ref, t_ref, m_ref, *, heads, qgw, scale
 ):
     i = pl.program_id(0)
     tile = q_ref.shape[0]
@@ -99,20 +99,23 @@
     mask = _slot_mask(lo_ref, hi_ref, base, rows)
     lane = lax.broadcasted_iota(jnp.int32, (1, STAT_LANES), 1)
     totals = jnp.zeros((tile, STAT_LANES), jnp.float32)
-    tops = jnp.transpose(m_ref[...])
+    maxes = jnp.full((tile, STAT_LANES), -jnp.inf, jnp.float32)
     for kv in range(heads // qgw):
         group = range(kv * qgw, (kv + 1) * qgw)
         keys = _slot_keys(kt_ref, blk_ref, base, kv)
         values = _slot_values(v_ref, blk_ref, base, kv)
-        sc = jnp.dot(_stacked(q_ref, kv, qgw), keys, preferred_element_type=jnp.float32) * scale
-        top = jnp.concatenate([tops[:, h : h + 1] for h in group], axis=0)
-        p = jnp.exp(jnp.where(mask, sc - top, -jnp.inf))
+        sc = jnp.dot(_stacked(q_ref, kv, qgw), keys, preferred_element_type=jnp.float32)
+        sc = jnp.where(mask, sc, -jnp.inf)
+        top = jnp.max(sc, axis=1, keepdims=True) * scale
+        p = jnp.exp(sc * scale - top)
         ctx = jnp.dot(p.astype(jnp.bfloat16), values, preferred_element_type=jnp.float32)
         tot = jnp.sum(p, axis=1, keepdims=True)
         for j, h in enumerate(group):
             o_ref[:, h * HEAD_SIZE : (h + 1) * HEAD_SIZE] = ctx[j * tile : (j + 1) * tile]
             totals = jnp.where(lane == h, tot[j * tile : (j + 1) * tile], totals)
+            maxes = jnp.where(lane == h, top[j * tile : (j + 1) * tile], maxes)
     t_ref[...] = jnp.transpose(totals)[: t_ref.shape[0], :]
+    m_ref[...] = jnp.transpose(maxes)[: m_ref.shape[0], :]
 
 
 def butterfly(x, axis, combine):
@@ -149,24 +152,23 @@
     s_spec = pl.BlockSpec((stat_rows, tok_dev), lambda i, *_: (i, 0))
     stat_shape = jax.ShapeDtypeStruct((n_tiles * stat_rows, tok_dev), jnp.float32)
     kw = dict(heads=heads, qgw=qgw, scale=scale)
-    local_max = pl.pallas_call(
-        functools.partial(max_kernel, **kw),
-        out_shape=stat_shape,
-        grid_spec=pltpu.PrefetchScalarGridSpec(
-            num_scalar_prefetch=3, grid=(n_tiles,), in_specs=[q_spec, kt_spec], out_specs=s_spec
-        ),
-    )(lo, hi, blk, gathered, keys_t)
-    far_max = butterfly(local_max, "blk", jnp.maximum)
-    partial, totals = pl.pallas_call(
+    partial, totals, local_max = pl.pallas_call(
         functools.partial(ctx_kernel, **kw),
-        out_shape=(jax.ShapeDtypeStruct((row_count, q_cols), jnp.float32), stat_shape),
+        out_shape=(jax.ShapeDtypeStruct((row_count, q_cols), jnp.float32), stat_shape, stat_shape),
         grid_spec=pltpu.PrefetchScalarGridSpec(
             num_scalar_prefetch=3,
             grid=(n_tiles,),
-            in_specs=[q_spec, kt_spec, v_spec, s_spec],
-            out_specs=(pl.BlockSpec((tok_dev, q_cols), lambda i, *_: (i, 0)), s_spec),
+            in_specs=[q_spec, kt_spec, v_spec],
+            out_specs=(pl.BlockSpec((tok_dev, q_cols), lambda i, *_: (i, 0)), s_spec, s_spec),
         ),
-    )(lo, hi, blk, gathered, keys_t, values, far_max)
+    )(lo, hi, blk, gathered, keys_t, values)
+    far_max = butterfly(local_max, "blk", jnp.maximum)
+    factor = jnp.exp(local_max - far_max)
+    row_factor = jnp.transpose(
+        factor.reshape(n_tiles, stat_rows, tok_dev)[:, :heads], (0, 2, 1)
+    ).reshape(row_count, heads, 1)
+    partial = (partial.reshape(row_count, heads, HEAD_SIZE) * row_factor).reshape(row_count, q_cols)
+    totals = totals * factor
     context = lax.psum_scatter(partial, "blk", scatter_dimension=0, tiled=True)
     totals = butterfly(totals, "blk", jnp.add)
     own = lambda a: jnp.transpose(

time: 310 us -> 312 us (level)
  Pallas kernels: 74.6 us -> 56.4 us
  other arithmetic: 5.44 us -> 21.1 us
  local copies, waits for them, and re-layouts: 13.9 us -> 18.5 us
    pallas_call x1 -> x0, Pallas kernels: 29.1 us -> none  [far_part(): pl.pallas_call(functools.partial(max_kernel, **kw), out_shape=stat_shape,...]
    mul x0 -> x3, other arithmetic: none -> 16.3 us  [the longest x2 15.3 us: far_part(): partial.reshape(row_count, heads, HEAD_SIZE) * row_factor]
    pallas_call x1, Pallas kernels: 45.5 us -> 56.4 us  [far_part(): pl.pallas_call(functools.partial(ctx_kernel, **kw), out_shape=(jax.ShapeD...]
    mul x0 -> x2, local copies, waits for them, and re-layouts: none -> 5.2 us  [far_part(): partial.reshape(row_count, heads, HEAD_SIZE) * row_factor]
  transfers between devices with their start and end apart: 21 -> 21, of which waited for: 15 -> 15; matrix products, arithmetic and copies ran while one was open for 5% -> 4% of each run, Pallas kernels for 0% -> 0%
where the time goes in v12:
time: 312 us
  waiting for transfers between devices  162 us (52%)
  Pallas kernels  56.4 us (18%)
  starting transfers between devices  34.5 us (11%)
  other arithmetic  21.1 us (7%)
  local copies, waits for them, and re-layouts  18.5 us (6%)
  between operations  13.7 us (4%)
  matrix products  5.36 us (2%)
    reduce_scatter x1, waiting for transfers between devices, far_part(): context = lax.psum_scatter(partial, 'blk', scatter_dimension=0, tiled=True)  86.3 us
    pallas_call x1, Pallas kernels, far_part(): pl.pallas_call(functools.partial(ctx_kernel, **kw), out_shape=(jax.ShapeD...  56.4 us
    all_gather x1, waiting for transfers between devices, far_part(): gathered = lax.all_gather(queries, 'blk', axis=0, tiled=True)  45.3 us
    ppermute x14, starting transfers between devices, butterfly(): lax.ppermute(x, axis, [(i, i + ((digit(i) + d) % radix - digit(i)) * stri...  23.3 us
    ppermute x14, waiting for transfers between devices, butterfly(): lax.ppermute(x, axis, [(i, i + ((digit(i) + d) % radix - digit(i)) * stri...  20.9 us
    mul x2, other arithmetic, far_part(): partial.reshape(row_count, heads, HEAD_SIZE) * row_factor  15.3 us
    ppermute x3, waiting for transfers between devices, column_sum(): got = lax.ppermute(sent, axis, [(i, (i + d) % n) for i in range(n)])  8.8 us
  transfers between devices with their start and end apart: 21, of which 15 were waited for; matrix products, arithmetic and copies ran while one was open for 4% of the time, Pallas kernels for 0%

profile of v12, /device:TPU:0, one launch (start us, length us, event | category | flops | bytes accessed | tf_op | source)
XLA Modules:
  0.0 311.7 jit_solution(16952232952180972624)
XLA Ops:
  9.3 1.6 gather_fusion.1
  10.9 1.6 gather_fusion
  14.1 1.5 gather_fusion.2
  17.4 2.1 gather_fusion.3
  19.5 45.3 %all-gather.2.cloned.1.call-done.q_ref = bf16[4096,1024]{1,0:T(8,128)(2,1)} async-done(((bf16[128,1024]{1,0:T(8,128)(2,1)}), bf16[4096,1024]{1,0:T(8,128)(2,1)}) %all-gather.2.cloned.1.call-update) | async-done | bytes 8388624 | tf_op jit(solution)/shard_map/all_gather | solution.py:145
  64.8 56.4 %shard_map.91 = (f32[4096,1024]{1,0:T(8,128)}, f32[256,128]{1,0:T(8,128)}, f32[256,128]{1,0:T(8,128)}) custom-call(s32[160]{0:T(256)} %select_n.90.lo_ref, s32[160]{0:T(256)} %select_n.92.hi_ref, s32[160]{0:T(256)} %gather_fusion.3, bf16[4096,1024]{1,0:T(8,128)(2,1)} %all-gather.2.cloned.1.call-done.q_ref, bf16[16,256,128]{2,1,0:T(8,128)(2,1)} %bitcast.56, ...), custom_call_target="tpu_custom_call" | custom-call | tf_op jit(solution)/shard_map/pallas_call | solution.py:155
  123.7 1.5 collective-permute-start.1
  125.2 2.7 collective-permute-start.2
  127.9 1.5 collective-permute-start.3
  130.6 3.7 %collective-permute-done.2 = f32[256,128]{1,0:T(8,128)S(1)} collective-permute-done((f32[256,128]{1,0:T(8,128)S(1)}, f32[256,128]{1,0:T(8,128)S(1)}, u32[]{:S(2)}, u32[]{:S(2)}) %collective-permute-start.2) | collective-permute-done | bytes 131104 | tf_op jit(solution)/shard_map/ppermute | solution.py:128
  135.4 2.7 collective-permute-start.5
  138.1 1.4 collective-permute-start.6
  139.5 2.5 collective-permute-done.4
  142.0 1.4 collective-permute-done.5
  146.4 4.6 %mul.76 = f32[4096,8,128]{2,1,0:T(8,128)S(1)} broadcast(f32[4096,8]{1,0:T(8,128)S(1)} %copy.28), dimensions={0,1} | broadcast | bytes 16908288 | tf_op jit(solution)/shard_map/mul | solution.py:170
  151.0 14.4 %bitcast_multiply_fusion = f32[4096,1024]{1,0:T(8,128)} fusion(f32[4096,1024]{1,0:T(8,128)} %get-tuple-element.8, f32[512,8,8,128]{3,2,1,0:T(8,128)S(1)} %bitcast.55), kind=kLoop, calls=%fused_computation.4 | loop fusion | flops 4194304 | bytes 50331648 | tf_op jit(solution)/shard_map/mul | solution.py:170
  167.7 4.0 %collective-permute-start.8 = (bf16[128,256]{1,0:T(8,128)(2,1)S(1)}, bf16[128,256]{1,0:T(8,128)(2,1)S(1)}, u32[]{:S(2)}, u32[]{:S(2)}) collective-permute-start(bf16[128,256]{1,0:T(8,128)(2,1)S(1)} %copy-done.5), channel_id=1, source_target_pairs={{0,1},{1,2},{2,3},{3,4},{4,5},{5,6},{6,7},{7,8},{8,9},{9,10},{10,1... | collective-permute-start | bytes 196616 | tf_op jit(solution)/shard_map/ppermute | solution.py:19
  174.9 3.3 %collective-permute-start.11 = (f32[256,128]{1,0:T(8,128)S(1)}, f32[256,128]{1,0:T(8,128)S(1)}, u32[]{:S(2)}, u32[]{:S(2)}) collective-permute-start(f32[256,128]{1,0:T(8,128)S(1)} %add.186), channel_id=1, source_target_pairs={{0,4},{1,5},{2,6},{3,7},{4,0},{5,1},{6,2},{7,3},{8,12},{9,13},{10,... | collective-permute-start | bytes 393224 | tf_op jit(solution)/shard_map/ppermute | solution.py:128
  178.2 1.5 collective-permute-start.12
  180.7 3.9 %collective-permute-done.11 = f32[256,128]{1,0:T(8,128)S(1)} collective-permute-done((f32[256,128]{1,0:T(8,128)S(1)}, f32[256,128]{1,0:T(8,128)S(1)}, u32[]{:S(2)}, u32[]{:S(2)}) %collective-permute-start.11) | collective-permute-done | bytes 131104 | tf_op jit(solution)/shard_map/ppermute | solution.py:128
  184.6 3.2 %collective-permute-start.13 = (f32[256,128]{1,0:T(8,128)S(1)}, f32[256,128]{1,0:T(8,128)S(1)}, u32[]{:S(2)}, u32[]{:S(2)}) collective-permute-start(f32[256,128]{1,0:T(8,128)S(1)} %add_add_fusion), channel_id=1, source_target_pairs={{0,8},{1,9},{2,10},{3,11},{4,12},{5,13},{6,14},{7,15},{8,16},{9,17... | collective-permute-start | bytes 393224 | tf_op jit(solution)/shard_map/ppermute | solution.py:128
  187.8 2.6 collective-permute-start.14
  191.0 1.9 collective-permute-done.13
  192.9 2.7 collective-permute-done.14
  195.6 86.3 %reduce-scatter.2.cloned.1.call-done = f32[128,1024]{1,0:T(8,128)} async-done(((f32[4096,1024]{1,0:T(8,128)}), f32[128,1024]{1,0:T(8,128)}) %reduce-scatter.2.cloned.1.call-update) | async-done | bytes 524304 | tf_op jit(solution)/shard_map/reduce_scatter | solution.py:172
  283.5 4.7 %fusion.15 = f32[128,4096]{1,0:T(8,128)S(1)} fusion(bf16[128,1024]{0,1:T(8,128)(2,1)S(1)} %bitcast.57, bf16[1024,4096]{1,0:T(8,128)(2,1)} %param.17), kind=kOutput, calls=%fused_computation.55 | convolution fusion | flops 1073741824 | bytes 10747904 | tf_op jit(solution)/shard_map/dot_general | solution.py:265
  288.3 1.6 collective-permute-start.16
  290.0 2.9 collective-permute-start.17
  292.8 1.4 collective-permute-start.18
  294.2 3.4 %collective-permute-done.16 = bf16[128,1024]{1,0:T(8,128)(2,1)S(1)} collective-permute-done((bf16[128,1024]{1,0:T(8,128)(2,1)S(1)}, bf16[128,1024]{1,0:T(8,128)(2,1)S(1)}, u32[]{:S(2)}, u32[]{:S(2)}) %collective-permute-start.16) | collective-permute-done | bytes 262176 | tf_op jit(solution)/shard_map/ppermute | solution.py:188
  297.6 5.4 %collective-permute-done.17 = bf16[128,1024]{1,0:T(8,128)(2,1)S(1)} collective-permute-done((bf16[128,1024]{1,0:T(8,128)(2,1)S(1)}, bf16[128,1024]{1,0:T(8,128)(2,1)S(1)}, u32[]{:S(2)}, u32[]{:S(2)}) %collective-permute-start.17) | collective-permute-done | bytes 262176 | tf_op jit(solution)/shard_map/ppermute | solution.py:188
  303.0 1.8 add_convert_fusion
  (82 shorter events, 22.4 us)
Async XLA Ops:
  6.5 7.5 %copy-start = (s32[64]{0:T(128)S(1)}, s32[64]{0:T(128)}, u32[]{:S(2)}) copy-start(s32[64]{0:T(128)} %param.16) | copy-start | bytes 772
  6.5 58.2 %all-gather.2.cloned.1.call-start = ((), (), s32[]{:S(2)}) async-start(), calls=%async_computation.1 | async-start | bytes 8650752 | tf_op jit(solution)/shard_map/all_gather | solution.py:145
  7.3 274.7 %reduce-scatter.2.cloned.1.call-start = ((), (), s32[]{:S(2)}) async-start(), calls=%async_computation.2 | async-start | bytes 17301504 | tf_op jit(solution)/shard_map/reduce_scatter | solution.py:172
  14.1 1.8 copy-start.2
  14.1 3.2 %copy-start.6 = (s32[16]{0:T(128)S(1)}, s32[16]{0:T(128)}, u32[]{:S(2)}) copy-start(s32[16]{0:T(128)} %param.14) | copy-start | bytes 196
  121.2 1.6 collective-permute-start
  123.7 6.9 %collective-permute-start.1 = (f32[256,128]{1,0:T(8,128)S(1)}, f32[256,128]{1,0:T(8,128)S(1)}, u32[]{:S(2)}, u32[]{:S(2)}) collective-permute-start(f32[256,128]{1,0:T(8,128)S(1)} %max.34), channel_id=1, source_target_pairs={{0,2},{1,3},{2,4},{3,5},{4,6},{5,7},{6,0},{7,1},{8,10},{9,11},{10,... | collective-permute-start | bytes 393224 | tf_op jit(solution)/shard_map/ppermute | solution.py:128
  125.2 9.1 %collective-permute-start.2 = (f32[256,128]{1,0:T(8,128)S(1)}, f32[256,128]{1,0:T(8,128)S(1)}, u32[]{:S(2)}, u32[]{:S(2)}) collective-permute-start(f32[256,128]{1,0:T(8,128)S(1)} %max.34), channel_id=1, source_target_pairs={{0,4},{1,5},{2,6},{3,7},{4,0},{5,1},{6,2},{7,3},{8,12},{9,13},{10,... | collective-permute-start | bytes 393224 | tf_op jit(solution)/shard_map/ppermute | solution.py:128
  127.9 6.4 %collective-permute-start.3 = (f32[256,128]{1,0:T(8,128)S(1)}, f32[256,128]{1,0:T(8,128)S(1)}, u32[]{:S(2)}, u32[]{:S(2)}) collective-permute-start(f32[256,128]{1,0:T(8,128)S(1)} %max.34), channel_id=1, source_target_pairs={{0,6},{1,7},{2,0},{3,1},{4,2},{5,3},{6,4},{7,5},{8,14},{9,15},{10,... | collective-permute-start | bytes 393224 | tf_op jit(solution)/shard_map/ppermute | solution.py:128
  134.4 7.6 %collective-permute-start.4 = (f32[256,128]{1,0:T(8,128)S(1)}, f32[256,128]{1,0:T(8,128)S(1)}, u32[]{:S(2)}, u32[]{:S(2)}) collective-permute-start(f32[256,128]{1,0:T(8,128)S(1)} %maximum_maximum_fusion.1), channel_id=1, source_target_pairs={{0,8},{1,9},{2,10},{3,11},{4,12},{5,13},{6,14},{7,15},{8,16},{9,17... | collective-permute-start | bytes 393224 | tf_op jit(solution)/shard_map/ppermute | solution.py:128
  135.4 8.0 %collective-permute-start.5 = (f32[256,128]{1,0:T(8,128)S(1)}, f32[256,128]{1,0:T(8,128)S(1)}, u32[]{:S(2)}, u32[]{:S(2)}) collective-permute-start(f32[256,128]{1,0:T(8,128)S(1)} %maximum_maximum_fusion.1), channel_id=1, source_target_pairs={{0,16},{1,17},{2,18},{3,19},{4,20},{5,21},{6,22},{7,23},{8,24},{9,... | collective-permute-start | bytes 393224 | tf_op jit(solution)/shard_map/ppermute | solution.py:128
  138.1 5.7 %collective-permute-start.6 = (f32[256,128]{1,0:T(8,128)S(1)}, f32[256,128]{1,0:T(8,128)S(1)}, u32[]{:S(2)}, u32[]{:S(2)}) collective-permute-start(f32[256,128]{1,0:T(8,128)S(1)} %maximum_maximum_fusion.1), channel_id=1, source_target_pairs={{0,24},{1,25},{2,26},{3,27},{4,28},{5,29},{6,30},{7,31},{8,0},{9,1... | collective-permute-start | bytes 393224 | tf_op jit(solution)/shard_map/ppermute | solution.py:128
  165.4 0.8 copy-start.4
  165.4 2.3 copy-start.5
  165.4 6.7 %copy-start.3 = (bf16[128,1024]{1,0:T(8,128)(2,1)S(1)}, bf16[128,1024]{1,0:T(8,128)(2,1)}, u32[]{:S(2)}) copy-start(bf16[128,1024]{1,0:T(8,128)(2,1)} %param.9) | copy-start | bytes 786436
  166.4 6.0 %collective-permute-start.7 = (bf16[128,256]{0,1:T(8,128)(2,1)S(1)}, bf16[128,256]{0,1:T(8,128)(2,1)S(1)}, u32[]{:S(2)}, u32[]{:S(2)}) collective-permute-start(bf16[128,256]{0,1:T(8,128)(2,1)S(1)} %copy.29), channel_id=1, source_target_pairs={{0,1},{1,2},{2,3},{3,4},{4,5},{5,6},{6,7},{7,8},{8,9},{9,10},{10,1... | collective-permute-start | bytes 196616 | tf_op jit(solution)/shard_map/ppermute | solution.py:19
  167.7 12.1 %collective-permute-start.8 = (bf16[128,256]{1,0:T(8,128)(2,1)S(1)}, bf16[128,256]{1,0:T(8,128)(2,1)S(1)}, u32[]{:S(2)}, u32[]{:S(2)}) collective-permute-start(bf16[128,256]{1,0:T(8,128)(2,1)S(1)} %copy-done.5), channel_id=1, source_target_pairs={{0,1},{1,2},{2,3},{3,4},{4,5},{5,6},{6,7},{7,8},{8,9},{9,10},{10,1... | collective-permute-start | bytes 196616 | tf_op jit(solution)/shard_map/ppermute | solution.py:19
  172.4 1.4 collective-permute-start.9
  173.8 6.8 %collective-permute-start.10 = (f32[256,128]{1,0:T(8,128)S(1)}, f32[256,128]{1,0:T(8,128)S(1)}, u32[]{:S(2)}, u32[]{:S(2)}) collective-permute-start(f32[256,128]{1,0:T(8,128)S(1)} %add.186), channel_id=1, source_target_pairs={{0,2},{1,3},{2,4},{3,5},{4,6},{5,7},{6,0},{7,1},{8,10},{9,11},{10,... | collective-permute-start | bytes 393224 | tf_op jit(solution)/shard_map/ppermute | solution.py:128
  174.9 9.6 %collective-permute-start.11 = (f32[256,128]{1,0:T(8,128)S(1)}, f32[256,128]{1,0:T(8,128)S(1)}, u32[]{:S(2)}, u32[]{:S(2)}) collective-permute-start(f32[256,128]{1,0:T(8,128)S(1)} %add.186), channel_id=1, source_target_pairs={{0,4},{1,5},{2,6},{3,7},{4,0},{5,1},{6,2},{7,3},{8,12},{9,13},{10,... | collective-permute-start | bytes 393224 | tf_op jit(solution)/shard_map/ppermute | solution.py:128
  178.2 6.3 %collective-permute-start.12 = (f32[256,128]{1,0:T(8,128)S(1)}, f32[256,128]{1,0:T(8,128)S(1)}, u32[]{:S(2)}, u32[]{:S(2)}) collective-permute-start(f32[256,128]{1,0:T(8,128)S(1)} %add.186), channel_id=1, source_target_pairs={{0,6},{1,7},{2,0},{3,1},{4,2},{5,3},{6,4},{7,5},{8,14},{9,15},{10,... | collective-permute-start | bytes 393224 | tf_op jit(solution)/shard_map/ppermute | solution.py:128
  184.6 8.3 %collective-permute-start.13 = (f32[256,128]{1,0:T(8,128)S(1)}, f32[256,128]{1,0:T(8,128)S(1)}, u32[]{:S(2)}, u32[]{:S(2)}) collective-permute-start(f32[256,128]{1,0:T(8,128)S(1)} %add_add_fusion), channel_id=1, source_target_pairs={{0,8},{1,9},{2,10},{3,11},{4,12},{5,13},{6,14},{7,15},{8,16},{9,17... | collective-permute-start | bytes 393224 | tf_op jit(solution)/shard_map/ppermute | solution.py:128
  187.8 7.8 %collective-permute-start.14 = (f32[256,128]{1,0:T(8,128)S(1)}, f32[256,128]{1,0:T(8,128)S(1)}, u32[]{:S(2)}, u32[]{:S(2)}) collective-permute-start(f32[256,128]{1,0:T(8,128)S(1)} %add_add_fusion), channel_id=1, source_target_pairs={{0,16},{1,17},{2,18},{3,19},{4,20},{5,21},{6,22},{7,23},{8,24},{9,... | collective-permute-start | bytes 393224 | tf_op jit(solution)/shard_map/ppermute | solution.py:128
  190.4 5.2 %collective-permute-start.15 = (f32[256,128]{1,0:T(8,128)S(1)}, f32[256,128]{1,0:T(8,128)S(1)}, u32[]{:S(2)}, u32[]{:S(2)}) collective-permute-start(f32[256,128]{1,0:T(8,128)S(1)} %add_add_fusion), channel_id=1, source_target_pairs={{0,24},{1,25},{2,26},{3,27},{4,28},{5,29},{6,30},{7,31},{8,0},{9,1... | collective-permute-start | bytes 393224 | tf_op jit(solution)/shard_map/ppermute | solution.py:128
  283.5 21.3 %copy-start.1 = (s32[64]{0:T(128)S(1)}, s32[64]{0:T(128)}, u32[]{:S(2)}) copy-start(s32[64]{0:T(128)} %param.16) | copy-start | bytes 772
  288.3 9.3 %collective-permute-start.16 = (bf16[128,1024]{1,0:T(8,128)(2,1)S(1)}, bf16[128,1024]{1,0:T(8,128)(2,1)S(1)}, u32[]{:S(2)}, u32[]{:S(2)}) collective-permute-start(bf16[128,1024]{1,0:T(8,128)(2,1)S(1)} %get-tuple-element.17), channel_id=1, source_target_pairs={{0,32},{32,64},{64,96},{96,0},{1,33},{33,65},{65,97},{97,1},{2,34}... | collective-permute-start | bytes 786440 | tf_op jit(solution)/shard_map/ppermute | solution.py:188
  290.0 13.1 %collective-permute-start.17 = (bf16[128,1024]{1,0:T(8,128)(2,1)S(1)}, bf16[128,1024]{1,0:T(8,128)(2,1)S(1)}, u32[]{:S(2)}, u32[]{:S(2)}) collective-permute-start(bf16[128,1024]{1,0:T(8,128)(2,1)S(1)} %get-tuple-element.19), channel_id=1, source_target_pairs={{0,64},{32,96},{64,0},{96,32},{1,65},{33,97},{65,1},{97,33},{2,66}... | collective-permute-start | bytes 786440 | tf_op jit(solution)/shard_map/ppermute | solution.py:188
  292.8 10.2 %collective-permute-start.18 = (bf16[128,1024]{1,0:T(8,128)(2,1)S(1)}, bf16[128,1024]{1,0:T(8,128)(2,1)}, u32[]{:S(2)}, u32[]{:S(2)}) collective-permute-start(bf16[128,1024]{1,0:T(8,128)(2,1)S(1)} %get-tuple-element.18), channel_id=1, source_target_pairs={{0,96},{32,0},{64,32},{96,64},{1,97},{33,1},{65,33},{97,65},{2,98}... | collective-permute-start | bytes 786440 | tf_op jit(solution)/shard_map/ppermute | solution.py:188
Sparse Core Ops, SparseCore 0:
  9.6 55.1 all-gather.1
  165.6 116.3 reduce-scatter.1

commit v13 on v11

--- a/solution.py
+++ b/solution.py
@@ -257,6 +257,9 @@
         preferred_element_type=jnp.float32,
     )
     far_scale = jnp.exp(own_far_max - top)
+    near_context, near_total, far_scale = lax.optimization_barrier(
+        (near_context, near_total, far_scale)
+    )
     context = far_context * far_scale[..., None] + near_context
     denominator = far_total * far_scale + near_total
     attention = (context / denominator[..., None]).reshape(tok_dev, q_cols).astype(jnp.bfloat16)

time: 310 us -> 310 us (level)
  transfers between devices with their start and end apart: 21 -> 21, of which waited for: 15 -> 16; matrix products, arithmetic and copies ran while one was open for 5% -> 5% of each run, Pallas kernels for 0% -> 0%
where the time goes in v13:
time: 310 us; the launch traced here: 309 us
  waiting for transfers between devices  160 us (52%)
  Pallas kernels  74.6 us (24%)
  starting transfers between devices  35.6 us (11%)
  local copies, waits for them, and re-layouts  13.9 us (4%)
  between operations  13.7 us (4%)
  other arithmetic  5.52 us (2%)
  matrix products  5.35 us (2%)
    reduce_scatter x1, waiting for transfers between devices, far_part(): context = lax.psum_scatter(partial, 'blk', scatter_dimension=0, tiled=True)  84.2 us
    pallas_call x1, Pallas kernels, far_part(): pl.pallas_call(functools.partial(ctx_kernel, **kw), out_shape=(jax.ShapeD...  45.5 us
    all_gather x1, waiting for transfers between devices, far_part(): gathered = lax.all_gather(queries, 'blk', axis=0, tiled=True)  45.3 us
    pallas_call x1, Pallas kernels, far_part(): pl.pallas_call(functools.partial(max_kernel, **kw), out_shape=stat_shape,...  29.1 us
    ppermute x14, starting transfers between devices, butterfly(): lax.ppermute(x, axis, [(i, i + ((digit(i) + d) % radix - digit(i)) * stri...  24.4 us
    ppermute x14, waiting for transfers between devices, butterfly(): lax.ppermute(x, axis, [(i, i + ((digit(i) + d) % radix - digit(i)) * stri...  20.7 us
    ppermute x3, waiting for transfers between devices, column_sum(): got = lax.ppermute(sent, axis, [(i, (i + d) % n) for i in range(n)])  8.88 us
  transfers between devices with their start and end apart: 21, of which 16 were waited for; matrix products, arithmetic and copies ran while one was open for 5% of the time, Pallas kernels for 0%

profile of v13, /device:TPU:0, one launch (start us, length us, event | category | flops | bytes accessed | tf_op | source)
XLA Modules:
  0.0 308.8 jit_solution(16057691530337261646)
XLA Ops:
  9.3 1.6 gather_fusion.1
  10.9 1.6 gather_fusion
  14.0 1.5 gather_fusion.2
  15.8 1.4 copy.26
  17.3 2.1 gather_fusion.3
  19.4 45.3 %all-gather.2.cloned.1.call-done.q_ref = bf16[4096,1024]{1,0:T(8,128)(2,1)} async-done(((bf16[128,1024]{1,0:T(8,128)(2,1)}), bf16[4096,1024]{1,0:T(8,128)(2,1)}) %all-gather.2.cloned.1.call-update) | async-done | bytes 8388624 | tf_op jit(solution)/shard_map/all_gather | solution.py:142
  64.8 29.1 %shard_map.91 = f32[256,128]{1,0:T(8,128)} custom-call(s32[160]{0:T(256)} %select_n.90.lo_ref, s32[160]{0:T(256)} %select_n.92.hi_ref, s32[160]{0:T(256)} %gather_fusion.3, bf16[4096,1024]{1,0:T(8,128)(2,1)} %all-gather.2.cloned.1.call-done.q_ref, bf16[16,256,128]{2,1,0:T(8,128)(2,1)} %bitcast.42), custom_call_target="tpu_custom_call" | custom-call | tf_op jit(solution)/shard_map/pallas_call | solution.py:152
  96.4 1.5 collective-permute-start.1
  97.9 2.7 collective-permute-start.2
  100.6 1.5 collective-permute-start.3
  103.3 3.7 %collective-permute-done.2 = f32[256,128]{1,0:T(8,128)S(1)} collective-permute-done((f32[256,128]{1,0:T(8,128)S(1)}, f32[256,128]{1,0:T(8,128)S(1)}, u32[]{:S(2)}, u32[]{:S(2)}) %collective-permute-start.2) | collective-permute-done | bytes 131104 | tf_op jit(solution)/shard_map/ppermute | solution.py:125
  108.1 2.7 collective-permute-start.5
  110.8 1.4 collective-permute-start.6
  112.2 2.5 collective-permute-done.4
  114.7 1.4 collective-permute-done.5
  117.2 45.5 %shard_map.92 = (f32[4096,1024]{1,0:T(8,128)}, f32[256,128]{1,0:T(8,128)}) custom-call(s32[160]{0:T(256)} %select_n.90.lo_ref, s32[160]{0:T(256)} %select_n.92.hi_ref, s32[160]{0:T(256)} %gather_fusion.3, bf16[4096,1024]{1,0:T(8,128)(2,1)} %all-gather.2.cloned.1.call-done.q_ref, bf16[16,256,128]{2,1,0:T(8,128)(2,1)} %bitcast.43, ...), custom_call_target="tpu_custom_call" | custom-call | tf_op jit(solution)/shard_map/pallas_call | solution.py:160
  165.0 4.0 %collective-permute-start.7 = (bf16[128,256]{1,0:T(8,128)(2,1)S(1)}, bf16[128,256]{1,0:T(8,128)(2,1)S(1)}, u32[]{:S(2)}, u32[]{:S(2)}) collective-permute-start(bf16[128,256]{1,0:T(8,128)(2,1)S(1)} %copy-done.5), channel_id=1, source_target_pairs={{0,1},{1,2},{2,3},{3,4},{4,5},{5,6},{6,7},{7,8},{8,9},{9,10},{10,1... | collective-permute-start | bytes 196616 | tf_op jit(solution)/shard_map/ppermute | solution.py:19
  171.9 2.7 collective-permute-start.10
  174.7 3.1 %collective-permute-start.11 = (f32[256,128]{1,0:T(8,128)S(1)}, f32[256,128]{1,0:T(8,128)S(1)}, u32[]{:S(2)}, u32[]{:S(2)}) collective-permute-start(f32[256,128]{1,0:T(8,128)S(1)} %add.182), channel_id=1, source_target_pairs={{0,4},{1,5},{2,6},{3,7},{4,0},{5,1},{6,2},{7,3},{8,12},{9,13},{10,... | collective-permute-start | bytes 393224 | tf_op jit(solution)/shard_map/ppermute | solution.py:125
  178.8 1.4 collective-permute-done.10
  180.2 4.0 %collective-permute-done.11 = f32[256,128]{1,0:T(8,128)S(1)} collective-permute-done((f32[256,128]{1,0:T(8,128)S(1)}, f32[256,128]{1,0:T(8,128)S(1)}, u32[]{:S(2)}, u32[]{:S(2)}) %collective-permute-start.11) | collective-permute-done | bytes 131104 | tf_op jit(solution)/shard_map/ppermute | solution.py:125
  184.2 3.0 collective-permute-start.13
  187.2 2.6 collective-permute-start.14
  190.6 1.7 collective-permute-done.13
  192.3 2.7 collective-permute-done.14
  195.1 84.2 %reduce-scatter.2.cloned.1.call-done = f32[128,1024]{1,0:T(8,128)} async-done(((f32[4096,1024]{1,0:T(8,128)}), f32[128,1024]{1,0:T(8,128)}) %reduce-scatter.2.cloned.1.call-update) | async-done | bytes 524304 | tf_op jit(solution)/shard_map/reduce_scatter | solution.py:170
  280.6 4.7 %fusion.10 = f32[128,4096]{1,0:T(8,128)S(1)} fusion(bf16[128,1024]{0,1:T(8,128)(2,1)S(1)} %bitcast.45, bf16[1024,4096]{1,0:T(8,128)(2,1)} %param.17), kind=kOutput, calls=%fused_computation.49 | convolution fusion | flops 1073741824 | bytes 10747904 | tf_op jit(solution)/shard_map/dot_general | solution.py:266
  285.4 1.6 collective-permute-start.16
  287.0 2.9 collective-permute-start.17
  291.2 3.5 %collective-permute-done.16 = bf16[128,1024]{1,0:T(8,128)(2,1)S(1)} collective-permute-done((bf16[128,1024]{1,0:T(8,128)(2,1)S(1)}, bf16[128,1024]{1,0:T(8,128)(2,1)S(1)}, u32[]{:S(2)}, u32[]{:S(2)}) %collective-permute-start.16) | collective-permute-done | bytes 262176 | tf_op jit(solution)/shard_map/ppermute | solution.py:186
  294.7 5.4 %collective-permute-done.17 = bf16[128,1024]{1,0:T(8,128)(2,1)S(1)} collective-permute-done((bf16[128,1024]{1,0:T(8,128)(2,1)S(1)}, bf16[128,1024]{1,0:T(8,128)(2,1)S(1)}, u32[]{:S(2)}, u32[]{:S(2)}) %collective-permute-start.17) | collective-permute-done | bytes 262176 | tf_op jit(solution)/shard_map/ppermute | solution.py:186
  300.1 1.8 add_convert_fusion
  (80 shorter events, 20.1 us)
Async XLA Ops:
  6.5 7.5 %copy-start = (s32[64]{0:T(128)S(1)}, s32[64]{0:T(128)}, u32[]{:S(2)}) copy-start(s32[64]{0:T(128)} %param.16) | copy-start | bytes 772
  6.5 58.2 %all-gather.2.cloned.1.call-start = ((), (), s32[]{:S(2)}) async-start(), calls=%async_computation.1 | async-start | bytes 8650752 | tf_op jit(solution)/shard_map/all_gather | solution.py:142
  7.3 272.0 %reduce-scatter.2.cloned.1.call-start = ((), (), s32[]{:S(2)}) async-start(), calls=%async_computation.2 | async-start | bytes 17301504 | tf_op jit(solution)/shard_map/reduce_scatter | solution.py:170
  14.0 1.8 copy-start.1
  14.0 3.2 %copy-start.6 = (s32[16]{0:T(128)S(1)}, s32[16]{0:T(128)}, u32[]{:S(2)}) copy-start(s32[16]{0:T(128)} %param.14) | copy-start | bytes 196
  93.9 1.6 collective-permute-start
  96.4 6.9 %collective-permute-start.1 = (f32[256,128]{1,0:T(8,128)S(1)}, f32[256,128]{1,0:T(8,128)S(1)}, u32[]{:S(2)}, u32[]{:S(2)}) collective-permute-start(f32[256,128]{1,0:T(8,128)S(1)} %max.28), channel_id=1, source_target_pairs={{0,2},{1,3},{2,4},{3,5},{4,6},{5,7},{6,0},{7,1},{8,10},{9,11},{10,... | collective-permute-start | bytes 393224 | tf_op jit(solution)/shard_map/ppermute | solution.py:125
  97.9 9.1 %collective-permute-start.2 = (f32[256,128]{1,0:T(8,128)S(1)}, f32[256,128]{1,0:T(8,128)S(1)}, u32[]{:S(2)}, u32[]{:S(2)}) collective-permute-start(f32[256,128]{1,0:T(8,128)S(1)} %max.28), channel_id=1, source_target_pairs={{0,4},{1,5},{2,6},{3,7},{4,0},{5,1},{6,2},{7,3},{8,12},{9,13},{10,... | collective-permute-start | bytes 393224 | tf_op jit(solution)/shard_map/ppermute | solution.py:125
  100.6 6.4 %collective-permute-start.3 = (f32[256,128]{1,0:T(8,128)S(1)}, f32[256,128]{1,0:T(8,128)S(1)}, u32[]{:S(2)}, u32[]{:S(2)}) collective-permute-start(f32[256,128]{1,0:T(8,128)S(1)} %max.28), channel_id=1, source_target_pairs={{0,6},{1,7},{2,0},{3,1},{4,2},{5,3},{6,4},{7,5},{8,14},{9,15},{10,... | collective-permute-start | bytes 393224 | tf_op jit(solution)/shard_map/ppermute | solution.py:125
  107.1 7.6 %collective-permute-start.4 = (f32[256,128]{1,0:T(8,128)S(1)}, f32[256,128]{1,0:T(8,128)S(1)}, u32[]{:S(2)}, u32[]{:S(2)}) collective-permute-start(f32[256,128]{1,0:T(8,128)S(1)} %maximum_maximum_fusion.1), channel_id=1, source_target_pairs={{0,8},{1,9},{2,10},{3,11},{4,12},{5,13},{6,14},{7,15},{8,16},{9,17... | collective-permute-start | bytes 393224 | tf_op jit(solution)/shard_map/ppermute | solution.py:125
  108.1 8.0 %collective-permute-start.5 = (f32[256,128]{1,0:T(8,128)S(1)}, f32[256,128]{1,0:T(8,128)S(1)}, u32[]{:S(2)}, u32[]{:S(2)}) collective-permute-start(f32[256,128]{1,0:T(8,128)S(1)} %maximum_maximum_fusion.1), channel_id=1, source_target_pairs={{0,16},{1,17},{2,18},{3,19},{4,20},{5,21},{6,22},{7,23},{8,24},{9,... | collective-permute-start | bytes 393224 | tf_op jit(solution)/shard_map/ppermute | solution.py:125
  110.8 5.7 %collective-permute-start.6 = (f32[256,128]{1,0:T(8,128)S(1)}, f32[256,128]{1,0:T(8,128)S(1)}, u32[]{:S(2)}, u32[]{:S(2)}) collective-permute-start(f32[256,128]{1,0:T(8,128)S(1)} %maximum_maximum_fusion.1), channel_id=1, source_target_pairs={{0,24},{1,25},{2,26},{3,27},{4,28},{5,29},{6,30},{7,31},{8,0},{9,1... | collective-permute-start | bytes 393224 | tf_op jit(solution)/shard_map/ppermute | solution.py:125
  162.7 0.8 copy-start.4
  162.7 2.3 copy-start.5
  162.7 6.7 %copy-start.2 = (bf16[128,1024]{1,0:T(8,128)(2,1)S(1)}, bf16[128,1024]{1,0:T(8,128)(2,1)}, u32[]{:S(2)}) copy-start(bf16[128,1024]{1,0:T(8,128)(2,1)} %param.9) | copy-start | bytes 786436
  162.7 7.7 %copy-start.3 = (f32[256,128]{1,0:T(8,128)S(1)}, f32[256,128]{1,0:T(8,128)}, u32[]{:S(2)}) copy-start(f32[256,128]{1,0:T(8,128)} %get-tuple-element.13) | copy-start | bytes 393220
  163.6 6.4 %collective-permute-start.8 = (bf16[128,256]{0,1:T(8,128)(2,1)S(1)}, bf16[128,256]{0,1:T(8,128)(2,1)S(1)}, u32[]{:S(2)}, u32[]{:S(2)}) collective-permute-start(bf16[128,256]{0,1:T(8,128)(2,1)S(1)} %copy.28), channel_id=1, source_target_pairs={{0,1},{1,2},{2,3},{3,4},{4,5},{5,6},{6,7},{7,8},{8,9},{9,10},{10,1... | collective-permute-start | bytes 196616 | tf_op jit(solution)/shard_map/ppermute | solution.py:19
  165.0 4.9 %collective-permute-start.7 = (bf16[128,256]{1,0:T(8,128)(2,1)S(1)}, bf16[128,256]{1,0:T(8,128)(2,1)S(1)}, u32[]{:S(2)}, u32[]{:S(2)}) collective-permute-start(bf16[128,256]{1,0:T(8,128)(2,1)S(1)} %copy-done.5), channel_id=1, source_target_pairs={{0,1},{1,2},{2,3},{3,4},{4,5},{5,6},{6,7},{7,8},{8,9},{9,10},{10,1... | collective-permute-start | bytes 196616 | tf_op jit(solution)/shard_map/ppermute | solution.py:19
  170.4 1.5 collective-permute-start.9
  171.9 8.2 %collective-permute-start.10 = (f32[256,128]{1,0:T(8,128)S(1)}, f32[256,128]{1,0:T(8,128)S(1)}, u32[]{:S(2)}, u32[]{:S(2)}) collective-permute-start(f32[256,128]{1,0:T(8,128)S(1)} %add.182), channel_id=1, source_target_pairs={{0,2},{1,3},{2,4},{3,5},{4,6},{5,7},{6,0},{7,1},{8,10},{9,11},{10,... | collective-permute-start | bytes 393224 | tf_op jit(solution)/shard_map/ppermute | solution.py:125
  174.7 9.5 %collective-permute-start.11 = (f32[256,128]{1,0:T(8,128)S(1)}, f32[256,128]{1,0:T(8,128)S(1)}, u32[]{:S(2)}, u32[]{:S(2)}) collective-permute-start(f32[256,128]{1,0:T(8,128)S(1)} %add.182), channel_id=1, source_target_pairs={{0,4},{1,5},{2,6},{3,7},{4,0},{5,1},{6,2},{7,3},{8,12},{9,13},{10,... | collective-permute-start | bytes 393224 | tf_op jit(solution)/shard_map/ppermute | solution.py:125
  177.8 6.3 %collective-permute-start.12 = (f32[256,128]{1,0:T(8,128)S(1)}, f32[256,128]{1,0:T(8,128)S(1)}, u32[]{:S(2)}, u32[]{:S(2)}) collective-permute-start(f32[256,128]{1,0:T(8,128)S(1)} %add.182), channel_id=1, source_target_pairs={{0,6},{1,7},{2,0},{3,1},{4,2},{5,3},{6,4},{7,5},{8,14},{9,15},{10,... | collective-permute-start | bytes 393224 | tf_op jit(solution)/shard_map/ppermute | solution.py:125
  184.2 8.1 %collective-permute-start.13 = (f32[256,128]{1,0:T(8,128)S(1)}, f32[256,128]{1,0:T(8,128)S(1)}, u32[]{:S(2)}, u32[]{:S(2)}) collective-permute-start(f32[256,128]{1,0:T(8,128)S(1)} %add_add_fusion), channel_id=1, source_target_pairs={{0,8},{1,9},{2,10},{3,11},{4,12},{5,13},{6,14},{7,15},{8,16},{9,17... | collective-permute-start | bytes 393224 | tf_op jit(solution)/shard_map/ppermute | solution.py:125
  187.2 7.9 %collective-permute-start.14 = (f32[256,128]{1,0:T(8,128)S(1)}, f32[256,128]{1,0:T(8,128)S(1)}, u32[]{:S(2)}, u32[]{:S(2)}) collective-permute-start(f32[256,128]{1,0:T(8,128)S(1)} %add_add_fusion), channel_id=1, source_target_pairs={{0,16},{1,17},{2,18},{3,19},{4,20},{5,21},{6,22},{7,23},{8,24},{9,... | collective-permute-start | bytes 393224 | tf_op jit(solution)/shard_map/ppermute | solution.py:125
  189.8 5.2 %collective-permute-start.15 = (f32[256,128]{1,0:T(8,128)S(1)}, f32[256,128]{1,0:T(8,128)S(1)}, u32[]{:S(2)}, u32[]{:S(2)}) collective-permute-start(f32[256,128]{1,0:T(8,128)S(1)} %add_add_fusion), channel_id=1, source_target_pairs={{0,24},{1,25},{2,26},{3,27},{4,28},{5,29},{6,30},{7,31},{8,0},{9,1... | collective-permute-start | bytes 393224 | tf_op jit(solution)/shard_map/ppermute | solution.py:125
  285.4 9.3 %collective-permute-start.16 = (bf16[128,1024]{1,0:T(8,128)(2,1)S(1)}, bf16[128,1024]{1,0:T(8,128)(2,1)S(1)}, u32[]{:S(2)}, u32[]{:S(2)}) collective-permute-start(bf16[128,1024]{1,0:T(8,128)(2,1)S(1)} %get-tuple-element.19), channel_id=1, source_target_pairs={{0,32},{32,64},{64,96},{96,0},{1,33},{33,65},{65,97},{97,1},{2,34}... | collective-permute-start | bytes 786440 | tf_op jit(solution)/shard_map/ppermute | solution.py:186
  287.0 13.1 %collective-permute-start.17 = (bf16[128,1024]{1,0:T(8,128)(2,1)S(1)}, bf16[128,1024]{1,0:T(8,128)(2,1)S(1)}, u32[]{:S(2)}, u32[]{:S(2)}) collective-permute-start(bf16[128,1024]{1,0:T(8,128)(2,1)S(1)} %get-tuple-element.21), channel_id=1, source_target_pairs={{0,64},{32,96},{64,0},{96,32},{1,65},{33,97},{65,1},{97,33},{2,66}... | collective-permute-start | bytes 786440 | tf_op jit(solution)/shard_map/ppermute | solution.py:186
  289.9 10.2 %collective-permute-start.18 = (bf16[128,1024]{1,0:T(8,128)(2,1)S(1)}, bf16[128,1024]{1,0:T(8,128)(2,1)}, u32[]{:S(2)}, u32[]{:S(2)}) collective-permute-start(bf16[128,1024]{1,0:T(8,128)(2,1)S(1)} %get-tuple-element.20), channel_id=1, source_target_pairs={{0,96},{32,0},{64,32},{96,64},{1,97},{33,1},{65,33},{97,65},{2,98}... | collective-permute-start | bytes 786440 | tf_op jit(solution)/shard_map/ppermute | solution.py:186
Sparse Core Ops, SparseCore 0:
  9.6 55.1 all-gather.1
  162.9 116.3 reduce-scatter.1

commit v14 on v13

--- a/solution.py
+++ b/solution.py
@@ -167,7 +167,9 @@
             out_specs=(pl.BlockSpec((tok_dev, q_cols), lambda i, *_: (i, 0)), s_spec),
         ),
     )(lo, hi, blk, gathered, keys_t, values, far_max)
-    context = lax.psum_scatter(partial, "blk", scatter_dimension=0, tiled=True)
+    context = lax.psum_scatter(
+        partial.astype(jnp.bfloat16), "blk", scatter_dimension=0, tiled=True
+    ).astype(jnp.float32)
     totals = butterfly(totals, "blk", jnp.add)
     own = lambda a: jnp.transpose(
         lax.dynamic_slice_in_dim(a, blk_index * stat_rows, stat_rows, 0)[:heads]

time: 310 us -> 296 us (0.955)
  waiting for transfers between devices: 160 us -> 137 us
  other arithmetic: 5.52 us -> 14.6 us
    reduce_scatter x1, waiting for transfers between devices: 84.2 us -> 61.5 us  [far_part(): lax.psum_scatter(partial.astype(jnp.bfloat16), 'blk', scatter_dimension=0...]
    convert_element_type x0 -> x1, other arithmetic: none -> 9.1 us  [far_part(): partial.astype(jnp.bfloat16)]
where the time goes in v14:
time: 296 us; the launch traced here: 295 us
  waiting for transfers between devices  137 us (46%)
  Pallas kernels  74.6 us (25%)
  starting transfers between devices  35.6 us (12%)
  other arithmetic  14.6 us (5%)
  local copies, waits for them, and re-layouts  13.8 us (5%)
  between operations  13.7 us (5%)
  matrix products  5.36 us (2%)
    reduce_scatter x1, waiting for transfers between devices, far_part(): lax.psum_scatter(partial.astype(jnp.bfloat16), 'blk', scatter_dimension=0...  61.5 us
    pallas_call x1, Pallas kernels, far_part(): pl.pallas_call(functools.partial(ctx_kernel, **kw), out_shape=(jax.ShapeD...  45.5 us
    all_gather x1, waiting for transfers between devices, far_part(): gathered = lax.all_gather(queries, 'blk', axis=0, tiled=True)  45.3 us
    pallas_call x1, Pallas kernels, far_part(): pl.pallas_call(functools.partial(max_kernel, **kw), out_shape=stat_shape,...  29.1 us
    ppermute x14, starting transfers between devices, butterfly(): lax.ppermute(x, axis, [(i, i + ((digit(i) + d) % radix - digit(i)) * stri...  24.4 us
    ppermute x14, waiting for transfers between devices, butterfly(): lax.ppermute(x, axis, [(i, i + ((digit(i) + d) % radix - digit(i)) * stri...  20.7 us
    convert_element_type x1, other arithmetic, far_part(): partial.astype(jnp.bfloat16)  9.1 us
    ppermute x3, waiting for transfers between devices, column_sum(): got = lax.ppermute(sent, axis, [(i, (i + d) % n) for i in range(n)])  8.46 us
  transfers between devices with their start and end apart: 21, of which 16 were waited for; matrix products, arithmetic and copies ran while one was open for 5% of the time, Pallas kernels for 0%

profile of v14, /device:TPU:0, one launch (start us, length us, event | category | flops | bytes accessed | tf_op | source)
XLA Modules:
  0.0 294.7 jit_solution(16787721994210042884)
XLA Ops:
  9.3 1.6 gather_fusion.1
  10.9 1.6 gather_fusion
  14.0 1.5 gather_fusion.2
  17.3 2.1 gather_fusion.3
  19.4 45.3 %all-gather.2.cloned.1.call-done.q_ref = bf16[4096,1024]{1,0:T(8,128)(2,1)} async-done(((bf16[128,1024]{1,0:T(8,128)(2,1)}), bf16[4096,1024]{1,0:T(8,128)(2,1)}) %all-gather.2.cloned.1.call-update) | async-done | bytes 8388624 | tf_op jit(solution)/shard_map/all_gather | solution.py:142
  64.8 29.1 %shard_map.91 = f32[256,128]{1,0:T(8,128)} custom-call(s32[160]{0:T(256)} %select_n.90.lo_ref, s32[160]{0:T(256)} %select_n.92.hi_ref, s32[160]{0:T(256)} %gather_fusion.3, bf16[4096,1024]{1,0:T(8,128)(2,1)} %all-gather.2.cloned.1.call-done.q_ref, bf16[16,256,128]{2,1,0:T(8,128)(2,1)} %bitcast.42), custom_call_target="tpu_custom_call" | custom-call | tf_op jit(solution)/shard_map/pallas_call | solution.py:152
  96.4 1.5 collective-permute-start.1
  97.9 2.7 collective-permute-start.2
  100.6 1.5 collective-permute-start.3
  103.3 3.7 %collective-permute-done.2 = f32[256,128]{1,0:T(8,128)S(1)} collective-permute-done((f32[256,128]{1,0:T(8,128)S(1)}, f32[256,128]{1,0:T(8,128)S(1)}, u32[]{:S(2)}, u32[]{:S(2)}) %collective-permute-start.2) | collective-permute-done | bytes 131104 | tf_op jit(solution)/shard_map/ppermute | solution.py:125
  108.1 2.7 collective-permute-start.5
  110.8 1.4 collective-permute-start.6
  112.2 2.5 collective-permute-done.4
  114.7 1.4 collective-permute-done.5
  117.2 45.5 %shard_map.92 = (f32[4096,1024]{1,0:T(8,128)}, f32[256,128]{1,0:T(8,128)}) custom-call(s32[160]{0:T(256)} %select_n.90.lo_ref, s32[160]{0:T(256)} %select_n.92.hi_ref, s32[160]{0:T(256)} %gather_fusion.3, bf16[4096,1024]{1,0:T(8,128)(2,1)} %all-gather.2.cloned.1.call-done.q_ref, bf16[16,256,128]{2,1,0:T(8,128)(2,1)} %bitcast.43, ...), custom_call_target="tpu_custom_call" | custom-call | tf_op jit(solution)/shard_map/pallas_call | solution.py:160
  162.7 9.1 %convert_element_type.42 = bf16[4096,1024]{1,0:T(8,128)(2,1)} convert(f32[4096,1024]{1,0:T(8,128)} %get-tuple-element.10) | non-fusion elementwise | flops 4194304 | bytes 25165824 | tf_op jit(solution)/shard_map/convert_element_type | solution.py:171
  174.1 4.0 %collective-permute-start.7 = (bf16[128,256]{1,0:T(8,128)(2,1)S(1)}, bf16[128,256]{1,0:T(8,128)(2,1)S(1)}, u32[]{:S(2)}, u32[]{:S(2)}) collective-permute-start(bf16[128,256]{1,0:T(8,128)(2,1)S(1)} %copy-done.5), channel_id=1, source_target_pairs={{0,1},{1,2},{2,3},{3,4},{4,5},{5,6},{6,7},{7,8},{8,9},{9,10},{10,1... | collective-permute-start | bytes 196616 | tf_op jit(solution)/shard_map/ppermute | solution.py:19
  181.0 2.7 collective-permute-start.10
  183.7 3.2 %collective-permute-start.11 = (f32[256,128]{1,0:T(8,128)S(1)}, f32[256,128]{1,0:T(8,128)S(1)}, u32[]{:S(2)}, u32[]{:S(2)}) collective-permute-start(f32[256,128]{1,0:T(8,128)S(1)} %add.182), channel_id=1, source_target_pairs={{0,4},{1,5},{2,6},{3,7},{4,0},{5,1},{6,2},{7,3},{8,12},{9,13},{10,... | collective-permute-start | bytes 393224 | tf_op jit(solution)/shard_map/ppermute | solution.py:125
  187.8 1.4 collective-permute-done.10
  189.3 4.0 %collective-permute-done.11 = f32[256,128]{1,0:T(8,128)S(1)} collective-permute-done((f32[256,128]{1,0:T(8,128)S(1)}, f32[256,128]{1,0:T(8,128)S(1)}, u32[]{:S(2)}, u32[]{:S(2)}) %collective-permute-start.11) | collective-permute-done | bytes 131104 | tf_op jit(solution)/shard_map/ppermute | solution.py:125
  193.3 3.0 %collective-permute-start.13 = (f32[256,128]{1,0:T(8,128)S(1)}, f32[256,128]{1,0:T(8,128)S(1)}, u32[]{:S(2)}, u32[]{:S(2)}) collective-permute-start(f32[256,128]{1,0:T(8,128)S(1)} %add_add_fusion), channel_id=1, source_target_pairs={{0,8},{1,9},{2,10},{3,11},{4,12},{5,13},{6,14},{7,15},{8,16},{9,17... | collective-permute-start | bytes 393224 | tf_op jit(solution)/shard_map/ppermute | solution.py:125
  196.3 2.6 collective-permute-start.14
  199.8 1.7 collective-permute-done.13
  201.4 2.7 collective-permute-done.14
  204.2 61.5 %reduce-scatter.2.cloned.1.call-done = bf16[128,1024]{1,0:T(8,128)(2,1)} async-done(((bf16[4096,1024]{1,0:T(8,128)(2,1)}), bf16[128,1024]{1,0:T(8,128)(2,1)}) %reduce-scatter.2.cloned.1.call-update) | async-done | bytes 262160 | tf_op jit(solution)/shard_map/reduce_scatter | solution.py:170
  266.9 4.7 %fusion.10 = f32[128,4096]{1,0:T(8,128)S(1)} fusion(bf16[128,1024]{0,1:T(8,128)(2,1)S(1)} %bitcast.45, bf16[1024,4096]{1,0:T(8,128)(2,1)} %param.17), kind=kOutput, calls=%fused_computation.49 | convolution fusion | flops 1073741824 | bytes 10747904 | tf_op jit(solution)/shard_map/dot_general | solution.py:268
  271.7 1.6 collective-permute-start.16
  273.3 2.9 collective-permute-start.17
  277.5 3.7 %collective-permute-done.16 = bf16[128,1024]{1,0:T(8,128)(2,1)S(1)} collective-permute-done((bf16[128,1024]{1,0:T(8,128)(2,1)S(1)}, bf16[128,1024]{1,0:T(8,128)(2,1)S(1)}, u32[]{:S(2)}, u32[]{:S(2)}) %collective-permute-start.16) | collective-permute-done | bytes 262176 | tf_op jit(solution)/shard_map/ppermute | solution.py:188
  281.2 4.8 %collective-permute-done.17 = bf16[128,1024]{1,0:T(8,128)(2,1)S(1)} collective-permute-done((bf16[128,1024]{1,0:T(8,128)(2,1)S(1)}, bf16[128,1024]{1,0:T(8,128)(2,1)S(1)}, u32[]{:S(2)}, u32[]{:S(2)}) %collective-permute-start.17) | collective-permute-done | bytes 262176 | tf_op jit(solution)/shard_map/ppermute | solution.py:188
  286.0 1.8 add_convert_fusion
  (81 shorter events, 21.4 us)
Async XLA Ops:
  6.5 7.5 %copy-start = (s32[64]{0:T(128)S(1)}, s32[64]{0:T(128)}, u32[]{:S(2)}) copy-start(s32[64]{0:T(128)} %param.16) | copy-start | bytes 772
  6.5 58.2 %all-gather.2.cloned.1.call-start = ((), (), s32[]{:S(2)}) async-start(), calls=%async_computation.1 | async-start | bytes 8650752 | tf_op jit(solution)/shard_map/all_gather | solution.py:142
  7.3 258.4 %reduce-scatter.2.cloned.1.call-start = ((), (), s32[]{:S(2)}) async-start(), calls=%async_computation.2 | async-start | bytes 8650752 | tf_op jit(solution)/shard_map/reduce_scatter | solution.py:170
  14.0 1.8 copy-start.1
  14.0 3.2 %copy-start.6 = (s32[16]{0:T(128)S(1)}, s32[16]{0:T(128)}, u32[]{:S(2)}) copy-start(s32[16]{0:T(128)} %param.14) | copy-start | bytes 196
  93.9 1.6 collective-permute-start
  96.4 6.9 %collective-permute-start.1 = (f32[256,128]{1,0:T(8,128)S(1)}, f32[256,128]{1,0:T(8,128)S(1)}, u32[]{:S(2)}, u32[]{:S(2)}) collective-permute-start(f32[256,128]{1,0:T(8,128)S(1)} %max.28), channel_id=1, source_target_pairs={{0,2},{1,3},{2,4},{3,5},{4,6},{5,7},{6,0},{7,1},{8,10},{9,11},{10,... | collective-permute-start | bytes 393224 | tf_op jit(solution)/shard_map/ppermute | solution.py:125
  97.9 9.1 %collective-permute-start.2 = (f32[256,128]{1,0:T(8,128)S(1)}, f32[256,128]{1,0:T(8,128)S(1)}, u32[]{:S(2)}, u32[]{:S(2)}) collective-permute-start(f32[256,128]{1,0:T(8,128)S(1)} %max.28), channel_id=1, source_target_pairs={{0,4},{1,5},{2,6},{3,7},{4,0},{5,1},{6,2},{7,3},{8,12},{9,13},{10,... | collective-permute-start | bytes 393224 | tf_op jit(solution)/shard_map/ppermute | solution.py:125
  100.6 6.4 %collective-permute-start.3 = (f32[256,128]{1,0:T(8,128)S(1)}, f32[256,128]{1,0:T(8,128)S(1)}, u32[]{:S(2)}, u32[]{:S(2)}) collective-permute-start(f32[256,128]{1,0:T(8,128)S(1)} %max.28), channel_id=1, source_target_pairs={{0,6},{1,7},{2,0},{3,1},{4,2},{5,3},{6,4},{7,5},{8,14},{9,15},{10,... | collective-permute-start | bytes 393224 | tf_op jit(solution)/shard_map/ppermute | solution.py:125
  107.1 7.6 %collective-permute-start.4 = (f32[256,128]{1,0:T(8,128)S(1)}, f32[256,128]{1,0:T(8,128)S(1)}, u32[]{:S(2)}, u32[]{:S(2)}) collective-permute-start(f32[256,128]{1,0:T(8,128)S(1)} %maximum_maximum_fusion.1), channel_id=1, source_target_pairs={{0,8},{1,9},{2,10},{3,11},{4,12},{5,13},{6,14},{7,15},{8,16},{9,17... | collective-permute-start | bytes 393224 | tf_op jit(solution)/shard_map/ppermute | solution.py:125
  108.1 8.0 %collective-permute-start.5 = (f32[256,128]{1,0:T(8,128)S(1)}, f32[256,128]{1,0:T(8,128)S(1)}, u32[]{:S(2)}, u32[]{:S(2)}) collective-permute-start(f32[256,128]{1,0:T(8,128)S(1)} %maximum_maximum_fusion.1), channel_id=1, source_target_pairs={{0,16},{1,17},{2,18},{3,19},{4,20},{5,21},{6,22},{7,23},{8,24},{9,... | collective-permute-start | bytes 393224 | tf_op jit(solution)/shard_map/ppermute | solution.py:125
  110.8 5.7 %collective-permute-start.6 = (f32[256,128]{1,0:T(8,128)S(1)}, f32[256,128]{1,0:T(8,128)S(1)}, u32[]{:S(2)}, u32[]{:S(2)}) collective-permute-start(f32[256,128]{1,0:T(8,128)S(1)} %maximum_maximum_fusion.1), channel_id=1, source_target_pairs={{0,24},{1,25},{2,26},{3,27},{4,28},{5,29},{6,30},{7,31},{8,0},{9,1... | collective-permute-start | bytes 393224 | tf_op jit(solution)/shard_map/ppermute | solution.py:125
  171.8 0.8 copy-start.4
  171.8 2.3 copy-start.5
  171.8 6.7 %copy-start.2 = (bf16[128,1024]{1,0:T(8,128)(2,1)S(1)}, bf16[128,1024]{1,0:T(8,128)(2,1)}, u32[]{:S(2)}) copy-start(bf16[128,1024]{1,0:T(8,128)(2,1)} %param.9) | copy-start | bytes 786436
  171.8 7.7 %copy-start.3 = (f32[256,128]{1,0:T(8,128)S(1)}, f32[256,128]{1,0:T(8,128)}, u32[]{:S(2)}) copy-start(f32[256,128]{1,0:T(8,128)} %get-tuple-element.13) | copy-start | bytes 393220
  172.7 6.4 %collective-permute-start.8 = (bf16[128,256]{0,1:T(8,128)(2,1)S(1)}, bf16[128,256]{0,1:T(8,128)(2,1)S(1)}, u32[]{:S(2)}, u32[]{:S(2)}) collective-permute-start(bf16[128,256]{0,1:T(8,128)(2,1)S(1)} %copy.28), channel_id=1, source_target_pairs={{0,1},{1,2},{2,3},{3,4},{4,5},{5,6},{6,7},{7,8},{8,9},{9,10},{10,1... | collective-permute-start | bytes 196616 | tf_op jit(solution)/shard_map/ppermute | solution.py:19
  174.1 4.9 %collective-permute-start.7 = (bf16[128,256]{1,0:T(8,128)(2,1)S(1)}, bf16[128,256]{1,0:T(8,128)(2,1)S(1)}, u32[]{:S(2)}, u32[]{:S(2)}) collective-permute-start(bf16[128,256]{1,0:T(8,128)(2,1)S(1)} %copy-done.5), channel_id=1, source_target_pairs={{0,1},{1,2},{2,3},{3,4},{4,5},{5,6},{6,7},{7,8},{8,9},{9,10},{10,1... | collective-permute-start | bytes 196616 | tf_op jit(solution)/shard_map/ppermute | solution.py:19
  179.5 1.5 collective-permute-start.9
  181.0 8.2 %collective-permute-start.10 = (f32[256,128]{1,0:T(8,128)S(1)}, f32[256,128]{1,0:T(8,128)S(1)}, u32[]{:S(2)}, u32[]{:S(2)}) collective-permute-start(f32[256,128]{1,0:T(8,128)S(1)} %add.182), channel_id=1, source_target_pairs={{0,2},{1,3},{2,4},{3,5},{4,6},{5,7},{6,0},{7,1},{8,10},{9,11},{10,... | collective-permute-start | bytes 393224 | tf_op jit(solution)/shard_map/ppermute | solution.py:125
  183.7 9.5 %collective-permute-start.11 = (f32[256,128]{1,0:T(8,128)S(1)}, f32[256,128]{1,0:T(8,128)S(1)}, u32[]{:S(2)}, u32[]{:S(2)}) collective-permute-start(f32[256,128]{1,0:T(8,128)S(1)} %add.182), channel_id=1, source_target_pairs={{0,4},{1,5},{2,6},{3,7},{4,0},{5,1},{6,2},{7,3},{8,12},{9,13},{10,... | collective-permute-start | bytes 393224 | tf_op jit(solution)/shard_map/ppermute | solution.py:125
  186.9 6.3 %collective-permute-start.12 = (f32[256,128]{1,0:T(8,128)S(1)}, f32[256,128]{1,0:T(8,128)S(1)}, u32[]{:S(2)}, u32[]{:S(2)}) collective-permute-start(f32[256,128]{1,0:T(8,128)S(1)} %add.182), channel_id=1, source_target_pairs={{0,6},{1,7},{2,0},{3,1},{4,2},{5,3},{6,4},{7,5},{8,14},{9,15},{10,... | collective-permute-start | bytes 393224 | tf_op jit(solution)/shard_map/ppermute | solution.py:125
  193.3 8.1 %collective-permute-start.13 = (f32[256,128]{1,0:T(8,128)S(1)}, f32[256,128]{1,0:T(8,128)S(1)}, u32[]{:S(2)}, u32[]{:S(2)}) collective-permute-start(f32[256,128]{1,0:T(8,128)S(1)} %add_add_fusion), channel_id=1, source_target_pairs={{0,8},{1,9},{2,10},{3,11},{4,12},{5,13},{6,14},{7,15},{8,16},{9,17... | collective-permute-start | bytes 393224 | tf_op jit(solution)/shard_map/ppermute | solution.py:125
  196.3 7.9 %collective-permute-start.14 = (f32[256,128]{1,0:T(8,128)S(1)}, f32[256,128]{1,0:T(8,128)S(1)}, u32[]{:S(2)}, u32[]{:S(2)}) collective-permute-start(f32[256,128]{1,0:T(8,128)S(1)} %add_add_fusion), channel_id=1, source_target_pairs={{0,16},{1,17},{2,18},{3,19},{4,20},{5,21},{6,22},{7,23},{8,24},{9,... | collective-permute-start | bytes 393224 | tf_op jit(solution)/shard_map/ppermute | solution.py:125
  198.9 5.2 %collective-permute-start.15 = (f32[256,128]{1,0:T(8,128)S(1)}, f32[256,128]{1,0:T(8,128)S(1)}, u32[]{:S(2)}, u32[]{:S(2)}) collective-permute-start(f32[256,128]{1,0:T(8,128)S(1)} %add_add_fusion), channel_id=1, source_target_pairs={{0,24},{1,25},{2,26},{3,27},{4,28},{5,29},{6,30},{7,31},{8,0},{9,1... | collective-permute-start | bytes 393224 | tf_op jit(solution)/shard_map/ppermute | solution.py:125
  271.7 9.5 %collective-permute-start.16 = (bf16[128,1024]{1,0:T(8,128)(2,1)S(1)}, bf16[128,1024]{1,0:T(8,128)(2,1)S(1)}, u32[]{:S(2)}, u32[]{:S(2)}) collective-permute-start(bf16[128,1024]{1,0:T(8,128)(2,1)S(1)} %get-tuple-element.19), channel_id=1, source_target_pairs={{0,32},{32,64},{64,96},{96,0},{1,33},{33,65},{65,97},{97,1},{2,34}... | collective-permute-start | bytes 786440 | tf_op jit(solution)/shard_map/ppermute | solution.py:188
  273.3 12.7 %collective-permute-start.17 = (bf16[128,1024]{1,0:T(8,128)(2,1)S(1)}, bf16[128,1024]{1,0:T(8,128)(2,1)S(1)}, u32[]{:S(2)}, u32[]{:S(2)}) collective-permute-start(bf16[128,1024]{1,0:T(8,128)(2,1)S(1)} %get-tuple-element.21), channel_id=1, source_target_pairs={{0,64},{32,96},{64,0},{96,32},{1,65},{33,97},{65,1},{97,33},{2,66}... | collective-permute-start | bytes 786440 | tf_op jit(solution)/shard_map/ppermute | solution.py:188
  276.2 9.8 %collective-permute-start.18 = (bf16[128,1024]{1,0:T(8,128)(2,1)S(1)}, bf16[128,1024]{1,0:T(8,128)(2,1)}, u32[]{:S(2)}, u32[]{:S(2)}) collective-permute-start(bf16[128,1024]{1,0:T(8,128)(2,1)S(1)} %get-tuple-element.20), channel_id=1, source_target_pairs={{0,96},{32,0},{64,32},{96,64},{1,97},{33,1},{65,33},{97,65},{2,98}... | collective-permute-start | bytes 786440 | tf_op jit(solution)/shard_map/ppermute | solution.py:188
Sparse Core Ops, SparseCore 0:
  9.6 55.1 all-gather.1
  172.0 93.6 reduce-scatter.1

commit v15 on v14

--- a/solution.py
+++ b/solution.py
@@ -119,7 +119,7 @@
     n = lax.axis_size(axis)
     stride = 1
     while stride < n:
-        radix = 2 if stride == 1 or n % (stride * 4) else 4
+        radix = 8 if stride == 1 and n % 8 == 0 else (4 if n % (stride * 4) == 0 else 2)
         digit = lambda i: (i // stride) % radix
         got = [
             lax.ppermute(

time: 296 us -> 301 us (1.017)
  starting transfers between devices: 35.6 us -> 43.8 us
    ppermute x14 -> x20, starting transfers between devices: 24.4 us -> 33.5 us  [butterfly(): lax.ppermute(x, axis, [(i, i + ((digit(i) + d) % radix - digit(i)) * stri...]
    reduce_scatter x1, waiting for transfers between devices: 61.5 us -> 55 us  [far_part(): lax.psum_scatter(partial.astype(jnp.bfloat16), 'blk', scatter_dimension=0...]
    ppermute x14 -> x20, waiting for transfers between devices: 20.7 us -> 23.9 us  [butterfly(): lax.ppermute(x, axis, [(i, i + ((digit(i) + d) % radix - digit(i)) * stri...]
  transfers between devices with their start and end apart: 21 -> 27, of which waited for: 16 -> 19; matrix products, arithmetic and copies ran while one was open for 5% -> 5% of each run, Pallas kernels for 0% -> 0%
where the time goes in v15:
time: 301 us; the launch traced here: 300 us
  waiting for transfers between devices  134 us (45%)
  Pallas kernels  74.6 us (25%)
  starting transfers between devices  43.8 us (15%)
  other arithmetic  14.6 us (5%)
  local copies, waits for them, and re-layouts  13.8 us (5%)
  between operations  13.7 us (5%)
  matrix products  5.35 us (2%)
    reduce_scatter x1, waiting for transfers between devices, far_part(): lax.psum_scatter(partial.astype(jnp.bfloat16), 'blk', scatter_dimension=0...  55 us
    pallas_call x1, Pallas kernels, far_part(): pl.pallas_call(functools.partial(ctx_kernel, **kw), out_shape=(jax.ShapeD...  45.5 us
    all_gather x1, waiting for transfers between devices, far_part(): gathered = lax.all_gather(queries, 'blk', axis=0, tiled=True)  45.3 us
    ppermute x20, starting transfers between devices, butterfly(): lax.ppermute(x, axis, [(i, i + ((digit(i) + d) % radix - digit(i)) * stri...  33.5 us
    pallas_call x1, Pallas kernels, far_part(): pl.pallas_call(functools.partial(max_kernel, **kw), out_shape=stat_shape,...  29.1 us
    ppermute x20, waiting for transfers between devices, butterfly(): lax.ppermute(x, axis, [(i, i + ((digit(i) + d) % radix - digit(i)) * stri...  23.9 us
    convert_element_type x1, other arithmetic, far_part(): partial.astype(jnp.bfloat16)  9.09 us
    ppermute x3, waiting for transfers between devices, column_sum(): got = lax.ppermute(sent, axis, [(i, (i + d) % n) for i in range(n)])  8.54 us
  transfers between devices with their start and end apart: 27, of which 19 were waited for; matrix products, arithmetic and copies ran while one was open for 5% of the time, Pallas kernels for 0%

profile of v15, /device:TPU:0, one launch (start us, length us, event | category | flops | bytes accessed | tf_op | source)
XLA Modules:
  0.0 299.6 jit_solution(1789059754568232670)
XLA Ops:
  9.3 1.6 gather_fusion.1
  10.9 1.6 gather_fusion
  17.3 2.1 gather_fusion.3
  19.4 45.3 %all-gather.2.cloned.1.call-done.q_ref = bf16[4096,1024]{1,0:T(8,128)(2,1)} async-done(((bf16[128,1024]{1,0:T(8,128)(2,1)}), bf16[4096,1024]{1,0:T(8,128)(2,1)}) %all-gather.2.cloned.1.call-update) | async-done | bytes 8388624 | tf_op jit(solution)/shard_map/all_gather | solution.py:142
  64.8 29.1 %shard_map.91 = f32[256,128]{1,0:T(8,128)} custom-call(s32[160]{0:T(256)} %select_n.90.lo_ref, s32[160]{0:T(256)} %select_n.92.hi_ref, s32[160]{0:T(256)} %gather_fusion.3, bf16[4096,1024]{1,0:T(8,128)(2,1)} %all-gather.2.cloned.1.call-done.q_ref, bf16[16,256,128]{2,1,0:T(8,128)(2,1)} %bitcast.42), custom_call_target="tpu_custom_call" | custom-call | tf_op jit(solution)/shard_map/pallas_call | solution.py:152
  95.6 1.8 collective-permute-start.2
  97.4 2.1 collective-permute-start.3
  99.5 1.8 collective-permute-start.4
  104.0 2.8 collective-permute-done.2
  106.8 1.7 collective-permute-done.3
  112.0 2.7 collective-permute-start.8
  116.2 2.8 collective-permute-done.7
  119.0 2.7 collective-permute-done.8
  122.9 45.5 %shard_map.92 = (f32[4096,1024]{1,0:T(8,128)}, f32[256,128]{1,0:T(8,128)}) custom-call(s32[160]{0:T(256)} %select_n.90.lo_ref, s32[160]{0:T(256)} %select_n.92.hi_ref, s32[160]{0:T(256)} %gather_fusion.3, bf16[4096,1024]{1,0:T(8,128)(2,1)} %all-gather.2.cloned.1.call-done.q_ref, bf16[16,256,128]{2,1,0:T(8,128)(2,1)} %bitcast.43, ...), custom_call_target="tpu_custom_call" | custom-call | tf_op jit(solution)/shard_map/pallas_call | solution.py:160
  168.4 9.1 %convert_element_type.42 = bf16[4096,1024]{1,0:T(8,128)(2,1)} convert(f32[4096,1024]{1,0:T(8,128)} %get-tuple-element.10) | non-fusion elementwise | flops 4194304 | bytes 25165824 | tf_op jit(solution)/shard_map/convert_element_type | solution.py:171
  179.9 2.9 collective-permute-start.10
  185.1 2.3 collective-permute-start.13
  187.4 1.7 collective-permute-start.14
  189.1 2.4 collective-permute-start.15
  193.6 1.7 collective-permute-start.17
  195.9 2.5 collective-permute-done.14
  199.9 1.6 collective-permute-done.17
  201.9 4.7 %collective-permute-start.19 = (f32[256,128]{1,0:T(8,128)S(1)}, f32[256,128]{1,0:T(8,128)S(1)}, u32[]{:S(2)}, u32[]{:S(2)}) collective-permute-start(f32[256,128]{1,0:T(8,128)S(1)} %add_add_fusion), channel_id=1, source_target_pairs={{0,8},{1,9},{2,10},{3,11},{4,12},{5,13},{6,14},{7,15},{8,16},{9,17... | collective-permute-start | bytes 393224 | tf_op jit(solution)/shard_map/ppermute | solution.py:125
  206.7 2.6 collective-permute-start.20
  210.8 4.1 %collective-permute-done.20 = f32[256,128]{1,0:T(8,128)S(1)} collective-permute-done((f32[256,128]{1,0:T(8,128)S(1)}, f32[256,128]{1,0:T(8,128)S(1)}, u32[]{:S(2)}, u32[]{:S(2)}) %collective-permute-start.20) | collective-permute-done | bytes 131104 | tf_op jit(solution)/shard_map/ppermute | solution.py:125
  215.6 55.0 %reduce-scatter.2.cloned.1.call-done = bf16[128,1024]{1,0:T(8,128)(2,1)} async-done(((bf16[4096,1024]{1,0:T(8,128)(2,1)}), bf16[128,1024]{1,0:T(8,128)(2,1)}) %reduce-scatter.2.cloned.1.call-update) | async-done | bytes 262160 | tf_op jit(solution)/shard_map/reduce_scatter | solution.py:170
  271.8 4.7 %fusion.10 = f32[128,4096]{1,0:T(8,128)S(1)} fusion(bf16[128,1024]{0,1:T(8,128)(2,1)S(1)} %bitcast.45, bf16[1024,4096]{1,0:T(8,128)(2,1)} %param.17), kind=kOutput, calls=%fused_computation.49 | convolution fusion | flops 1073741824 | bytes 10747904 | tf_op jit(solution)/shard_map/dot_general | solution.py:268
  276.6 1.6 collective-permute-start.22
  278.2 2.8 collective-permute-start.23
  282.4 3.6 %collective-permute-done.22 = bf16[128,1024]{1,0:T(8,128)(2,1)S(1)} collective-permute-done((bf16[128,1024]{1,0:T(8,128)(2,1)S(1)}, bf16[128,1024]{1,0:T(8,128)(2,1)S(1)}, u32[]{:S(2)}, u32[]{:S(2)}) %collective-permute-start.22) | collective-permute-done | bytes 262176 | tf_op jit(solution)/shard_map/ppermute | solution.py:188
  286.0 5.0 %collective-permute-done.23 = bf16[128,1024]{1,0:T(8,128)(2,1)S(1)} collective-permute-done((bf16[128,1024]{1,0:T(8,128)(2,1)S(1)}, bf16[128,1024]{1,0:T(8,128)(2,1)S(1)}, u32[]{:S(2)}, u32[]{:S(2)}) %collective-permute-start.23) | collective-permute-done | bytes 262176 | tf_op jit(solution)/shard_map/ppermute | solution.py:188
  291.0 1.8 add_convert_fusion
  (91 shorter events, 32.3 us)
Async XLA Ops:
  6.5 7.5 %copy-start = (s32[64]{0:T(128)S(1)}, s32[64]{0:T(128)}, u32[]{:S(2)}) copy-start(s32[64]{0:T(128)} %param.16) | copy-start | bytes 772
  6.5 58.2 %all-gather.2.cloned.1.call-start = ((), (), s32[]{:S(2)}) async-start(), calls=%async_computation.1 | async-start | bytes 8650752 | tf_op jit(solution)/shard_map/all_gather | solution.py:142
  7.3 263.4 %reduce-scatter.2.cloned.1.call-start = ((), (), s32[]{:S(2)}) async-start(), calls=%async_computation.2 | async-start | bytes 8650752 | tf_op jit(solution)/shard_map/reduce_scatter | solution.py:170
  14.0 3.2 %copy-start.6 = (s32[16]{0:T(128)S(1)}, s32[16]{0:T(128)}, u32[]{:S(2)}) copy-start(s32[16]{0:T(128)} %param.14) | copy-start | bytes 196
  93.9 7.4 %collective-permute-start = (f32[256,128]{1,0:T(8,128)}, f32[256,128]{1,0:T(8,128)S(1)}, u32[]{:S(2)}, u32[]{:S(2)}) collective-permute-start(f32[256,128]{1,0:T(8,128)} %shard_map.91), channel_id=1, source_target_pairs={{0,1},{1,2},{2,3},{3,4},{4,5},{5,6},{6,7},{7,0},{8,9},{9,10},{10,1... | collective-permute-start | bytes 393224 | tf_op jit(solution)/shard_map/ppermute | solution.py:125
  94.1 8.6 %collective-permute-start.1 = (f32[256,128]{1,0:T(8,128)}, f32[256,128]{1,0:T(8,128)S(1)}, u32[]{:S(2)}, u32[]{:S(2)}) collective-permute-start(f32[256,128]{1,0:T(8,128)} %shard_map.91), channel_id=1, source_target_pairs={{0,2},{1,3},{2,4},{3,5},{4,6},{5,7},{6,0},{7,1},{8,10},{9,11},{10,... | collective-permute-start | bytes 393224 | tf_op jit(solution)/shard_map/ppermute | solution.py:125
  95.6 11.2 %collective-permute-start.2 = (f32[256,128]{1,0:T(8,128)}, f32[256,128]{1,0:T(8,128)S(1)}, u32[]{:S(2)}, u32[]{:S(2)}) collective-permute-start(f32[256,128]{1,0:T(8,128)} %shard_map.91), channel_id=1, source_target_pairs={{0,3},{1,4},{2,5},{3,6},{4,7},{5,0},{6,1},{7,2},{8,11},{9,12},{10,... | collective-permute-start | bytes 393224 | tf_op jit(solution)/shard_map/ppermute | solution.py:125
  97.4 11.0 %collective-permute-start.3 = (f32[256,128]{1,0:T(8,128)}, f32[256,128]{1,0:T(8,128)S(1)}, u32[]{:S(2)}, u32[]{:S(2)}) collective-permute-start(f32[256,128]{1,0:T(8,128)} %shard_map.91), channel_id=1, source_target_pairs={{0,4},{1,5},{2,6},{3,7},{4,0},{5,1},{6,2},{7,3},{8,12},{9,13},{10,... | collective-permute-start | bytes 393224 | tf_op jit(solution)/shard_map/ppermute | solution.py:125
  99.5 9.0 %collective-permute-start.4 = (f32[256,128]{1,0:T(8,128)}, f32[256,128]{1,0:T(8,128)S(1)}, u32[]{:S(2)}, u32[]{:S(2)}) collective-permute-start(f32[256,128]{1,0:T(8,128)} %shard_map.91), channel_id=1, source_target_pairs={{0,5},{1,6},{2,7},{3,0},{4,1},{5,2},{6,3},{7,4},{8,13},{9,14},{10,... | collective-permute-start | bytes 393224 | tf_op jit(solution)/shard_map/ppermute | solution.py:125
  101.3 8.7 %collective-permute-start.5 = (f32[256,128]{1,0:T(8,128)}, f32[256,128]{1,0:T(8,128)S(1)}, u32[]{:S(2)}, u32[]{:S(2)}) collective-permute-start(f32[256,128]{1,0:T(8,128)} %shard_map.91), channel_id=1, source_target_pairs={{0,6},{1,7},{2,0},{3,1},{4,2},{5,3},{6,4},{7,5},{8,14},{9,15},{10,... | collective-permute-start | bytes 393224 | tf_op jit(solution)/shard_map/ppermute | solution.py:125
  102.7 7.7 %collective-permute-start.6 = (f32[256,128]{1,0:T(8,128)}, f32[256,128]{1,0:T(8,128)S(1)}, u32[]{:S(2)}, u32[]{:S(2)}) collective-permute-start(f32[256,128]{1,0:T(8,128)} %shard_map.91), channel_id=1, source_target_pairs={{0,7},{1,0},{2,1},{3,2},{4,3},{5,4},{6,5},{7,6},{8,15},{9,8},{10,9... | collective-permute-start | bytes 393224 | tf_op jit(solution)/shard_map/ppermute | solution.py:125
  111.4 7.6 %collective-permute-start.7 = (f32[256,128]{1,0:T(8,128)S(1)}, f32[256,128]{1,0:T(8,128)S(1)}, u32[]{:S(2)}, u32[]{:S(2)}) collective-permute-start(f32[256,128]{1,0:T(8,128)S(1)} %maximum_maximum_fusion.1), channel_id=1, source_target_pairs={{0,8},{1,9},{2,10},{3,11},{4,12},{5,13},{6,14},{7,15},{8,16},{9,17... | collective-permute-start | bytes 393224 | tf_op jit(solution)/shard_map/ppermute | solution.py:125
  112.0 9.6 %collective-permute-start.8 = (f32[256,128]{1,0:T(8,128)S(1)}, f32[256,128]{1,0:T(8,128)S(1)}, u32[]{:S(2)}, u32[]{:S(2)}) collective-permute-start(f32[256,128]{1,0:T(8,128)S(1)} %maximum_maximum_fusion.1), channel_id=1, source_target_pairs={{0,16},{1,17},{2,18},{3,19},{4,20},{5,21},{6,22},{7,23},{8,24},{9,... | collective-permute-start | bytes 393224 | tf_op jit(solution)/shard_map/ppermute | solution.py:125
  114.8 7.4 %collective-permute-start.9 = (f32[256,128]{1,0:T(8,128)S(1)}, f32[256,128]{1,0:T(8,128)S(1)}, u32[]{:S(2)}, u32[]{:S(2)}) collective-permute-start(f32[256,128]{1,0:T(8,128)S(1)} %maximum_maximum_fusion.1), channel_id=1, source_target_pairs={{0,24},{1,25},{2,26},{3,27},{4,28},{5,29},{6,30},{7,31},{8,0},{9,1... | collective-permute-start | bytes 393224 | tf_op jit(solution)/shard_map/ppermute | solution.py:125
  177.5 2.5 copy-start.5
  177.5 5.8 %copy-start.2 = (bf16[128,1024]{1,0:T(8,128)(2,1)S(1)}, bf16[128,1024]{1,0:T(8,128)(2,1)}, u32[]{:S(2)}) copy-start(bf16[128,1024]{1,0:T(8,128)(2,1)} %param.9) | copy-start | bytes 786436
  177.5 6.8 %copy-start.3 = (f32[256,128]{1,0:T(8,128)S(1)}, f32[256,128]{1,0:T(8,128)}, u32[]{:S(2)}) copy-start(f32[256,128]{1,0:T(8,128)} %get-tuple-element.13) | copy-start | bytes 393220
  178.4 5.4 %collective-permute-start.11 = (bf16[128,256]{0,1:T(8,128)(2,1)S(1)}, bf16[128,256]{0,1:T(8,128)(2,1)S(1)}, u32[]{:S(2)}, u32[]{:S(2)}) collective-permute-start(bf16[128,256]{0,1:T(8,128)(2,1)S(1)} %copy.28), channel_id=1, source_target_pairs={{0,1},{1,2},{2,3},{3,4},{4,5},{5,6},{6,7},{7,8},{8,9},{9,10},{10,1... | collective-permute-start | bytes 196616 | tf_op jit(solution)/shard_map/ppermute | solution.py:19
  179.9 3.8 %collective-permute-start.10 = (bf16[128,256]{1,0:T(8,128)(2,1)S(1)}, bf16[128,256]{1,0:T(8,128)(2,1)S(1)}, u32[]{:S(2)}, u32[]{:S(2)}) collective-permute-start(bf16[128,256]{1,0:T(8,128)(2,1)S(1)} %copy-done.5), channel_id=1, source_target_pairs={{0,1},{1,2},{2,3},{3,4},{4,5},{5,6},{6,7},{7,8},{8,9},{9,10},{10,1... | collective-permute-start | bytes 196616 | tf_op jit(solution)/shard_map/ppermute | solution.py:19
  184.2 9.3 %collective-permute-start.12 = (f32[256,128]{1,0:T(8,128)S(1)}, f32[256,128]{1,0:T(8,128)S(1)}, u32[]{:S(2)}, u32[]{:S(2)}) collective-permute-start(f32[256,128]{1,0:T(8,128)S(1)} %copy-done.3), channel_id=1, source_target_pairs={{0,1},{1,2},{2,3},{3,4},{4,5},{5,6},{6,7},{7,0},{8,9},{9,10},{10,1... | collective-permute-start | bytes 393224 | tf_op jit(solution)/shard_map/ppermute | solution.py:125
  185.1 10.1 %collective-permute-start.13 = (f32[256,128]{1,0:T(8,128)S(1)}, f32[256,128]{1,0:T(8,128)S(1)}, u32[]{:S(2)}, u32[]{:S(2)}) collective-permute-start(f32[256,128]{1,0:T(8,128)S(1)} %copy-done.3), channel_id=1, source_target_pairs={{0,2},{1,3},{2,4},{3,5},{4,6},{5,7},{6,0},{7,1},{8,10},{9,11},{10,... | collective-permute-start | bytes 393224 | tf_op jit(solution)/shard_map/ppermute | solution.py:125
  187.4 10.9 %collective-permute-start.14 = (f32[256,128]{1,0:T(8,128)S(1)}, f32[256,128]{1,0:T(8,128)S(1)}, u32[]{:S(2)}, u32[]{:S(2)}) collective-permute-start(f32[256,128]{1,0:T(8,128)S(1)} %copy-done.3), channel_id=1, source_target_pairs={{0,3},{1,4},{2,5},{3,6},{4,7},{5,0},{6,1},{7,2},{8,11},{9,12},{10,... | collective-permute-start | bytes 393224 | tf_op jit(solution)/shard_map/ppermute | solution.py:125
  189.1 10.7 %collective-permute-start.15 = (f32[256,128]{1,0:T(8,128)S(1)}, f32[256,128]{1,0:T(8,128)S(1)}, u32[]{:S(2)}, u32[]{:S(2)}) collective-permute-start(f32[256,128]{1,0:T(8,128)S(1)} %copy-done.3), channel_id=1, source_target_pairs={{0,4},{1,5},{2,6},{3,7},{4,0},{5,1},{6,2},{7,3},{8,12},{9,13},{10,... | collective-permute-start | bytes 393224 | tf_op jit(solution)/shard_map/ppermute | solution.py:125
  191.5 8.4 %collective-permute-start.16 = (f32[256,128]{1,0:T(8,128)S(1)}, f32[256,128]{1,0:T(8,128)S(1)}, u32[]{:S(2)}, u32[]{:S(2)}) collective-permute-start(f32[256,128]{1,0:T(8,128)S(1)} %copy-done.3), channel_id=1, source_target_pairs={{0,5},{1,6},{2,7},{3,0},{4,1},{5,2},{6,3},{7,4},{8,13},{9,14},{10,... | collective-permute-start | bytes 393224 | tf_op jit(solution)/shard_map/ppermute | solution.py:125
  193.6 7.9 %collective-permute-start.17 = (f32[256,128]{1,0:T(8,128)S(1)}, f32[256,128]{1,0:T(8,128)S(1)}, u32[]{:S(2)}, u32[]{:S(2)}) collective-permute-start(f32[256,128]{1,0:T(8,128)S(1)} %copy-done.3), channel_id=1, source_target_pairs={{0,6},{1,7},{2,0},{3,1},{4,2},{5,3},{6,4},{7,5},{8,14},{9,15},{10,... | collective-permute-start | bytes 393224 | tf_op jit(solution)/shard_map/ppermute | solution.py:125
  195.3 6.6 %collective-permute-start.18 = (f32[256,128]{1,0:T(8,128)S(1)}, f32[256,128]{1,0:T(8,128)S(1)}, u32[]{:S(2)}, u32[]{:S(2)}) collective-permute-start(f32[256,128]{1,0:T(8,128)S(1)} %copy-done.3), channel_id=1, source_target_pairs={{0,7},{1,0},{2,1},{3,2},{4,3},{5,4},{6,5},{7,6},{8,15},{9,8},{10,9... | collective-permute-start | bytes 393224 | tf_op jit(solution)/shard_map/ppermute | solution.py:125
  201.9 8.8 %collective-permute-start.19 = (f32[256,128]{1,0:T(8,128)S(1)}, f32[256,128]{1,0:T(8,128)S(1)}, u32[]{:S(2)}, u32[]{:S(2)}) collective-permute-start(f32[256,128]{1,0:T(8,128)S(1)} %add_add_fusion), channel_id=1, source_target_pairs={{0,8},{1,9},{2,10},{3,11},{4,12},{5,13},{6,14},{7,15},{8,16},{9,17... | collective-permute-start | bytes 393224 | tf_op jit(solution)/shard_map/ppermute | solution.py:125
  206.7 8.2 %collective-permute-start.20 = (f32[256,128]{1,0:T(8,128)S(1)}, f32[256,128]{1,0:T(8,128)S(1)}, u32[]{:S(2)}, u32[]{:S(2)}) collective-permute-start(f32[256,128]{1,0:T(8,128)S(1)} %add_add_fusion), channel_id=1, source_target_pairs={{0,16},{1,17},{2,18},{3,19},{4,20},{5,21},{6,22},{7,23},{8,24},{9,... | collective-permute-start | bytes 393224 | tf_op jit(solution)/shard_map/ppermute | solution.py:125
  209.3 6.3 %collective-permute-start.21 = (f32[256,128]{1,0:T(8,128)S(1)}, f32[256,128]{1,0:T(8,128)S(1)}, u32[]{:S(2)}, u32[]{:S(2)}) collective-permute-start(f32[256,128]{1,0:T(8,128)S(1)} %add_add_fusion), channel_id=1, source_target_pairs={{0,24},{1,25},{2,26},{3,27},{4,28},{5,29},{6,30},{7,31},{8,0},{9,1... | collective-permute-start | bytes 393224 | tf_op jit(solution)/shard_map/ppermute | solution.py:125
  276.6 9.4 %collective-permute-start.22 = (bf16[128,1024]{1,0:T(8,128)(2,1)S(1)}, bf16[128,1024]{1,0:T(8,128)(2,1)S(1)}, u32[]{:S(2)}, u32[]{:S(2)}) collective-permute-start(bf16[128,1024]{1,0:T(8,128)(2,1)S(1)} %get-tuple-element.19), channel_id=1, source_target_pairs={{0,32},{32,64},{64,96},{96,0},{1,33},{33,65},{65,97},{97,1},{2,34}... | collective-permute-start | bytes 786440 | tf_op jit(solution)/shard_map/ppermute | solution.py:188
  278.2 12.7 %collective-permute-start.23 = (bf16[128,1024]{1,0:T(8,128)(2,1)S(1)}, bf16[128,1024]{1,0:T(8,128)(2,1)S(1)}, u32[]{:S(2)}, u32[]{:S(2)}) collective-permute-start(bf16[128,1024]{1,0:T(8,128)(2,1)S(1)} %get-tuple-element.21), channel_id=1, source_target_pairs={{0,64},{32,96},{64,0},{96,32},{1,65},{33,97},{65,1},{97,33},{2,66}... | collective-permute-start | bytes 786440 | tf_op jit(solution)/shard_map/ppermute | solution.py:188
  281.1 9.9 %collective-permute-start.24 = (bf16[128,1024]{1,0:T(8,128)(2,1)S(1)}, bf16[128,1024]{1,0:T(8,128)(2,1)}, u32[]{:S(2)}, u32[]{:S(2)}) collective-permute-start(bf16[128,1024]{1,0:T(8,128)(2,1)S(1)} %get-tuple-element.20), channel_id=1, source_target_pairs={{0,96},{32,0},{64,32},{96,64},{1,97},{33,1},{65,33},{97,65},{2,98}... | collective-permute-start | bytes 786440 | tf_op jit(solution)/shard_map/ppermute | solution.py:188
  (2 other events, 2.6 us)
Sparse Core Ops, SparseCore 0:
  9.6 55.1 all-gather.1
  177.6 92.9 reduce-scatter.1

commit v16 on v14

--- a/solution.py
+++ b/solution.py
@@ -110,7 +110,9 @@
         ctx = jnp.dot(p.astype(jnp.bfloat16), values, preferred_element_type=jnp.float32)
         tot = jnp.sum(p, axis=1, keepdims=True)
         for j, h in enumerate(group):
-            o_ref[:, h * HEAD_SIZE : (h + 1) * HEAD_SIZE] = ctx[j * tile : (j + 1) * tile]
+            o_ref[:, h * HEAD_SIZE : (h + 1) * HEAD_SIZE] = ctx[j * tile : (j + 1) * tile].astype(
+                o_ref.dtype
+            )
             totals = jnp.where(lane == h, tot[j * tile : (j + 1) * tile], totals)
     t_ref[...] = jnp.transpose(totals)[: t_ref.shape[0], :]
 
@@ -159,7 +161,7 @@
     far_max = butterfly(local_max, "blk", jnp.maximum)
     partial, totals = pl.pallas_call(
         functools.partial(ctx_kernel, **kw),
-        out_shape=(jax.ShapeDtypeStruct((row_count, q_cols), jnp.float32), stat_shape),
+        out_shape=(jax.ShapeDtypeStruct((row_count, q_cols), jnp.bfloat16), stat_shape),
         grid_spec=pltpu.PrefetchScalarGridSpec(
             num_scalar_prefetch=3,
             grid=(n_tiles,),
@@ -168,7 +170,7 @@
         ),
     )(lo, hi, blk, gathered, keys_t, values, far_max)
     context = lax.psum_scatter(
-        partial.astype(jnp.bfloat16), "blk", scatter_dimension=0, tiled=True
+        partial, "blk", scatter_dimension=0, tiled=True
     ).astype(jnp.float32)
     totals = butterfly(totals, "blk", jnp.add)
     own = lambda a: jnp.transpose(

time: 296 us -> 287 us (0.970)
  other arithmetic: 14.6 us -> 5.52 us
    convert_element_type x1 -> x0, other arithmetic: 9.1 us -> none  [far_part(): partial.astype(jnp.bfloat16)]
where the time goes in v16:
time: 287 us; the launch traced here: 286 us
  waiting for transfers between devices  138 us (48%)
  Pallas kernels  74.7 us (26%)
  starting transfers between devices  35.3 us (12%)
  between operations  13.7 us (5%)
  local copies, waits for them, and re-layouts  13 us (5%)
  other arithmetic  5.52 us (2%)
  matrix products  5.36 us (2%)
    reduce_scatter x1, waiting for transfers between devices, far_part(): lax.psum_scatter(partial, 'blk', scatter_dimension=0, tiled=True)  62.3 us
    pallas_call x1, Pallas kernels, far_part(): pl.pallas_call(functools.partial(ctx_kernel, **kw), out_shape=(jax.ShapeD...  45.5 us
    all_gather x1, waiting for transfers between devices, far_part(): gathered = lax.all_gather(queries, 'blk', axis=0, tiled=True)  45.3 us
    pallas_call x1, Pallas kernels, far_part(): pl.pallas_call(functools.partial(max_kernel, **kw), out_shape=stat_shape,...  29.1 us
    ppermute x14, starting transfers between devices, butterfly(): lax.ppermute(x, axis, [(i, i + ((digit(i) + d) % radix - digit(i)) * stri...  24.1 us
    ppermute x14, waiting for transfers between devices, butterfly(): lax.ppermute(x, axis, [(i, i + ((digit(i) + d) % radix - digit(i)) * stri...  20.9 us
    ppermute x3, waiting for transfers between devices, column_sum(): got = lax.ppermute(sent, axis, [(i, (i + d) % n) for i in range(n)])  8.51 us
    ppermute x3, starting transfers between devices, column_sum(): got = lax.ppermute(sent, axis, [(i, (i + d) % n) for i in range(n)])  5.8 us
  transfers between devices with their start and end apart: 21, of which 16 were waited for; matrix products, arithmetic and copies ran while one was open for 5% of the time, Pallas kernels for 0%

profile of v16, /device:TPU:0, one launch (start us, length us, event | category | flops | bytes accessed | tf_op | source)
XLA Modules:
  0.0 285.6 jit_solution(17174774076441385568)
XLA Ops:
  9.3 1.6 gather_fusion.1
  10.9 1.6 gather_fusion
  14.1 1.5 gather_fusion.2
  17.3 2.1 gather_fusion.3
  19.4 45.3 %all-gather.2.cloned.1.call-done.q_ref = bf16[4096,1024]{1,0:T(8,128)(2,1)} async-done(((bf16[128,1024]{1,0:T(8,128)(2,1)}), bf16[4096,1024]{1,0:T(8,128)(2,1)}) %all-gather.2.cloned.1.call-update) | async-done | bytes 8388624 | tf_op jit(solution)/shard_map/all_gather | solution.py:144
  64.8 29.1 %shard_map.91 = f32[256,128]{1,0:T(8,128)} custom-call(s32[160]{0:T(256)} %select_n.90.lo_ref, s32[160]{0:T(256)} %select_n.92.hi_ref, s32[160]{0:T(256)} %gather_fusion.3, bf16[4096,1024]{1,0:T(8,128)(2,1)} %all-gather.2.cloned.1.call-done.q_ref, bf16[16,256,128]{2,1,0:T(8,128)(2,1)} %bitcast.42), custom_call_target="tpu_custom_call" | custom-call | tf_op jit(solution)/shard_map/pallas_call | solution.py:154
  96.4 1.5 collective-permute-start.1
  97.9 2.7 collective-permute-start.2
  100.6 1.5 collective-permute-start.3
  103.3 3.7 %collective-permute-done.2 = f32[256,128]{1,0:T(8,128)S(1)} collective-permute-done((f32[256,128]{1,0:T(8,128)S(1)}, f32[256,128]{1,0:T(8,128)S(1)}, u32[]{:S(2)}, u32[]{:S(2)}) %collective-permute-start.2) | collective-permute-done | bytes 131104 | tf_op jit(solution)/shard_map/ppermute | solution.py:127
  108.1 2.7 collective-permute-start.5
  110.8 1.4 collective-permute-start.6
  112.2 2.5 collective-permute-done.4
  114.7 1.4 collective-permute-done.5
  117.2 45.5 %shard_map.92 = (bf16[4096,1024]{1,0:T(8,128)(2,1)}, f32[256,128]{1,0:T(8,128)}) custom-call(s32[160]{0:T(256)} %select_n.90.lo_ref, s32[160]{0:T(256)} %select_n.92.hi_ref, s32[160]{0:T(256)} %gather_fusion.3, bf16[4096,1024]{1,0:T(8,128)(2,1)} %all-gather.2.cloned.1.call-done.q_ref, bf16[16,256,128]{2,1,0:T(8,128)(2,1)} %bitcast.43, ...), custom_call_target="tpu_custom_call" | custom-call | tf_op jit(solution)/shard_map/pallas_call | solution.py:162
  164.2 4.0 %collective-permute-start.7 = (bf16[128,256]{1,0:T(8,128)(2,1)S(1)}, bf16[128,256]{1,0:T(8,128)(2,1)S(1)}, u32[]{:S(2)}, u32[]{:S(2)}) collective-permute-start(bf16[128,256]{1,0:T(8,128)(2,1)S(1)} %copy-done.5), channel_id=1, source_target_pairs={{0,1},{1,2},{2,3},{3,4},{4,5},{5,6},{6,7},{7,8},{8,9},{9,10},{10,1... | collective-permute-start | bytes 196616 | tf_op jit(solution)/shard_map/ppermute | solution.py:19
  171.2 2.8 collective-permute-start.10
  174.0 3.1 %collective-permute-start.11 = (f32[256,128]{1,0:T(8,128)S(1)}, f32[256,128]{1,0:T(8,128)S(1)}, u32[]{:S(2)}, u32[]{:S(2)}) collective-permute-start(f32[256,128]{1,0:T(8,128)S(1)} %add.182), channel_id=1, source_target_pairs={{0,4},{1,5},{2,6},{3,7},{4,0},{5,1},{6,2},{7,3},{8,12},{9,13},{10,... | collective-permute-start | bytes 393224 | tf_op jit(solution)/shard_map/ppermute | solution.py:127
  177.9 1.6 collective-permute-done.10
  179.5 4.0 %collective-permute-done.11 = f32[256,128]{1,0:T(8,128)S(1)} collective-permute-done((f32[256,128]{1,0:T(8,128)S(1)}, f32[256,128]{1,0:T(8,128)S(1)}, u32[]{:S(2)}, u32[]{:S(2)}) %collective-permute-start.11) | collective-permute-done | bytes 131104 | tf_op jit(solution)/shard_map/ppermute | solution.py:127
  183.5 3.0 %collective-permute-start.13 = (f32[256,128]{1,0:T(8,128)S(1)}, f32[256,128]{1,0:T(8,128)S(1)}, u32[]{:S(2)}, u32[]{:S(2)}) collective-permute-start(f32[256,128]{1,0:T(8,128)S(1)} %add_add_fusion), channel_id=1, source_target_pairs={{0,8},{1,9},{2,10},{3,11},{4,12},{5,13},{6,14},{7,15},{8,16},{9,17... | collective-permute-start | bytes 393224 | tf_op jit(solution)/shard_map/ppermute | solution.py:127
  186.4 2.7 collective-permute-start.14
  189.8 1.7 collective-permute-done.13
  191.6 2.7 collective-permute-done.14
  194.4 62.3 %reduce-scatter.2.cloned.1.call-done = bf16[128,1024]{1,0:T(8,128)(2,1)} async-done(((bf16[4096,1024]{1,0:T(8,128)(2,1)}), bf16[128,1024]{1,0:T(8,128)(2,1)}) %reduce-scatter.2.cloned.1.call-update) | async-done | bytes 262160 | tf_op jit(solution)/shard_map/reduce_scatter | solution.py:172
  257.9 4.7 %fusion.10 = f32[128,4096]{1,0:T(8,128)S(1)} fusion(bf16[128,1024]{0,1:T(8,128)(2,1)S(1)} %bitcast.45, bf16[1024,4096]{1,0:T(8,128)(2,1)} %param.17), kind=kOutput, calls=%fused_computation.49 | convolution fusion | flops 1073741824 | bytes 10747904 | tf_op jit(solution)/shard_map/dot_general | solution.py:270
  262.7 1.6 collective-permute-start.16
  264.3 2.8 collective-permute-start.17
  267.1 1.4 collective-permute-start.18
  268.5 3.7 %collective-permute-done.16 = bf16[128,1024]{1,0:T(8,128)(2,1)S(1)} collective-permute-done((bf16[128,1024]{1,0:T(8,128)(2,1)S(1)}, bf16[128,1024]{1,0:T(8,128)(2,1)S(1)}, u32[]{:S(2)}, u32[]{:S(2)}) %collective-permute-start.16) | collective-permute-done | bytes 262176 | tf_op jit(solution)/shard_map/ppermute | solution.py:190
  272.2 4.8 %collective-permute-done.17 = bf16[128,1024]{1,0:T(8,128)(2,1)S(1)} collective-permute-done((bf16[128,1024]{1,0:T(8,128)(2,1)S(1)}, bf16[128,1024]{1,0:T(8,128)(2,1)S(1)}, u32[]{:S(2)}, u32[]{:S(2)}) %collective-permute-start.17) | collective-permute-done | bytes 262176 | tf_op jit(solution)/shard_map/ppermute | solution.py:190
  277.0 1.8 add_convert_fusion
  (80 shorter events, 19.0 us)
Async XLA Ops:
  6.5 7.6 %copy-start = (s32[64]{0:T(128)S(1)}, s32[64]{0:T(128)}, u32[]{:S(2)}) copy-start(s32[64]{0:T(128)} %param.16) | copy-start | bytes 772
  6.5 58.2 %all-gather.2.cloned.1.call-start = ((), (), s32[]{:S(2)}) async-start(), calls=%async_computation.1 | async-start | bytes 8650752 | tf_op jit(solution)/shard_map/all_gather | solution.py:144
  7.3 249.4 %reduce-scatter.2.cloned.1.call-start = ((), (), s32[]{:S(2)}) async-start(), calls=%async_computation.2 | async-start | bytes 8650752 | tf_op jit(solution)/shard_map/reduce_scatter | solution.py:172
  14.1 1.8 copy-start.1
  14.1 3.1 %copy-start.6 = (s32[16]{0:T(128)S(1)}, s32[16]{0:T(128)}, u32[]{:S(2)}) copy-start(s32[16]{0:T(128)} %param.14) | copy-start | bytes 196
  93.9 1.6 collective-permute-start
  96.4 6.9 %collective-permute-start.1 = (f32[256,128]{1,0:T(8,128)S(1)}, f32[256,128]{1,0:T(8,128)S(1)}, u32[]{:S(2)}, u32[]{:S(2)}) collective-permute-start(f32[256,128]{1,0:T(8,128)S(1)} %max.28), channel_id=1, source_target_pairs={{0,2},{1,3},{2,4},{3,5},{4,6},{5,7},{6,0},{7,1},{8,10},{9,11},{10,... | collective-permute-start | bytes 393224 | tf_op jit(solution)/shard_map/ppermute | solution.py:127
  97.9 9.1 %collective-permute-start.2 = (f32[256,128]{1,0:T(8,128)S(1)}, f32[256,128]{1,0:T(8,128)S(1)}, u32[]{:S(2)}, u32[]{:S(2)}) collective-permute-start(f32[256,128]{1,0:T(8,128)S(1)} %max.28), channel_id=1, source_target_pairs={{0,4},{1,5},{2,6},{3,7},{4,0},{5,1},{6,2},{7,3},{8,12},{9,13},{10,... | collective-permute-start | bytes 393224 | tf_op jit(solution)/shard_map/ppermute | solution.py:127
  100.6 6.4 %collective-permute-start.3 = (f32[256,128]{1,0:T(8,128)S(1)}, f32[256,128]{1,0:T(8,128)S(1)}, u32[]{:S(2)}, u32[]{:S(2)}) collective-permute-start(f32[256,128]{1,0:T(8,128)S(1)} %max.28), channel_id=1, source_target_pairs={{0,6},{1,7},{2,0},{3,1},{4,2},{5,3},{6,4},{7,5},{8,14},{9,15},{10,... | collective-permute-start | bytes 393224 | tf_op jit(solution)/shard_map/ppermute | solution.py:127
  107.1 7.6 %collective-permute-start.4 = (f32[256,128]{1,0:T(8,128)S(1)}, f32[256,128]{1,0:T(8,128)S(1)}, u32[]{:S(2)}, u32[]{:S(2)}) collective-permute-start(f32[256,128]{1,0:T(8,128)S(1)} %maximum_maximum_fusion.1), channel_id=1, source_target_pairs={{0,8},{1,9},{2,10},{3,11},{4,12},{5,13},{6,14},{7,15},{8,16},{9,17... | collective-permute-start | bytes 393224 | tf_op jit(solution)/shard_map/ppermute | solution.py:127
  108.1 8.0 %collective-permute-start.5 = (f32[256,128]{1,0:T(8,128)S(1)}, f32[256,128]{1,0:T(8,128)S(1)}, u32[]{:S(2)}, u32[]{:S(2)}) collective-permute-start(f32[256,128]{1,0:T(8,128)S(1)} %maximum_maximum_fusion.1), channel_id=1, source_target_pairs={{0,16},{1,17},{2,18},{3,19},{4,20},{5,21},{6,22},{7,23},{8,24},{9,... | collective-permute-start | bytes 393224 | tf_op jit(solution)/shard_map/ppermute | solution.py:127
  110.8 5.7 %collective-permute-start.6 = (f32[256,128]{1,0:T(8,128)S(1)}, f32[256,128]{1,0:T(8,128)S(1)}, u32[]{:S(2)}, u32[]{:S(2)}) collective-permute-start(f32[256,128]{1,0:T(8,128)S(1)} %maximum_maximum_fusion.1), channel_id=1, source_target_pairs={{0,24},{1,25},{2,26},{3,27},{4,28},{5,29},{6,30},{7,31},{8,0},{9,1... | collective-permute-start | bytes 393224 | tf_op jit(solution)/shard_map/ppermute | solution.py:127
  117.2 45.6 %copy-start.4 = (bf16[128,256]{1,0:T(8,128)(2,1)S(1)}, bf16[128,256]{1,0:T(8,128)(2,1)}, u32[]{:S(2)}) copy-start(bf16[128,256]{1,0:T(8,128)(2,1)} %param.10) | copy-start | bytes 196612
  117.2 47.0 %copy-start.5 = (bf16[128,256]{1,0:T(8,128)(2,1)S(1)}, bf16[128,256]{1,0:T(8,128)(2,1)}, u32[]{:S(2)}) copy-start(bf16[128,256]{1,0:T(8,128)(2,1)} %param.11) | copy-start | bytes 196612
  117.2 51.5 %copy-start.2 = (bf16[128,1024]{1,0:T(8,128)(2,1)S(1)}, bf16[128,1024]{1,0:T(8,128)(2,1)}, u32[]{:S(2)}) copy-start(bf16[128,1024]{1,0:T(8,128)(2,1)} %param.9) | copy-start | bytes 786436
  162.8 6.9 %copy-start.3 = (f32[256,128]{1,0:T(8,128)S(1)}, f32[256,128]{1,0:T(8,128)}, u32[]{:S(2)}) copy-start(f32[256,128]{1,0:T(8,128)} %get-tuple-element.13) | copy-start | bytes 393220
  162.9 6.4 %collective-permute-start.8 = (bf16[128,256]{0,1:T(8,128)(2,1)S(1)}, bf16[128,256]{0,1:T(8,128)(2,1)S(1)}, u32[]{:S(2)}, u32[]{:S(2)}) collective-permute-start(bf16[128,256]{0,1:T(8,128)(2,1)S(1)} %copy.28), channel_id=1, source_target_pairs={{0,1},{1,2},{2,3},{3,4},{4,5},{5,6},{6,7},{7,8},{8,9},{9,10},{10,1... | collective-permute-start | bytes 196616 | tf_op jit(solution)/shard_map/ppermute | solution.py:19
  164.2 4.9 %collective-permute-start.7 = (bf16[128,256]{1,0:T(8,128)(2,1)S(1)}, bf16[128,256]{1,0:T(8,128)(2,1)S(1)}, u32[]{:S(2)}, u32[]{:S(2)}) collective-permute-start(bf16[128,256]{1,0:T(8,128)(2,1)S(1)} %copy-done.5), channel_id=1, source_target_pairs={{0,1},{1,2},{2,3},{3,4},{4,5},{5,6},{6,7},{7,8},{8,9},{9,10},{10,1... | collective-permute-start | bytes 196616 | tf_op jit(solution)/shard_map/ppermute | solution.py:19
  169.7 1.5 collective-permute-start.9
  171.2 8.3 %collective-permute-start.10 = (f32[256,128]{1,0:T(8,128)S(1)}, f32[256,128]{1,0:T(8,128)S(1)}, u32[]{:S(2)}, u32[]{:S(2)}) collective-permute-start(f32[256,128]{1,0:T(8,128)S(1)} %add.182), channel_id=1, source_target_pairs={{0,2},{1,3},{2,4},{3,5},{4,6},{5,7},{6,0},{7,1},{8,10},{9,11},{10,... | collective-permute-start | bytes 393224 | tf_op jit(solution)/shard_map/ppermute | solution.py:127
  174.0 9.5 %collective-permute-start.11 = (f32[256,128]{1,0:T(8,128)S(1)}, f32[256,128]{1,0:T(8,128)S(1)}, u32[]{:S(2)}, u32[]{:S(2)}) collective-permute-start(f32[256,128]{1,0:T(8,128)S(1)} %add.182), channel_id=1, source_target_pairs={{0,4},{1,5},{2,6},{3,7},{4,0},{5,1},{6,2},{7,3},{8,12},{9,13},{10,... | collective-permute-start | bytes 393224 | tf_op jit(solution)/shard_map/ppermute | solution.py:127
  177.1 6.4 %collective-permute-start.12 = (f32[256,128]{1,0:T(8,128)S(1)}, f32[256,128]{1,0:T(8,128)S(1)}, u32[]{:S(2)}, u32[]{:S(2)}) collective-permute-start(f32[256,128]{1,0:T(8,128)S(1)} %add.182), channel_id=1, source_target_pairs={{0,6},{1,7},{2,0},{3,1},{4,2},{5,3},{6,4},{7,5},{8,14},{9,15},{10,... | collective-permute-start | bytes 393224 | tf_op jit(solution)/shard_map/ppermute | solution.py:127
  183.5 8.1 %collective-permute-start.13 = (f32[256,128]{1,0:T(8,128)S(1)}, f32[256,128]{1,0:T(8,128)S(1)}, u32[]{:S(2)}, u32[]{:S(2)}) collective-permute-start(f32[256,128]{1,0:T(8,128)S(1)} %add_add_fusion), channel_id=1, source_target_pairs={{0,8},{1,9},{2,10},{3,11},{4,12},{5,13},{6,14},{7,15},{8,16},{9,17... | collective-permute-start | bytes 393224 | tf_op jit(solution)/shard_map/ppermute | solution.py:127
  186.4 7.9 %collective-permute-start.14 = (f32[256,128]{1,0:T(8,128)S(1)}, f32[256,128]{1,0:T(8,128)S(1)}, u32[]{:S(2)}, u32[]{:S(2)}) collective-permute-start(f32[256,128]{1,0:T(8,128)S(1)} %add_add_fusion), channel_id=1, source_target_pairs={{0,16},{1,17},{2,18},{3,19},{4,20},{5,21},{6,22},{7,23},{8,24},{9,... | collective-permute-start | bytes 393224 | tf_op jit(solution)/shard_map/ppermute | solution.py:127
  189.1 5.2 %collective-permute-start.15 = (f32[256,128]{1,0:T(8,128)S(1)}, f32[256,128]{1,0:T(8,128)S(1)}, u32[]{:S(2)}, u32[]{:S(2)}) collective-permute-start(f32[256,128]{1,0:T(8,128)S(1)} %add_add_fusion), channel_id=1, source_target_pairs={{0,24},{1,25},{2,26},{3,27},{4,28},{5,29},{6,30},{7,31},{8,0},{9,1... | collective-permute-start | bytes 393224 | tf_op jit(solution)/shard_map/ppermute | solution.py:127
  262.7 9.5 %collective-permute-start.16 = (bf16[128,1024]{1,0:T(8,128)(2,1)S(1)}, bf16[128,1024]{1,0:T(8,128)(2,1)S(1)}, u32[]{:S(2)}, u32[]{:S(2)}) collective-permute-start(bf16[128,1024]{1,0:T(8,128)(2,1)S(1)} %get-tuple-element.19), channel_id=1, source_target_pairs={{0,32},{32,64},{64,96},{96,0},{1,33},{33,65},{65,97},{97,1},{2,34}... | collective-permute-start | bytes 786440 | tf_op jit(solution)/shard_map/ppermute | solution.py:190
  264.3 12.7 %collective-permute-start.17 = (bf16[128,1024]{1,0:T(8,128)(2,1)S(1)}, bf16[128,1024]{1,0:T(8,128)(2,1)S(1)}, u32[]{:S(2)}, u32[]{:S(2)}) collective-permute-start(bf16[128,1024]{1,0:T(8,128)(2,1)S(1)} %get-tuple-element.21), channel_id=1, source_target_pairs={{0,64},{32,96},{64,0},{96,32},{1,65},{33,97},{65,1},{97,33},{2,66}... | collective-permute-start | bytes 786440 | tf_op jit(solution)/shard_map/ppermute | solution.py:190
  267.1 9.9 %collective-permute-start.18 = (bf16[128,1024]{1,0:T(8,128)(2,1)S(1)}, bf16[128,1024]{1,0:T(8,128)(2,1)}, u32[]{:S(2)}, u32[]{:S(2)}) collective-permute-start(bf16[128,1024]{1,0:T(8,128)(2,1)S(1)} %get-tuple-element.20), channel_id=1, source_target_pairs={{0,96},{32,0},{64,32},{96,64},{1,97},{33,1},{65,33},{97,65},{2,98}... | collective-permute-start | bytes 786440 | tf_op jit(solution)/shard_map/ppermute | solution.py:190
Sparse Core Ops, SparseCore 0:
  9.6 55.1 all-gather.1
  162.9 93.7 reduce-scatter.1
